TPU v7x, 768 devices: a whole 4x8x12 slice. The times are simulated.
768 devices in a mesh: bx: 12 (over x, z_hi), by: 64 (over z_lo, y, core).
Axes of the slice: x: 4, y: 8, z: 12 (z_hi: 3, z_lo: 4; z = z_hi * 4 + z_lo), core: 2. Of those that a mesh axis runs over, the one named last changes fastest.
Arguments:
- cotangent: float32 [36, 384, 384], P('bx', 'by'), may hold values from -45 to 45
- pointwise: bfloat16 [7, 4, 4, 4, 12, 128, 128], P(None, None, None, None, 'bx', 'by'), may hold values from -1.25 to 8, as said below
Outputs:
- adjoint: float32 [36, 384, 384], P('bx', 'by')
- residual: float32 [36, 384, 384], P('bx', 'by')
Inputs may be any that keep to these rules, and one draw needn't show every extreme that they name: `pointwise`: entry 0 of every point is positive; entries 1 to 6 form a symmetric positive definite tensor whose off-diagonal entries are at most 0.31 times the geometric mean of the two matching diagonal entries.
All inputs are finite; a program needn't handle non-finite values.
Results may differ from a plain program's by a relative error of at most 0.0003.
Values sent between devices are 32-bit elements; how exact they have to be, the bound alone decides.
No kernel may reach another device: no remote copies, remote signals or barrier semaphores. Data moves between devices by JAX's collectives and lax.ppermute only.
A program may use at most 32 MiB of HBM per device.

v0:
```python
import math

import jax
import jax.numpy as jnp
import numpy as np
from jax import lax
from jax.sharding import Mesh
from jax.sharding import PartitionSpec as P

ITERS = 2
BX = ("bx_0", "bx_1")
BY = ("by_0", "by_1", "by_2")
BX_BY = ("bx_0", "bx_1", "by_0", "by_1", "by_2")


EINSUM_FORMS = ("pa,abcxyz->pbcxyz", "pb,abcxyz->apcxyz", "pc,abcxyz->abpxyz")


def shifted(value, axis, steps):
    count = lax.axis_size(axis)
    initial, last = (max(0, -steps), min(count, count - steps))
    return lax.ppermute(value, axis, [(source, source + steps) for source in range(initial, last)])


def over_axes(value, axes):
    for axis in axes:
        value = lax.psum(value, axis)
    return value


def gauss_tables():
    inner_point = math.sqrt(3.0 / 7.0 - 2.0 / 7.0 * math.sqrt(6.0 / 5.0))
    outer_point = math.sqrt(3.0 / 7.0 + 2.0 / 7.0 * math.sqrt(6.0 / 5.0))
    points = [-outer_point, -inner_point, inner_point, outer_point]
    lobatto = [-1.0, -1.0 / math.sqrt(5.0), 1.0 / math.sqrt(5.0), 1.0]
    values = np.zeros((4, 4))
    slopes = np.zeros((4, 4))
    for a in range(4):
        others = [lobatto[k] for k in range(4) if k != a]
        scaling = (lobatto[a] - others[0]) * (lobatto[a] - others[1]) * (lobatto[a] - others[2])
        for q in range(4):
            sample = points[q]
            values[q, a] = (
                (sample - others[0]) * (sample - others[1]) * (sample - others[2]) / scaling
            )
            slopes[q, a] = (
                (sample - others[1]) * (sample - others[2])
                + (sample - others[0]) * (sample - others[2])
                + (sample - others[0]) * (sample - others[1])
            ) / scaling
    return (values, slopes)


def apply_table(weights_1d, operand, stack_pos):
    return jnp.einsum(EINSUM_FORMS[stack_pos], weights_1d, operand, precision=lax.Precision.HIGHEST)


def split_axis(dof_field, axis_pos, stack_pos):
    elem_count = (dof_field.shape[axis_pos] - 1) // 3
    widths = [(0, 0)] * dof_field.ndim
    widths[axis_pos] = (0, 2)
    padded = jnp.pad(dof_field, widths)
    shaped = padded.reshape(
        dof_field.shape[:axis_pos] + (elem_count + 1, 3) + dof_field.shape[axis_pos + 1 :]
    )
    lower_rows = lax.slice_in_dim(shaped, 0, elem_count, axis=axis_pos)
    upper_rows = lax.slice_in_dim(shaped, 1, elem_count + 1, axis=axis_pos)
    pieces = [lax.index_in_dim(lower_rows, k, axis_pos + 1, keepdims=False) for k in range(3)]
    pieces.append(lax.index_in_dim(upper_rows, 0, axis_pos + 1, keepdims=False))
    return jnp.stack(pieces, stack_pos)


def merge_axis(parts, axis_pos, stack_pos):
    pieces = [lax.index_in_dim(parts, k, stack_pos, keepdims=False) for k in range(4)]
    target = axis_pos - 1
    extent = pieces[0].shape
    elem_count = extent[target]
    ending = [(0, 0)] * len(extent)
    ending[target] = (0, 1)
    leading = [(0, 0)] * len(extent)
    leading[target] = (1, 0)
    head_piece = jnp.pad(pieces[0], ending) + jnp.pad(pieces[3], leading)
    stacked = jnp.stack(
        [head_piece, jnp.pad(pieces[1], ending), jnp.pad(pieces[2], ending)], target + 1
    )
    merged = stacked.reshape(extent[:target] + (3 * (elem_count + 1),) + extent[target + 1 :])
    return lax.slice_in_dim(merged, 0, 3 * elem_count + 1, axis=target)


def element_action(elements, pointwise):
    table_pair = gauss_tables()
    values = jnp.asarray(table_pair[0], jnp.float32)
    slopes = jnp.asarray(table_pair[1], jnp.float32)
    coeffs = pointwise.astype(jnp.float32)
    x_value = apply_table(values, elements, 0)
    x_slope = apply_table(slopes, elements, 0)
    value_value = apply_table(values, x_value, 1)
    value_slope = apply_table(slopes, x_value, 1)
    slope_value = apply_table(values, x_slope, 1)
    point_value = apply_table(values, value_value, 2)
    grad_z = apply_table(slopes, value_value, 2)
    grad_y = apply_table(values, value_slope, 2)
    grad_x = apply_table(values, slope_value, 2)
    flux_x = coeffs[1] * grad_x + coeffs[4] * grad_y + coeffs[5] * grad_z
    flux_y = coeffs[4] * grad_x + coeffs[2] * grad_y + coeffs[6] * grad_z
    flux_z = coeffs[5] * grad_x + coeffs[6] * grad_y + coeffs[3] * grad_z
    mass_term = coeffs[0] * point_value
    back_plain = apply_table(values.T, mass_term, 2) + apply_table(slopes.T, flux_z, 2)
    back_fluxx = apply_table(values.T, flux_x, 2)
    back_fluxy = apply_table(values.T, flux_y, 2)
    near_sum = apply_table(values.T, back_plain, 1) + apply_table(slopes.T, back_fluxy, 1)
    far_sum = apply_table(values.T, back_fluxx, 1)
    return apply_table(values.T, near_sum, 0) + apply_table(slopes.T, far_sum, 0)


def diagonal_action(pointwise):
    table_pair = gauss_tables()
    values = jnp.asarray(table_pair[0], jnp.float32)
    slopes = jnp.asarray(table_pair[1], jnp.float32)
    coeffs = pointwise.astype(jnp.float32)
    square_v = values * values
    square_s = slopes * slopes
    mixed_vs = values * slopes

    def triple(table_x, table_y, table_z, term):
        return apply_table(table_x.T, apply_table(table_y.T, apply_table(table_z.T, term, 2), 1), 0)

    running_total = triple(square_v, square_v, square_v, coeffs[0])
    running_total = running_total + triple(square_s, square_v, square_v, coeffs[1])
    running_total = running_total + triple(square_v, square_s, square_v, coeffs[2])
    running_total = running_total + triple(square_v, square_v, square_s, coeffs[3])
    running_total = running_total + 2.0 * triple(mixed_vs, mixed_vs, square_v, coeffs[4])
    running_total = running_total + 2.0 * triple(mixed_vs, square_v, mixed_vs, coeffs[5])
    running_total = running_total + 2.0 * triple(square_v, mixed_vs, mixed_vs, coeffs[6])
    return running_total


def to_dofs(parts):
    return merge_axis(merge_axis(merge_axis(parts, 5, 2), 3, 1), 1, 0)


def element_block(dof_block, pointwise):
    elements = split_axis(split_axis(split_axis(dof_block, 0, 0), 2, 1), 4, 2)
    return to_dofs(element_action(elements, pointwise))


def upper_x(plane):
    return shifted(plane, BX, -1)


def upper_y(plane):
    return shifted(plane, BY, -1)


def lower_x(plane):
    return shifted(plane, BX, 1)


def lower_y(plane):
    return shifted(plane, BY, 1)


def global_sums(terms):
    return (over_axes(terms[0], BX_BY), over_axes(terms[1], BX_BY))


def widen(dof_field):
    widened = jnp.concatenate([dof_field, upper_x(dof_field[0:1])], 0)
    widened = jnp.concatenate([widened, upper_y(widened[:, 0:1])], 1)
    return widened


def pad_top(dof_field):
    return jnp.pad(dof_field, ((0, 0), (0, 0), (0, 1)))


def collect(contributions, rows_x, rows_y, rows_z):
    summed = contributions[:, :, :rows_z]
    arrived = lower_y(summed[:, rows_y:])
    summed = jnp.concatenate([summed[:, 0:1] + arrived, summed[:, 1:rows_y]], 1)
    arrived = lower_x(summed[rows_x:])
    summed = jnp.concatenate([summed[0:1] + arrived, summed[1:rows_x]], 0)
    return summed


def shards(cotangent, pointwise):
    rows_x, rows_y, rows_z = cotangent.shape
    total_x = rows_x * lax.axis_size(BX)
    total_y = rows_y * lax.axis_size(BY)
    extent = cotangent.shape
    place_x = lax.broadcasted_iota(jnp.int32, extent, 0) + lax.axis_index(BX) * rows_x
    place_y = lax.broadcasted_iota(jnp.int32, extent, 1) + lax.axis_index(BY) * rows_y
    place_z = lax.broadcasted_iota(jnp.int32, extent, 2)
    inside = (
        (place_x > 0) & (place_y > 0) & (place_z > 0) & (place_x < total_x) & (place_y < total_y)
    )
    interior = jnp.where(inside, 1.0, 0.0).astype(jnp.float32)
    diagonal = collect(to_dofs(diagonal_action(pointwise)), rows_x, rows_y, rows_z)

    def operator(dof_field):
        return (
            collect(element_block(pad_top(widen(dof_field)), pointwise), rows_x, rows_y, rows_z)
            * interior
        )

    def local_dot(left, right):
        return jnp.sum(left * right)

    adjoint = jnp.zeros(cotangent.shape, jnp.float32)
    residual = cotangent * interior
    precond = residual / diagonal
    image = operator(precond)
    rz_now, curvature = global_sums((local_dot(residual, precond), local_dot(precond, image)))
    alpha = rz_now / curvature
    direction = precond
    direction_image = image
    for sweep in range(ITERS):
        adjoint = adjoint + alpha * direction
        residual = residual - alpha * direction_image
        if sweep + 1 < ITERS:
            precond = residual / diagonal
            image = operator(precond)
            fresh, curvature = global_sums(
                (local_dot(residual, precond), local_dot(precond, image))
            )
            ratio = fresh / rz_now
            alpha = fresh / (curvature - ratio * fresh / alpha)
            direction = precond + ratio * direction
            direction_image = image + ratio * direction_image
            rz_now = fresh
    return (adjoint, residual)


def solution(mesh):
    split = Mesh(mesh.devices.reshape(4, 3, 4, 8, 2), ("bx_0", "bx_1", "by_0", "by_1", "by_2"))
    in_specs = (P(BX, BY, None), P(None, None, None, None, BX, BY, None))
    out_specs = (P(BX, BY, None), P(BX, BY, None))
    return jax.shard_map(
        shards, mesh=split, in_specs=in_specs, out_specs=out_specs, check_vma=False
    )
```

profile of v0, /device:TPU:1, one launch (start us, length us, event | category | flops | bytes accessed | tf_op | source)
XLA Modules:
  0.0 253.0 jit_solution(3841538437232366506)
XLA Ops:
  0.7 1.1 copy_convert_fusion
  1.8 0.9 convolution_bitcast_fusion.21
  2.6 0.9 convolution_bitcast_fusion.23
  4.4 0.9 convolution_bitcast_fusion.29
  5.3 0.9 convolution_bitcast_fusion.31
  7.1 0.9 convolution_bitcast_fusion.20
  8.0 0.9 convolution_bitcast_fusion.22
  9.0 0.9 convolution_bitcast_fusion.24
  9.9 0.9 convolution_bitcast_fusion.27
  10.8 0.9 convolution_bitcast_fusion.26
  15.4 1.1 reshape.306
  16.9 4.6 %collective-permute-start = (f32[4,1,384]{2,1,0:T(1,128)S(1)}, f32[4,1,384]{2,1,0:T(1,128)S(1)}, u32[]{:S(2)}, u32[]{:S(2)}) collective-permute-start(f32[4,1,384]{2,1,0:T(1,128)S(1)} %slice.523), channel_id=1, source_target_pairs={{0,1},{1,2},{2,3},{3,4},{4,5},{5,6},{6,7},{7,8},{8,9},{9,10},{10,1... | collective-permute-start | bytes 18440 | tf_op jit(solution)/shard_map/ppermute | solution.py:22
  21.5 7.8 %collective-permute-done = f32[4,1,384]{2,1,0:T(1,128)S(1)} collective-permute-done((f32[4,1,384]{2,1,0:T(1,128)S(1)}, f32[4,1,384]{2,1,0:T(1,128)S(1)}, u32[]{:S(2)}, u32[]{:S(2)}) %collective-permute-start) | collective-permute-done | bytes 6176 | tf_op jit(solution)/shard_map/ppermute | solution.py:22
  29.3 3.5 %collective-permute-start.1 = (f32[1,6,384]{2,1,0:T(8,128)S(1)}, f32[1,6,384]{2,1,0:T(8,128)S(1)}, u32[]{:S(2)}, u32[]{:S(2)}) collective-permute-start(f32[1,6,384]{2,1,0:T(8,128)S(1)} %pad_maximum_fusion.13), channel_id=1, source_target_pairs={{0,64},{64,128},{128,192},{192,256},{256,320},{320,384},{384,448},... | collective-permute-start | bytes 27656 | tf_op jit(solution)/shard_map/ppermute | solution.py:22
  33.8 1.3 collective-permute-start.2
  35.1 8.0 %collective-permute-done.2 = f32[1,6,384]{2,1,0:T(8,128)S(1)} collective-permute-done((f32[1,6,384]{2,1,0:T(8,128)S(1)}, f32[1,6,384]{2,1,0:T(8,128)S(1)}, u32[]{:S(2)}, u32[]{:S(2)}) %collective-permute-start.2) | collective-permute-done | bytes 9248 | tf_op jit(solution)/shard_map/ppermute | solution.py:22
  43.2 2.5 collective-permute-start.3
  45.6 4.7 %collective-permute-done.3 = f32[4,1,384]{2,1,0:T(1,128)S(1)} collective-permute-done((f32[4,1,384]{2,1,0:T(1,128)S(1)}, f32[4,1,384]{2,1,0:T(1,128)S(1)}, u32[]{:S(2)}, u32[]{:S(2)}) %collective-permute-start.3) | collective-permute-done | bytes 6176 | tf_op jit(solution)/shard_map/ppermute | solution.py:22
  51.2 4.5 %fusion.113 = (f32[4,4,1,2,128,1]{5,4,0,3,1,2:T(8,128)}, f32[4,4,1,2,128,1]{5,4,0,3,1,2:T(8,128)}, f32[4,4,1,2,128,1]{5,4,0,3,1,2:T(8,128)}, f32[4,4,1,2,128,1]{5,4,0,3,1,2:T(8,128)}) fusion(f32[4,4,1,2,129,3]{5,4,0,3,1,2:T(8,128)S(1)} %reshape.368), kind=kLoop, calls=%fused_computation.303 | loop fusion | bytes 131072 | tf_op jit(solution)/shard_map/slice | solution.py:68
  55.7 2.2 copy.372
  57.9 2.4 copy.374
  60.3 2.2 copy.373
  69.4 1.1 reshape.324
  70.9 1.9 collective-permute-start.4
  72.9 1.1 collective-permute-done.4
  74.0 7.9 %collective-permute-start.5 = (f32[1,6,384]{2,1,0:T(8,128)S(1)}, f32[1,6,384]{2,1,0:T(8,128)S(1)}, u32[]{:S(2)}, u32[]{:S(2)}) collective-permute-start(f32[1,6,384]{2,1,0:T(8,128)S(1)} %pad_maximum_fusion.12), channel_id=1, source_target_pairs={{0,64},{64,128},{128,192},{192,256},{256,320},{320,384},{384,448},... | collective-permute-start | bytes 27656 | tf_op jit(solution)/shard_map/ppermute | solution.py:22
  83.4 13.5 %all-reduce.49 = (f32[]{:T(128)}, f32[]{:T(128)}) all-reduce(f32[]{:T(128)} %get-tuple-element.5, f32[]{:T(128)} %get-tuple-element.4), channel_id=1, replica_groups=mesh['bx_0'=4,'bx_1'=3,'by_0'=4,'by_1'=8,'by_2'=2] {'bx_0'}, use_global_device_ids=true, to_apply=%region_1.2 | all-reduce | flops 2 | bytes 16 | tf_op jit(solution)/shard_map/psum | solution.py:27
  96.8 9.8 %all-reduce.51 = (f32[]{:T(128)}, f32[]{:T(128)}) all-reduce(f32[]{:T(128)} %get-tuple-element.16, f32[]{:T(128)} %get-tuple-element.17), channel_id=1, replica_groups=mesh['bx_0'=4,'bx_1'=3,'by_0'=4,'by_1'=8,'by_2'=2] {'bx_1'}, use_global_device_ids=true, to_apply=%region_2.3 | all-reduce | flops 2 | bytes 16 | tf_op jit(solution)/shard_map/psum | solution.py:27
  106.6 11.0 %all-reduce.47 = (f32[]{:T(128)}, f32[]{:T(128)}) all-reduce(f32[]{:T(128)} %get-tuple-element.20, f32[]{:T(128)} %get-tuple-element.21), channel_id=1, replica_groups=mesh['bx_0'=4,'bx_1'=3,'by_0'=4,'by_1'=8,'by_2'=2] {'by_0'}, use_global_device_ids=true, to_apply=%region_3.4 | all-reduce | flops 2 | bytes 16 | tf_op jit(solution)/shard_map/psum | solution.py:27
  117.7 14.7 %all-reduce.45 = (f32[]{:T(128)}, f32[]{:T(128)}) all-reduce(f32[]{:T(128)} %get-tuple-element.12, f32[]{:T(128)} %get-tuple-element.13), channel_id=1, replica_groups=mesh['bx_0'=4,'bx_1'=3,'by_0'=4,'by_1'=8,'by_2'=2] {'by_1'}, use_global_device_ids=true, to_apply=%region_4.5 | all-reduce | flops 2 | bytes 16 | tf_op jit(solution)/shard_map/psum | solution.py:27
  132.4 13.2 %all-reduce.53 = (f32[]{:T(128)}, f32[]{:T(128)}) all-reduce(f32[]{:T(128)} %get-tuple-element.8, f32[]{:T(128)} %get-tuple-element.9), channel_id=1, replica_groups=mesh['bx_0'=4,'bx_1'=3,'by_0'=4,'by_1'=8,'by_2'=2] {'by_2'}, use_global_device_ids=true, to_apply=%region_5.6 | all-reduce | flops 2 | bytes 16 | tf_op jit(solution)/shard_map/psum | solution.py:27
  147.1 1.3 collective-permute-start.6
  148.4 7.2 %collective-permute-done.6 = f32[1,6,384]{2,1,0:T(8,128)S(1)} collective-permute-done((f32[1,6,384]{2,1,0:T(8,128)S(1)}, f32[1,6,384]{2,1,0:T(8,128)S(1)}, u32[]{:S(2)}, u32[]{:S(2)}) %collective-permute-start.6) | collective-permute-done | bytes 9248 | tf_op jit(solution)/shard_map/ppermute | solution.py:22
  155.5 3.5 %collective-permute-start.7 = (f32[4,1,384]{2,1,0:T(1,128)S(1)}, f32[4,1,384]{2,1,0:T(1,128)S(1)}, u32[]{:S(2)}, u32[]{:S(2)}) collective-permute-start(f32[4,1,384]{2,1,0:T(1,128)S(1)} %pad_maximum_fusion.14), channel_id=1, source_target_pairs={{1,0},{2,1},{3,2},{4,3},{5,4},{6,5},{7,6},{8,7},{9,8},{10,9},{11,1... | collective-permute-start | bytes 18440 | tf_op jit(solution)/shard_map/ppermute | solution.py:22
  159.0 2.7 %collective-permute-done.7 = f32[4,1,384]{2,1,0:T(1,128)S(1)} collective-permute-done((f32[4,1,384]{2,1,0:T(1,128)S(1)}, f32[4,1,384]{2,1,0:T(1,128)S(1)}, u32[]{:S(2)}, u32[]{:S(2)}) %collective-permute-start.7) | collective-permute-done | bytes 6176 | tf_op jit(solution)/shard_map/ppermute | solution.py:22
  162.6 4.5 %fusion.112 = (f32[4,4,1,2,128,1]{5,4,0,3,1,2:T(8,128)}, f32[4,4,1,2,128,1]{5,4,0,3,1,2:T(8,128)}, f32[4,4,1,2,128,1]{5,4,0,3,1,2:T(8,128)}, f32[4,4,1,2,128,1]{5,4,0,3,1,2:T(8,128)}) fusion(f32[4,4,1,2,129,3]{5,4,0,3,1,2:T(8,128)S(1)} %reshape.369), kind=kLoop, calls=%fused_computation.302 | loop fusion | bytes 131072 | tf_op jit(solution)/shard_map/slice | solution.py:68
  167.1 2.2 copy.385
  169.3 2.4 copy.387
  171.6 2.2 copy.386
  180.8 1.1 reshape.342
  182.2 1.9 collective-permute-start.8
  184.2 1.1 collective-permute-done.8
  185.3 4.6 %collective-permute-start.9 = (f32[1,6,384]{2,1,0:T(8,128)S(1)}, f32[1,6,384]{2,1,0:T(8,128)S(1)}, u32[]{:S(2)}, u32[]{:S(2)}) collective-permute-start(f32[1,6,384]{2,1,0:T(8,128)S(1)} %pad_maximum_fusion.11), channel_id=1, source_target_pairs={{0,64},{64,128},{128,192},{192,256},{256,320},{320,384},{384,448},... | collective-permute-start | bytes 27656 | tf_op jit(solution)/shard_map/ppermute | solution.py:22
  191.5 11.1 %all-reduce.48 = (f32[]{:T(128)}, f32[]{:T(128)}) all-reduce(f32[]{:T(128)} %get-tuple-element.3, f32[]{:T(128)} %get-tuple-element.2), channel_id=1, replica_groups=mesh['bx_0'=4,'bx_1'=3,'by_0'=4,'by_1'=8,'by_2'=2] {'bx_0'}, use_global_device_ids=true, to_apply=%region_13.14 | all-reduce | flops 2 | bytes 16 | tf_op jit(solution)/shard_map/psum | solution.py:27
  202.6 8.4 %all-reduce.50 = (f32[]{:T(128)}, f32[]{:T(128)}) all-reduce(f32[]{:T(128)} %get-tuple-element.14, f32[]{:T(128)} %get-tuple-element.15), channel_id=1, replica_groups=mesh['bx_0'=4,'bx_1'=3,'by_0'=4,'by_1'=8,'by_2'=2] {'bx_1'}, use_global_device_ids=true, to_apply=%region_14.15 | all-reduce | flops 2 | bytes 16 | tf_op jit(solution)/shard_map/psum | solution.py:27
  211.0 8.0 %all-reduce.46 = (f32[]{:T(128)}, f32[]{:T(128)}) all-reduce(f32[]{:T(128)} %get-tuple-element.18, f32[]{:T(128)} %get-tuple-element.19), channel_id=1, replica_groups=mesh['bx_0'=4,'bx_1'=3,'by_0'=4,'by_1'=8,'by_2'=2] {'by_0'}, use_global_device_ids=true, to_apply=%region_15.16 | all-reduce | flops 2 | bytes 16 | tf_op jit(solution)/shard_map/psum | solution.py:27
  219.0 14.0 %all-reduce.44 = (f32[]{:T(128)}, f32[]{:T(128)}) all-reduce(f32[]{:T(128)} %get-tuple-element.10, f32[]{:T(128)} %get-tuple-element.11), channel_id=1, replica_groups=mesh['bx_0'=4,'bx_1'=3,'by_0'=4,'by_1'=8,'by_2'=2] {'by_1'}, use_global_device_ids=true, to_apply=%region_16.17 | all-reduce | flops 2 | bytes 16 | tf_op jit(solution)/shard_map/psum | solution.py:27
  232.9 14.2 %all-reduce.52 = (f32[]{:T(128)}, f32[]{:T(128)}) all-reduce(f32[]{:T(128)} %get-tuple-element.6, f32[]{:T(128)} %get-tuple-element.7), channel_id=1, replica_groups=mesh['bx_0'=4,'bx_1'=3,'by_0'=4,'by_1'=8,'by_2'=2] {'by_2'}, use_global_device_ids=true, to_apply=%region_17.18 | all-reduce | flops 2 | bytes 16 | tf_op jit(solution)/shard_map/psum | solution.py:27
  (170 shorter events, 26.6 us)
Async XLA Ops:
  0.6 13.0 %copy-start.6 = (f32[4,4,1,1,1]{0,1,4,3,2:T(4,128)S(1)}, f32[4,4,1,1,1]{0,1,4,3,2:T(4,128)}, u32[]{:S(2)}) copy-start(f32[4,4,1,1,1]{0,1,4,3,2:T(4,128)} %constant.144) | copy-start | bytes 196
  0.6 11.4 %copy-start.4 = (f32[4,4,1,1,1]{0,1,4,3,2:T(4,128)S(1)}, f32[4,4,1,1,1]{0,1,4,3,2:T(4,128)}, u32[]{:S(2)}) copy-start(f32[4,4,1,1,1]{0,1,4,3,2:T(4,128)} %constant.142) | copy-start | bytes 196
  0.7 11.1 %copy-start.7 = (f32[4,4,1,1,1]{0,1,4,3,2:T(4,128)S(1)}, f32[4,4,1,1,1]{0,1,4,3,2:T(4,128)}, u32[]{:S(2)}) copy-start(f32[4,4,1,1,1]{0,1,4,3,2:T(4,128)} %constant.143) | copy-start | bytes 196
  15.4 18.3 %copy-start.3 = (f32[3,6,384]{2,1,0:T(8,128)S(1)}, f32[3,6,384]{2,1,0:T(8,128)}, u32[]{:S(2)}) copy-start(f32[3,6,384]{2,1,0:T(8,128)} %param.8) | copy-start | bytes 82948
  16.9 12.5 %collective-permute-start = (f32[4,1,384]{2,1,0:T(1,128)S(1)}, f32[4,1,384]{2,1,0:T(1,128)S(1)}, u32[]{:S(2)}, u32[]{:S(2)}) collective-permute-start(f32[4,1,384]{2,1,0:T(1,128)S(1)} %slice.523), channel_id=1, source_target_pairs={{0,1},{1,2},{2,3},{3,4},{4,5},{5,6},{6,7},{7,8},{8,9},{9,10},{10,1... | collective-permute-start | bytes 18440 | tf_op jit(solution)/shard_map/ppermute | solution.py:22
  29.3 4.3 %collective-permute-start.1 = (f32[1,6,384]{2,1,0:T(8,128)S(1)}, f32[1,6,384]{2,1,0:T(8,128)S(1)}, u32[]{:S(2)}, u32[]{:S(2)}) collective-permute-start(f32[1,6,384]{2,1,0:T(8,128)S(1)} %pad_maximum_fusion.13), channel_id=1, source_target_pairs={{0,64},{64,128},{128,192},{192,256},{256,320},{320,384},{384,448},... | collective-permute-start | bytes 27656 | tf_op jit(solution)/shard_map/ppermute | solution.py:22
  33.8 9.3 %collective-permute-start.2 = (f32[1,6,384]{2,1,0:T(8,128)S(1)}, f32[1,6,384]{2,1,0:T(8,128)S(1)}, u32[]{:S(2)}, u32[]{:S(2)}) collective-permute-start(f32[1,6,384]{2,1,0:T(8,128)S(1)} %slice.526), channel_id=1, source_target_pairs={{64,0},{128,64},{192,128},{256,192},{320,256},{384,320},{448,384},... | collective-permute-start | bytes 27656 | tf_op jit(solution)/shard_map/ppermute | solution.py:22
  43.2 7.2 %collective-permute-start.3 = (f32[4,1,384]{2,1,0:T(1,128)S(1)}, f32[4,1,384]{2,1,0:T(1,128)S(1)}, u32[]{:S(2)}, u32[]{:S(2)}) collective-permute-start(f32[4,1,384]{2,1,0:T(1,128)S(1)} %pad_maximum_fusion.15), channel_id=1, source_target_pairs={{1,0},{2,1},{3,2},{4,3},{5,4},{6,5},{7,6},{8,7},{9,8},{10,9},{11,1... | collective-permute-start | bytes 18440 | tf_op jit(solution)/shard_map/ppermute | solution.py:22
  57.9 4.6 %copy-start = (f32[4,4,1,2,128,1]{5,4,0,3,1,2:T(8,128)S(1)}, f32[4,4,1,2,128,1]{5,4,0,3,1,2:T(8,128)}, u32[]{:S(2)}) copy-start(f32[4,4,1,2,128,1]{5,4,0,3,1,2:T(8,128)} %get-tuple-element.34) | copy-start | bytes 49156
  60.3 2.9 %copy-start.2 = (f32[4,4,1,1,1]{1,0,4,3,2:T(4,128)S(1)}, f32[4,4,1,1,1]{1,0,4,3,2:T(4,128)}, u32[]{:S(2)}) copy-start(f32[4,4,1,1,1]{1,0,4,3,2:T(4,128)} %constant.145) | copy-start | bytes 196
  60.3 3.2 %copy-start.5 = (f32[4,4,1,1,1]{1,0,4,3,2:T(4,128)S(1)}, f32[4,4,1,1,1]{1,0,4,3,2:T(4,128)}, u32[]{:S(2)}) copy-start(f32[4,4,1,1,1]{1,0,4,3,2:T(4,128)} %constant.146) | copy-start | bytes 196
  70.9 3.1 %collective-permute-start.4 = (f32[4,1,384]{2,1,0:T(1,128)S(1)}, f32[4,1,384]{2,1,0:T(1,128)S(1)}, u32[]{:S(2)}, u32[]{:S(2)}) collective-permute-start(f32[4,1,384]{2,1,0:T(1,128)S(1)} %slice.559), channel_id=1, source_target_pairs={{0,1},{1,2},{2,3},{3,4},{4,5},{5,6},{6,7},{7,8},{8,9},{9,10},{10,1... | collective-permute-start | bytes 18440 | tf_op jit(solution)/shard_map/ppermute | solution.py:22
  74.0 8.7 %collective-permute-start.5 = (f32[1,6,384]{2,1,0:T(8,128)S(1)}, f32[1,6,384]{2,1,0:T(8,128)S(1)}, u32[]{:S(2)}, u32[]{:S(2)}) collective-permute-start(f32[1,6,384]{2,1,0:T(8,128)S(1)} %pad_maximum_fusion.12), channel_id=1, source_target_pairs={{0,64},{64,128},{128,192},{192,256},{256,320},{320,384},{384,448},... | collective-permute-start | bytes 27656 | tf_op jit(solution)/shard_map/ppermute | solution.py:22
  147.1 8.5 %collective-permute-start.6 = (f32[1,6,384]{2,1,0:T(8,128)S(1)}, f32[1,6,384]{2,1,0:T(8,128)S(1)}, u32[]{:S(2)}, u32[]{:S(2)}) collective-permute-start(f32[1,6,384]{2,1,0:T(8,128)S(1)} %slice.561), channel_id=1, source_target_pairs={{64,0},{128,64},{192,128},{256,192},{320,256},{384,320},{448,384},... | collective-permute-start | bytes 27656 | tf_op jit(solution)/shard_map/ppermute | solution.py:22
  155.5 6.2 %collective-permute-start.7 = (f32[4,1,384]{2,1,0:T(1,128)S(1)}, f32[4,1,384]{2,1,0:T(1,128)S(1)}, u32[]{:S(2)}, u32[]{:S(2)}) collective-permute-start(f32[4,1,384]{2,1,0:T(1,128)S(1)} %pad_maximum_fusion.14), channel_id=1, source_target_pairs={{1,0},{2,1},{3,2},{4,3},{5,4},{6,5},{7,6},{8,7},{9,8},{10,9},{11,1... | collective-permute-start | bytes 18440 | tf_op jit(solution)/shard_map/ppermute | solution.py:22
  169.3 4.6 %copy-start.1 = (f32[4,4,1,2,128,1]{5,4,0,3,1,2:T(8,128)S(1)}, f32[4,4,1,2,128,1]{5,4,0,3,1,2:T(8,128)}, u32[]{:S(2)}) copy-start(f32[4,4,1,2,128,1]{5,4,0,3,1,2:T(8,128)} %get-tuple-element.30) | copy-start | bytes 49156
  182.2 3.1 %collective-permute-start.8 = (f32[4,1,384]{2,1,0:T(1,128)S(1)}, f32[4,1,384]{2,1,0:T(1,128)S(1)}, u32[]{:S(2)}, u32[]{:S(2)}) collective-permute-start(f32[4,1,384]{2,1,0:T(1,128)S(1)} %slice.588), channel_id=1, source_target_pairs={{0,1},{1,2},{2,3},{3,4},{4,5},{5,6},{6,7},{7,8},{8,9},{9,10},{10,1... | collective-permute-start | bytes 18440 | tf_op jit(solution)/shard_map/ppermute | solution.py:22
  185.3 5.4 %collective-permute-start.9 = (f32[1,6,384]{2,1,0:T(8,128)S(1)}, f32[1,6,384]{2,1,0:T(8,128)S(1)}, u32[]{:S(2)}, u32[]{:S(2)}) collective-permute-start(f32[1,6,384]{2,1,0:T(8,128)S(1)} %pad_maximum_fusion.11), channel_id=1, source_target_pairs={{0,64},{64,128},{128,192},{192,256},{256,320},{320,384},{384,448},... | collective-permute-start | bytes 27656 | tf_op jit(solution)/shard_map/ppermute | solution.py:22
where the time goes:
time: 254 us; the launch traced here: 253 us
  blocking collectives  118 us (46%)
  waiting for transfers between devices  35 us (14%)
  starting transfers between devices  33 us (13%)
  local copies, waits for them, and re-layouts  31.4 us (12%)
  matrix products  22.9 us (9%)
  between operations  7.87 us (3%)
  other arithmetic  4.93 us (2%)
    psum x10, blocking collectives, over_axes(): value = lax.psum(value, axis)  118 us
    ppermute x10, waiting for transfers between devices, shifted(): lax.ppermute(value, axis, [(source, source + steps) for source in range(i...  35 us
    ppermute x10, starting transfers between devices, shifted(): lax.ppermute(value, axis, [(source, source + steps) for source in range(i...  33 us
    dot_general x57, matrix products, apply_table(): jnp.einsum(EINSUM_FORMS[stack_pos], weights_1d, operand, precision=lax.Pr...  22.9 us
    unnamed x26, local copies, waits for them, and re-layouts  15 us
    slice x4, local copies, waits for them, and re-layouts, split_axis(): lax.index_in_dim(lower_rows, k, axis_pos + 1, keepdims=False)  9.03 us
  transfers between devices with their start and end apart: 10, of which 10 were waited for; matrix products, arithmetic and copies ran while one was open for 0% of the time, Pallas kernels for 0%

commit v1 on v0

--- a/solution.py
+++ b/solution.py
@@ -161,7 +161,8 @@
 
 
 def global_sums(terms):
-    return (over_axes(terms[0], BX_BY), over_axes(terms[1], BX_BY))
+    summed = lax.psum(jnp.stack(terms), BX_BY)
+    return (summed[0], summed[1])
 
 
 def widen(dof_field):

time: 254 us -> 369 us (1.45)
  blocking collectives: 118 us -> 231 us
    psum x10 -> x2, blocking collectives: 118 us -> 231 us  [global_sums(): summed = lax.psum(jnp.stack(terms), BX_BY)]
where the time goes in v1:
time: 369 us; the launch traced here: 368 us
  blocking collectives  231 us (63%)
  waiting for transfers between devices  33.1 us (9%)
  starting transfers between devices  33 us (9%)
  local copies, waits for them, and re-layouts  32.6 us (9%)
  matrix products  22.9 us (6%)
  between operations  7.76 us (2%)
  other arithmetic  7.65 us (2%)
    psum x2, blocking collectives, global_sums(): summed = lax.psum(jnp.stack(terms), BX_BY)  231 us
    ppermute x10, waiting for transfers between devices, shifted(): lax.ppermute(value, axis, [(source, source + steps) for source in range(i...  33.1 us
    ppermute x10, starting transfers between devices, shifted(): lax.ppermute(value, axis, [(source, source + steps) for source in range(i...  33 us
    dot_general x57, matrix products, apply_table(): jnp.einsum(EINSUM_FORMS[stack_pos], weights_1d, operand, precision=lax.Pr...  22.9 us
    unnamed x26, local copies, waits for them, and re-layouts  15 us
    slice x4, local copies, waits for them, and re-layouts, split_axis(): lax.index_in_dim(lower_rows, k, axis_pos + 1, keepdims=False)  9.05 us
  transfers between devices with their start and end apart: 10, of which 10 were waited for; matrix products, arithmetic and copies ran while one was open for 0% of the time, Pallas kernels for 0%

profile of v1, /device:TPU:1, one launch (start us, length us, event | category | flops | bytes accessed | tf_op | source)
XLA Modules:
  0.0 368.3 jit_solution(15937994726773428056)
XLA Ops:
  0.7 1.1 copy_convert_fusion
  1.8 0.9 convolution_bitcast_fusion.21
  2.6 0.9 convolution_bitcast_fusion.23
  3.5 0.9 convolution_bitcast_fusion.25
  4.4 0.9 convolution_bitcast_fusion.29
  5.3 0.9 convolution_bitcast_fusion.31
  6.2 0.9 convolution_bitcast_fusion.33
  7.1 0.9 convolution_bitcast_fusion.20
  8.0 0.9 convolution_bitcast_fusion.22
  9.0 0.9 convolution_bitcast_fusion.24
  9.9 0.9 convolution_bitcast_fusion.27
  10.8 0.9 convolution_bitcast_fusion.26
  15.4 1.1 reshape.306
  16.9 4.6 %collective-permute-start = (f32[4,1,384]{2,1,0:T(1,128)S(1)}, f32[4,1,384]{2,1,0:T(1,128)S(1)}, u32[]{:S(2)}, u32[]{:S(2)}) collective-permute-start(f32[4,1,384]{2,1,0:T(1,128)S(1)} %slice.539), channel_id=1, source_target_pairs={{0,1},{1,2},{2,3},{3,4},{4,5},{5,6},{6,7},{7,8},{8,9},{9,10},{10,1... | collective-permute-start | bytes 18440 | tf_op jit(solution)/shard_map/ppermute | solution.py:22
  21.5 7.8 %collective-permute-done = f32[4,1,384]{2,1,0:T(1,128)S(1)} collective-permute-done((f32[4,1,384]{2,1,0:T(1,128)S(1)}, f32[4,1,384]{2,1,0:T(1,128)S(1)}, u32[]{:S(2)}, u32[]{:S(2)}) %collective-permute-start) | collective-permute-done | bytes 6176 | tf_op jit(solution)/shard_map/ppermute | solution.py:22
  29.3 3.5 collective-permute-start.1
  32.9 0.8 collective-permute-done.1
  33.8 1.3 collective-permute-start.2
  35.1 8.0 %collective-permute-done.2 = f32[1,6,384]{2,1,0:T(8,128)S(1)} collective-permute-done((f32[1,6,384]{2,1,0:T(8,128)S(1)}, f32[1,6,384]{2,1,0:T(8,128)S(1)}, u32[]{:S(2)}, u32[]{:S(2)}) %collective-permute-start.2) | collective-permute-done | bytes 9248 | tf_op jit(solution)/shard_map/ppermute | solution.py:22
  43.2 2.5 collective-permute-start.3
  45.6 4.7 %collective-permute-done.3 = f32[4,1,384]{2,1,0:T(1,128)S(1)} collective-permute-done((f32[4,1,384]{2,1,0:T(1,128)S(1)}, f32[4,1,384]{2,1,0:T(1,128)S(1)}, u32[]{:S(2)}, u32[]{:S(2)}) %collective-permute-start.3) | collective-permute-done | bytes 6176 | tf_op jit(solution)/shard_map/ppermute | solution.py:22
  51.2 4.5 %fusion.113 = (f32[4,4,1,2,128,1]{5,4,0,3,1,2:T(8,128)}, f32[4,4,1,2,128,1]{5,4,0,3,1,2:T(8,128)}, f32[4,4,1,2,128,1]{5,4,0,3,1,2:T(8,128)}, f32[4,4,1,2,128,1]{5,4,0,3,1,2:T(8,128)}) fusion(f32[4,4,1,2,129,3]{5,4,0,3,1,2:T(8,128)S(1)} %reshape.368), kind=kLoop, calls=%fused_computation.305 | loop fusion | bytes 131072 | tf_op jit(solution)/shard_map/slice | solution.py:68
  55.7 2.2 copy.372
  57.9 2.4 copy.374
  60.3 2.2 copy.373
  69.4 1.1 reshape.324
  70.9 1.9 collective-permute-start.4
  72.9 1.1 collective-permute-done.4
  74.0 7.9 %collective-permute-start.5 = (f32[1,6,384]{2,1,0:T(8,128)S(1)}, f32[1,6,384]{2,1,0:T(8,128)S(1)}, u32[]{:S(2)}, u32[]{:S(2)}) collective-permute-start(f32[1,6,384]{2,1,0:T(8,128)S(1)} %pad_maximum_fusion.12), channel_id=1, source_target_pairs={{0,64},{64,128},{128,192},{192,256},{256,320},{320,384},{384,448},... | collective-permute-start | bytes 27656 | tf_op jit(solution)/shard_map/ppermute | solution.py:22
  81.9 0.8 collective-permute-done.5
  83.4 1.4 pad_maximum_fusion.16
  84.7 118.3 %psum.14 = f32[2]{0:T(128)S(1)} all-reduce(f32[2]{0:T(128)S(1)} %pad_maximum_fusion.16), channel_id=1, replica_groups=mesh['bx_0'=4,'bx_1'=3,'by_0'=4,'by_1'=8,'by_2'=2] {'bx_0','bx_1','by_0'..., use_global_device_ids=true, to_apply=%region_2.3 | all-reduce | flops 2 | bytes 16 | tf_op jit(solution)/shard_map/psum | solution.py:164
  205.0 1.3 collective-permute-start.6
  206.3 7.0 %collective-permute-done.6 = f32[1,6,384]{2,1,0:T(8,128)S(1)} collective-permute-done((f32[1,6,384]{2,1,0:T(8,128)S(1)}, f32[1,6,384]{2,1,0:T(8,128)S(1)}, u32[]{:S(2)}, u32[]{:S(2)}) %collective-permute-start.6) | collective-permute-done | bytes 9248 | tf_op jit(solution)/shard_map/ppermute | solution.py:22
  213.4 4.0 %collective-permute-start.7 = (f32[4,1,384]{2,1,0:T(1,128)S(1)}, f32[4,1,384]{2,1,0:T(1,128)S(1)}, u32[]{:S(2)}, u32[]{:S(2)}) collective-permute-start(f32[4,1,384]{2,1,0:T(1,128)S(1)} %pad_maximum_fusion.14), channel_id=1, source_target_pairs={{1,0},{2,1},{3,2},{4,3},{5,4},{6,5},{7,6},{8,7},{9,8},{10,9},{11,1... | collective-permute-start | bytes 18440 | tf_op jit(solution)/shard_map/ppermute | solution.py:22
  217.4 0.9 collective-permute-done.7
  219.2 4.5 %fusion.112 = (f32[4,4,1,2,128,1]{5,4,0,3,1,2:T(8,128)}, f32[4,4,1,2,128,1]{5,4,0,3,1,2:T(8,128)}, f32[4,4,1,2,128,1]{5,4,0,3,1,2:T(8,128)}, f32[4,4,1,2,128,1]{5,4,0,3,1,2:T(8,128)}) fusion(f32[4,4,1,2,129,3]{5,4,0,3,1,2:T(8,128)S(1)} %reshape.369), kind=kLoop, calls=%fused_computation.304 | loop fusion | bytes 131072 | tf_op jit(solution)/shard_map/slice | solution.py:68
  223.7 2.2 copy.385
  225.9 2.4 copy.387
  228.3 2.2 copy.386
  237.4 1.1 reshape.342
  238.8 1.9 collective-permute-start.8
  240.8 1.1 collective-permute-done.8
  241.9 4.0 %collective-permute-start.9 = (f32[1,6,384]{2,1,0:T(8,128)S(1)}, f32[1,6,384]{2,1,0:T(8,128)S(1)}, u32[]{:S(2)}, u32[]{:S(2)}) collective-permute-start(f32[1,6,384]{2,1,0:T(8,128)S(1)} %pad_maximum_fusion.11), channel_id=1, source_target_pairs={{0,64},{64,128},{128,192},{192,256},{256,320},{320,384},{384,448},... | collective-permute-start | bytes 27656 | tf_op jit(solution)/shard_map/ppermute | solution.py:22
  245.9 0.8 collective-permute-done.9
  246.8 0.8 multiply_reduce_fusion.1
  247.5 1.3 pad_maximum_fusion.17
  248.9 113.0 %psum.15 = f32[2]{0:T(128)S(1)} all-reduce(f32[2]{0:T(128)S(1)} %pad_maximum_fusion.17), channel_id=1, replica_groups=mesh['bx_0'=4,'bx_1'=3,'by_0'=4,'by_1'=8,'by_2'=2] {'bx_0','bx_1','by_0'..., use_global_device_ids=true, to_apply=%region_5.6 | all-reduce | flops 2 | bytes 16 | tf_op jit(solution)/shard_map/psum | solution.py:164
  (166 shorter events, 22.9 us)
Async XLA Ops:
  0.6 13.0 %copy-start.6 = (f32[4,4,1,1,1]{0,1,4,3,2:T(4,128)S(1)}, f32[4,4,1,1,1]{0,1,4,3,2:T(4,128)}, u32[]{:S(2)}) copy-start(f32[4,4,1,1,1]{0,1,4,3,2:T(4,128)} %constant.144) | copy-start | bytes 196
  0.6 11.4 %copy-start.4 = (f32[4,4,1,1,1]{0,1,4,3,2:T(4,128)S(1)}, f32[4,4,1,1,1]{0,1,4,3,2:T(4,128)}, u32[]{:S(2)}) copy-start(f32[4,4,1,1,1]{0,1,4,3,2:T(4,128)} %constant.142) | copy-start | bytes 196
  0.7 11.1 %copy-start.7 = (f32[4,4,1,1,1]{0,1,4,3,2:T(4,128)S(1)}, f32[4,4,1,1,1]{0,1,4,3,2:T(4,128)}, u32[]{:S(2)}) copy-start(f32[4,4,1,1,1]{0,1,4,3,2:T(4,128)} %constant.143) | copy-start | bytes 196
  15.4 18.3 %copy-start.3 = (f32[3,6,384]{2,1,0:T(8,128)S(1)}, f32[3,6,384]{2,1,0:T(8,128)}, u32[]{:S(2)}) copy-start(f32[3,6,384]{2,1,0:T(8,128)} %param.8) | copy-start | bytes 82948
  16.9 12.5 %collective-permute-start = (f32[4,1,384]{2,1,0:T(1,128)S(1)}, f32[4,1,384]{2,1,0:T(1,128)S(1)}, u32[]{:S(2)}, u32[]{:S(2)}) collective-permute-start(f32[4,1,384]{2,1,0:T(1,128)S(1)} %slice.539), channel_id=1, source_target_pairs={{0,1},{1,2},{2,3},{3,4},{4,5},{5,6},{6,7},{7,8},{8,9},{9,10},{10,1... | collective-permute-start | bytes 18440 | tf_op jit(solution)/shard_map/ppermute | solution.py:22
  29.3 4.3 %collective-permute-start.1 = (f32[1,6,384]{2,1,0:T(8,128)S(1)}, f32[1,6,384]{2,1,0:T(8,128)S(1)}, u32[]{:S(2)}, u32[]{:S(2)}) collective-permute-start(f32[1,6,384]{2,1,0:T(8,128)S(1)} %pad_maximum_fusion.13), channel_id=1, source_target_pairs={{0,64},{64,128},{128,192},{192,256},{256,320},{320,384},{384,448},... | collective-permute-start | bytes 27656 | tf_op jit(solution)/shard_map/ppermute | solution.py:22
  33.8 9.3 %collective-permute-start.2 = (f32[1,6,384]{2,1,0:T(8,128)S(1)}, f32[1,6,384]{2,1,0:T(8,128)S(1)}, u32[]{:S(2)}, u32[]{:S(2)}) collective-permute-start(f32[1,6,384]{2,1,0:T(8,128)S(1)} %slice.542), channel_id=1, source_target_pairs={{64,0},{128,64},{192,128},{256,192},{320,256},{384,320},{448,384},... | collective-permute-start | bytes 27656 | tf_op jit(solution)/shard_map/ppermute | solution.py:22
  43.2 7.2 %collective-permute-start.3 = (f32[4,1,384]{2,1,0:T(1,128)S(1)}, f32[4,1,384]{2,1,0:T(1,128)S(1)}, u32[]{:S(2)}, u32[]{:S(2)}) collective-permute-start(f32[4,1,384]{2,1,0:T(1,128)S(1)} %pad_maximum_fusion.15), channel_id=1, source_target_pairs={{1,0},{2,1},{3,2},{4,3},{5,4},{6,5},{7,6},{8,7},{9,8},{10,9},{11,1... | collective-permute-start | bytes 18440 | tf_op jit(solution)/shard_map/ppermute | solution.py:22
  57.9 4.6 %copy-start = (f32[4,4,1,2,128,1]{5,4,0,3,1,2:T(8,128)S(1)}, f32[4,4,1,2,128,1]{5,4,0,3,1,2:T(8,128)}, u32[]{:S(2)}) copy-start(f32[4,4,1,2,128,1]{5,4,0,3,1,2:T(8,128)} %get-tuple-element.14) | copy-start | bytes 49156
  60.3 2.9 copy-start.2
  60.3 3.2 copy-start.5
  70.9 3.1 collective-permute-start.4
  74.0 8.7 %collective-permute-start.5 = (f32[1,6,384]{2,1,0:T(8,128)S(1)}, f32[1,6,384]{2,1,0:T(8,128)S(1)}, u32[]{:S(2)}, u32[]{:S(2)}) collective-permute-start(f32[1,6,384]{2,1,0:T(8,128)S(1)} %pad_maximum_fusion.12), channel_id=1, source_target_pairs={{0,64},{64,128},{128,192},{192,256},{256,320},{320,384},{384,448},... | collective-permute-start | bytes 27656 | tf_op jit(solution)/shard_map/ppermute | solution.py:22
  205.0 8.3 %collective-permute-start.6 = (f32[1,6,384]{2,1,0:T(8,128)S(1)}, f32[1,6,384]{2,1,0:T(8,128)S(1)}, u32[]{:S(2)}, u32[]{:S(2)}) collective-permute-start(f32[1,6,384]{2,1,0:T(8,128)S(1)} %slice.577), channel_id=1, source_target_pairs={{64,0},{128,64},{192,128},{256,192},{320,256},{384,320},{448,384},... | collective-permute-start | bytes 27656 | tf_op jit(solution)/shard_map/ppermute | solution.py:22
  213.4 4.9 %collective-permute-start.7 = (f32[4,1,384]{2,1,0:T(1,128)S(1)}, f32[4,1,384]{2,1,0:T(1,128)S(1)}, u32[]{:S(2)}, u32[]{:S(2)}) collective-permute-start(f32[4,1,384]{2,1,0:T(1,128)S(1)} %pad_maximum_fusion.14), channel_id=1, source_target_pairs={{1,0},{2,1},{3,2},{4,3},{5,4},{6,5},{7,6},{8,7},{9,8},{10,9},{11,1... | collective-permute-start | bytes 18440 | tf_op jit(solution)/shard_map/ppermute | solution.py:22
  225.9 4.6 %copy-start.1 = (f32[4,4,1,2,128,1]{5,4,0,3,1,2:T(8,128)S(1)}, f32[4,4,1,2,128,1]{5,4,0,3,1,2:T(8,128)}, u32[]{:S(2)}) copy-start(f32[4,4,1,2,128,1]{5,4,0,3,1,2:T(8,128)} %get-tuple-element.10) | copy-start | bytes 49156
  238.8 3.1 collective-permute-start.8
  241.9 4.8 %collective-permute-start.9 = (f32[1,6,384]{2,1,0:T(8,128)S(1)}, f32[1,6,384]{2,1,0:T(8,128)S(1)}, u32[]{:S(2)}, u32[]{:S(2)}) collective-permute-start(f32[1,6,384]{2,1,0:T(8,128)S(1)} %pad_maximum_fusion.11), channel_id=1, source_target_pairs={{0,64},{64,128},{128,192},{192,256},{256,320},{320,384},{384,448},... | collective-permute-start | bytes 27656 | tf_op jit(solution)/shard_map/ppermute | solution.py:22

commit v2 on v0

--- a/solution.py
+++ b/solution.py
@@ -206,28 +206,34 @@
     def local_dot(left, right):
         return jnp.sum(left * right)
 
-    adjoint = jnp.zeros(cotangent.shape, jnp.float32)
     residual = cotangent * interior
     precond = residual / diagonal
     image = operator(precond)
-    rz_now, curvature = global_sums((local_dot(residual, precond), local_dot(precond, image)))
+    scaled = image / diagonal
+    second = operator(scaled)
+    terms = [
+        local_dot(residual, precond),
+        local_dot(precond, image),
+        local_dot(residual, scaled),
+        local_dot(image, scaled),
+        local_dot(precond, second),
+        local_dot(scaled, second),
+    ]
+    summed = over_axes(jnp.stack(terms), BX_BY)
+    rz_now, curvature, cross_r, cross_q, cross_z, curvature_w = [summed[k] for k in range(6)]
     alpha = rz_now / curvature
-    direction = precond
-    direction_image = image
-    for sweep in range(ITERS):
-        adjoint = adjoint + alpha * direction
-        residual = residual - alpha * direction_image
-        if sweep + 1 < ITERS:
-            precond = residual / diagonal
-            image = operator(precond)
-            fresh, curvature = global_sums(
-                (local_dot(residual, precond), local_dot(precond, image))
-            )
-            ratio = fresh / rz_now
-            alpha = fresh / (curvature - ratio * fresh / alpha)
-            direction = precond + ratio * direction
-            direction_image = image + ratio * direction_image
-            rz_now = fresh
+    fresh = rz_now - alpha * cross_r - alpha * curvature + alpha * alpha * cross_q
+    ratio = fresh / rz_now
+    grow = 1.0 + ratio
+    next_curvature = (
+        grow * grow * curvature - alpha * grow * (cross_z + cross_q) + alpha * alpha * curvature_w
+    )
+    next_alpha = fresh / next_curvature
+    residual = residual - alpha * image
+    direction = residual / diagonal + ratio * precond
+    direction_image = image - alpha * second + ratio * image
+    adjoint = alpha * precond + next_alpha * direction
+    residual = residual - next_alpha * direction_image
     return (adjoint, residual)
 
 

time: 254 us -> 206 us (0.81)
  blocking collectives: 118 us -> 61.2 us
  local copies, waits for them, and re-layouts: 31.4 us -> 35.9 us
  starting transfers between devices: 33 us -> 36.8 us
    psum x10 -> x5, blocking collectives: 118 us -> 61.2 us  [over_axes(): value = lax.psum(value, axis)]
    another operation x0 -> x1, local copies, waits for them, and re-layouts: none -> 3.82 us  [shards(): summed = over_axes(jnp.stack(terms), BX_BY)]
    ppermute x10, starting transfers between devices: 33 us -> 36.8 us  [shifted(): lax.ppermute(value, axis, [(source, source + steps) for source in range(i...]
where the time goes in v2:
time: 206 us; the launch traced here: 205 us
  blocking collectives  61.2 us (30%)
  starting transfers between devices  36.8 us (18%)
  waiting for transfers between devices  36.2 us (18%)
  local copies, waits for them, and re-layouts  35.9 us (17%)
  matrix products  22.9 us (11%)
  between operations  8.88 us (4%)
  other arithmetic  3.65 us (2%)
    psum x5, blocking collectives, over_axes(): value = lax.psum(value, axis)  61.2 us
    ppermute x10, starting transfers between devices, shifted(): lax.ppermute(value, axis, [(source, source + steps) for source in range(i...  36.8 us
    ppermute x10, waiting for transfers between devices, shifted(): lax.ppermute(value, axis, [(source, source + steps) for source in range(i...  36.2 us
    dot_general x57, matrix products, apply_table(): jnp.einsum(EINSUM_FORMS[stack_pos], weights_1d, operand, precision=lax.Pr...  22.9 us
    unnamed x26, local copies, waits for them, and re-layouts  15 us
    slice x4, local copies, waits for them, and re-layouts, split_axis(): lax.index_in_dim(lower_rows, k, axis_pos + 1, keepdims=False)  9.04 us
  transfers between devices with their start and end apart: 10, of which 10 were waited for; matrix products, arithmetic and copies ran while one was open for 0% of the time, Pallas kernels for 0%

profile of v2, /device:TPU:1, one launch (start us, length us, event | category | flops | bytes accessed | tf_op | source)
XLA Modules:
  0.0 205.5 jit_solution(11862041456635361706)
XLA Ops:
  0.7 1.1 copy_convert_fusion
  1.8 0.9 convolution_bitcast_fusion.21
  2.6 0.9 convolution_bitcast_fusion.23
  3.5 0.9 convolution_bitcast_fusion.25
  4.4 0.9 convolution_bitcast_fusion.29
  5.3 0.9 convolution_bitcast_fusion.31
  6.2 0.9 convolution_bitcast_fusion.33
  7.1 0.9 convolution_bitcast_fusion.20
  8.0 0.9 convolution_bitcast_fusion.22
  9.0 0.9 convolution_bitcast_fusion.24
  9.9 0.9 convolution_bitcast_fusion.27
  10.8 0.9 convolution_bitcast_fusion.26
  15.4 1.1 reshape.306
  16.9 4.6 %collective-permute-start = (f32[4,1,384]{2,1,0:T(1,128)S(1)}, f32[4,1,384]{2,1,0:T(1,128)S(1)}, u32[]{:S(2)}, u32[]{:S(2)}) collective-permute-start(f32[4,1,384]{2,1,0:T(1,128)S(1)} %slice.547), channel_id=1, source_target_pairs={{0,1},{1,2},{2,3},{3,4},{4,5},{5,6},{6,7},{7,8},{8,9},{9,10},{10,1... | collective-permute-start | bytes 18440 | tf_op jit(solution)/shard_map/ppermute | solution.py:22
  21.5 7.8 %collective-permute-done = f32[4,1,384]{2,1,0:T(1,128)S(1)} collective-permute-done((f32[4,1,384]{2,1,0:T(1,128)S(1)}, f32[4,1,384]{2,1,0:T(1,128)S(1)}, u32[]{:S(2)}, u32[]{:S(2)}) %collective-permute-start) | collective-permute-done | bytes 6176 | tf_op jit(solution)/shard_map/ppermute | solution.py:22
  29.3 3.5 %collective-permute-start.1 = (f32[1,6,384]{2,1,0:T(8,128)S(1)}, f32[1,6,384]{2,1,0:T(8,128)S(1)}, u32[]{:S(2)}, u32[]{:S(2)}) collective-permute-start(f32[1,6,384]{2,1,0:T(8,128)S(1)} %pad_maximum_fusion.13), channel_id=1, source_target_pairs={{0,64},{64,128},{128,192},{192,256},{256,320},{320,384},{384,448},... | collective-permute-start | bytes 27656 | tf_op jit(solution)/shard_map/ppermute | solution.py:22
  33.8 1.3 collective-permute-start.2
  35.1 8.0 %collective-permute-done.2 = f32[1,6,384]{2,1,0:T(8,128)S(1)} collective-permute-done((f32[1,6,384]{2,1,0:T(8,128)S(1)}, f32[1,6,384]{2,1,0:T(8,128)S(1)}, u32[]{:S(2)}, u32[]{:S(2)}) %collective-permute-start.2) | collective-permute-done | bytes 9248 | tf_op jit(solution)/shard_map/ppermute | solution.py:22
  43.2 2.5 %collective-permute-start.3 = (f32[4,1,384]{2,1,0:T(1,128)S(1)}, f32[4,1,384]{2,1,0:T(1,128)S(1)}, u32[]{:S(2)}, u32[]{:S(2)}) collective-permute-start(f32[4,1,384]{2,1,0:T(1,128)S(1)} %pad_maximum_fusion.15), channel_id=1, source_target_pairs={{1,0},{2,1},{3,2},{4,3},{5,4},{6,5},{7,6},{8,7},{9,8},{10,9},{11,1... | collective-permute-start | bytes 18440 | tf_op jit(solution)/shard_map/ppermute | solution.py:22
  45.6 4.7 %collective-permute-done.3 = f32[4,1,384]{2,1,0:T(1,128)S(1)} collective-permute-done((f32[4,1,384]{2,1,0:T(1,128)S(1)}, f32[4,1,384]{2,1,0:T(1,128)S(1)}, u32[]{:S(2)}, u32[]{:S(2)}) %collective-permute-start.3) | collective-permute-done | bytes 6176 | tf_op jit(solution)/shard_map/ppermute | solution.py:22
  51.2 4.5 %fusion.113 = (f32[4,4,1,2,128,1]{5,4,0,3,1,2:T(8,128)}, f32[4,4,1,2,128,1]{5,4,0,3,1,2:T(8,128)}, f32[4,4,1,2,128,1]{5,4,0,3,1,2:T(8,128)}, f32[4,4,1,2,128,1]{5,4,0,3,1,2:T(8,128)}) fusion(f32[4,4,1,2,129,3]{5,4,0,3,1,2:T(8,128)S(1)} %reshape.368), kind=kLoop, calls=%fused_computation.305 | loop fusion | bytes 131072 | tf_op jit(solution)/shard_map/slice | solution.py:68
  55.7 2.2 %copy.372 = f32[4,4,1,2,128,1]{4,0,3,1,5,2:T(4,128)S(1)} copy(f32[4,4,1,2,128,1]{5,4,0,3,1,2:T(8,128)} %get-tuple-element.14) | data formatting | bytes 32768
  57.9 2.4 %copy.374 = f32[4,4,1,2,128,1]{4,0,3,1,5,2:T(4,128)S(1)} copy(f32[4,4,1,2,128,1]{5,4,0,3,1,2:T(8,128)} %get-tuple-element.15) | data formatting | bytes 32768
  60.3 2.2 %copy.373 = f32[4,4,1,2,128,1]{4,0,3,1,5,2:T(4,128)S(1)} copy(f32[4,4,1,2,128,1]{5,4,0,3,1,2:T(8,128)} %get-tuple-element.16) | data formatting | bytes 32768
  69.4 1.1 reshape.324
  70.9 1.9 collective-permute-start.4
  72.9 1.1 collective-permute-done.4
  74.0 7.9 %collective-permute-start.5 = (f32[1,6,384]{2,1,0:T(8,128)S(1)}, f32[1,6,384]{2,1,0:T(8,128)S(1)}, u32[]{:S(2)}, u32[]{:S(2)}) collective-permute-start(f32[1,6,384]{2,1,0:T(8,128)S(1)} %pad_maximum_fusion.12), channel_id=1, source_target_pairs={{0,64},{64,128},{128,192},{192,256},{256,320},{320,384},{384,448},... | collective-permute-start | bytes 27656 | tf_op jit(solution)/shard_map/ppermute | solution.py:22
  81.9 0.8 collective-permute-done.5
  82.8 1.3 collective-permute-start.6
  84.1 8.2 %collective-permute-done.6 = f32[1,6,384]{2,1,0:T(8,128)S(1)} collective-permute-done((f32[1,6,384]{2,1,0:T(8,128)S(1)}, f32[1,6,384]{2,1,0:T(8,128)S(1)}, u32[]{:S(2)}, u32[]{:S(2)}) %collective-permute-start.6) | collective-permute-done | bytes 9248 | tf_op jit(solution)/shard_map/ppermute | solution.py:22
  92.3 4.0 %collective-permute-start.7 = (f32[4,1,384]{2,1,0:T(1,128)S(1)}, f32[4,1,384]{2,1,0:T(1,128)S(1)}, u32[]{:S(2)}, u32[]{:S(2)}) collective-permute-start(f32[4,1,384]{2,1,0:T(1,128)S(1)} %pad_maximum_fusion.14), channel_id=1, source_target_pairs={{1,0},{2,1},{3,2},{4,3},{5,4},{6,5},{7,6},{8,7},{9,8},{10,9},{11,1... | collective-permute-start | bytes 18440 | tf_op jit(solution)/shard_map/ppermute | solution.py:22
  96.3 2.8 %collective-permute-done.7 = f32[4,1,384]{2,1,0:T(1,128)S(1)} collective-permute-done((f32[4,1,384]{2,1,0:T(1,128)S(1)}, f32[4,1,384]{2,1,0:T(1,128)S(1)}, u32[]{:S(2)}, u32[]{:S(2)}) %collective-permute-start.7) | collective-permute-done | bytes 6176 | tf_op jit(solution)/shard_map/ppermute | solution.py:22
  100.0 4.5 %fusion.112 = (f32[4,4,1,2,128,1]{5,4,0,3,1,2:T(8,128)}, f32[4,4,1,2,128,1]{5,4,0,3,1,2:T(8,128)}, f32[4,4,1,2,128,1]{5,4,0,3,1,2:T(8,128)}, f32[4,4,1,2,128,1]{5,4,0,3,1,2:T(8,128)}) fusion(f32[4,4,1,2,129,3]{5,4,0,3,1,2:T(8,128)S(1)} %reshape.369), kind=kLoop, calls=%fused_computation.304 | loop fusion | bytes 131072 | tf_op jit(solution)/shard_map/slice | solution.py:68
  104.5 2.2 %copy.385 = f32[4,4,1,2,128,1]{4,0,3,1,5,2:T(4,128)S(1)} copy(f32[4,4,1,2,128,1]{5,4,0,3,1,2:T(8,128)} %get-tuple-element.10) | data formatting | bytes 32768
  106.7 2.4 %copy.387 = f32[4,4,1,2,128,1]{4,0,3,1,5,2:T(4,128)S(1)} copy(f32[4,4,1,2,128,1]{5,4,0,3,1,2:T(8,128)} %get-tuple-element.11) | data formatting | bytes 32768
  109.1 2.2 %copy.386 = f32[4,4,1,2,128,1]{4,0,3,1,5,2:T(4,128)S(1)} copy(f32[4,4,1,2,128,1]{5,4,0,3,1,2:T(8,128)} %get-tuple-element.12) | data formatting | bytes 32768
  118.2 1.1 reshape.342
  119.7 2.0 collective-permute-start.8
  121.7 1.1 collective-permute-done.8
  122.8 7.8 %collective-permute-start.9 = (f32[1,6,384]{2,1,0:T(8,128)S(1)}, f32[1,6,384]{2,1,0:T(8,128)S(1)}, u32[]{:S(2)}, u32[]{:S(2)}) collective-permute-start(f32[1,6,384]{2,1,0:T(8,128)S(1)} %pad_maximum_fusion.11), channel_id=1, source_target_pairs={{0,64},{64,128},{128,192},{192,256},{256,320},{320,384},{384,448},... | collective-permute-start | bytes 27656 | tf_op jit(solution)/shard_map/ppermute | solution.py:22
  130.6 0.8 collective-permute-done.9
  132.2 3.8 %stack.195 = f32[6]{0:T(128)S(1)} concatenate(f32[1]{0:T(128)} %bitcast.89, f32[1]{0:T(128)} %bitcast.191, f32[1]{0:T(128)} %bitcast.192, f32[1]{0:T(128)} %bitcast.193, f32[1]{0:T(128)} %bitcast.282, f32[1]{0:T(128)} %bitcast.283), dimensions={0} | concatenate | bytes 48 | tf_op jit(solution)/shard_map/stack | solution.py:222
  136.0 12.9 %psum.35 = f32[6]{0:T(128)S(1)} all-reduce(f32[6]{0:T(128)S(1)} %stack.195), channel_id=1, replica_groups=mesh['bx_0'=4,'bx_1'=3,'by_0'=4,'by_1'=8,'by_2'=2] {'bx_0'}, use_global_device_ids=true, to_apply=%region_6.7 | all-reduce | flops 6 | bytes 48 | tf_op jit(solution)/shard_map/psum | solution.py:27
  148.9 9.0 %psum.36 = f32[6]{0:T(128)S(1)} all-reduce(f32[6]{0:T(128)S(1)} %psum.35), channel_id=1, replica_groups=mesh['bx_0'=4,'bx_1'=3,'by_0'=4,'by_1'=8,'by_2'=2] {'bx_1'}, use_global_device_ids=true, to_apply=%region_7.8 | all-reduce | flops 6 | bytes 48 | tf_op jit(solution)/shard_map/psum | solution.py:27
  158.0 12.2 %psum.37 = f32[6]{0:T(128)S(1)} all-reduce(f32[6]{0:T(128)S(1)} %psum.36), channel_id=1, replica_groups=mesh['bx_0'=4,'bx_1'=3,'by_0'=4,'by_1'=8,'by_2'=2] {'by_0'}, use_global_device_ids=true, to_apply=%region_8.9 | all-reduce | flops 6 | bytes 48 | tf_op jit(solution)/shard_map/psum | solution.py:27
  170.1 13.7 %psum.38 = f32[6]{0:T(128)S(1)} all-reduce(f32[6]{0:T(128)S(1)} %psum.37), channel_id=1, replica_groups=mesh['bx_0'=4,'bx_1'=3,'by_0'=4,'by_1'=8,'by_2'=2] {'by_1'}, use_global_device_ids=true, to_apply=%region_9.10 | all-reduce | flops 6 | bytes 48 | tf_op jit(solution)/shard_map/psum | solution.py:27
  183.9 13.3 %psum.39 = f32[6]{0:T(128)S(1)} all-reduce(f32[6]{0:T(128)S(1)} %psum.38), channel_id=1, replica_groups=mesh['bx_0'=4,'bx_1'=3,'by_0'=4,'by_1'=8,'by_2'=2] {'by_2'}, use_global_device_ids=true, to_apply=%region_10.11 | all-reduce | flops 6 | bytes 48 | tf_op jit(solution)/shard_map/psum | solution.py:27
  (165 shorter events, 22.6 us)
Async XLA Ops:
  0.6 13.0 %copy-start.6 = (f32[4,4,1,1,1]{0,1,4,3,2:T(4,128)S(1)}, f32[4,4,1,1,1]{0,1,4,3,2:T(4,128)}, u32[]{:S(2)}) copy-start(f32[4,4,1,1,1]{0,1,4,3,2:T(4,128)} %constant.144) | copy-start | bytes 196
  0.6 11.4 %copy-start.4 = (f32[4,4,1,1,1]{0,1,4,3,2:T(4,128)S(1)}, f32[4,4,1,1,1]{0,1,4,3,2:T(4,128)}, u32[]{:S(2)}) copy-start(f32[4,4,1,1,1]{0,1,4,3,2:T(4,128)} %constant.142) | copy-start | bytes 196
  0.7 11.1 %copy-start.7 = (f32[4,4,1,1,1]{0,1,4,3,2:T(4,128)S(1)}, f32[4,4,1,1,1]{0,1,4,3,2:T(4,128)}, u32[]{:S(2)}) copy-start(f32[4,4,1,1,1]{0,1,4,3,2:T(4,128)} %constant.143) | copy-start | bytes 196
  15.4 18.3 %copy-start.3 = (f32[3,6,384]{2,1,0:T(8,128)S(1)}, f32[3,6,384]{2,1,0:T(8,128)}, u32[]{:S(2)}) copy-start(f32[3,6,384]{2,1,0:T(8,128)} %param.8) | copy-start | bytes 82948
  16.9 12.5 %collective-permute-start = (f32[4,1,384]{2,1,0:T(1,128)S(1)}, f32[4,1,384]{2,1,0:T(1,128)S(1)}, u32[]{:S(2)}, u32[]{:S(2)}) collective-permute-start(f32[4,1,384]{2,1,0:T(1,128)S(1)} %slice.547), channel_id=1, source_target_pairs={{0,1},{1,2},{2,3},{3,4},{4,5},{5,6},{6,7},{7,8},{8,9},{9,10},{10,1... | collective-permute-start | bytes 18440 | tf_op jit(solution)/shard_map/ppermute | solution.py:22
  29.3 4.3 %collective-permute-start.1 = (f32[1,6,384]{2,1,0:T(8,128)S(1)}, f32[1,6,384]{2,1,0:T(8,128)S(1)}, u32[]{:S(2)}, u32[]{:S(2)}) collective-permute-start(f32[1,6,384]{2,1,0:T(8,128)S(1)} %pad_maximum_fusion.13), channel_id=1, source_target_pairs={{0,64},{64,128},{128,192},{192,256},{256,320},{320,384},{384,448},... | collective-permute-start | bytes 27656 | tf_op jit(solution)/shard_map/ppermute | solution.py:22
  33.8 9.3 %collective-permute-start.2 = (f32[1,6,384]{2,1,0:T(8,128)S(1)}, f32[1,6,384]{2,1,0:T(8,128)S(1)}, u32[]{:S(2)}, u32[]{:S(2)}) collective-permute-start(f32[1,6,384]{2,1,0:T(8,128)S(1)} %slice.550), channel_id=1, source_target_pairs={{64,0},{128,64},{192,128},{256,192},{320,256},{384,320},{448,384},... | collective-permute-start | bytes 27656 | tf_op jit(solution)/shard_map/ppermute | solution.py:22
  43.2 7.2 %collective-permute-start.3 = (f32[4,1,384]{2,1,0:T(1,128)S(1)}, f32[4,1,384]{2,1,0:T(1,128)S(1)}, u32[]{:S(2)}, u32[]{:S(2)}) collective-permute-start(f32[4,1,384]{2,1,0:T(1,128)S(1)} %pad_maximum_fusion.15), channel_id=1, source_target_pairs={{1,0},{2,1},{3,2},{4,3},{5,4},{6,5},{7,6},{8,7},{9,8},{10,9},{11,1... | collective-permute-start | bytes 18440 | tf_op jit(solution)/shard_map/ppermute | solution.py:22
  57.9 4.6 %copy-start = (f32[4,4,1,2,128,1]{5,4,0,3,1,2:T(8,128)S(1)}, f32[4,4,1,2,128,1]{5,4,0,3,1,2:T(8,128)}, u32[]{:S(2)}) copy-start(f32[4,4,1,2,128,1]{5,4,0,3,1,2:T(8,128)} %get-tuple-element.17) | copy-start | bytes 49156
  60.3 2.9 %copy-start.2 = (f32[4,4,1,1,1]{1,0,4,3,2:T(4,128)S(1)}, f32[4,4,1,1,1]{1,0,4,3,2:T(4,128)}, u32[]{:S(2)}) copy-start(f32[4,4,1,1,1]{1,0,4,3,2:T(4,128)} %constant.145) | copy-start | bytes 196
  60.3 3.2 %copy-start.5 = (f32[4,4,1,1,1]{1,0,4,3,2:T(4,128)S(1)}, f32[4,4,1,1,1]{1,0,4,3,2:T(4,128)}, u32[]{:S(2)}) copy-start(f32[4,4,1,1,1]{1,0,4,3,2:T(4,128)} %constant.146) | copy-start | bytes 196
  70.9 3.1 %collective-permute-start.4 = (f32[4,1,384]{2,1,0:T(1,128)S(1)}, f32[4,1,384]{2,1,0:T(1,128)S(1)}, u32[]{:S(2)}, u32[]{:S(2)}) collective-permute-start(f32[4,1,384]{2,1,0:T(1,128)S(1)} %slice.583), channel_id=1, source_target_pairs={{0,1},{1,2},{2,3},{3,4},{4,5},{5,6},{6,7},{7,8},{8,9},{9,10},{10,1... | collective-permute-start | bytes 18440 | tf_op jit(solution)/shard_map/ppermute | solution.py:22
  74.0 8.7 %collective-permute-start.5 = (f32[1,6,384]{2,1,0:T(8,128)S(1)}, f32[1,6,384]{2,1,0:T(8,128)S(1)}, u32[]{:S(2)}, u32[]{:S(2)}) collective-permute-start(f32[1,6,384]{2,1,0:T(8,128)S(1)} %pad_maximum_fusion.12), channel_id=1, source_target_pairs={{0,64},{64,128},{128,192},{192,256},{256,320},{320,384},{384,448},... | collective-permute-start | bytes 27656 | tf_op jit(solution)/shard_map/ppermute | solution.py:22
  82.8 9.5 %collective-permute-start.6 = (f32[1,6,384]{2,1,0:T(8,128)S(1)}, f32[1,6,384]{2,1,0:T(8,128)S(1)}, u32[]{:S(2)}, u32[]{:S(2)}) collective-permute-start(f32[1,6,384]{2,1,0:T(8,128)S(1)} %slice.585), channel_id=1, source_target_pairs={{64,0},{128,64},{192,128},{256,192},{320,256},{384,320},{448,384},... | collective-permute-start | bytes 27656 | tf_op jit(solution)/shard_map/ppermute | solution.py:22
  92.3 6.9 %collective-permute-start.7 = (f32[4,1,384]{2,1,0:T(1,128)S(1)}, f32[4,1,384]{2,1,0:T(1,128)S(1)}, u32[]{:S(2)}, u32[]{:S(2)}) collective-permute-start(f32[4,1,384]{2,1,0:T(1,128)S(1)} %pad_maximum_fusion.14), channel_id=1, source_target_pairs={{1,0},{2,1},{3,2},{4,3},{5,4},{6,5},{7,6},{8,7},{9,8},{10,9},{11,1... | collective-permute-start | bytes 18440 | tf_op jit(solution)/shard_map/ppermute | solution.py:22
  106.7 4.6 %copy-start.1 = (f32[4,4,1,2,128,1]{5,4,0,3,1,2:T(8,128)S(1)}, f32[4,4,1,2,128,1]{5,4,0,3,1,2:T(8,128)}, u32[]{:S(2)}) copy-start(f32[4,4,1,2,128,1]{5,4,0,3,1,2:T(8,128)} %get-tuple-element.13) | copy-start | bytes 49156
  119.7 3.1 %collective-permute-start.8 = (f32[4,1,384]{2,1,0:T(1,128)S(1)}, f32[4,1,384]{2,1,0:T(1,128)S(1)}, u32[]{:S(2)}, u32[]{:S(2)}) collective-permute-start(f32[4,1,384]{2,1,0:T(1,128)S(1)} %slice.612), channel_id=1, source_target_pairs={{0,1},{1,2},{2,3},{3,4},{4,5},{5,6},{6,7},{7,8},{8,9},{9,10},{10,1... | collective-permute-start | bytes 18440 | tf_op jit(solution)/shard_map/ppermute | solution.py:22
  122.8 8.7 %collective-permute-start.9 = (f32[1,6,384]{2,1,0:T(8,128)S(1)}, f32[1,6,384]{2,1,0:T(8,128)S(1)}, u32[]{:S(2)}, u32[]{:S(2)}) collective-permute-start(f32[1,6,384]{2,1,0:T(8,128)S(1)} %pad_maximum_fusion.11), channel_id=1, source_target_pairs={{0,64},{64,128},{128,192},{192,256},{256,320},{320,384},{384,448},... | collective-permute-start | bytes 27656 | tf_op jit(solution)/shard_map/ppermute | solution.py:22

commit v3 on v2

--- a/solution.py
+++ b/solution.py
@@ -144,6 +144,88 @@
     return to_dofs(element_action(elements, pointwise))
 
 
+def banded(table, count):
+    band = np.zeros((3 * count + 1, 4, count))
+    for index in range(count):
+        band[3 * index : 3 * index + 4, :, index] = table.T
+    return band
+
+
+def planar(table_x, table_y, count_x, count_y):
+    kron = np.einsum("xpi,yqj->piqjxy", banded(table_x, count_x), banded(table_y, count_y))
+    return jnp.asarray(kron.reshape(16 * count_x * count_y, -1), jnp.float32)
+
+
+def long_axis(table, count):
+    place = lax.broadcasted_iota(jnp.int32, (3 * count + 1, 4, count), 0)
+    first = lax.broadcasted_iota(jnp.int32, (3 * count + 1, 4, count), 2) * 3
+    point = lax.broadcasted_iota(jnp.int32, (3 * count + 1, 4, count), 1)
+    place, first, point = lax.optimization_barrier((place, first, point))
+    offset = place - first
+    band = jnp.zeros(place.shape, jnp.float32)
+    for node in range(4):
+        column = jnp.asarray(table[:, node], jnp.float32)[point]
+        band = band + jnp.where(offset == node, column, 0.0)
+    return band.reshape(3 * count + 1, 4 * count)
+
+
+def mat(left, right):
+    return jnp.matmul(left, right, precision=lax.Precision.HIGHEST)
+
+
+def point_layout(pointwise):
+    count_x, count_y, count_z = pointwise.shape[4:]
+    coeffs = pointwise.astype(jnp.float32).transpose(0, 1, 4, 2, 5, 3, 6)
+    return coeffs.reshape(7, 16 * count_x * count_y, 4 * count_z)
+
+
+def band_operator(field, coeffs, counts):
+    count_x, count_y, count_z = counts
+    values, slopes = gauss_tables()
+    plain = planar(values, values, count_x, count_y)
+    along_x = planar(slopes, values, count_x, count_y)
+    along_y = planar(values, slopes, count_x, count_y)
+    z_tables = jnp.concatenate([long_axis(values, count_z), long_axis(slopes, count_z)], 1)
+    rows = field.shape[0] * field.shape[1]
+    width = 4 * count_z
+    through_z = mat(field.reshape(rows, field.shape[2]), z_tables)
+    z_value = through_z[:, :width]
+    point_value = mat(plain, z_value)
+    grad_x = mat(along_x, z_value)
+    grad_y = mat(along_y, z_value)
+    grad_z = mat(plain, through_z[:, width:])
+    flux_x = coeffs[1] * grad_x + coeffs[4] * grad_y + coeffs[5] * grad_z
+    flux_y = coeffs[4] * grad_x + coeffs[2] * grad_y + coeffs[6] * grad_z
+    flux_z = coeffs[5] * grad_x + coeffs[6] * grad_y + coeffs[3] * grad_z
+    mass_term = coeffs[0] * point_value
+    backward = jnp.concatenate([plain, along_x, along_y], 0).T
+    near = mat(backward, jnp.concatenate([mass_term, flux_x, flux_y], 0))
+    far = mat(plain.T, flux_z)
+    merged = mat(jnp.concatenate([near, far], 1), z_tables.T)
+    return merged.reshape(field.shape)
+
+
+def band_diagonal(coeffs, counts):
+    count_x, count_y, count_z = counts
+    values, slopes = gauss_tables()
+    square_v = values * values
+    square_s = slopes * slopes
+    mixed = values * slopes
+    groups = [
+        (square_v, [(square_v, square_v, 0, 1.0), (square_s, square_v, 1, 1.0),
+                    (square_v, square_s, 2, 1.0), (mixed, mixed, 4, 2.0)]),
+        (square_s, [(square_v, square_v, 3, 1.0)]),
+        (mixed, [(mixed, square_v, 5, 2.0), (square_v, mixed, 6, 2.0)]),
+    ]
+    total = 0.0
+    for z_table, members in groups:
+        inner = 0.0
+        for table_x, table_y, entry, factor in members:
+            inner = inner + mat(factor * planar(table_x, table_y, count_x, count_y).T, coeffs[entry])
+        total = total + mat(inner, long_axis(z_table, count_z).T)
+    return total.reshape(3 * count_x + 1, 3 * count_y + 1, 3 * count_z + 1)
+
+
 def upper_x(plane):
     return shifted(plane, BX, -1)
 
@@ -195,11 +277,13 @@
         (place_x > 0) & (place_y > 0) & (place_z > 0) & (place_x < total_x) & (place_y < total_y)
     )
     interior = jnp.where(inside, 1.0, 0.0).astype(jnp.float32)
-    diagonal = collect(to_dofs(diagonal_action(pointwise)), rows_x, rows_y, rows_z)
+    counts = pointwise.shape[4:]
+    coeffs = point_layout(pointwise)
+    diagonal = collect(band_diagonal(coeffs, counts), rows_x, rows_y, rows_z)
 
     def operator(dof_field):
         return (
-            collect(element_block(pad_top(widen(dof_field)), pointwise), rows_x, rows_y, rows_z)
+            collect(band_operator(pad_top(widen(dof_field)), coeffs, counts), rows_x, rows_y, rows_z)
             * interior
         )
 

time: 206 us -> 174 us (0.84)
  local copies, waits for them, and re-layouts: 35.9 us -> 8.17 us
  matrix products: 22.9 us -> 12.5 us
  other arithmetic: 3.65 us -> 10.4 us
    unnamed x26 -> x33, local copies, waits for them, and re-layouts: 15 us -> 2.71 us
    dot_general x57 -> x30, matrix products: 22.9 us -> 12.5 us  [mat(): return jnp.matmul(left, right, precision=lax.Precision.HIGHEST)]
    slice x8 -> x16, local copies, waits for them, and re-layouts: 9.07 us -> 0.41 us  [band_diagonal(): coeffs[entry]]
    add x0 -> x2, other arithmetic: none -> 8.36 us  [long_axis(): band = band + jnp.where(offset == node, column, 0.0)]
    reshape x5, local copies, waits for them, and re-layouts: 4.5 us -> 0.05 us  [the longest x2 0.02 us: band_operator(): through_z = mat(field.reshape(rows, field.shape[2]), z_tables)]
    another operation x28 -> x0, local copies, waits for them, and re-layouts: 2.59 us -> none  [the longest x26 2.57 us: merge_axis(): jnp.stack([head_piece, jnp.pad(pieces[1], ending), jnp.pad(pieces[2], end...]
  transfers between devices with their start and end apart: 10 -> 10, of which waited for: 10 -> 10; matrix products, arithmetic and copies ran while one was open for 0% -> 1% of each run, Pallas kernels for 0% -> 0%
where the time goes in v3:
time: 174 us; the launch traced here: 173 us
  blocking collectives  61.2 us (35%)
  starting transfers between devices  36.6 us (21%)
  waiting for transfers between devices  35.3 us (20%)
  matrix products  12.5 us (7%)
  other arithmetic  10.4 us (6%)
  between operations  8.7 us (5%)
  local copies, waits for them, and re-layouts  8.17 us (5%)
    psum x5, blocking collectives, over_axes(): value = lax.psum(value, axis)  61.2 us
    ppermute x10, starting transfers between devices, shifted(): lax.ppermute(value, axis, [(source, source + steps) for source in range(i...  36.6 us
    ppermute x10, waiting for transfers between devices, shifted(): lax.ppermute(value, axis, [(source, source + steps) for source in range(i...  35.3 us
    dot_general x30, matrix products, mat(): return jnp.matmul(left, right, precision=lax.Precision.HIGHEST)  12.5 us
    add x2, other arithmetic, long_axis(): band = band + jnp.where(offset == node, column, 0.0)  8.36 us
    another operation x1, local copies, waits for them, and re-layouts, shards(): summed = over_axes(jnp.stack(terms), BX_BY)  3.89 us
  transfers between devices with their start and end apart: 10, of which 10 were waited for; matrix products, arithmetic and copies ran while one was open for 1% of the time, Pallas kernels for 0%

profile of v3, /device:TPU:1, one launch (start us, length us, event | category | flops | bytes accessed | tf_op | source)
XLA Modules:
  0.0 172.8 jit_solution(17575253858483666963)
XLA Ops:
  1.0 2.7 %fusion = (f32[385,4,128]{2,1,0:T(4,128)S(1)}, pred[385,4,128]{2,1,0:T(4,128)(4,1)S(1)}, pred[385,4,128]{2,1,0:T(4,128)(4,1)S(1)}, pred[385,4,128]{2,1,0:T(4,128...) fusion(s32[385,4,128]{2,1,0:T(4,128)S(1)} %iota.37, ...), kind=kLoop, calls=%fused_computation.14 | loop fusion | flops 5913600 | bytes 4533760 | tf_op jit(solution)/shard_map/add | solution.py:168
  3.7 5.7 %fusion.3 = (f32[385,4,128]{2,1,0:T(4,128)S(1)}, f32[385,4,128]{2,1,0:T(4,128)S(1)}, f32[385,4,128]{2,1,0:T(4,128)S(1)}, f32[385,4,128]{2,1,0:T(4,128)S(1)}) fusion(pred[385,4,128]{2,1,0:T(4,128)(4,1)S(1)} %get-tuple-element.23, pred[385,4,128]{2,1,0:T(4,128)(4,1)S(1)} %get-tuple-element.22, pred[385,4,128]{2,1,0:T(4,128)(4,1)S(1)} %get-tuple-element.21, ...), kind=kLoop, calls=%fused_computation.21 | loop fusion | flops 14981120 | bytes 4533760 | tf_op jit(solution)/shard_map/add | solution.py:168
  9.6 0.7 copy-done.1
  10.8 0.5 copy-done.5
  12.0 0.4 copy-done.10
  13.1 0.8 fusion.112
  14.1 0.8 convolution_add_fusion.6
  15.2 0.8 convolution_add_fusion.4
  16.0 4.6 %collective-permute-start = (f32[4,1,384]{2,1,0:T(1,128)S(1)}, f32[4,1,384]{2,1,0:T(1,128)S(1)}, u32[]{:S(2)}, u32[]{:S(2)}) collective-permute-start(f32[4,1,384]{2,1,0:T(1,128)S(1)} %slice.337), channel_id=1, source_target_pairs={{0,1},{1,2},{2,3},{3,4},{4,5},{5,6},{6,7},{7,8},{8,9},{9,10},{10,1... | collective-permute-start | bytes 18440 | tf_op jit(solution)/shard_map/ppermute | solution.py:22
  21.0 7.5 %collective-permute-done = f32[4,1,384]{2,1,0:T(1,128)S(1)} collective-permute-done((f32[4,1,384]{2,1,0:T(1,128)S(1)}, f32[4,1,384]{2,1,0:T(1,128)S(1)}, u32[]{:S(2)}, u32[]{:S(2)}) %collective-permute-start) | collective-permute-done | bytes 6176 | tf_op jit(solution)/shard_map/ppermute | solution.py:22
  28.5 3.5 %collective-permute-start.1 = (f32[1,6,384]{2,1,0:T(8,128)S(1)}, f32[1,6,384]{2,1,0:T(8,128)S(1)}, u32[]{:S(2)}, u32[]{:S(2)}) collective-permute-start(f32[1,6,384]{2,1,0:T(8,128)S(1)} %pad_maximum_fusion.2), channel_id=1, source_target_pairs={{0,64},{64,128},{128,192},{192,256},{256,320},{320,384},{384,448},... | collective-permute-start | bytes 27656 | tf_op jit(solution)/shard_map/ppermute | solution.py:22
  32.2 0.6 collective-permute-done.1
  32.9 1.3 collective-permute-start.2
  34.5 7.8 %collective-permute-done.2 = f32[1,6,384]{2,1,0:T(8,128)S(1)} collective-permute-done((f32[1,6,384]{2,1,0:T(8,128)S(1)}, f32[1,6,384]{2,1,0:T(8,128)S(1)}, u32[]{:S(2)}, u32[]{:S(2)}) %collective-permute-start.2) | collective-permute-done | bytes 9248 | tf_op jit(solution)/shard_map/ppermute | solution.py:22
  42.3 2.3 %collective-permute-start.3 = (f32[4,1,384]{2,1,0:T(1,128)S(1)}, f32[4,1,384]{2,1,0:T(1,128)S(1)}, u32[]{:S(2)}, u32[]{:S(2)}) collective-permute-start(f32[4,1,384]{2,1,0:T(1,128)S(1)} %pad_maximum_fusion.4), channel_id=1, source_target_pairs={{1,0},{2,1},{3,2},{4,3},{5,4},{6,5},{7,6},{8,7},{9,8},{10,9},{11,1... | collective-permute-start | bytes 18440 | tf_op jit(solution)/shard_map/ppermute | solution.py:22
  44.9 4.6 %collective-permute-done.3 = f32[4,1,384]{2,1,0:T(1,128)S(1)} collective-permute-done((f32[4,1,384]{2,1,0:T(1,128)S(1)}, f32[4,1,384]{2,1,0:T(1,128)S(1)}, u32[]{:S(2)}, u32[]{:S(2)}) %collective-permute-start.3) | collective-permute-done | bytes 6176 | tf_op jit(solution)/shard_map/ppermute | solution.py:22
  49.5 1.0 fusion.113
  50.9 0.3 fusion.114
  51.6 0.3 fusion.24
  51.9 0.3 convolution_add_fusion.3
  52.1 0.3 convolution_add_fusion.2
  52.4 1.5 fusion.15
  53.9 1.9 %collective-permute-start.4 = (f32[4,1,384]{2,1,0:T(1,128)S(1)}, f32[4,1,384]{2,1,0:T(1,128)S(1)}, u32[]{:S(2)}, u32[]{:S(2)}) collective-permute-start(f32[4,1,384]{2,1,0:T(1,128)S(1)} %slice.350), channel_id=1, source_target_pairs={{0,1},{1,2},{2,3},{3,4},{4,5},{5,6},{6,7},{7,8},{8,9},{9,10},{10,1... | collective-permute-start | bytes 18440 | tf_op jit(solution)/shard_map/ppermute | solution.py:22
  55.9 1.1 collective-permute-done.4
  57.0 7.9 %collective-permute-start.5 = (f32[1,6,384]{2,1,0:T(8,128)S(1)}, f32[1,6,384]{2,1,0:T(8,128)S(1)}, u32[]{:S(2)}, u32[]{:S(2)}) collective-permute-start(f32[1,6,384]{2,1,0:T(8,128)S(1)} %pad_maximum_fusion.1), channel_id=1, source_target_pairs={{0,64},{64,128},{128,192},{192,256},{256,320},{320,384},{384,448},... | collective-permute-start | bytes 27656 | tf_op jit(solution)/shard_map/ppermute | solution.py:22
  64.9 0.8 collective-permute-done.5
  65.8 1.3 collective-permute-start.6
  67.1 8.2 %collective-permute-done.6 = f32[1,6,384]{2,1,0:T(8,128)S(1)} collective-permute-done((f32[1,6,384]{2,1,0:T(8,128)S(1)}, f32[1,6,384]{2,1,0:T(8,128)S(1)}, u32[]{:S(2)}, u32[]{:S(2)}) %collective-permute-start.6) | collective-permute-done | bytes 9248 | tf_op jit(solution)/shard_map/ppermute | solution.py:22
  75.4 4.0 %collective-permute-start.7 = (f32[4,1,384]{2,1,0:T(1,128)S(1)}, f32[4,1,384]{2,1,0:T(1,128)S(1)}, u32[]{:S(2)}, u32[]{:S(2)}) collective-permute-start(f32[4,1,384]{2,1,0:T(1,128)S(1)} %pad_maximum_fusion.3), channel_id=1, source_target_pairs={{1,0},{2,1},{3,2},{4,3},{5,4},{6,5},{7,6},{8,7},{9,8},{10,9},{11,1... | collective-permute-start | bytes 18440 | tf_op jit(solution)/shard_map/ppermute | solution.py:22
  79.3 2.9 %collective-permute-done.7 = f32[4,1,384]{2,1,0:T(1,128)S(1)} collective-permute-done((f32[4,1,384]{2,1,0:T(1,128)S(1)}, f32[4,1,384]{2,1,0:T(1,128)S(1)}, u32[]{:S(2)}, u32[]{:S(2)}) %collective-permute-start.7) | collective-permute-done | bytes 6176 | tf_op jit(solution)/shard_map/ppermute | solution.py:22
  82.3 1.0 fusion.115
  84.1 0.3 fusion.116
  84.6 0.3 convolution_add_fusion.1
  84.9 0.3 convolution_add_fusion
  85.1 1.5 fusion.19
  86.7 1.9 %collective-permute-start.8 = (f32[4,1,384]{2,1,0:T(1,128)S(1)}, f32[4,1,384]{2,1,0:T(1,128)S(1)}, u32[]{:S(2)}, u32[]{:S(2)}) collective-permute-start(f32[4,1,384]{2,1,0:T(1,128)S(1)} %slice.356), channel_id=1, source_target_pairs={{0,1},{1,2},{2,3},{3,4},{4,5},{5,6},{6,7},{7,8},{8,9},{9,10},{10,1... | collective-permute-start | bytes 18440 | tf_op jit(solution)/shard_map/ppermute | solution.py:22
  88.6 1.1 collective-permute-done.8
  89.7 7.8 %collective-permute-start.9 = (f32[1,6,384]{2,1,0:T(8,128)S(1)}, f32[1,6,384]{2,1,0:T(8,128)S(1)}, u32[]{:S(2)}, u32[]{:S(2)}) collective-permute-start(f32[1,6,384]{2,1,0:T(8,128)S(1)} %pad_maximum_fusion), channel_id=1, source_target_pairs={{0,64},{64,128},{128,192},{192,256},{256,320},{320,384},{384,448},... | collective-permute-start | bytes 27656 | tf_op jit(solution)/shard_map/ppermute | solution.py:22
  97.6 0.8 collective-permute-done.9
  98.4 0.8 multiply_reduce_fusion
  99.2 3.9 %stack.27 = f32[6]{0:T(128)S(1)} concatenate(f32[1]{0:T(128)} %bitcast.1, f32[1]{0:T(128)} %bitcast.2, f32[1]{0:T(128)} %bitcast.3, f32[1]{0:T(128)} %bitcast.4, f32[1]{0:T(128)} %bitcast.5, f32[1]{0:T(128)} %bitcast.6), dimensions={0} | concatenate | bytes 48 | tf_op jit(solution)/shard_map/stack | solution.py:306
  103.1 12.9 %psum.35 = f32[6]{0:T(128)S(1)} all-reduce(f32[6]{0:T(128)S(1)} %stack.27), channel_id=1, replica_groups=mesh['bx_0'=4,'bx_1'=3,'by_0'=4,'by_1'=8,'by_2'=2] {'bx_0'}, use_global_device_ids=true, to_apply=%region_6.7 | all-reduce | flops 6 | bytes 48 | tf_op jit(solution)/shard_map/psum | solution.py:27
  116.0 9.0 %psum.36 = f32[6]{0:T(128)S(1)} all-reduce(f32[6]{0:T(128)S(1)} %psum.35), channel_id=1, replica_groups=mesh['bx_0'=4,'bx_1'=3,'by_0'=4,'by_1'=8,'by_2'=2] {'bx_1'}, use_global_device_ids=true, to_apply=%region_7.8 | all-reduce | flops 6 | bytes 48 | tf_op jit(solution)/shard_map/psum | solution.py:27
  125.0 12.2 %psum.37 = f32[6]{0:T(128)S(1)} all-reduce(f32[6]{0:T(128)S(1)} %psum.36), channel_id=1, replica_groups=mesh['bx_0'=4,'bx_1'=3,'by_0'=4,'by_1'=8,'by_2'=2] {'by_0'}, use_global_device_ids=true, to_apply=%region_8.9 | all-reduce | flops 6 | bytes 48 | tf_op jit(solution)/shard_map/psum | solution.py:27
  137.2 13.7 %psum.38 = f32[6]{0:T(128)S(1)} all-reduce(f32[6]{0:T(128)S(1)} %psum.37), channel_id=1, replica_groups=mesh['bx_0'=4,'bx_1'=3,'by_0'=4,'by_1'=8,'by_2'=2] {'by_1'}, use_global_device_ids=true, to_apply=%region_9.10 | all-reduce | flops 6 | bytes 48 | tf_op jit(solution)/shard_map/psum | solution.py:27
  150.9 13.3 %psum.39 = f32[6]{0:T(128)S(1)} all-reduce(f32[6]{0:T(128)S(1)} %psum.38), channel_id=1, replica_groups=mesh['bx_0'=4,'bx_1'=3,'by_0'=4,'by_1'=8,'by_2'=2] {'by_2'}, use_global_device_ids=true, to_apply=%region_10.11 | all-reduce | flops 6 | bytes 48 | tf_op jit(solution)/shard_map/psum | solution.py:27
  164.3 0.7 fusion.111
  172.1 0.7 multiply_subtract_fusion
  (99 shorter events, 5.9 us)
Async XLA Ops:
  9.3 0.9 copy-start.1
  10.5 0.7 copy-start.5
  11.7 0.7 copy-start.10
  11.7 0.9 copy-start.9
  11.7 1.2 copy-start.8
  11.9 2.0 %copy-start.6 = (f32[32,28]{1,0:T(8,128)S(1)}, f32[32,28]{1,0:T(8,128)}, u32[]{:S(2)}) copy-start(f32[32,28]{1,0:T(8,128)} %constant.144) | copy-start | bytes 10756
  12.0 3.0 %copy-start.7 = (f32[32,28]{1,0:T(8,128)S(1)}, f32[32,28]{1,0:T(8,128)}, u32[]{:S(2)}) copy-start(f32[32,28]{1,0:T(8,128)} %constant.145) | copy-start | bytes 10756
  16.0 12.5 %collective-permute-start = (f32[4,1,384]{2,1,0:T(1,128)S(1)}, f32[4,1,384]{2,1,0:T(1,128)S(1)}, u32[]{:S(2)}, u32[]{:S(2)}) collective-permute-start(f32[4,1,384]{2,1,0:T(1,128)S(1)} %slice.337), channel_id=1, source_target_pairs={{0,1},{1,2},{2,3},{3,4},{4,5},{5,6},{6,7},{7,8},{8,9},{9,10},{10,1... | collective-permute-start | bytes 18440 | tf_op jit(solution)/shard_map/ppermute | solution.py:22
  28.5 4.3 %collective-permute-start.1 = (f32[1,6,384]{2,1,0:T(8,128)S(1)}, f32[1,6,384]{2,1,0:T(8,128)S(1)}, u32[]{:S(2)}, u32[]{:S(2)}) collective-permute-start(f32[1,6,384]{2,1,0:T(8,128)S(1)} %pad_maximum_fusion.2), channel_id=1, source_target_pairs={{0,64},{64,128},{128,192},{192,256},{256,320},{320,384},{384,448},... | collective-permute-start | bytes 27656 | tf_op jit(solution)/shard_map/ppermute | solution.py:22
  32.0 0.8 copy-start.2
  32.9 9.3 %collective-permute-start.2 = (f32[1,6,384]{2,1,0:T(8,128)S(1)}, f32[1,6,384]{2,1,0:T(8,128)S(1)}, u32[]{:S(2)}, u32[]{:S(2)}) collective-permute-start(f32[1,6,384]{2,1,0:T(8,128)S(1)} %slice.340), channel_id=1, source_target_pairs={{64,0},{128,64},{192,128},{256,192},{320,256},{384,320},{448,384},... | collective-permute-start | bytes 27656 | tf_op jit(solution)/shard_map/ppermute | solution.py:22
  42.3 7.2 %collective-permute-start.3 = (f32[4,1,384]{2,1,0:T(1,128)S(1)}, f32[4,1,384]{2,1,0:T(1,128)S(1)}, u32[]{:S(2)}, u32[]{:S(2)}) collective-permute-start(f32[4,1,384]{2,1,0:T(1,128)S(1)} %pad_maximum_fusion.4), channel_id=1, source_target_pairs={{1,0},{2,1},{3,2},{4,3},{5,4},{6,5},{7,6},{8,7},{9,8},{10,9},{11,1... | collective-permute-start | bytes 18440 | tf_op jit(solution)/shard_map/ppermute | solution.py:22
  44.7 5.9 %copy-start = (f32[32,28]{1,0:T(8,128)S(1)}, f32[32,28]{1,0:T(8,128)}, u32[]{:S(2)}) copy-start(f32[32,28]{1,0:T(8,128)} %constant.126.clone) | copy-start | bytes 10756
  44.7 6.5 %copy-start.3 = (f32[32,28]{1,0:T(8,128)S(1)}, f32[32,28]{1,0:T(8,128)}, u32[]{:S(2)}) copy-start(f32[32,28]{1,0:T(8,128)} %constant.128.clone) | copy-start | bytes 10756
  44.8 6.6 %copy-start.4 = (f32[32,28]{1,0:T(8,128)S(1)}, f32[32,28]{1,0:T(8,128)}, u32[]{:S(2)}) copy-start(f32[32,28]{1,0:T(8,128)} %constant.127.clone) | copy-start | bytes 10756
  53.9 3.1 %collective-permute-start.4 = (f32[4,1,384]{2,1,0:T(1,128)S(1)}, f32[4,1,384]{2,1,0:T(1,128)S(1)}, u32[]{:S(2)}, u32[]{:S(2)}) collective-permute-start(f32[4,1,384]{2,1,0:T(1,128)S(1)} %slice.350), channel_id=1, source_target_pairs={{0,1},{1,2},{2,3},{3,4},{4,5},{5,6},{6,7},{7,8},{8,9},{9,10},{10,1... | collective-permute-start | bytes 18440 | tf_op jit(solution)/shard_map/ppermute | solution.py:22
  57.0 8.7 %collective-permute-start.5 = (f32[1,6,384]{2,1,0:T(8,128)S(1)}, f32[1,6,384]{2,1,0:T(8,128)S(1)}, u32[]{:S(2)}, u32[]{:S(2)}) collective-permute-start(f32[1,6,384]{2,1,0:T(8,128)S(1)} %pad_maximum_fusion.1), channel_id=1, source_target_pairs={{0,64},{64,128},{128,192},{192,256},{256,320},{320,384},{384,448},... | collective-permute-start | bytes 27656 | tf_op jit(solution)/shard_map/ppermute | solution.py:22
  65.8 9.5 %collective-permute-start.6 = (f32[1,6,384]{2,1,0:T(8,128)S(1)}, f32[1,6,384]{2,1,0:T(8,128)S(1)}, u32[]{:S(2)}, u32[]{:S(2)}) collective-permute-start(f32[1,6,384]{2,1,0:T(8,128)S(1)} %slice.352), channel_id=1, source_target_pairs={{64,0},{128,64},{192,128},{256,192},{320,256},{384,320},{448,384},... | collective-permute-start | bytes 27656 | tf_op jit(solution)/shard_map/ppermute | solution.py:22
  75.4 6.9 %collective-permute-start.7 = (f32[4,1,384]{2,1,0:T(1,128)S(1)}, f32[4,1,384]{2,1,0:T(1,128)S(1)}, u32[]{:S(2)}, u32[]{:S(2)}) collective-permute-start(f32[4,1,384]{2,1,0:T(1,128)S(1)} %pad_maximum_fusion.3), channel_id=1, source_target_pairs={{1,0},{2,1},{3,2},{4,3},{5,4},{6,5},{7,6},{8,7},{9,8},{10,9},{11,1... | collective-permute-start | bytes 18440 | tf_op jit(solution)/shard_map/ppermute | solution.py:22
  86.7 3.1 %collective-permute-start.8 = (f32[4,1,384]{2,1,0:T(1,128)S(1)}, f32[4,1,384]{2,1,0:T(1,128)S(1)}, u32[]{:S(2)}, u32[]{:S(2)}) collective-permute-start(f32[4,1,384]{2,1,0:T(1,128)S(1)} %slice.356), channel_id=1, source_target_pairs={{0,1},{1,2},{2,3},{3,4},{4,5},{5,6},{6,7},{7,8},{8,9},{9,10},{10,1... | collective-permute-start | bytes 18440 | tf_op jit(solution)/shard_map/ppermute | solution.py:22
  89.7 8.7 %collective-permute-start.9 = (f32[1,6,384]{2,1,0:T(8,128)S(1)}, f32[1,6,384]{2,1,0:T(8,128)S(1)}, u32[]{:S(2)}, u32[]{:S(2)}) collective-permute-start(f32[1,6,384]{2,1,0:T(8,128)S(1)} %pad_maximum_fusion), channel_id=1, source_target_pairs={{0,64},{64,128},{128,192},{192,256},{256,320},{320,384},{384,448},... | collective-permute-start | bytes 27656 | tf_op jit(solution)/shard_map/ppermute | solution.py:22

commit v4 on v3

--- a/solution.py
+++ b/solution.py
@@ -226,6 +226,64 @@
     return total.reshape(3 * count_x + 1, 3 * count_y + 1, 3 * count_z + 1)
 
 
+def moved(value, steps_x, steps_y):
+    count_x = lax.axis_size(BX)
+    count_y = lax.axis_size(BY)
+    pairs = []
+    for source_x in range(count_x):
+        for source_y in range(count_y):
+            target_x, target_y = source_x + steps_x, source_y + steps_y
+            if 0 <= target_x < count_x and 0 <= target_y < count_y:
+                pairs.append((source_x * count_y + source_y, target_x * count_y + target_y))
+    return lax.ppermute(value, BX_BY, pairs)
+
+
+def surround(dof_field):
+    rows_x, rows_y = dof_field.shape[:2]
+    top_x, top_y = rows_x - 3, rows_y - 3
+    lower_row = jnp.concatenate(
+        [
+            moved(dof_field[top_x:, top_y:], 1, 1),
+            moved(dof_field[top_x:], 1, 0),
+            moved(dof_field[top_x:, 0:1], 1, -1),
+        ],
+        1,
+    )
+    own_row = jnp.concatenate(
+        [moved(dof_field[:, top_y:], 0, 1), dof_field, moved(dof_field[:, 0:1], 0, -1)], 1
+    )
+    upper_row = jnp.concatenate(
+        [
+            moved(dof_field[0:1, top_y:], -1, 1),
+            moved(dof_field[0:1], -1, 0),
+            moved(dof_field[0:1, 0:1], -1, -1),
+        ],
+        1,
+    )
+    return jnp.concatenate([lower_row, own_row, upper_row], 0)
+
+
+def ghost_points(pointwise):
+    points = pointwise.astype(jnp.float32)
+    corner = moved(points[:, :, :, :, -1:, -1:], 1, 1)
+    below_x = moved(points[:, :, :, :, -1:], 1, 0)
+    below_y = moved(points[:, :, :, :, :, -1:], 0, 1)
+    lower_row = jnp.concatenate([corner, below_x], 5)
+    own_row = jnp.concatenate([below_y, points], 5)
+    return jnp.concatenate([lower_row, own_row], 4)
+
+
+def gather_contributions(contributions, rows_x, rows_y, rows_z):
+    own = contributions[:rows_x, :rows_y, :rows_z]
+    from_x = moved(contributions[rows_x:, :rows_y, :rows_z], 1, 0)
+    from_y = moved(contributions[:rows_x, rows_y:, :rows_z], 0, 1)
+    from_corner = moved(contributions[rows_x:, rows_y:, :rows_z], 1, 1)
+    head = own[0:1] + from_x
+    head = jnp.concatenate([head[:, 0:1] + from_corner, head[:, 1:]], 1)
+    own = jnp.concatenate([head, own[1:]], 0)
+    return jnp.concatenate([own[:, 0:1] + from_y, own[:, 1:]], 1)
+
+
 def upper_x(plane):
     return shifted(plane, BX, -1)
 
@@ -279,13 +337,13 @@
     interior = jnp.where(inside, 1.0, 0.0).astype(jnp.float32)
     counts = pointwise.shape[4:]
     coeffs = point_layout(pointwise)
-    diagonal = collect(band_diagonal(coeffs, counts), rows_x, rows_y, rows_z)
+    diagonal = gather_contributions(band_diagonal(coeffs, counts), rows_x, rows_y, rows_z)
+    wide_counts = (counts[0] + 1, counts[1] + 1, counts[2])
+    wide_coeffs = point_layout(ghost_points(pointwise))
 
     def operator(dof_field):
-        return (
-            collect(band_operator(pad_top(widen(dof_field)), coeffs, counts), rows_x, rows_y, rows_z)
-            * interior
-        )
+        wide = band_operator(pad_top(surround(dof_field)), wide_coeffs, wide_counts)
+        return wide[3 : 3 + rows_x, 3 : 3 + rows_y, :rows_z] * interior
 
     def local_dot(left, right):
         return jnp.sum(left * right)

time: 174 us -> 277 us (1.59)
  starting transfers between devices: 36.6 us -> 133 us
  blocking collectives: 61.2 us -> 51.7 us
  waiting for transfers between devices: 35.3 us -> 39.9 us
  other arithmetic: 10.4 us -> 14.1 us
  matrix products: 12.5 us -> 16 us
  local copies, waits for them, and re-layouts: 8.17 us -> 11.3 us
    ppermute x10 -> x22, starting transfers between devices: 36.6 us -> 133 us  [moved(): return lax.ppermute(value, BX_BY, pairs)]
    psum x5, blocking collectives: 61.2 us -> 51.7 us  [over_axes(): value = lax.psum(value, axis)]
    ppermute x10 -> x22, waiting for transfers between devices: 35.3 us -> 39.9 us  [moved(): return lax.ppermute(value, BX_BY, pairs)]
    dot_general x30, matrix products: 12.5 us -> 16 us  [mat(): return jnp.matmul(left, right, precision=lax.Precision.HIGHEST)]
  transfers between devices with their start and end apart: 10 -> 22, of which waited for: 10 -> 5; matrix products, arithmetic and copies ran while one was open for 1% -> 1% of each run, Pallas kernels for 0% -> 0%
where the time goes in v4:
time: 277 us; the launch traced here: 275 us
  starting transfers between devices  133 us (48%)
  blocking collectives  51.7 us (19%)
  waiting for transfers between devices  39.9 us (14%)
  matrix products  16 us (6%)
  other arithmetic  14.1 us (5%)
  local copies, waits for them, and re-layouts  11.3 us (4%)
  between operations  8.87 us (3%)
    ppermute x22, starting transfers between devices, moved(): return lax.ppermute(value, BX_BY, pairs)  133 us
    psum x5, blocking collectives, over_axes(): value = lax.psum(value, axis)  51.7 us
    ppermute x22, waiting for transfers between devices, moved(): return lax.ppermute(value, BX_BY, pairs)  39.9 us
    dot_general x30, matrix products, mat(): return jnp.matmul(left, right, precision=lax.Precision.HIGHEST)  16 us
    add x2, other arithmetic, long_axis(): band = band + jnp.where(offset == node, column, 0.0)  8.36 us
  transfers between devices with their start and end apart: 22, of which 5 were waited for; matrix products, arithmetic and copies ran while one was open for 1% of the time, Pallas kernels for 0%

profile of v4, /device:TPU:1, one launch (start us, length us, event | category | flops | bytes accessed | tf_op | source)
XLA Modules:
  0.0 275.2 jit_solution(4715891009184297319)
XLA Ops:
  1.0 2.7 fusion
  3.7 5.7 %fusion.3 = (f32[385,4,128]{2,1,0:T(4,128)S(1)}, f32[385,4,128]{2,1,0:T(4,128)S(1)}, f32[385,4,128]{2,1,0:T(4,128)S(1)}, f32[385,4,128]{2,1,0:T(4,128)S(1)}) fusion(pred[385,4,128]{2,1,0:T(4,128)(4,1)S(1)} %get-tuple-element.23, pred[385,4,128]{2,1,0:T(4,128)(4,1)S(1)} %get-tuple-element.22, pred[385,4,128]{2,1,0:T(4,128)(4,1)S(1)} %get-tuple-element.21, ...), kind=kLoop, calls=%fused_computation.22 | loop fusion | flops 14981120 | bytes 4533760 | tf_op jit(solution)/shard_map/add | solution.py:168
  9.6 0.7 copy-done.1
  13.1 0.8 fusion.114
  14.1 0.8 convolution_add_fusion.6
  15.2 0.8 convolution_add_fusion.4
  16.0 11.5 %collective-permute-start = (f32[1,6,384]{2,1,0:T(8,128)S(1)}, f32[1,6,384]{2,1,0:T(8,128)S(1)}, u32[]{:S(2)}, u32[]{:S(2)}) collective-permute-start(f32[1,6,384]{2,1,0:T(8,128)S(1)} %slice.333), channel_id=1, source_target_pairs={{0,64},{1,65},{2,66},{3,67},{4,68},{5,69},{6,70},{7,71},{8,72},{9,... | collective-permute-start | bytes 27656 | tf_op jit(solution)/shard_map/ppermute | solution.py:238
  27.5 10.1 %collective-permute-start.1 = (f32[1,1,384]{2,1,0:T(1,128)S(1)}, f32[1,1,384]{2,1,0:T(1,128)S(1)}, u32[]{:S(2)}, u32[]{:S(2)}) collective-permute-start(f32[1,1,384]{2,1,0:T(1,128)S(1)} %slice.335), channel_id=1, source_target_pairs={{0,65},{1,66},{2,67},{3,68},{4,69},{5,70},{6,71},{7,72},{8,73},{9,... | collective-permute-start | bytes 4616 | tf_op jit(solution)/shard_map/ppermute | solution.py:238
  37.6 1.9 collective-permute-start.2
  39.9 0.8 collective-permute-done.2
  40.8 1.3 collective-permute-start.11
  42.1 1.9 collective-permute-start.10
  44.0 1.3 collective-permute-start.13
  45.6 10.1 %collective-permute-start.7 = (f32[3,6,384]{2,1,0:T(8,128)S(1)}, f32[3,6,384]{2,1,0:T(8,128)S(1)}, u32[]{:S(2)}, u32[]{:S(2)}) collective-permute-start(f32[3,6,384]{2,1,0:T(8,128)S(1)} %fusion.103), channel_id=1, source_target_pairs={{0,64},{1,65},{2,66},{3,67},{4,68},{5,69},{6,70},{7,71},{8,72},{9,... | collective-permute-start | bytes 82952 | tf_op jit(solution)/shard_map/ppermute | solution.py:238
  55.8 8.7 %collective-permute-start.6 = (f32[3,3,384]{2,1,0:T(4,128)S(1)}, f32[3,3,384]{2,1,0:T(4,128)S(1)}, u32[]{:S(2)}, u32[]{:S(2)}) collective-permute-start(f32[3,3,384]{2,1,0:T(4,128)S(1)} %slice.341), channel_id=1, source_target_pairs={{0,65},{1,66},{2,67},{3,68},{4,69},{5,70},{6,71},{7,72},{8,73},{9,... | collective-permute-start | bytes 41480 | tf_op jit(solution)/shard_map/ppermute | solution.py:238
  64.5 2.5 collective-permute-start.9
  67.0 5.8 %collective-permute-start.8 = (f32[3,1,384]{2,1,0:T(1,128)S(1)}, f32[3,1,384]{2,1,0:T(1,128)S(1)}, u32[]{:S(2)}, u32[]{:S(2)}) collective-permute-start(f32[3,1,384]{2,1,0:T(1,128)S(1)} %slice.342), channel_id=1, source_target_pairs={{1,64},{2,65},{3,66},{4,67},{5,68},{6,69},{7,70},{8,71},{9,72},{10... | collective-permute-start | bytes 13832 | tf_op jit(solution)/shard_map/ppermute | solution.py:238
  72.8 1.3 collective-permute-start.12
  74.4 0.9 slice.339
  75.3 9.6 %collective-permute-start.3 = (f32[7,4,4,4,1,1,128]{6,5,4,3,2,1,0:T(1,128)}, f32[7,4,4,4,1,1,128]{6,5,4,3,2,1,0:T(1,128)S(1)}, u32[]{:S(2)}, u32[]{:S(2)}) collective-permute-start(f32[7,4,4,4,1,1,128]{6,5,4,3,2,1,0:T(1,128)} %slice.339), channel_id=1, source_target_pairs={{0,65},{1,66},{2,67},{3,68},{4,69},{5,70},{6,71},{7,72},{8,73},{9,... | collective-permute-start | bytes 688136 | tf_op jit(solution)/shard_map/ppermute | solution.py:238
  85.0 1.9 collective-permute-start.5
  86.9 3.0 %collective-permute-start.4 = (f32[7,4,4,4,1,2,128]{6,5,4,3,2,1,0:T(2,128)S(1)}, f32[7,4,4,4,1,2,128]{6,5,4,3,2,1,0:T(2,128)}, u32[]{:S(2)}, u32[]{:S(2)}) collective-permute-start(f32[7,4,4,4,1,2,128]{6,5,4,3,2,1,0:T(2,128)S(1)} %convert_element_type.7), channel_id=1, source_target_pairs={{0,64},{1,65},{2,66},{3,67},{4,68},{5,69},{6,70},{7,71},{8,72},{9,... | collective-permute-start | bytes 1376264 | tf_op jit(solution)/shard_map/ppermute | solution.py:238
  90.0 1.1 fusion.115
  92.1 25.6 %collective-permute-done.4 = f32[7,4,4,4,1,2,128]{6,5,4,3,2,1,0:T(2,128)} collective-permute-done((f32[7,4,4,4,1,2,128]{6,5,4,3,2,1,0:T(2,128)S(1)}, f32[7,4,4,4,1,2,128]{6,5,4,3,2,1,0:T(2,128)}, u32[]{:S(2)}, u32[]{:S(2)}) %collective-permute-start.4) | collective-permute-done | bytes 458784 | tf_op jit(solution)/shard_map/ppermute | solution.py:238
  117.7 1.9 maximum_bitcast_fusion
  122.1 2.2 fusion.15
  124.3 0.9 reshape.77
  125.4 9.0 %collective-permute-start.15 = (f32[3,6,384]{2,1,0:T(8,128)S(1)}, f32[3,6,384]{2,1,0:T(8,128)S(1)}, u32[]{:S(2)}, u32[]{:S(2)}) collective-permute-start(f32[3,6,384]{2,1,0:T(8,128)S(1)} %fusion.110), channel_id=1, source_target_pairs={{0,64},{1,65},{2,66},{3,67},{4,68},{5,69},{6,70},{7,71},{8,72},{9,... | collective-permute-start | bytes 82952 | tf_op jit(solution)/shard_map/ppermute | solution.py:238
  134.4 1.3 collective-permute-start.19
  135.7 36.4 %collective-permute-start.14 = (f32[3,3,384]{2,1,0:T(4,128)S(1)}, f32[3,3,384]{2,1,0:T(4,128)S(1)}, u32[]{:S(2)}, u32[]{:S(2)}) collective-permute-start(f32[3,3,384]{2,1,0:T(4,128)S(1)} %slice.355), channel_id=1, source_target_pairs={{0,65},{1,66},{2,67},{3,68},{4,69},{5,70},{6,71},{7,72},{8,73},{9,... | collective-permute-start | bytes 41480 | tf_op jit(solution)/shard_map/ppermute | solution.py:238
  172.1 9.9 %collective-permute-start.17 = (f32[3,3,384]{2,1,0:T(4,128)S(1)}, f32[3,3,384]{2,1,0:T(4,128)S(1)}, u32[]{:S(2)}, u32[]{:S(2)}) collective-permute-start(f32[3,3,384]{2,1,0:T(4,128)S(1)} %slice.355), channel_id=1, source_target_pairs={{0,1},{1,2},{2,3},{3,4},{4,5},{5,6},{6,7},{7,8},{8,9},{9,10},{10,1... | collective-permute-start | bytes 41480 | tf_op jit(solution)/shard_map/ppermute | solution.py:238
  182.1 1.3 collective-permute-start.21
  183.4 8.4 %collective-permute-done.21 = f32[1,1,384]{2,1,0:T(1,128)S(1)} collective-permute-done((f32[1,1,384]{2,1,0:T(1,128)S(1)}, f32[1,1,384]{2,1,0:T(1,128)S(1)}, u32[]{:S(2)}, u32[]{:S(2)}) %collective-permute-start.21) | collective-permute-done | bytes 1568 | tf_op jit(solution)/shard_map/ppermute | solution.py:238
  191.8 1.3 collective-permute-start.16
  193.1 1.3 collective-permute-start.20
  194.4 1.9 collective-permute-start.18
  196.3 3.1 %collective-permute-done.18 = f32[3,1,384]{2,1,0:T(1,128)S(1)} collective-permute-done((f32[3,1,384]{2,1,0:T(1,128)S(1)}, f32[3,1,384]{2,1,0:T(1,128)S(1)}, u32[]{:S(2)}, u32[]{:S(2)}) %collective-permute-start.18) | collective-permute-done | bytes 4640 | tf_op jit(solution)/shard_map/ppermute | solution.py:238
  199.4 2.0 collective-permute-done.20
  202.1 2.0 fusion.117
  206.9 1.5 fusion.19
  208.4 1.7 multiply_reduce_fusion.2
  210.1 3.9 %stack.27 = f32[6]{0:T(128)S(1)} concatenate(f32[1]{0:T(128)} %bitcast.1, f32[1]{0:T(128)} %bitcast.3, f32[1]{0:T(128)} %bitcast.4, f32[1]{0:T(128)} %bitcast.5, f32[1]{0:T(128)} %bitcast.6, f32[1]{0:T(128)} %bitcast.7), dimensions={0} | concatenate | bytes 48 | tf_op jit(solution)/shard_map/stack | solution.py:364
  214.1 13.1 %psum.35 = f32[6]{0:T(128)S(1)} all-reduce(f32[6]{0:T(128)S(1)} %stack.27), channel_id=1, replica_groups=mesh['bx_0'=4,'bx_1'=3,'by_0'=4,'by_1'=8,'by_2'=2] {'bx_0'}, use_global_device_ids=true, to_apply=%region_6.7 | all-reduce | flops 6 | bytes 48 | tf_op jit(solution)/shard_map/psum | solution.py:27
  227.2 7.7 %psum.36 = f32[6]{0:T(128)S(1)} all-reduce(f32[6]{0:T(128)S(1)} %psum.35), channel_id=1, replica_groups=mesh['bx_0'=4,'bx_1'=3,'by_0'=4,'by_1'=8,'by_2'=2] {'bx_1'}, use_global_device_ids=true, to_apply=%region_7.8 | all-reduce | flops 6 | bytes 48 | tf_op jit(solution)/shard_map/psum | solution.py:27
  234.8 8.4 %psum.37 = f32[6]{0:T(128)S(1)} all-reduce(f32[6]{0:T(128)S(1)} %psum.36), channel_id=1, replica_groups=mesh['bx_0'=4,'bx_1'=3,'by_0'=4,'by_1'=8,'by_2'=2] {'by_0'}, use_global_device_ids=true, to_apply=%region_8.9 | all-reduce | flops 6 | bytes 48 | tf_op jit(solution)/shard_map/psum | solution.py:27
  243.2 12.8 %psum.38 = f32[6]{0:T(128)S(1)} all-reduce(f32[6]{0:T(128)S(1)} %psum.37), channel_id=1, replica_groups=mesh['bx_0'=4,'bx_1'=3,'by_0'=4,'by_1'=8,'by_2'=2] {'by_1'}, use_global_device_ids=true, to_apply=%region_9.10 | all-reduce | flops 6 | bytes 48 | tf_op jit(solution)/shard_map/psum | solution.py:27
  256.1 9.7 %psum.39 = f32[6]{0:T(128)S(1)} all-reduce(f32[6]{0:T(128)S(1)} %psum.38), channel_id=1, replica_groups=mesh['bx_0'=4,'bx_1'=3,'by_0'=4,'by_1'=8,'by_2'=2] {'by_2'}, use_global_device_ids=true, to_apply=%region_10.11 | all-reduce | flops 6 | bytes 48 | tf_op jit(solution)/shard_map/psum | solution.py:27
  273.5 1.6 multiply_subtract_fusion
  (126 shorter events, 12.2 us)
Async XLA Ops:
  9.3 0.9 copy-start.1
  10.5 0.7 copy-start.6
  11.7 0.7 copy-start.11
  11.7 0.9 copy-start.10
  11.7 1.2 copy-start.9
  11.9 2.0 copy-start.7
  12.0 3.0 %copy-start.8 = (f32[32,28]{1,0:T(8,128)S(1)}, f32[32,28]{1,0:T(8,128)}, u32[]{:S(2)}) copy-start(f32[32,28]{1,0:T(8,128)} %constant.145) | copy-start | bytes 10756
  16.0 23.8 %collective-permute-start = (f32[1,6,384]{2,1,0:T(8,128)S(1)}, f32[1,6,384]{2,1,0:T(8,128)S(1)}, u32[]{:S(2)}, u32[]{:S(2)}) collective-permute-start(f32[1,6,384]{2,1,0:T(8,128)S(1)} %slice.333), channel_id=1, source_target_pairs={{0,64},{1,65},{2,66},{3,67},{4,68},{5,69},{6,70},{7,71},{8,72},{9,... | collective-permute-start | bytes 27656 | tf_op jit(solution)/shard_map/ppermute | solution.py:238
  27.5 12.4 %collective-permute-start.1 = (f32[1,1,384]{2,1,0:T(1,128)S(1)}, f32[1,1,384]{2,1,0:T(1,128)S(1)}, u32[]{:S(2)}, u32[]{:S(2)}) collective-permute-start(f32[1,1,384]{2,1,0:T(1,128)S(1)} %slice.335), channel_id=1, source_target_pairs={{0,65},{1,66},{2,67},{3,68},{4,69},{5,70},{6,71},{7,72},{8,73},{9,... | collective-permute-start | bytes 4616 | tf_op jit(solution)/shard_map/ppermute | solution.py:238
  37.6 3.1 %collective-permute-start.2 = (f32[3,1,384]{2,1,0:T(1,128)S(1)}, f32[3,1,384]{2,1,0:T(1,128)S(1)}, u32[]{:S(2)}, u32[]{:S(2)}) collective-permute-start(f32[3,1,384]{2,1,0:T(1,128)S(1)} %slice.338), channel_id=1, source_target_pairs={{0,1},{1,2},{2,3},{3,4},{4,5},{5,6},{6,7},{7,8},{8,9},{9,10},{10,1... | collective-permute-start | bytes 13832 | tf_op jit(solution)/shard_map/ppermute | solution.py:238
  39.6 1.1 copy-start.5
  40.8 26.2 %collective-permute-start.11 = (f32[1,3,384]{2,1,0:T(4,128)S(1)}, f32[1,3,384]{2,1,0:T(4,128)S(1)}, u32[]{:S(2)}, u32[]{:S(2)}) collective-permute-start(f32[1,3,384]{2,1,0:T(4,128)S(1)} %slice.343), channel_id=1, source_target_pairs={{64,1},{65,2},{66,3},{67,4},{68,5},{69,6},{70,7},{71,8},{72,9},{73... | collective-permute-start | bytes 13832 | tf_op jit(solution)/shard_map/ppermute | solution.py:238
  42.1 30.7 %collective-permute-start.10 = (f32[3,1,384]{2,1,0:T(1,128)S(1)}, f32[3,1,384]{2,1,0:T(1,128)S(1)}, u32[]{:S(2)}, u32[]{:S(2)}) collective-permute-start(f32[3,1,384]{2,1,0:T(1,128)S(1)} %slice.342), channel_id=1, source_target_pairs={{1,0},{2,1},{3,2},{4,3},{5,4},{6,5},{7,6},{8,7},{9,8},{10,9},{11,1... | collective-permute-start | bytes 13832 | tf_op jit(solution)/shard_map/ppermute | solution.py:238
  44.0 20.5 %collective-permute-start.13 = (f32[1,1,384]{2,1,0:T(1,128)S(1)}, f32[1,1,384]{2,1,0:T(1,128)S(1)}, u32[]{:S(2)}, u32[]{:S(2)}) collective-permute-start(f32[1,1,384]{2,1,0:T(1,128)S(1)} %slice.345), channel_id=1, source_target_pairs={{65,0},{66,1},{67,2},{68,3},{69,4},{70,5},{71,6},{72,7},{73,8},{74... | collective-permute-start | bytes 4616 | tf_op jit(solution)/shard_map/ppermute | solution.py:238
  45.6 44.3 %collective-permute-start.7 = (f32[3,6,384]{2,1,0:T(8,128)S(1)}, f32[3,6,384]{2,1,0:T(8,128)S(1)}, u32[]{:S(2)}, u32[]{:S(2)}) collective-permute-start(f32[3,6,384]{2,1,0:T(8,128)S(1)} %fusion.103), channel_id=1, source_target_pairs={{0,64},{1,65},{2,66},{3,67},{4,68},{5,69},{6,70},{7,71},{8,72},{9,... | collective-permute-start | bytes 82952 | tf_op jit(solution)/shard_map/ppermute | solution.py:238
  55.8 31.2 %collective-permute-start.6 = (f32[3,3,384]{2,1,0:T(4,128)S(1)}, f32[3,3,384]{2,1,0:T(4,128)S(1)}, u32[]{:S(2)}, u32[]{:S(2)}) collective-permute-start(f32[3,3,384]{2,1,0:T(4,128)S(1)} %slice.341), channel_id=1, source_target_pairs={{0,65},{1,66},{2,67},{3,68},{4,69},{5,70},{6,71},{7,72},{8,73},{9,... | collective-permute-start | bytes 41480 | tf_op jit(solution)/shard_map/ppermute | solution.py:238
  64.5 25.4 %collective-permute-start.9 = (f32[3,3,384]{2,1,0:T(4,128)S(1)}, f32[3,3,384]{2,1,0:T(4,128)S(1)}, u32[]{:S(2)}, u32[]{:S(2)}) collective-permute-start(f32[3,3,384]{2,1,0:T(4,128)S(1)} %slice.341), channel_id=1, source_target_pairs={{0,1},{1,2},{2,3},{3,4},{4,5},{5,6},{6,7},{7,8},{8,9},{9,10},{10,1... | collective-permute-start | bytes 41480 | tf_op jit(solution)/shard_map/ppermute | solution.py:238
  67.0 8.4 %collective-permute-start.8 = (f32[3,1,384]{2,1,0:T(1,128)S(1)}, f32[3,1,384]{2,1,0:T(1,128)S(1)}, u32[]{:S(2)}, u32[]{:S(2)}) collective-permute-start(f32[3,1,384]{2,1,0:T(1,128)S(1)} %slice.342), channel_id=1, source_target_pairs={{1,64},{2,65},{3,66},{4,67},{5,68},{6,69},{7,70},{8,71},{9,72},{10... | collective-permute-start | bytes 13832 | tf_op jit(solution)/shard_map/ppermute | solution.py:238
  72.8 12.2 %collective-permute-start.12 = (f32[1,6,384]{2,1,0:T(8,128)S(1)}, f32[1,6,384]{2,1,0:T(8,128)S(1)}, u32[]{:S(2)}, u32[]{:S(2)}) collective-permute-start(f32[1,6,384]{2,1,0:T(8,128)S(1)} %slice.344), channel_id=1, source_target_pairs={{64,0},{65,1},{66,2},{67,3},{68,4},{69,5},{70,6},{71,7},{72,8},{73... | collective-permute-start | bytes 27656 | tf_op jit(solution)/shard_map/ppermute | solution.py:238
  74.4 16.7 %copy-start = (f32[96,70]{1,0:T(8,128)S(1)}, f32[96,70]{1,0:T(8,128)}, u32[]{:S(2)}) copy-start(f32[96,70]{1,0:T(8,128)} %constant.126.clone) | copy-start | bytes 80644
  75.3 16.1 %copy-start.2 = (f32[96,70]{1,0:T(8,128)S(1)}, f32[96,70]{1,0:T(8,128)}, u32[]{:S(2)}) copy-start(f32[96,70]{1,0:T(8,128)} %constant.128.clone) | copy-start | bytes 80644
  75.3 16.7 %collective-permute-start.3 = (f32[7,4,4,4,1,1,128]{6,5,4,3,2,1,0:T(1,128)}, f32[7,4,4,4,1,1,128]{6,5,4,3,2,1,0:T(1,128)S(1)}, u32[]{:S(2)}, u32[]{:S(2)}) collective-permute-start(f32[7,4,4,4,1,1,128]{6,5,4,3,2,1,0:T(1,128)} %slice.339), channel_id=1, source_target_pairs={{0,65},{1,66},{2,67},{3,68},{4,69},{5,70},{6,71},{7,72},{8,73},{9,... | collective-permute-start | bytes 688136 | tf_op jit(solution)/shard_map/ppermute | solution.py:238
  85.0 7.1 %collective-permute-start.5 = (f32[7,4,4,4,1,1,128]{6,5,4,3,2,1,0:T(1,128)}, f32[7,4,4,4,1,1,128]{6,5,4,3,2,1,0:T(1,128)S(1)}, u32[]{:S(2)}, u32[]{:S(2)}) collective-permute-start(f32[7,4,4,4,1,1,128]{6,5,4,3,2,1,0:T(1,128)} %slice.339), channel_id=1, source_target_pairs={{0,1},{1,2},{2,3},{3,4},{4,5},{5,6},{6,7},{7,8},{8,9},{9,10},{10,1... | collective-permute-start | bytes 688136 | tf_op jit(solution)/shard_map/ppermute | solution.py:238
  86.9 30.8 %collective-permute-start.4 = (f32[7,4,4,4,1,2,128]{6,5,4,3,2,1,0:T(2,128)S(1)}, f32[7,4,4,4,1,2,128]{6,5,4,3,2,1,0:T(2,128)}, u32[]{:S(2)}, u32[]{:S(2)}) collective-permute-start(f32[7,4,4,4,1,2,128]{6,5,4,3,2,1,0:T(2,128)S(1)} %convert_element_type.7), channel_id=1, source_target_pairs={{0,64},{1,65},{2,66},{3,67},{4,68},{5,69},{6,70},{7,71},{8,72},{9,... | collective-permute-start | bytes 1376264 | tf_op jit(solution)/shard_map/ppermute | solution.py:238
  90.0 1.8 copy-start.3
  125.3 76.1 %copy-start.4 = (f32[7,10,385]{2,1,0:T(8,128)}, f32[7,10,385]{2,1,0:T(8,128)S(1)}, u32[]{:S(2)}) copy-start(f32[7,10,385]{2,1,0:T(8,128)S(1)} %reshape.77) | copy-start | bytes 323404
  125.4 76.1 %collective-permute-start.15 = (f32[3,6,384]{2,1,0:T(8,128)S(1)}, f32[3,6,384]{2,1,0:T(8,128)S(1)}, u32[]{:S(2)}, u32[]{:S(2)}) collective-permute-start(f32[3,6,384]{2,1,0:T(8,128)S(1)} %fusion.110), channel_id=1, source_target_pairs={{0,64},{1,65},{2,66},{3,67},{4,68},{5,69},{6,70},{7,71},{8,72},{9,... | collective-permute-start | bytes 82952 | tf_op jit(solution)/shard_map/ppermute | solution.py:238
  134.4 58.7 %collective-permute-start.19 = (f32[1,3,384]{2,1,0:T(4,128)S(1)}, f32[1,3,384]{2,1,0:T(4,128)S(1)}, u32[]{:S(2)}, u32[]{:S(2)}) collective-permute-start(f32[1,3,384]{2,1,0:T(4,128)S(1)} %slice.357), channel_id=1, source_target_pairs={{64,1},{65,2},{66,3},{67,4},{68,5},{69,6},{70,7},{71,8},{72,9},{73... | collective-permute-start | bytes 13832 | tf_op jit(solution)/shard_map/ppermute | solution.py:238
  135.7 65.7 %collective-permute-start.14 = (f32[3,3,384]{2,1,0:T(4,128)S(1)}, f32[3,3,384]{2,1,0:T(4,128)S(1)}, u32[]{:S(2)}, u32[]{:S(2)}) collective-permute-start(f32[3,3,384]{2,1,0:T(4,128)S(1)} %slice.355), channel_id=1, source_target_pairs={{0,65},{1,66},{2,67},{3,68},{4,69},{5,70},{6,71},{7,72},{8,73},{9,... | collective-permute-start | bytes 41480 | tf_op jit(solution)/shard_map/ppermute | solution.py:238
  172.1 29.3 %collective-permute-start.17 = (f32[3,3,384]{2,1,0:T(4,128)S(1)}, f32[3,3,384]{2,1,0:T(4,128)S(1)}, u32[]{:S(2)}, u32[]{:S(2)}) collective-permute-start(f32[3,3,384]{2,1,0:T(4,128)S(1)} %slice.355), channel_id=1, source_target_pairs={{0,1},{1,2},{2,3},{3,4},{4,5},{5,6},{6,7},{7,8},{8,9},{9,10},{10,1... | collective-permute-start | bytes 41480 | tf_op jit(solution)/shard_map/ppermute | solution.py:238
  182.1 9.7 %collective-permute-start.21 = (f32[1,1,384]{2,1,0:T(1,128)S(1)}, f32[1,1,384]{2,1,0:T(1,128)S(1)}, u32[]{:S(2)}, u32[]{:S(2)}) collective-permute-start(f32[1,1,384]{2,1,0:T(1,128)S(1)} %slice.359), channel_id=1, source_target_pairs={{65,0},{66,1},{67,2},{68,3},{69,4},{70,5},{71,6},{72,7},{73,8},{74... | collective-permute-start | bytes 4616 | tf_op jit(solution)/shard_map/ppermute | solution.py:238
  191.8 2.6 collective-permute-start.16
  193.1 8.3 %collective-permute-start.20 = (f32[1,6,384]{2,1,0:T(8,128)S(1)}, f32[1,6,384]{2,1,0:T(8,128)S(1)}, u32[]{:S(2)}, u32[]{:S(2)}) collective-permute-start(f32[1,6,384]{2,1,0:T(8,128)S(1)} %slice.358), channel_id=1, source_target_pairs={{64,0},{65,1},{66,2},{67,3},{68,4},{69,5},{70,6},{71,7},{72,8},{73... | collective-permute-start | bytes 27656 | tf_op jit(solution)/shard_map/ppermute | solution.py:238
  194.4 5.0 %collective-permute-start.18 = (f32[3,1,384]{2,1,0:T(1,128)S(1)}, f32[3,1,384]{2,1,0:T(1,128)S(1)}, u32[]{:S(2)}, u32[]{:S(2)}) collective-permute-start(f32[3,1,384]{2,1,0:T(1,128)S(1)} %slice.356), channel_id=1, source_target_pairs={{1,0},{2,1},{3,2},{4,3},{5,4},{6,5},{7,6},{8,7},{9,8},{10,9},{11,1... | collective-permute-start | bytes 13832 | tf_op jit(solution)/shard_map/ppermute | solution.py:238

commit v5 on v3

--- a/solution.py
+++ b/solution.py
@@ -226,6 +226,20 @@
     return total.reshape(3 * count_x + 1, 3 * count_y + 1, 3 * count_z + 1)
 
 
+def surround(dof_field):
+    rows_x, rows_y = dof_field.shape[:2]
+    wide = jnp.concatenate(
+        [lower_x(dof_field[rows_x - 3 :]), dof_field, upper_x(dof_field[0:1])], 0
+    )
+    return jnp.concatenate([lower_y(wide[:, rows_y - 3 :]), wide, upper_y(wide[:, 0:1])], 1)
+
+
+def ghost_points(pointwise):
+    points = pointwise.astype(jnp.float32)
+    points = jnp.concatenate([lower_x(points[:, :, :, :, -1:]), points], 4)
+    return jnp.concatenate([lower_y(points[:, :, :, :, :, -1:]), points], 5)
+
+
 def upper_x(plane):
     return shifted(plane, BX, -1)
 
@@ -280,12 +294,12 @@
     counts = pointwise.shape[4:]
     coeffs = point_layout(pointwise)
     diagonal = collect(band_diagonal(coeffs, counts), rows_x, rows_y, rows_z)
+    wide_counts = (counts[0] + 1, counts[1] + 1, counts[2])
+    wide_coeffs = point_layout(ghost_points(pointwise))
 
     def operator(dof_field):
-        return (
-            collect(band_operator(pad_top(widen(dof_field)), coeffs, counts), rows_x, rows_y, rows_z)
-            * interior
-        )
+        wide = band_operator(pad_top(surround(dof_field)), wide_coeffs, wide_counts)
+        return wide[3 : 3 + rows_x, 3 : 3 + rows_y, :rows_z] * interior
 
     def local_dot(left, right):
         return jnp.sum(left * right)

time: 174 us -> 218 us (1.25)
  starting transfers between devices: 36.6 us -> 88.2 us
  waiting for transfers between devices: 35.3 us -> 26.4 us
  blocking collectives: 61.2 us -> 54 us
  matrix products: 12.5 us -> 16 us
  other arithmetic: 10.4 us -> 13.2 us
    ppermute x10 -> x12, starting transfers between devices: 36.6 us -> 88.2 us  [shifted(): lax.ppermute(value, axis, [(source, source + steps) for source in range(i...]
    ppermute x10 -> x12, waiting for transfers between devices: 35.3 us -> 26.4 us  [shifted(): lax.ppermute(value, axis, [(source, source + steps) for source in range(i...]
    psum x5, blocking collectives: 61.2 us -> 54 us  [over_axes(): value = lax.psum(value, axis)]
    dot_general x30, matrix products: 12.5 us -> 16 us  [mat(): return jnp.matmul(left, right, precision=lax.Precision.HIGHEST)]
  transfers between devices with their start and end apart: 10 -> 12, of which waited for: 10 -> 6; matrix products, arithmetic and copies ran while one was open for 1% -> 1% of each run, Pallas kernels for 0% -> 0%
where the time goes in v5:
time: 218 us; the launch traced here: 217 us
  starting transfers between devices  88.2 us (40%)
  blocking collectives  54 us (25%)
  waiting for transfers between devices  26.4 us (12%)
  matrix products  16 us (7%)
  other arithmetic  13.2 us (6%)
  local copies, waits for them, and re-layouts  10.2 us (5%)
  between operations  8.98 us (4%)
    ppermute x12, starting transfers between devices, shifted(): lax.ppermute(value, axis, [(source, source + steps) for source in range(i...  88.2 us
    psum x5, blocking collectives, over_axes(): value = lax.psum(value, axis)  54 us
    ppermute x12, waiting for transfers between devices, shifted(): lax.ppermute(value, axis, [(source, source + steps) for source in range(i...  26.4 us
    dot_general x30, matrix products, mat(): return jnp.matmul(left, right, precision=lax.Precision.HIGHEST)  16 us
    add x2, other arithmetic, long_axis(): band = band + jnp.where(offset == node, column, 0.0)  8.36 us
  transfers between devices with their start and end apart: 12, of which 6 were waited for; matrix products, arithmetic and copies ran while one was open for 1% of the time, Pallas kernels for 0%

profile of v5, /device:TPU:1, one launch (start us, length us, event | category | flops | bytes accessed | tf_op | source)
XLA Modules:
  0.0 217.0 jit_solution(11073992379863678344)
XLA Ops:
  1.0 2.7 %fusion = (f32[385,4,128]{2,1,0:T(4,128)S(1)}, pred[385,4,128]{2,1,0:T(4,128)(4,1)S(1)}, pred[385,4,128]{2,1,0:T(4,128)(4,1)S(1)}, pred[385,4,128]{2,1,0:T(4,128...) fusion(s32[385,4,128]{2,1,0:T(4,128)S(1)} %iota.37, ...), kind=kLoop, calls=%fused_computation.15 | loop fusion | flops 5913600 | bytes 4533760 | tf_op jit(solution)/shard_map/add | solution.py:168
  3.7 5.7 %fusion.3 = (f32[385,4,128]{2,1,0:T(4,128)S(1)}, f32[385,4,128]{2,1,0:T(4,128)S(1)}, f32[385,4,128]{2,1,0:T(4,128)S(1)}, f32[385,4,128]{2,1,0:T(4,128)S(1)}) fusion(pred[385,4,128]{2,1,0:T(4,128)(4,1)S(1)} %get-tuple-element.23, pred[385,4,128]{2,1,0:T(4,128)(4,1)S(1)} %get-tuple-element.22, pred[385,4,128]{2,1,0:T(4,128)(4,1)S(1)} %get-tuple-element.21, ...), kind=kLoop, calls=%fused_computation.22 | loop fusion | flops 14981120 | bytes 4533760 | tf_op jit(solution)/shard_map/add | solution.py:168
  9.6 0.7 copy-done.1
  10.8 0.5 copy-done.6
  12.0 0.4 copy-done.11
  13.1 0.8 fusion.115
  14.1 0.8 convolution_add_fusion.6
  15.2 0.8 convolution_add_fusion.4
  16.0 4.6 %collective-permute-start = (f32[4,1,384]{2,1,0:T(1,128)S(1)}, f32[4,1,384]{2,1,0:T(1,128)S(1)}, u32[]{:S(2)}, u32[]{:S(2)}) collective-permute-start(f32[4,1,384]{2,1,0:T(1,128)S(1)} %slice.301), channel_id=1, source_target_pairs={{0,1},{1,2},{2,3},{3,4},{4,5},{5,6},{6,7},{7,8},{8,9},{9,10},{10,1... | collective-permute-start | bytes 18440 | tf_op jit(solution)/shard_map/ppermute | solution.py:22
  20.7 10.7 %collective-permute-start.2 = (f32[7,4,4,4,1,2,128]{6,3,5,4,2,1,0:T(4,128)S(1)}, f32[7,4,4,4,1,2,128]{6,3,5,4,2,1,0:T(4,128)S(1)}, u32[]{:S(2)}, u32[]{:S(2)}) collective-permute-start(f32[7,4,4,4,1,2,128]{6,3,5,4,2,1,0:T(4,128)S(1)} %copy_convert_fusion), channel_id=1, source_target_pairs={{0,64},{64,128},{128,192},{192,256},{256,320},{320,384},{384,448},... | collective-permute-start | bytes 1376264 | tf_op jit(solution)/shard_map/ppermute | solution.py:22
  31.5 8.2 %collective-permute-start.1 = (f32[1,6,384]{2,1,0:T(8,128)S(1)}, f32[1,6,384]{2,1,0:T(8,128)S(1)}, u32[]{:S(2)}, u32[]{:S(2)}) collective-permute-start(f32[1,6,384]{2,1,0:T(8,128)S(1)} %pad_maximum_fusion.3), channel_id=1, source_target_pairs={{0,64},{64,128},{128,192},{192,256},{256,320},{320,384},{384,448},... | collective-permute-start | bytes 27656 | tf_op jit(solution)/shard_map/ppermute | solution.py:22
  40.0 1.5 collective-permute-done.1
  41.7 38.3 %collective-permute-start.4 = (f32[3,6,384]{2,1,0:T(8,128)S(1)}, f32[3,6,384]{2,1,0:T(8,128)S(1)}, u32[]{:S(2)}, u32[]{:S(2)}) collective-permute-start(f32[3,6,384]{2,1,0:T(8,128)S(1)} %fusion.104), channel_id=1, source_target_pairs={{0,64},{64,128},{128,192},{192,256},{256,320},{320,384},{384,448},... | collective-permute-start | bytes 82952 | tf_op jit(solution)/shard_map/ppermute | solution.py:22
  80.0 1.3 collective-permute-start.5
  81.5 7.2 %collective-permute-done.5 = f32[1,6,384]{2,1,0:T(8,128)S(1)} collective-permute-done((f32[1,6,384]{2,1,0:T(8,128)S(1)}, f32[1,6,384]{2,1,0:T(8,128)S(1)}, u32[]{:S(2)}, u32[]{:S(2)}) %collective-permute-start.5) | collective-permute-done | bytes 9248 | tf_op jit(solution)/shard_map/ppermute | solution.py:22
  88.8 4.5 %collective-permute-start.6 = (f32[7,3,384]{2,1,0:T(4,128)S(1)}, f32[7,3,384]{2,1,0:T(4,128)S(1)}, u32[]{:S(2)}, u32[]{:S(2)}) collective-permute-start(f32[7,3,384]{2,1,0:T(4,128)S(1)} %slice.305), channel_id=1, source_target_pairs={{0,1},{1,2},{2,3},{3,4},{4,5},{5,6},{6,7},{7,8},{8,9},{9,10},{10,1... | collective-permute-start | bytes 96776 | tf_op jit(solution)/shard_map/ppermute | solution.py:22
  93.4 1.9 collective-permute-start.7
  95.4 3.0 %collective-permute-done.7 = f32[7,1,384]{2,1,0:T(1,128)S(1)} collective-permute-done((f32[7,1,384]{2,1,0:T(1,128)S(1)}, f32[7,1,384]{2,1,0:T(1,128)S(1)}, u32[]{:S(2)}, u32[]{:S(2)}) %collective-permute-start.7) | collective-permute-done | bytes 10784 | tf_op jit(solution)/shard_map/ppermute | solution.py:22
  98.5 1.1 fusion.116
  100.0 2.1 collective-permute-start.3
  102.8 4.6 %collective-permute-done.3 = f32[7,4,4,4,2,1,128]{6,3,5,4,2,1,0:T(4,128)S(1)} collective-permute-done((f32[7,4,4,4,2,1,128]{6,3,5,4,2,1,0:T(4,128)S(1)}, f32[7,4,4,4,2,1,128]{6,3,5,4,2,1,0:T(4,128)S(1)}, u32[]{:S(2)}, u32[]{:S(2)}) %collective-permute-start.3) | collective-permute-done | bytes 458784 | tf_op jit(solution)/shard_map/ppermute | solution.py:22
  108.8 0.4 fusion.29
  109.2 0.4 convolution_add_fusion.3
  109.6 0.4 convolution_add_fusion.2
  110.0 2.2 %fusion.15 = f32[70,385]{1,0:T(8,128)} fusion(f32[385,1024]{1,0:T(8,128)S(1)} %constant_dynamic-update-slice_fusion, f32[70,512]{1,0:T(8,128)S(1)} %fusion.29, f32[70,512]{1,0:T(8,128)S(1)} %convolution_add_fusion.2), kind=kOutput, calls=%fused_computation.57 | convolution fusion | flops 331233280 | bytes 1971480 | tf_op jit(solution)/shard_map/dot_general | solution.py:173
  112.2 0.9 reshape.77
  113.2 0.7 fusion.111
  113.9 7.5 %collective-permute-start.8 = (f32[3,6,384]{2,1,0:T(8,128)S(1)}, f32[3,6,384]{2,1,0:T(8,128)S(1)}, u32[]{:S(2)}, u32[]{:S(2)}) collective-permute-start(f32[3,6,384]{2,1,0:T(8,128)S(1)} %fusion.111), channel_id=1, source_target_pairs={{0,64},{64,128},{128,192},{192,256},{256,320},{320,384},{384,448},... | collective-permute-start | bytes 82952 | tf_op jit(solution)/shard_map/ppermute | solution.py:22
  121.5 1.3 collective-permute-start.9
  122.8 7.0 %collective-permute-done.9 = f32[1,6,384]{2,1,0:T(8,128)S(1)} collective-permute-done((f32[1,6,384]{2,1,0:T(8,128)S(1)}, f32[1,6,384]{2,1,0:T(8,128)S(1)}, u32[]{:S(2)}, u32[]{:S(2)}) %collective-permute-start.9) | collective-permute-done | bytes 9248 | tf_op jit(solution)/shard_map/ppermute | solution.py:22
  129.9 5.8 %collective-permute-start.10 = (f32[7,3,384]{2,1,0:T(4,128)S(1)}, f32[7,3,384]{2,1,0:T(4,128)S(1)}, u32[]{:S(2)}, u32[]{:S(2)}) collective-permute-start(f32[7,3,384]{2,1,0:T(4,128)S(1)} %slice.316), channel_id=1, source_target_pairs={{0,1},{1,2},{2,3},{3,4},{4,5},{5,6},{6,7},{7,8},{8,9},{9,10},{10,1... | collective-permute-start | bytes 96776 | tf_op jit(solution)/shard_map/ppermute | solution.py:22
  135.7 1.9 collective-permute-start.11
  137.7 3.1 %collective-permute-done.11 = f32[7,1,384]{2,1,0:T(1,128)S(1)} collective-permute-done((f32[7,1,384]{2,1,0:T(1,128)S(1)}, f32[7,1,384]{2,1,0:T(1,128)S(1)}, u32[]{:S(2)}, u32[]{:S(2)}) %collective-permute-start.11) | collective-permute-done | bytes 10784 | tf_op jit(solution)/shard_map/ppermute | solution.py:22
  140.8 0.7 reshape.78
  141.5 2.0 fusion.118
  145.1 0.4 fusion.32
  145.4 0.4 convolution_add_fusion.1
  145.8 0.4 convolution_add_fusion
  146.2 1.5 fusion.19
  147.8 1.7 multiply_reduce_fusion.2
  149.5 4.0 %stack.27 = f32[6]{0:T(128)S(1)} concatenate(f32[1]{0:T(128)} %bitcast.1, f32[1]{0:T(128)} %bitcast.3, f32[1]{0:T(128)} %bitcast.4, f32[1]{0:T(128)} %bitcast.5, f32[1]{0:T(128)} %bitcast.6, f32[1]{0:T(128)} %bitcast.7), dimensions={0} | concatenate | bytes 48 | tf_op jit(solution)/shard_map/stack | solution.py:320
  153.5 9.8 %psum.35 = f32[6]{0:T(128)S(1)} all-reduce(f32[6]{0:T(128)S(1)} %stack.27), channel_id=1, replica_groups=mesh['bx_0'=4,'bx_1'=3,'by_0'=4,'by_1'=8,'by_2'=2] {'bx_0'}, use_global_device_ids=true, to_apply=%region_6.7 | all-reduce | flops 6 | bytes 48 | tf_op jit(solution)/shard_map/psum | solution.py:27
  163.3 7.7 %psum.36 = f32[6]{0:T(128)S(1)} all-reduce(f32[6]{0:T(128)S(1)} %psum.35), channel_id=1, replica_groups=mesh['bx_0'=4,'bx_1'=3,'by_0'=4,'by_1'=8,'by_2'=2] {'bx_1'}, use_global_device_ids=true, to_apply=%region_7.8 | all-reduce | flops 6 | bytes 48 | tf_op jit(solution)/shard_map/psum | solution.py:27
  171.0 10.7 %psum.37 = f32[6]{0:T(128)S(1)} all-reduce(f32[6]{0:T(128)S(1)} %psum.36), channel_id=1, replica_groups=mesh['bx_0'=4,'bx_1'=3,'by_0'=4,'by_1'=8,'by_2'=2] {'by_0'}, use_global_device_ids=true, to_apply=%region_8.9 | all-reduce | flops 6 | bytes 48 | tf_op jit(solution)/shard_map/psum | solution.py:27
  181.7 15.5 %psum.38 = f32[6]{0:T(128)S(1)} all-reduce(f32[6]{0:T(128)S(1)} %psum.37), channel_id=1, replica_groups=mesh['bx_0'=4,'bx_1'=3,'by_0'=4,'by_1'=8,'by_2'=2] {'by_1'}, use_global_device_ids=true, to_apply=%region_9.10 | all-reduce | flops 6 | bytes 48 | tf_op jit(solution)/shard_map/psum | solution.py:27
  197.1 10.4 %psum.39 = f32[6]{0:T(128)S(1)} all-reduce(f32[6]{0:T(128)S(1)} %psum.38), channel_id=1, replica_groups=mesh['bx_0'=4,'bx_1'=3,'by_0'=4,'by_1'=8,'by_2'=2] {'by_2'}, use_global_device_ids=true, to_apply=%region_10.11 | all-reduce | flops 6 | bytes 48 | tf_op jit(solution)/shard_map/psum | solution.py:27
  207.5 0.7 fusion.114
  215.4 1.6 multiply_subtract_fusion
  (127 shorter events, 7.7 us)
Async XLA Ops:
  9.3 0.9 copy-start.1
  10.5 0.7 copy-start.6
  11.7 0.7 copy-start.11
  11.7 0.9 copy-start.10
  11.7 1.2 copy-start.9
  11.9 2.0 copy-start.7
  12.0 3.0 %copy-start.8 = (f32[32,28]{1,0:T(8,128)S(1)}, f32[32,28]{1,0:T(8,128)}, u32[]{:S(2)}) copy-start(f32[32,28]{1,0:T(8,128)} %constant.145) | copy-start | bytes 10756
  16.0 15.5 %collective-permute-start = (f32[4,1,384]{2,1,0:T(1,128)S(1)}, f32[4,1,384]{2,1,0:T(1,128)S(1)}, u32[]{:S(2)}, u32[]{:S(2)}) collective-permute-start(f32[4,1,384]{2,1,0:T(1,128)S(1)} %slice.301), channel_id=1, source_target_pairs={{0,1},{1,2},{2,3},{3,4},{4,5},{5,6},{6,7},{7,8},{8,9},{9,10},{10,1... | collective-permute-start | bytes 18440 | tf_op jit(solution)/shard_map/ppermute | solution.py:22
  20.7 79.2 %collective-permute-start.2 = (f32[7,4,4,4,1,2,128]{6,3,5,4,2,1,0:T(4,128)S(1)}, f32[7,4,4,4,1,2,128]{6,3,5,4,2,1,0:T(4,128)S(1)}, u32[]{:S(2)}, u32[]{:S(2)}) collective-permute-start(f32[7,4,4,4,1,2,128]{6,3,5,4,2,1,0:T(4,128)S(1)} %copy_convert_fusion), channel_id=1, source_target_pairs={{0,64},{64,128},{128,192},{192,256},{256,320},{320,384},{384,448},... | collective-permute-start | bytes 1376264 | tf_op jit(solution)/shard_map/ppermute | solution.py:22
  31.4 10.1 %copy-start.12 = (pred[6]{0:T(512)(128)(4,1)}, pred[6]{0:T(512)(128)(4,1)S(1)}, u32[]{:S(2)}) copy-start(pred[6]{0:T(512)(128)(4,1)S(1)} %get-tuple-element.50) | copy-start | bytes 22
  31.4 10.1 %copy-start.14 = (pred[6]{0:T(512)(128)(4,1)}, pred[6]{0:T(512)(128)(4,1)S(1)}, u32[]{:S(2)}) copy-start(pred[6]{0:T(512)(128)(4,1)S(1)} %get-tuple-element.51) | copy-start | bytes 22
  31.4 10.1 %copy-start.17 = (pred[3]{0:T(512)(128)(4,1)}, pred[3]{0:T(512)(128)(4,1)S(1)}, u32[]{:S(2)}) copy-start(pred[3]{0:T(512)(128)(4,1)S(1)} %get-tuple-element.52) | copy-start | bytes 13
  31.5 10.1 %copy-start.20 = (pred[3]{0:T(512)(128)(4,1)}, pred[3]{0:T(512)(128)(4,1)S(1)}, u32[]{:S(2)}) copy-start(pred[3]{0:T(512)(128)(4,1)S(1)} %get-tuple-element.53) | copy-start | bytes 13
  31.5 10.0 %collective-permute-start.1 = (f32[1,6,384]{2,1,0:T(8,128)S(1)}, f32[1,6,384]{2,1,0:T(8,128)S(1)}, u32[]{:S(2)}, u32[]{:S(2)}) collective-permute-start(f32[1,6,384]{2,1,0:T(8,128)S(1)} %pad_maximum_fusion.3), channel_id=1, source_target_pairs={{0,64},{64,128},{128,192},{192,256},{256,320},{320,384},{384,448},... | collective-permute-start | bytes 27656 | tf_op jit(solution)/shard_map/ppermute | solution.py:22
  39.7 1.8 copy-start.23
  39.8 1.8 copy-start.5
  41.7 47.1 %collective-permute-start.4 = (f32[3,6,384]{2,1,0:T(8,128)S(1)}, f32[3,6,384]{2,1,0:T(8,128)S(1)}, u32[]{:S(2)}, u32[]{:S(2)}) collective-permute-start(f32[3,6,384]{2,1,0:T(8,128)S(1)} %fusion.104), channel_id=1, source_target_pairs={{0,64},{64,128},{128,192},{192,256},{256,320},{320,384},{384,448},... | collective-permute-start | bytes 82952 | tf_op jit(solution)/shard_map/ppermute | solution.py:22
  80.0 8.8 %collective-permute-start.5 = (f32[1,6,384]{2,1,0:T(8,128)S(1)}, f32[1,6,384]{2,1,0:T(8,128)S(1)}, u32[]{:S(2)}, u32[]{:S(2)}) collective-permute-start(f32[1,6,384]{2,1,0:T(8,128)S(1)} %slice.304), channel_id=1, source_target_pairs={{64,0},{128,64},{192,128},{256,192},{320,256},{384,320},{448,384},... | collective-permute-start | bytes 27656 | tf_op jit(solution)/shard_map/ppermute | solution.py:22
  88.8 9.5 %collective-permute-start.6 = (f32[7,3,384]{2,1,0:T(4,128)S(1)}, f32[7,3,384]{2,1,0:T(4,128)S(1)}, u32[]{:S(2)}, u32[]{:S(2)}) collective-permute-start(f32[7,3,384]{2,1,0:T(4,128)S(1)} %slice.305), channel_id=1, source_target_pairs={{0,1},{1,2},{2,3},{3,4},{4,5},{5,6},{6,7},{7,8},{8,9},{9,10},{10,1... | collective-permute-start | bytes 96776 | tf_op jit(solution)/shard_map/ppermute | solution.py:22
  93.4 5.0 %collective-permute-start.7 = (f32[7,1,384]{2,1,0:T(1,128)S(1)}, f32[7,1,384]{2,1,0:T(1,128)S(1)}, u32[]{:S(2)}, u32[]{:S(2)}) collective-permute-start(f32[7,1,384]{2,1,0:T(1,128)S(1)} %pad_maximum_fusion.5), channel_id=1, source_target_pairs={{1,0},{2,1},{3,2},{4,3},{5,4},{6,5},{7,6},{8,7},{9,8},{10,9},{11,1... | collective-permute-start | bytes 32264 | tf_op jit(solution)/shard_map/ppermute | solution.py:22
  95.4 4.2 %copy-start = (f32[96,70]{1,0:T(8,128)S(1)}, f32[96,70]{1,0:T(8,128)}, u32[]{:S(2)}) copy-start(f32[96,70]{1,0:T(8,128)} %constant.126.clone) | copy-start | bytes 80644
  98.4 3.7 %copy-start.2 = (f32[96,70]{1,0:T(8,128)S(1)}, f32[96,70]{1,0:T(8,128)}, u32[]{:S(2)}) copy-start(f32[96,70]{1,0:T(8,128)} %constant.128.clone) | copy-start | bytes 80644
  98.4 4.0 %copy-start.3 = (f32[96,70]{1,0:T(8,128)S(1)}, f32[96,70]{1,0:T(8,128)}, u32[]{:S(2)}) copy-start(f32[96,70]{1,0:T(8,128)} %constant.127.clone) | copy-start | bytes 80644
  100.0 7.4 %collective-permute-start.3 = (f32[7,4,4,4,2,1,128]{6,3,5,4,2,1,0:T(4,128)S(1)}, f32[7,4,4,4,2,1,128]{6,3,5,4,2,1,0:T(4,128)S(1)}, u32[]{:S(2)}, u32[]{:S(2)}) collective-permute-start(f32[7,4,4,4,2,1,128]{6,3,5,4,2,1,0:T(4,128)S(1)} %pad_maximum_fusion), channel_id=1, source_target_pairs={{0,1},{1,2},{2,3},{3,4},{4,5},{5,6},{6,7},{7,8},{8,9},{9,10},{10,1... | collective-permute-start | bytes 1376264 | tf_op jit(solution)/shard_map/ppermute | solution.py:22
  109.6 3.6 %copy-start.13 = (pred[6]{0:T(512)(128)(4,1)S(1)}, pred[6]{0:T(512)(128)(4,1)}, u32[]{:S(2)}) copy-start(pred[6]{0:T(512)(128)(4,1)} %copy-done.12) | copy-start | bytes 22
  109.6 3.6 %copy-start.15 = (pred[6]{0:T(512)(128)(4,1)S(1)}, pred[6]{0:T(512)(128)(4,1)}, u32[]{:S(2)}) copy-start(pred[6]{0:T(512)(128)(4,1)} %copy-done.14) | copy-start | bytes 22
  109.6 3.6 %copy-start.18 = (pred[3]{0:T(512)(128)(4,1)S(1)}, pred[3]{0:T(512)(128)(4,1)}, u32[]{:S(2)}) copy-start(pred[3]{0:T(512)(128)(4,1)} %copy-done.17) | copy-start | bytes 13
  109.6 3.6 %copy-start.21 = (pred[3]{0:T(512)(128)(4,1)S(1)}, pred[3]{0:T(512)(128)(4,1)}, u32[]{:S(2)}) copy-start(pred[3]{0:T(512)(128)(4,1)} %copy-done.20) | copy-start | bytes 13
  113.2 27.6 %copy-start.4 = (f32[7,10,385]{2,1,0:T(8,128)}, f32[7,10,385]{2,1,0:T(8,128)S(1)}, u32[]{:S(2)}) copy-start(f32[7,10,385]{2,1,0:T(8,128)S(1)} %reshape.77) | copy-start | bytes 323404
  113.9 15.9 %collective-permute-start.8 = (f32[3,6,384]{2,1,0:T(8,128)S(1)}, f32[3,6,384]{2,1,0:T(8,128)S(1)}, u32[]{:S(2)}, u32[]{:S(2)}) collective-permute-start(f32[3,6,384]{2,1,0:T(8,128)S(1)} %fusion.111), channel_id=1, source_target_pairs={{0,64},{64,128},{128,192},{192,256},{256,320},{320,384},{384,448},... | collective-permute-start | bytes 82952 | tf_op jit(solution)/shard_map/ppermute | solution.py:22
  121.5 8.3 %collective-permute-start.9 = (f32[1,6,384]{2,1,0:T(8,128)S(1)}, f32[1,6,384]{2,1,0:T(8,128)S(1)}, u32[]{:S(2)}, u32[]{:S(2)}) collective-permute-start(f32[1,6,384]{2,1,0:T(8,128)S(1)} %slice.315), channel_id=1, source_target_pairs={{64,0},{128,64},{192,128},{256,192},{320,256},{384,320},{448,384},... | collective-permute-start | bytes 27656 | tf_op jit(solution)/shard_map/ppermute | solution.py:22
  129.9 10.8 %collective-permute-start.10 = (f32[7,3,384]{2,1,0:T(4,128)S(1)}, f32[7,3,384]{2,1,0:T(4,128)S(1)}, u32[]{:S(2)}, u32[]{:S(2)}) collective-permute-start(f32[7,3,384]{2,1,0:T(4,128)S(1)} %slice.316), channel_id=1, source_target_pairs={{0,1},{1,2},{2,3},{3,4},{4,5},{5,6},{6,7},{7,8},{8,9},{9,10},{10,1... | collective-permute-start | bytes 96776 | tf_op jit(solution)/shard_map/ppermute | solution.py:22
  135.7 5.0 %collective-permute-start.11 = (f32[7,1,384]{2,1,0:T(1,128)S(1)}, f32[7,1,384]{2,1,0:T(1,128)S(1)}, u32[]{:S(2)}, u32[]{:S(2)}) collective-permute-start(f32[7,1,384]{2,1,0:T(1,128)S(1)} %pad_maximum_fusion.4), channel_id=1, source_target_pairs={{1,0},{2,1},{3,2},{4,3},{5,4},{6,5},{7,6},{8,7},{9,8},{10,9},{11,1... | collective-permute-start | bytes 32264 | tf_op jit(solution)/shard_map/ppermute | solution.py:22
  145.8 2.0 copy-start.16
  145.8 2.0 copy-start.19
  145.8 2.0 copy-start.22
  145.8 2.0 copy-start.24

commit v6 on v3

--- a/solution.py
+++ b/solution.py
@@ -157,16 +157,12 @@
 
 
 def long_axis(table, count):
-    place = lax.broadcasted_iota(jnp.int32, (3 * count + 1, 4, count), 0)
-    first = lax.broadcasted_iota(jnp.int32, (3 * count + 1, 4, count), 2) * 3
-    point = lax.broadcasted_iota(jnp.int32, (3 * count + 1, 4, count), 1)
-    place, first, point = lax.optimization_barrier((place, first, point))
-    offset = place - first
-    band = jnp.zeros(place.shape, jnp.float32)
-    for node in range(4):
-        column = jnp.asarray(table[:, node], jnp.float32)[point]
-        band = band + jnp.where(offset == node, column, 0.0)
-    return band.reshape(3 * count + 1, 4 * count)
+    length = 3 * count + 1
+    rows = jnp.asarray(table, jnp.float32)[:, None, :] + jnp.zeros((4, count, 4), jnp.float32)
+    rows = lax.optimization_barrier(rows)
+    rows = jnp.pad(rows, ((0, 0), (0, 0), (0, length - 1)))
+    band = rows.reshape(4, count * (length + 3))[:, : count * length]
+    return band.reshape(4 * count, length)
 
 
 def mat(left, right):
@@ -185,10 +181,10 @@
     plain = planar(values, values, count_x, count_y)
     along_x = planar(slopes, values, count_x, count_y)
     along_y = planar(values, slopes, count_x, count_y)
-    z_tables = jnp.concatenate([long_axis(values, count_z), long_axis(slopes, count_z)], 1)
+    z_tables = jnp.concatenate([long_axis(values, count_z), long_axis(slopes, count_z)], 0)
     rows = field.shape[0] * field.shape[1]
     width = 4 * count_z
-    through_z = mat(field.reshape(rows, field.shape[2]), z_tables)
+    through_z = mat(field.reshape(rows, field.shape[2]), z_tables.T)
     z_value = through_z[:, :width]
     point_value = mat(plain, z_value)
     grad_x = mat(along_x, z_value)
@@ -201,7 +197,7 @@
     backward = jnp.concatenate([plain, along_x, along_y], 0).T
     near = mat(backward, jnp.concatenate([mass_term, flux_x, flux_y], 0))
     far = mat(plain.T, flux_z)
-    merged = mat(jnp.concatenate([near, far], 1), z_tables.T)
+    merged = mat(jnp.concatenate([near, far], 1), z_tables)
     return merged.reshape(field.shape)
 
 
@@ -222,7 +218,7 @@
         inner = 0.0
         for table_x, table_y, entry, factor in members:
             inner = inner + mat(factor * planar(table_x, table_y, count_x, count_y).T, coeffs[entry])
-        total = total + mat(inner, long_axis(z_table, count_z).T)
+        total = total + mat(inner, long_axis(z_table, count_z))
     return total.reshape(3 * count_x + 1, 3 * count_y + 1, 3 * count_z + 1)
 
 
@@ -295,15 +291,18 @@
     image = operator(precond)
     scaled = image / diagonal
     second = operator(scaled)
-    terms = [
-        local_dot(residual, precond),
-        local_dot(precond, image),
-        local_dot(residual, scaled),
-        local_dot(image, scaled),
-        local_dot(precond, second),
-        local_dot(scaled, second),
-    ]
-    summed = over_axes(jnp.stack(terms), BX_BY)
+    products = jnp.stack(
+        [
+            residual * precond,
+            precond * image,
+            residual * scaled,
+            image * scaled,
+            precond * second,
+            scaled * second,
+        ]
+    )
+    terms = jnp.sum(products.reshape(6, -1, products.shape[-1]), axis=(1, 2))
+    summed = over_axes(terms, BX_BY)
     rz_now, curvature, cross_r, cross_q, cross_z, curvature_w = [summed[k] for k in range(6)]
     alpha = rz_now / curvature
     fresh = rz_now - alpha * cross_r - alpha * curvature + alpha * alpha * cross_q

time: 174 us -> 189 us (1.086)
  local copies, waits for them, and re-layouts: 8.17 us -> 28.2 us
  waiting for transfers between devices: 35.3 us -> 24.5 us
  starting transfers between devices: 36.6 us -> 43.9 us
  other arithmetic: 10.4 us -> 6.66 us
  matrix products: 12.5 us -> 14.6 us
    reshape x2 -> x12, local copies, waits for them, and re-layouts: 0.02 us -> 15.2 us  [the longest x5 8.47 us: long_axis(): return band.reshape(4 * count, length)]
    ppermute x10, waiting for transfers between devices: 35.3 us -> 24.5 us  [shifted(): lax.ppermute(value, axis, [(source, source + steps) for source in range(i...]
    add x2 -> x0, other arithmetic: 8.36 us -> none  [long_axis(): band = band + jnp.where(offset == node, column, 0.0)]
    ppermute x10, starting transfers between devices: 36.6 us -> 43.9 us  [shifted(): lax.ppermute(value, axis, [(source, source + steps) for source in range(i...]
    slice x0 -> x5, local copies, waits for them, and re-layouts: none -> 5.29 us  [long_axis(): band = rows.reshape(4, count * (length + 3))[:, :count * length]]
    another operation x1 -> x4, local copies, waits for them, and re-layouts: 3.89 us -> 0.03 us  [shards(): jnp.stack([residual * precond, precond * image, residual * scaled, image...]
    slice x16, local copies, waits for them, and re-layouts: 0.41 us -> 3 us  [band_diagonal(): coeffs[entry]]
    unnamed x33 -> x55, local copies, waits for them, and re-layouts: 2.71 us -> 0.22 us
  transfers between devices with their start and end apart: 10 -> 10, of which waited for: 10 -> 9; matrix products, arithmetic and copies ran while one was open for 1% -> 8% of each run, Pallas kernels for 0% -> 0%
where the time goes in v6:
time: 189 us; the launch traced here: 188 us
  blocking collectives  61.3 us (32%)
  starting transfers between devices  43.9 us (23%)
  local copies, waits for them, and re-layouts  28.2 us (15%)
  waiting for transfers between devices  24.5 us (13%)
  matrix products  14.6 us (8%)
  between operations  9.07 us (5%)
  other arithmetic  6.66 us (4%)
    psum x5, blocking collectives, over_axes(): value = lax.psum(value, axis)  61.3 us
    ppermute x10, starting transfers between devices, shifted(): lax.ppermute(value, axis, [(source, source + steps) for source in range(i...  43.9 us
    ppermute x10, waiting for transfers between devices, shifted(): lax.ppermute(value, axis, [(source, source + steps) for source in range(i...  24.5 us
    dot_general x30, matrix products, mat(): return jnp.matmul(left, right, precision=lax.Precision.HIGHEST)  14.6 us
    reshape x5, local copies, waits for them, and re-layouts, long_axis(): return band.reshape(4 * count, length)  8.47 us
    reshape x5, local copies, waits for them, and re-layouts, long_axis(): band = rows.reshape(4, count * (length + 3))[:, :count * length]  6.7 us
    slice x5, local copies, waits for them, and re-layouts, long_axis(): band = rows.reshape(4, count * (length + 3))[:, :count * length]  5.29 us
  transfers between devices with their start and end apart: 10, of which 9 were waited for; matrix products, arithmetic and copies ran while one was open for 8% of the time, Pallas kernels for 0%

profile of v6, /device:TPU:1, one launch (start us, length us, event | category | flops | bytes accessed | tf_op | source)
XLA Modules:
  0.0 188.1 jit_solution(17566069840407690590)
XLA Ops:
  0.6 1.0 fusion.101
  2.6 1.0 reshape.321
  3.6 1.0 reshape.322
  5.3 1.0 reshape.323
  6.3 0.9 slice.263
  7.3 2.1 %reshape.324 = f32[512,385]{1,0:T(8,128)S(1)} reshape(f32[4,49280]{1,0:T(4,128)} %slice.263) | data formatting | bytes 1576960 | tf_op jit(solution)/shard_map/reshape | solution.py:165
  9.6 1.9 reshape.325
  11.5 2.1 %slice.266 = f32[4,49280]{1,0:T(4,128)} slice(f32[4,49664]{1,0:T(4,128)} %reshape.325), slice={[0:4], [0:49280]} | slice | bytes 1576960 | tf_op jit(solution)/shard_map/slice | solution.py:164
  13.6 2.2 %reshape.326 = f32[512,385]{1,0:T(8,128)S(1)} reshape(f32[4,49280]{1,0:T(4,128)} %slice.266) | data formatting | bytes 1576960 | tf_op jit(solution)/shard_map/reshape | solution.py:165
  15.8 0.9 convolution_add_fusion.9
  19.9 4.8 %collective-permute-start = (f32[4,1,384]{2,1,0:T(1,128)S(1)}, f32[4,1,384]{2,1,0:T(1,128)S(1)}, u32[]{:S(2)}, u32[]{:S(2)}) collective-permute-start(f32[4,1,384]{2,1,0:T(1,128)S(1)} %slice.268), channel_id=1, source_target_pairs={{0,1},{1,2},{2,3},{3,4},{4,5},{5,6},{6,7},{7,8},{8,9},{9,10},{10,1... | collective-permute-start | bytes 18440 | tf_op jit(solution)/shard_map/ppermute | solution.py:22
  24.7 1.0 bitcast_convert_fusion
  25.9 1.0 reshape.329
  26.9 1.0 reshape.330
  28.6 1.8 fusion.100
  31.2 1.9 reshape.331
  33.0 2.1 %slice.273 = f32[4,49280]{1,0:T(4,128)} slice(f32[4,49664]{1,0:T(4,128)} %reshape.331), slice={[0:4], [0:49280]} | slice | bytes 1576960 | tf_op jit(solution)/shard_map/slice | solution.py:164
  35.1 2.1 %reshape.332 = f32[512,385]{1,0:T(8,128)S(1)} reshape(f32[4,49280]{1,0:T(4,128)} %slice.273) | data formatting | bytes 1576960 | tf_op jit(solution)/shard_map/reshape | solution.py:165
  37.4 0.9 slice_add_fusion.2
  38.2 10.6 %collective-permute-start.1 = (f32[1,6,384]{2,1,0:T(8,128)S(1)}, f32[1,6,384]{2,1,0:T(8,128)S(1)}, u32[]{:S(2)}, u32[]{:S(2)}) collective-permute-start(f32[1,6,384]{2,1,0:T(8,128)S(1)} %pad_maximum_fusion.9), channel_id=1, source_target_pairs={{0,64},{64,128},{128,192},{192,256},{256,320},{320,384},{384,448},... | collective-permute-start | bytes 27656 | tf_op jit(solution)/shard_map/ppermute | solution.py:22
  48.9 0.8 collective-permute-done.1
  49.7 0.8 fusion.90
  51.1 1.3 collective-permute-start.2
  54.3 6.4 %collective-permute-done.2 = f32[1,6,384]{2,1,0:T(8,128)} collective-permute-done((f32[1,6,384]{2,1,0:T(8,128)}, f32[1,6,384]{2,1,0:T(8,128)}, u32[]{:S(2)}, u32[]{:S(2)}) %collective-permute-start.2) | collective-permute-done | bytes 9248 | tf_op jit(solution)/shard_map/ppermute | solution.py:22
  61.4 2.3 %collective-permute-start.3 = (f32[4,1,384]{2,1,0:T(1,128)S(1)}, f32[4,1,384]{2,1,0:T(1,128)S(1)}, u32[]{:S(2)}, u32[]{:S(2)}) collective-permute-start(f32[4,1,384]{2,1,0:T(1,128)S(1)} %pad_maximum_fusion.11), channel_id=1, source_target_pairs={{1,0},{2,1},{3,2},{4,3},{5,4},{6,5},{7,6},{8,7},{9,8},{10,9},{11,1... | collective-permute-start | bytes 18440 | tf_op jit(solution)/shard_map/ppermute | solution.py:22
  63.8 2.6 %collective-permute-done.3 = f32[4,1,384]{2,1,0:T(1,128)S(1)} collective-permute-done((f32[4,1,384]{2,1,0:T(1,128)S(1)}, f32[4,1,384]{2,1,0:T(1,128)S(1)}, u32[]{:S(2)}, u32[]{:S(2)}) %collective-permute-start.3) | collective-permute-done | bytes 6176 | tf_op jit(solution)/shard_map/ppermute | solution.py:22
  67.1 2.0 %fusion.104 = f32[28,1024]{1,0:T(8,128)S(1)} fusion(f32[28,385]{1,0:T(8,128)S(1)} %reshape.328, f32[1024,385]{1,0:T(8,128)S(1)} %constant_dynamic-update-slice_fusion), kind=kOutput, calls=%fused_computation.165 | convolution fusion | flops 132464640 | bytes 1734768 | tf_op jit(solution)/shard_map/dot_general | solution.py:169
  71.0 1.3 fusion
  72.4 2.0 %collective-permute-start.4 = (f32[4,1,384]{2,1,0:T(1,128)S(1)}, f32[4,1,384]{2,1,0:T(1,128)S(1)}, u32[]{:S(2)}, u32[]{:S(2)}) collective-permute-start(f32[4,1,384]{2,1,0:T(1,128)S(1)} %slice.283), channel_id=1, source_target_pairs={{0,1},{1,2},{2,3},{3,4},{4,5},{5,6},{6,7},{7,8},{8,9},{9,10},{10,1... | collective-permute-start | bytes 18440 | tf_op jit(solution)/shard_map/ppermute | solution.py:22
  74.4 1.1 collective-permute-done.4
  75.5 7.9 %collective-permute-start.5 = (f32[1,6,384]{2,1,0:T(8,128)S(1)}, f32[1,6,384]{2,1,0:T(8,128)S(1)}, u32[]{:S(2)}, u32[]{:S(2)}) collective-permute-start(f32[1,6,384]{2,1,0:T(8,128)S(1)} %pad_maximum_fusion.8), channel_id=1, source_target_pairs={{0,64},{64,128},{128,192},{192,256},{256,320},{320,384},{384,448},... | collective-permute-start | bytes 27656 | tf_op jit(solution)/shard_map/ppermute | solution.py:22
  83.4 0.8 collective-permute-done.5
  84.3 1.3 collective-permute-start.6
  85.7 8.2 %collective-permute-done.6 = f32[1,6,384]{2,1,0:T(8,128)S(1)} collective-permute-done((f32[1,6,384]{2,1,0:T(8,128)S(1)}, f32[1,6,384]{2,1,0:T(8,128)S(1)}, u32[]{:S(2)}, u32[]{:S(2)}) %collective-permute-start.6) | collective-permute-done | bytes 9248 | tf_op jit(solution)/shard_map/ppermute | solution.py:22
  93.8 4.0 %collective-permute-start.7 = (f32[4,1,384]{2,1,0:T(1,128)S(1)}, f32[4,1,384]{2,1,0:T(1,128)S(1)}, u32[]{:S(2)}, u32[]{:S(2)}) collective-permute-start(f32[4,1,384]{2,1,0:T(1,128)S(1)} %pad_maximum_fusion.10), channel_id=1, source_target_pairs={{1,0},{2,1},{3,2},{4,3},{5,4},{6,5},{7,6},{8,7},{9,8},{10,9},{11,1... | collective-permute-start | bytes 18440 | tf_op jit(solution)/shard_map/ppermute | solution.py:22
  97.9 2.8 %collective-permute-done.7 = f32[4,1,384]{2,1,0:T(1,128)S(1)} collective-permute-done((f32[4,1,384]{2,1,0:T(1,128)S(1)}, f32[4,1,384]{2,1,0:T(1,128)S(1)}, u32[]{:S(2)}, u32[]{:S(2)}) %collective-permute-start.7) | collective-permute-done | bytes 6176 | tf_op jit(solution)/shard_map/ppermute | solution.py:22
  100.7 2.0 %fusion.106 = f32[28,1024]{1,0:T(8,128)S(1)} fusion(f32[28,385]{1,0:T(8,128)S(1)} %reshape.334, f32[1024,385]{1,0:T(8,128)S(1)} %constant_dynamic-update-slice_fusion), kind=kOutput, calls=%fused_computation.167 | convolution fusion | flops 132464640 | bytes 1734768 | tf_op jit(solution)/shard_map/dot_general | solution.py:169
  104.6 1.3 fusion.4
  105.9 1.9 %collective-permute-start.8 = (f32[4,1,384]{2,1,0:T(1,128)S(1)}, f32[4,1,384]{2,1,0:T(1,128)S(1)}, u32[]{:S(2)}, u32[]{:S(2)}) collective-permute-start(f32[4,1,384]{2,1,0:T(1,128)S(1)} %slice.289), channel_id=1, source_target_pairs={{0,1},{1,2},{2,3},{3,4},{4,5},{5,6},{6,7},{7,8},{8,9},{9,10},{10,1... | collective-permute-start | bytes 18440 | tf_op jit(solution)/shard_map/ppermute | solution.py:22
  108.0 1.0 collective-permute-done.8
  109.0 7.8 %collective-permute-start.9 = (f32[1,6,384]{2,1,0:T(8,128)S(1)}, f32[1,6,384]{2,1,0:T(8,128)S(1)}, u32[]{:S(2)}, u32[]{:S(2)}) collective-permute-start(f32[1,6,384]{2,1,0:T(8,128)S(1)} %pad_maximum_fusion.7), channel_id=1, source_target_pairs={{0,64},{64,128},{128,192},{192,256},{256,320},{320,384},{384,448},... | collective-permute-start | bytes 27656 | tf_op jit(solution)/shard_map/ppermute | solution.py:22
  116.9 0.8 collective-permute-done.9
  118.2 12.9 %psum.35 = f32[6]{0:T(128)S(1)} all-reduce(f32[6]{0:T(128)S(1)} %reduce_sum.9), channel_id=1, replica_groups=mesh['bx_0'=4,'bx_1'=3,'by_0'=4,'by_1'=8,'by_2'=2] {'bx_0'}, use_global_device_ids=true, to_apply=%region_1.2 | all-reduce | flops 6 | bytes 48 | tf_op jit(solution)/shard_map/psum | solution.py:27
  131.2 9.1 %psum.36 = f32[6]{0:T(128)S(1)} all-reduce(f32[6]{0:T(128)S(1)} %psum.35), channel_id=1, replica_groups=mesh['bx_0'=4,'bx_1'=3,'by_0'=4,'by_1'=8,'by_2'=2] {'bx_1'}, use_global_device_ids=true, to_apply=%region_2.3 | all-reduce | flops 6 | bytes 48 | tf_op jit(solution)/shard_map/psum | solution.py:27
  140.3 12.1 %psum.37 = f32[6]{0:T(128)S(1)} all-reduce(f32[6]{0:T(128)S(1)} %psum.36), channel_id=1, replica_groups=mesh['bx_0'=4,'bx_1'=3,'by_0'=4,'by_1'=8,'by_2'=2] {'by_0'}, use_global_device_ids=true, to_apply=%region_3.4 | all-reduce | flops 6 | bytes 48 | tf_op jit(solution)/shard_map/psum | solution.py:27
  152.4 13.1 %psum.38 = f32[6]{0:T(128)S(1)} all-reduce(f32[6]{0:T(128)S(1)} %psum.37), channel_id=1, replica_groups=mesh['bx_0'=4,'bx_1'=3,'by_0'=4,'by_1'=8,'by_2'=2] {'by_1'}, use_global_device_ids=true, to_apply=%region_4.5 | all-reduce | flops 6 | bytes 48 | tf_op jit(solution)/shard_map/psum | solution.py:27
  165.5 14.0 %psum.39 = f32[6]{0:T(128)S(1)} all-reduce(f32[6]{0:T(128)S(1)} %psum.38), channel_id=1, replica_groups=mesh['bx_0'=4,'bx_1'=3,'by_0'=4,'by_1'=8,'by_2'=2] {'by_2'}, use_global_device_ids=true, to_apply=%region_5.6 | all-reduce | flops 6 | bytes 48 | tf_op jit(solution)/shard_map/psum | solution.py:27
  187.4 0.7 multiply_subtract_fusion
  (164 shorter events, 15.3 us)
Async XLA Ops:
  3.6 1.1 copy-start.11
  3.6 1.6 copy-start.24
  6.3 3.1 %copy-start.23 = (f32[4,4]{1,0:T(4,128)S(1)}, f32[4,4]{1,0:T(4,128)}, u32[]{:S(2)}) copy-start(f32[4,4]{1,0:T(4,128)} %constant.79.clone) | copy-start | bytes 196
  11.5 5.3 %copy-start.15 = (f32[32,28]{1,0:T(8,128)S(1)}, f32[32,28]{1,0:T(8,128)}, u32[]{:S(2)}) copy-start(f32[32,28]{1,0:T(8,128)} %constant.73.clone) | copy-start | bytes 10756
  11.5 5.5 %copy-start.14 = (f32[32,28]{1,0:T(8,128)S(1)}, f32[32,28]{1,0:T(8,128)}, u32[]{:S(2)}) copy-start(f32[32,28]{1,0:T(8,128)} %constant.105) | copy-start | bytes 10756
  13.6 4.3 %copy-start.12 = (f32[32,28]{1,0:T(8,128)S(1)}, f32[32,28]{1,0:T(8,128)}, u32[]{:S(2)}) copy-start(f32[32,28]{1,0:T(8,128)} %constant.106) | copy-start | bytes 10756
  15.8 3.1 %copy-start.13 = (f32[32,28]{1,0:T(8,128)S(1)}, f32[32,28]{1,0:T(8,128)}, u32[]{:S(2)}) copy-start(f32[32,28]{1,0:T(8,128)} %constant.107) | copy-start | bytes 10756
  17.2 7.5 %copy-start.1 = (bf16[7,4,4,4,1,2,128]{6,5,4,3,2,1,0:T(2,128)(2,1)S(1)}, bf16[7,4,4,4,1,2,128]{6,5,4,3,2,1,0:T(2,128)(2,1)}, u32[]{:S(2)}) copy-start(bf16[7,4,4,4,1,2,128]{6,5,4,3,2,1,0:T(2,128)(2,1)} %param.23) | copy-start | bytes 688132
  17.9 7.8 %copy-start.22 = (f32[4,4]{1,0:T(4,128)S(1)}, f32[4,4]{1,0:T(4,128)}, u32[]{:S(2)}) copy-start(f32[4,4]{1,0:T(4,128)} %constant.83.clone) | copy-start | bytes 196
  19.9 5.9 %copy-start.9 = (f32[4,7,385]{2,1,0:T(8,128)}, f32[4,7,385]{2,1,0:T(8,128)S(1)}, u32[]{:S(2)}) copy-start(f32[4,7,385]{2,1,0:T(8,128)S(1)} %reshape.327) | copy-start | bytes 129364
  19.9 17.4 %collective-permute-start = (f32[4,1,384]{2,1,0:T(1,128)S(1)}, f32[4,1,384]{2,1,0:T(1,128)S(1)}, u32[]{:S(2)}, u32[]{:S(2)}) collective-permute-start(f32[4,1,384]{2,1,0:T(1,128)S(1)} %slice.268), channel_id=1, source_target_pairs={{0,1},{1,2},{2,3},{3,4},{4,5},{5,6},{6,7},{7,8},{8,9},{9,10},{10,1... | collective-permute-start | bytes 18440 | tf_op jit(solution)/shard_map/ppermute | solution.py:22
  26.9 4.0 %copy-start.10 = (f32[4,7,385]{2,1,0:T(8,128)S(1)}, f32[4,7,385]{2,1,0:T(8,128)}, u32[]{:S(2)}) copy-start(f32[4,7,385]{2,1,0:T(8,128)} %copy-done.9) | copy-start | bytes 129364
  26.9 4.0 %copy-start.21 = (f32[4,4]{1,0:T(4,128)S(1)}, f32[4,4]{1,0:T(4,128)}, u32[]{:S(2)}) copy-start(f32[4,4]{1,0:T(4,128)} %constant.84.clone) | copy-start | bytes 196
  28.1 3.1 %copy-start.16 = (pred[6]{0:T(512)(128)(4,1)}, pred[6]{0:T(512)(128)(4,1)S(1)}, u32[]{:S(2)}) copy-start(pred[6]{0:T(512)(128)(4,1)S(1)} %get-tuple-element.31) | copy-start | bytes 22
  28.6 2.5 %copy-start.19 = (pred[3]{0:T(512)(128)(4,1)}, pred[3]{0:T(512)(128)(4,1)S(1)}, u32[]{:S(2)}) copy-start(pred[3]{0:T(512)(128)(4,1)S(1)} %get-tuple-element.33) | copy-start | bytes 13
  33.0 16.7 %copy-start.2 = (f32[3,6,384]{2,1,0:T(8,128)S(1)}, f32[3,6,384]{2,1,0:T(8,128)}, u32[]{:S(2)}) copy-start(f32[3,6,384]{2,1,0:T(8,128)} %param.22) | copy-start | bytes 82948
  37.3 15.2 %copy-start.6 = (f32[1,4,1,4,2,4,128]{6,4,2,5,3,1,0:T(2,128)S(1)}, f32[1,4,1,4,2,4,128]{6,4,2,5,3,1,0:T(2,128)}, u32[]{:S(2)}) copy-start(f32[1,4,1,4,2,4,128]{6,4,2,5,3,1,0:T(2,128)} %get-tuple-element.7) | copy-start | bytes 196612
  37.3 15.2 %copy-start.5 = (f32[1,4,1,4,2,4,128]{6,4,2,5,3,1,0:T(2,128)S(1)}, f32[1,4,1,4,2,4,128]{6,4,2,5,3,1,0:T(2,128)}, u32[]{:S(2)}) copy-start(f32[1,4,1,4,2,4,128]{6,4,2,5,3,1,0:T(2,128)} %get-tuple-element.8) | copy-start | bytes 196612
  37.3 15.3 %copy-start.4 = (f32[1,4,1,4,2,4,128]{6,4,2,5,3,1,0:T(2,128)S(1)}, f32[1,4,1,4,2,4,128]{6,4,2,5,3,1,0:T(2,128)}, u32[]{:S(2)}) copy-start(f32[1,4,1,4,2,4,128]{6,4,2,5,3,1,0:T(2,128)} %get-tuple-element.9) | copy-start | bytes 196612
  37.3 15.3 %copy-start.3 = (f32[1,4,1,4,2,4,128]{6,4,2,5,3,1,0:T(2,128)S(1)}, f32[1,4,1,4,2,4,128]{6,4,2,5,3,1,0:T(2,128)}, u32[]{:S(2)}) copy-start(f32[1,4,1,4,2,4,128]{6,4,2,5,3,1,0:T(2,128)} %get-tuple-element.12) | copy-start | bytes 196612
  38.2 11.5 %collective-permute-start.1 = (f32[1,6,384]{2,1,0:T(8,128)S(1)}, f32[1,6,384]{2,1,0:T(8,128)S(1)}, u32[]{:S(2)}, u32[]{:S(2)}) collective-permute-start(f32[1,6,384]{2,1,0:T(8,128)S(1)} %pad_maximum_fusion.9), channel_id=1, source_target_pairs={{0,64},{64,128},{128,192},{192,256},{256,320},{320,384},{384,448},... | collective-permute-start | bytes 27656 | tf_op jit(solution)/shard_map/ppermute | solution.py:22
  51.1 9.6 %collective-permute-start.2 = (f32[1,6,384]{2,1,0:T(8,128)}, f32[1,6,384]{2,1,0:T(8,128)}, u32[]{:S(2)}, u32[]{:S(2)}) collective-permute-start(f32[1,6,384]{2,1,0:T(8,128)} %slice.271), channel_id=1, source_target_pairs={{64,0},{128,64},{192,128},{256,192},{320,256},{384,320},{448,384},... | collective-permute-start | bytes 27656 | tf_op jit(solution)/shard_map/ppermute | solution.py:22
  52.5 16.7 %copy-start = (f32[32,28]{1,0:T(8,128)S(1)}, f32[32,28]{1,0:T(8,128)}, u32[]{:S(2)}) copy-start(f32[32,28]{1,0:T(8,128)} %constant.80.clone) | copy-start | bytes 10756
  52.5 16.9 %copy-start.7 = (f32[32,28]{1,0:T(8,128)S(1)}, f32[32,28]{1,0:T(8,128)}, u32[]{:S(2)}) copy-start(f32[32,28]{1,0:T(8,128)} %constant.82.clone) | copy-start | bytes 10756
  52.5 17.1 %copy-start.8 = (f32[32,28]{1,0:T(8,128)S(1)}, f32[32,28]{1,0:T(8,128)}, u32[]{:S(2)}) copy-start(f32[32,28]{1,0:T(8,128)} %constant.81.clone) | copy-start | bytes 10756
  61.4 4.9 %collective-permute-start.3 = (f32[4,1,384]{2,1,0:T(1,128)S(1)}, f32[4,1,384]{2,1,0:T(1,128)S(1)}, u32[]{:S(2)}, u32[]{:S(2)}) collective-permute-start(f32[4,1,384]{2,1,0:T(1,128)S(1)} %pad_maximum_fusion.11), channel_id=1, source_target_pairs={{1,0},{2,1},{3,2},{4,3},{5,4},{6,5},{7,6},{8,7},{9,8},{10,9},{11,1... | collective-permute-start | bytes 18440 | tf_op jit(solution)/shard_map/ppermute | solution.py:22
  70.2 14.0 %copy-start.17 = (pred[6]{0:T(512)(128)(4,1)S(1)}, pred[6]{0:T(512)(128)(4,1)}, u32[]{:S(2)}) copy-start(pred[6]{0:T(512)(128)(4,1)} %copy-done.16) | copy-start | bytes 22
  70.2 14.0 %copy-start.18 = (pred[3]{0:T(512)(128)(4,1)S(1)}, pred[3]{0:T(512)(128)(4,1)}, u32[]{:S(2)}) copy-start(pred[3]{0:T(512)(128)(4,1)} %get-tuple-element.32) | copy-start | bytes 13
  70.2 14.0 %copy-start.20 = (pred[3]{0:T(512)(128)(4,1)S(1)}, pred[3]{0:T(512)(128)(4,1)}, u32[]{:S(2)}) copy-start(pred[3]{0:T(512)(128)(4,1)} %copy-done.19) | copy-start | bytes 13
  72.4 3.1 %collective-permute-start.4 = (f32[4,1,384]{2,1,0:T(1,128)S(1)}, f32[4,1,384]{2,1,0:T(1,128)S(1)}, u32[]{:S(2)}, u32[]{:S(2)}) collective-permute-start(f32[4,1,384]{2,1,0:T(1,128)S(1)} %slice.283), channel_id=1, source_target_pairs={{0,1},{1,2},{2,3},{3,4},{4,5},{5,6},{6,7},{7,8},{8,9},{9,10},{10,1... | collective-permute-start | bytes 18440 | tf_op jit(solution)/shard_map/ppermute | solution.py:22
  75.5 8.7 %collective-permute-start.5 = (f32[1,6,384]{2,1,0:T(8,128)S(1)}, f32[1,6,384]{2,1,0:T(8,128)S(1)}, u32[]{:S(2)}, u32[]{:S(2)}) collective-permute-start(f32[1,6,384]{2,1,0:T(8,128)S(1)} %pad_maximum_fusion.8), channel_id=1, source_target_pairs={{0,64},{64,128},{128,192},{192,256},{256,320},{320,384},{384,448},... | collective-permute-start | bytes 27656 | tf_op jit(solution)/shard_map/ppermute | solution.py:22
  84.3 9.5 %collective-permute-start.6 = (f32[1,6,384]{2,1,0:T(8,128)S(1)}, f32[1,6,384]{2,1,0:T(8,128)S(1)}, u32[]{:S(2)}, u32[]{:S(2)}) collective-permute-start(f32[1,6,384]{2,1,0:T(8,128)S(1)} %slice.285), channel_id=1, source_target_pairs={{64,0},{128,64},{192,128},{256,192},{320,256},{384,320},{448,384},... | collective-permute-start | bytes 27656 | tf_op jit(solution)/shard_map/ppermute | solution.py:22
  93.8 6.9 %collective-permute-start.7 = (f32[4,1,384]{2,1,0:T(1,128)S(1)}, f32[4,1,384]{2,1,0:T(1,128)S(1)}, u32[]{:S(2)}, u32[]{:S(2)}) collective-permute-start(f32[4,1,384]{2,1,0:T(1,128)S(1)} %pad_maximum_fusion.10), channel_id=1, source_target_pairs={{1,0},{2,1},{3,2},{4,3},{5,4},{6,5},{7,6},{8,7},{9,8},{10,9},{11,1... | collective-permute-start | bytes 18440 | tf_op jit(solution)/shard_map/ppermute | solution.py:22
  105.9 3.1 %collective-permute-start.8 = (f32[4,1,384]{2,1,0:T(1,128)S(1)}, f32[4,1,384]{2,1,0:T(1,128)S(1)}, u32[]{:S(2)}, u32[]{:S(2)}) collective-permute-start(f32[4,1,384]{2,1,0:T(1,128)S(1)} %slice.289), channel_id=1, source_target_pairs={{0,1},{1,2},{2,3},{3,4},{4,5},{5,6},{6,7},{7,8},{8,9},{9,10},{10,1... | collective-permute-start | bytes 18440 | tf_op jit(solution)/shard_map/ppermute | solution.py:22
  109.0 8.7 %collective-permute-start.9 = (f32[1,6,384]{2,1,0:T(8,128)S(1)}, f32[1,6,384]{2,1,0:T(8,128)S(1)}, u32[]{:S(2)}, u32[]{:S(2)}) collective-permute-start(f32[1,6,384]{2,1,0:T(8,128)S(1)} %pad_maximum_fusion.7), channel_id=1, source_target_pairs={{0,64},{64,128},{128,192},{192,256},{256,320},{320,384},{384,448},... | collective-permute-start | bytes 27656 | tf_op jit(solution)/shard_map/ppermute | solution.py:22

commit v7 on v6

--- a/solution.py
+++ b/solution.py
@@ -156,13 +156,15 @@
     return jnp.asarray(kron.reshape(16 * count_x * count_y, -1), jnp.float32)
 
 
-def long_axis(table, count):
-    length = 3 * count + 1
-    rows = jnp.asarray(table, jnp.float32)[:, None, :] + jnp.zeros((4, count, 4), jnp.float32)
-    rows = lax.optimization_barrier(rows)
-    rows = jnp.pad(rows, ((0, 0), (0, 0), (0, length - 1)))
-    band = rows.reshape(4, count * (length + 3))[:, : count * length]
-    return band.reshape(4 * count, length)
+def long_axis(table, count, anchor):
+    shape = (3 * count + 1, 4, count)
+    offset = lax.broadcasted_iota(jnp.int32, shape, 0) - 3 * lax.broadcasted_iota(jnp.int32, shape, 2)
+    offset = offset + anchor
+    band = jnp.zeros(shape, jnp.float32)
+    for node in range(4):
+        column = jnp.asarray(table[:, node], jnp.float32)[None, :, None]
+        band = band + jnp.where(offset == node, column, 0.0)
+    return band.reshape(3 * count + 1, 4 * count)
 
 
 def mat(left, right):
@@ -175,16 +177,16 @@
     return coeffs.reshape(7, 16 * count_x * count_y, 4 * count_z)
 
 
-def band_operator(field, coeffs, counts):
+def band_operator(field, coeffs, counts, anchor):
     count_x, count_y, count_z = counts
     values, slopes = gauss_tables()
     plain = planar(values, values, count_x, count_y)
     along_x = planar(slopes, values, count_x, count_y)
     along_y = planar(values, slopes, count_x, count_y)
-    z_tables = jnp.concatenate([long_axis(values, count_z), long_axis(slopes, count_z)], 0)
+    z_tables = jnp.concatenate([long_axis(values, count_z, anchor), long_axis(slopes, count_z, anchor)], 1)
     rows = field.shape[0] * field.shape[1]
     width = 4 * count_z
-    through_z = mat(field.reshape(rows, field.shape[2]), z_tables.T)
+    through_z = mat(field.reshape(rows, field.shape[2]), z_tables)
     z_value = through_z[:, :width]
     point_value = mat(plain, z_value)
     grad_x = mat(along_x, z_value)
@@ -197,11 +199,11 @@
     backward = jnp.concatenate([plain, along_x, along_y], 0).T
     near = mat(backward, jnp.concatenate([mass_term, flux_x, flux_y], 0))
     far = mat(plain.T, flux_z)
-    merged = mat(jnp.concatenate([near, far], 1), z_tables)
+    merged = mat(jnp.concatenate([near, far], 1), z_tables.T)
     return merged.reshape(field.shape)
 
 
-def band_diagonal(coeffs, counts):
+def band_diagonal(coeffs, counts, anchor):
     count_x, count_y, count_z = counts
     values, slopes = gauss_tables()
     square_v = values * values
@@ -218,7 +220,7 @@
         inner = 0.0
         for table_x, table_y, entry, factor in members:
             inner = inner + mat(factor * planar(table_x, table_y, count_x, count_y).T, coeffs[entry])
-        total = total + mat(inner, long_axis(z_table, count_z))
+        total = total + mat(inner, long_axis(z_table, count_z, anchor).T)
     return total.reshape(3 * count_x + 1, 3 * count_y + 1, 3 * count_z + 1)
 
 
@@ -275,11 +277,12 @@
     interior = jnp.where(inside, 1.0, 0.0).astype(jnp.float32)
     counts = pointwise.shape[4:]
     coeffs = point_layout(pointwise)
-    diagonal = collect(band_diagonal(coeffs, counts), rows_x, rows_y, rows_z)
+    anchor = (cotangent[0, 0, 0] * 0.0).astype(jnp.int32)
+    diagonal = collect(band_diagonal(coeffs, counts, anchor), rows_x, rows_y, rows_z)
 
     def operator(dof_field):
         return (
-            collect(band_operator(pad_top(widen(dof_field)), coeffs, counts), rows_x, rows_y, rows_z)
+            collect(band_operator(pad_top(widen(dof_field)), coeffs, counts, anchor), rows_x, rows_y, rows_z)
             * interior
         )
 

time: 189 us -> 163 us (0.86)
  local copies, waits for them, and re-layouts: 28.2 us -> 4.83 us
  waiting for transfers between devices: 24.5 us -> 33.5 us
  starting transfers between devices: 43.9 us -> 37.2 us
  other arithmetic: 6.66 us -> 2.41 us
    reshape x12 -> x2, local copies, waits for them, and re-layouts: 15.2 us -> 0.02 us  [band_operator(): through_z = mat(field.reshape(rows, field.shape[2]), z_tables)]
    ppermute x10, waiting for transfers between devices: 24.5 us -> 33.5 us  [shifted(): lax.ppermute(value, axis, [(source, source + steps) for source in range(i...]
    ppermute x10, starting transfers between devices: 43.9 us -> 37.2 us  [shifted(): lax.ppermute(value, axis, [(source, source + steps) for source in range(i...]
    slice x5 -> x1, local copies, waits for them, and re-layouts: 5.29 us -> 1.2 us  [shards(): anchor = (cotangent[0, 0, 0] * 0.0).astype(jnp.int32)]
  transfers between devices with their start and end apart: 10 -> 10, of which waited for: 9 -> 10; matrix products, arithmetic and copies ran while one was open for 8% -> 1% of each run, Pallas kernels for 0% -> 0%
where the time goes in v7:
time: 163 us; the launch traced here: 162 us
  blocking collectives  61.2 us (38%)
  starting transfers between devices  37.2 us (23%)
  waiting for transfers between devices  33.5 us (21%)
  matrix products  13.4 us (8%)
  between operations  9.4 us (6%)
  local copies, waits for them, and re-layouts  4.83 us (3%)
  other arithmetic  2.41 us (1%)
    psum x5, blocking collectives, over_axes(): value = lax.psum(value, axis)  61.2 us
    ppermute x10, starting transfers between devices, shifted(): lax.ppermute(value, axis, [(source, source + steps) for source in range(i...  37.2 us
    ppermute x10, waiting for transfers between devices, shifted(): lax.ppermute(value, axis, [(source, source + steps) for source in range(i...  33.5 us
    dot_general x30, matrix products, mat(): return jnp.matmul(left, right, precision=lax.Precision.HIGHEST)  13.4 us
  transfers between devices with their start and end apart: 10, of which 10 were waited for; matrix products, arithmetic and copies ran while one was open for 1% of the time, Pallas kernels for 0%

profile of v7, /device:TPU:1, one launch (start us, length us, event | category | flops | bytes accessed | tf_op | source)
XLA Modules:
  0.0 162.0 jit_solution(13096422645685155821)
XLA Ops:
  0.9 1.1 fusion.173
  2.0 1.2 slice.184
  4.7 0.2 fusion.125
  6.1 1.1 fusion.14
  7.2 1.1 convolution_add_fusion.6
  8.3 1.1 convolution_add_fusion.4
  9.4 4.6 %collective-permute-start = (f32[4,1,384]{2,1,0:T(1,128)S(1)}, f32[4,1,384]{2,1,0:T(1,128)S(1)}, u32[]{:S(2)}, u32[]{:S(2)}) collective-permute-start(f32[4,1,384]{2,1,0:T(1,128)S(1)} %slice.241), channel_id=1, source_target_pairs={{0,1},{1,2},{2,3},{3,4},{4,5},{5,6},{6,7},{7,8},{8,9},{9,10},{10,1... | collective-permute-start | bytes 18440 | tf_op jit(solution)/shard_map/ppermute | solution.py:22
  14.1 0.2 bitcast_convert_fusion
  14.5 0.2 copy-done.17
  15.0 0.5 select_add_fusion.1
  15.6 6.3 %collective-permute-done = f32[4,1,384]{2,1,0:T(1,128)S(1)} collective-permute-done((f32[4,1,384]{2,1,0:T(1,128)S(1)}, f32[4,1,384]{2,1,0:T(1,128)S(1)}, u32[]{:S(2)}, u32[]{:S(2)}) %collective-permute-start) | collective-permute-done | bytes 6176 | tf_op jit(solution)/shard_map/ppermute | solution.py:22
  21.9 4.4 %collective-permute-start.1 = (f32[1,6,384]{2,1,0:T(8,128)S(1)}, f32[1,6,384]{2,1,0:T(8,128)S(1)}, u32[]{:S(2)}, u32[]{:S(2)}) collective-permute-start(f32[1,6,384]{2,1,0:T(8,128)S(1)} %pad_maximum_fusion.14), channel_id=1, source_target_pairs={{0,64},{64,128},{128,192},{192,256},{256,320},{320,384},{384,448},... | collective-permute-start | bytes 27656 | tf_op jit(solution)/shard_map/ppermute | solution.py:22
  26.3 0.8 collective-permute-done.1
  27.2 1.3 collective-permute-start.2
  29.1 7.4 %collective-permute-done.2 = f32[1,6,384]{2,1,0:T(8,128)S(1)} collective-permute-done((f32[1,6,384]{2,1,0:T(8,128)S(1)}, f32[1,6,384]{2,1,0:T(8,128)S(1)}, u32[]{:S(2)}, u32[]{:S(2)}) %collective-permute-start.2) | collective-permute-done | bytes 9248 | tf_op jit(solution)/shard_map/ppermute | solution.py:22
  36.5 2.3 %collective-permute-start.3 = (f32[4,1,384]{2,1,0:T(1,128)S(1)}, f32[4,1,384]{2,1,0:T(1,128)S(1)}, u32[]{:S(2)}, u32[]{:S(2)}) collective-permute-start(f32[4,1,384]{2,1,0:T(1,128)S(1)} %pad_maximum_fusion.16), channel_id=1, source_target_pairs={{1,0},{2,1},{3,2},{4,3},{5,4},{6,5},{7,6},{8,7},{9,8},{10,9},{11,1... | collective-permute-start | bytes 18440 | tf_op jit(solution)/shard_map/ppermute | solution.py:22
  38.8 4.1 %collective-permute-done.3 = f32[4,1,384]{2,1,0:T(1,128)S(1)} collective-permute-done((f32[4,1,384]{2,1,0:T(1,128)S(1)}, f32[4,1,384]{2,1,0:T(1,128)S(1)}, u32[]{:S(2)}, u32[]{:S(2)}) %collective-permute-start.3) | collective-permute-done | bytes 6176 | tf_op jit(solution)/shard_map/ppermute | solution.py:22
  43.0 1.0 fusion.29
  44.4 0.3 fusion.175
  45.1 0.3 fusion.64
  45.4 0.3 convolution_add_fusion.3
  45.6 0.3 convolution_add_fusion.2
  45.9 1.5 fusion.28
  47.4 1.9 %collective-permute-start.4 = (f32[4,1,384]{2,1,0:T(1,128)S(1)}, f32[4,1,384]{2,1,0:T(1,128)S(1)}, u32[]{:S(2)}, u32[]{:S(2)}) collective-permute-start(f32[4,1,384]{2,1,0:T(1,128)S(1)} %slice.254), channel_id=1, source_target_pairs={{0,1},{1,2},{2,3},{3,4},{4,5},{5,6},{6,7},{7,8},{8,9},{9,10},{10,1... | collective-permute-start | bytes 18440 | tf_op jit(solution)/shard_map/ppermute | solution.py:22
  49.4 1.1 collective-permute-done.4
  50.5 7.8 %collective-permute-start.5 = (f32[1,6,384]{2,1,0:T(8,128)S(1)}, f32[1,6,384]{2,1,0:T(8,128)S(1)}, u32[]{:S(2)}, u32[]{:S(2)}) collective-permute-start(f32[1,6,384]{2,1,0:T(8,128)S(1)} %pad_maximum_fusion.13), channel_id=1, source_target_pairs={{0,64},{64,128},{128,192},{192,256},{256,320},{320,384},{384,448},... | collective-permute-start | bytes 27656 | tf_op jit(solution)/shard_map/ppermute | solution.py:22
  58.4 0.8 collective-permute-done.5
  59.3 1.3 collective-permute-start.6
  60.6 8.2 %collective-permute-done.6 = f32[1,6,384]{2,1,0:T(8,128)S(1)} collective-permute-done((f32[1,6,384]{2,1,0:T(8,128)S(1)}, f32[1,6,384]{2,1,0:T(8,128)S(1)}, u32[]{:S(2)}, u32[]{:S(2)}) %collective-permute-start.6) | collective-permute-done | bytes 9248 | tf_op jit(solution)/shard_map/ppermute | solution.py:22
  68.8 3.8 %collective-permute-start.7 = (f32[4,1,384]{2,1,0:T(1,128)S(1)}, f32[4,1,384]{2,1,0:T(1,128)S(1)}, u32[]{:S(2)}, u32[]{:S(2)}) collective-permute-start(f32[4,1,384]{2,1,0:T(1,128)S(1)} %pad_maximum_fusion.15), channel_id=1, source_target_pairs={{1,0},{2,1},{3,2},{4,3},{5,4},{6,5},{7,6},{8,7},{9,8},{10,9},{11,1... | collective-permute-start | bytes 18440 | tf_op jit(solution)/shard_map/ppermute | solution.py:22
  72.6 3.0 %collective-permute-done.7 = f32[4,1,384]{2,1,0:T(1,128)S(1)} collective-permute-done((f32[4,1,384]{2,1,0:T(1,128)S(1)}, f32[4,1,384]{2,1,0:T(1,128)S(1)}, u32[]{:S(2)}, u32[]{:S(2)}) %collective-permute-start.7) | collective-permute-done | bytes 6176 | tf_op jit(solution)/shard_map/ppermute | solution.py:22
  75.7 1.0 fusion.27
  77.5 0.3 fusion.176
  77.8 0.3 fusion.67
  78.1 0.3 convolution_add_fusion.1
  78.3 0.3 convolution_add_fusion
  78.6 1.5 fusion.26
  80.1 1.9 %collective-permute-start.8 = (f32[4,1,384]{2,1,0:T(1,128)S(1)}, f32[4,1,384]{2,1,0:T(1,128)S(1)}, u32[]{:S(2)}, u32[]{:S(2)}) collective-permute-start(f32[4,1,384]{2,1,0:T(1,128)S(1)} %slice.260), channel_id=1, source_target_pairs={{0,1},{1,2},{2,3},{3,4},{4,5},{5,6},{6,7},{7,8},{8,9},{9,10},{10,1... | collective-permute-start | bytes 18440 | tf_op jit(solution)/shard_map/ppermute | solution.py:22
  82.1 1.0 collective-permute-done.8
  83.2 7.8 %collective-permute-start.9 = (f32[1,6,384]{2,1,0:T(8,128)S(1)}, f32[1,6,384]{2,1,0:T(8,128)S(1)}, u32[]{:S(2)}, u32[]{:S(2)}) collective-permute-start(f32[1,6,384]{2,1,0:T(8,128)S(1)} %pad_maximum_fusion.12), channel_id=1, source_target_pairs={{0,64},{64,128},{128,192},{192,256},{256,320},{320,384},{384,448},... | collective-permute-start | bytes 27656 | tf_op jit(solution)/shard_map/ppermute | solution.py:22
  91.1 0.8 collective-permute-done.9
  92.4 12.9 %psum.35 = f32[6]{0:T(128)S(1)} all-reduce(f32[6]{0:T(128)S(1)} %reduce_sum.9), channel_id=1, replica_groups=mesh['bx_0'=4,'bx_1'=3,'by_0'=4,'by_1'=8,'by_2'=2] {'bx_0'}, use_global_device_ids=true, to_apply=%region_1.2 | all-reduce | flops 6 | bytes 48 | tf_op jit(solution)/shard_map/psum | solution.py:27
  105.3 9.0 %psum.36 = f32[6]{0:T(128)S(1)} all-reduce(f32[6]{0:T(128)S(1)} %psum.35), channel_id=1, replica_groups=mesh['bx_0'=4,'bx_1'=3,'by_0'=4,'by_1'=8,'by_2'=2] {'bx_1'}, use_global_device_ids=true, to_apply=%region_2.3 | all-reduce | flops 6 | bytes 48 | tf_op jit(solution)/shard_map/psum | solution.py:27
  114.3 12.2 %psum.37 = f32[6]{0:T(128)S(1)} all-reduce(f32[6]{0:T(128)S(1)} %psum.36), channel_id=1, replica_groups=mesh['bx_0'=4,'bx_1'=3,'by_0'=4,'by_1'=8,'by_2'=2] {'by_0'}, use_global_device_ids=true, to_apply=%region_3.4 | all-reduce | flops 6 | bytes 48 | tf_op jit(solution)/shard_map/psum | solution.py:27
  126.5 13.7 %psum.38 = f32[6]{0:T(128)S(1)} all-reduce(f32[6]{0:T(128)S(1)} %psum.37), channel_id=1, replica_groups=mesh['bx_0'=4,'bx_1'=3,'by_0'=4,'by_1'=8,'by_2'=2] {'by_1'}, use_global_device_ids=true, to_apply=%region_4.5 | all-reduce | flops 6 | bytes 48 | tf_op jit(solution)/shard_map/psum | solution.py:27
  140.3 13.4 %psum.39 = f32[6]{0:T(128)S(1)} all-reduce(f32[6]{0:T(128)S(1)} %psum.38), channel_id=1, replica_groups=mesh['bx_0'=4,'bx_1'=3,'by_0'=4,'by_1'=8,'by_2'=2] {'by_2'}, use_global_device_ids=true, to_apply=%region_5.6 | all-reduce | flops 6 | bytes 48 | tf_op jit(solution)/shard_map/psum | solution.py:27
  153.6 0.7 fusion.174
  161.2 0.7 multiply_subtract_fusion
  (163 shorter events, 5.5 us)
Async XLA Ops:
  0.6 3.3 %copy-start.5 = (f32[32,28]{1,0:T(8,128)S(1)}, f32[32,28]{1,0:T(8,128)}, u32[]{:S(2)}) copy-start(f32[32,28]{1,0:T(8,128)} %constant.108.clone) | copy-start | bytes 10756
  0.6 3.8 %copy-start.29 = (f32[4]{0:T(128)S(1)}, f32[4]{0:T(128)}, u32[]{:S(2)}) copy-start(f32[4]{0:T(128)} %constant.114.clone) | copy-start | bytes 52
  0.7 3.8 %copy-start.30 = (f32[4]{0:T(128)S(1)}, f32[4]{0:T(128)}, u32[]{:S(2)}) copy-start(f32[4]{0:T(128)} %constant.115.clone) | copy-start | bytes 52
  0.7 3.8 %copy-start.27 = (f32[4]{0:T(128)S(1)}, f32[4]{0:T(128)}, u32[]{:S(2)}) copy-start(f32[4]{0:T(128)} %constant.112.clone) | copy-start | bytes 52
  0.7 3.8 %copy-start.28 = (f32[4]{0:T(128)S(1)}, f32[4]{0:T(128)}, u32[]{:S(2)}) copy-start(f32[4]{0:T(128)} %constant.113.clone) | copy-start | bytes 52
  0.7 3.9 %copy-start.25 = (f32[4]{0:T(128)S(1)}, f32[4]{0:T(128)}, u32[]{:S(2)}) copy-start(f32[4]{0:T(128)} %constant.118.clone) | copy-start | bytes 52
  0.7 3.9 %copy-start.26 = (f32[4]{0:T(128)S(1)}, f32[4]{0:T(128)}, u32[]{:S(2)}) copy-start(f32[4]{0:T(128)} %constant.119.clone) | copy-start | bytes 52
  0.7 3.9 %copy-start.23 = (f32[4]{0:T(128)S(1)}, f32[4]{0:T(128)}, u32[]{:S(2)}) copy-start(f32[4]{0:T(128)} %constant.116.clone) | copy-start | bytes 52
  0.7 3.9 %copy-start.24 = (f32[4]{0:T(128)S(1)}, f32[4]{0:T(128)}, u32[]{:S(2)}) copy-start(f32[4]{0:T(128)} %constant.117.clone) | copy-start | bytes 52
  0.7 4.0 %copy-start.6 = (f32[32,28]{1,0:T(8,128)S(1)}, f32[32,28]{1,0:T(8,128)}, u32[]{:S(2)}) copy-start(f32[32,28]{1,0:T(8,128)} %constant.144) | copy-start | bytes 10756
  0.8 4.2 %copy-start.21 = (f32[4]{0:T(128)S(1)}, f32[4]{0:T(128)}, u32[]{:S(2)}) copy-start(f32[4]{0:T(128)} %constant.124.clone) | copy-start | bytes 52
  0.8 4.2 %copy-start.22 = (f32[4]{0:T(128)S(1)}, f32[4]{0:T(128)}, u32[]{:S(2)}) copy-start(f32[4]{0:T(128)} %constant.125.clone) | copy-start | bytes 52
  0.8 4.3 %copy-start.19 = (f32[4]{0:T(128)S(1)}, f32[4]{0:T(128)}, u32[]{:S(2)}) copy-start(f32[4]{0:T(128)} %constant.122.clone) | copy-start | bytes 52
  0.8 4.3 %copy-start.20 = (f32[4]{0:T(128)S(1)}, f32[4]{0:T(128)}, u32[]{:S(2)}) copy-start(f32[4]{0:T(128)} %constant.123.clone) | copy-start | bytes 52
  0.8 4.3 %copy-start.10 = (f32[32,28]{1,0:T(8,128)S(1)}, f32[32,28]{1,0:T(8,128)}, u32[]{:S(2)}) copy-start(f32[32,28]{1,0:T(8,128)} %constant.109.clone) | copy-start | bytes 10756
  0.8 4.5 %copy-start.9 = (f32[32,28]{1,0:T(8,128)S(1)}, f32[32,28]{1,0:T(8,128)}, u32[]{:S(2)}) copy-start(f32[32,28]{1,0:T(8,128)} %constant.110.clone) | copy-start | bytes 10756
  0.8 4.8 %copy-start.8 = (f32[32,28]{1,0:T(8,128)S(1)}, f32[32,28]{1,0:T(8,128)}, u32[]{:S(2)}) copy-start(f32[32,28]{1,0:T(8,128)} %constant.143) | copy-start | bytes 10756
  1.9 3.9 %copy-start.7 = (f32[32,28]{1,0:T(8,128)S(1)}, f32[32,28]{1,0:T(8,128)}, u32[]{:S(2)}) copy-start(f32[32,28]{1,0:T(8,128)} %constant.145) | copy-start | bytes 10756
  8.3 5.8 %copy-start.1 = (bf16[7,4,4,4,1,2,128]{6,5,4,3,2,1,0:T(2,128)(2,1)S(1)}, bf16[7,4,4,4,1,2,128]{6,5,4,3,2,1,0:T(2,128)(2,1)}, u32[]{:S(2)}) copy-start(bf16[7,4,4,4,1,2,128]{6,5,4,3,2,1,0:T(2,128)(2,1)} %param.44) | copy-start | bytes 688132
  9.4 12.5 %collective-permute-start = (f32[4,1,384]{2,1,0:T(1,128)S(1)}, f32[4,1,384]{2,1,0:T(1,128)S(1)}, u32[]{:S(2)}, u32[]{:S(2)}) collective-permute-start(f32[4,1,384]{2,1,0:T(1,128)S(1)} %slice.241), channel_id=1, source_target_pairs={{0,1},{1,2},{2,3},{3,4},{4,5},{5,6},{6,7},{7,8},{8,9},{9,10},{10,1... | collective-permute-start | bytes 18440 | tf_op jit(solution)/shard_map/ppermute | solution.py:22
  14.0 0.7 copy-start.17
  14.1 0.7 copy-start.18
  14.1 0.7 copy-start.15
  14.1 0.7 copy-start.16
  14.1 0.8 copy-start.13
  14.1 0.8 copy-start.14
  14.1 0.8 copy-start.11
  14.1 0.8 copy-start.12
  15.0 12.1 %copy-start.2 = (f32[3,6,384]{2,1,0:T(8,128)S(1)}, f32[3,6,384]{2,1,0:T(8,128)}, u32[]{:S(2)}) copy-start(f32[3,6,384]{2,1,0:T(8,128)} %param.43) | copy-start | bytes 82948
  21.9 5.2 %collective-permute-start.1 = (f32[1,6,384]{2,1,0:T(8,128)S(1)}, f32[1,6,384]{2,1,0:T(8,128)S(1)}, u32[]{:S(2)}, u32[]{:S(2)}) collective-permute-start(f32[1,6,384]{2,1,0:T(8,128)S(1)} %pad_maximum_fusion.14), channel_id=1, source_target_pairs={{0,64},{64,128},{128,192},{192,256},{256,320},{320,384},{384,448},... | collective-permute-start | bytes 27656 | tf_op jit(solution)/shard_map/ppermute | solution.py:22
  27.2 9.3 %collective-permute-start.2 = (f32[1,6,384]{2,1,0:T(8,128)S(1)}, f32[1,6,384]{2,1,0:T(8,128)S(1)}, u32[]{:S(2)}, u32[]{:S(2)}) collective-permute-start(f32[1,6,384]{2,1,0:T(8,128)S(1)} %slice.244), channel_id=1, source_target_pairs={{64,0},{128,64},{192,128},{256,192},{320,256},{384,320},{448,384},... | collective-permute-start | bytes 27656 | tf_op jit(solution)/shard_map/ppermute | solution.py:22
  36.5 6.4 %collective-permute-start.3 = (f32[4,1,384]{2,1,0:T(1,128)S(1)}, f32[4,1,384]{2,1,0:T(1,128)S(1)}, u32[]{:S(2)}, u32[]{:S(2)}) collective-permute-start(f32[4,1,384]{2,1,0:T(1,128)S(1)} %pad_maximum_fusion.16), channel_id=1, source_target_pairs={{1,0},{2,1},{3,2},{4,3},{5,4},{6,5},{7,6},{8,7},{9,8},{10,9},{11,1... | collective-permute-start | bytes 18440 | tf_op jit(solution)/shard_map/ppermute | solution.py:22
  43.0 1.1 copy-start
  43.0 1.7 %copy-start.3 = (f32[32,28]{1,0:T(8,128)S(1)}, f32[32,28]{1,0:T(8,128)}, u32[]{:S(2)}) copy-start(f32[32,28]{1,0:T(8,128)} %constant.128.clone) | copy-start | bytes 10756
  43.0 1.9 %copy-start.4 = (f32[32,28]{1,0:T(8,128)S(1)}, f32[32,28]{1,0:T(8,128)}, u32[]{:S(2)}) copy-start(f32[32,28]{1,0:T(8,128)} %constant.127.clone) | copy-start | bytes 10756
  47.4 3.1 %collective-permute-start.4 = (f32[4,1,384]{2,1,0:T(1,128)S(1)}, f32[4,1,384]{2,1,0:T(1,128)S(1)}, u32[]{:S(2)}, u32[]{:S(2)}) collective-permute-start(f32[4,1,384]{2,1,0:T(1,128)S(1)} %slice.254), channel_id=1, source_target_pairs={{0,1},{1,2},{2,3},{3,4},{4,5},{5,6},{6,7},{7,8},{8,9},{9,10},{10,1... | collective-permute-start | bytes 18440 | tf_op jit(solution)/shard_map/ppermute | solution.py:22
  50.5 8.7 %collective-permute-start.5 = (f32[1,6,384]{2,1,0:T(8,128)S(1)}, f32[1,6,384]{2,1,0:T(8,128)S(1)}, u32[]{:S(2)}, u32[]{:S(2)}) collective-permute-start(f32[1,6,384]{2,1,0:T(8,128)S(1)} %pad_maximum_fusion.13), channel_id=1, source_target_pairs={{0,64},{64,128},{128,192},{192,256},{256,320},{320,384},{384,448},... | collective-permute-start | bytes 27656 | tf_op jit(solution)/shard_map/ppermute | solution.py:22
  59.3 9.5 %collective-permute-start.6 = (f32[1,6,384]{2,1,0:T(8,128)S(1)}, f32[1,6,384]{2,1,0:T(8,128)S(1)}, u32[]{:S(2)}, u32[]{:S(2)}) collective-permute-start(f32[1,6,384]{2,1,0:T(8,128)S(1)} %slice.256), channel_id=1, source_target_pairs={{64,0},{128,64},{192,128},{256,192},{320,256},{384,320},{448,384},... | collective-permute-start | bytes 27656 | tf_op jit(solution)/shard_map/ppermute | solution.py:22
  68.8 6.9 %collective-permute-start.7 = (f32[4,1,384]{2,1,0:T(1,128)S(1)}, f32[4,1,384]{2,1,0:T(1,128)S(1)}, u32[]{:S(2)}, u32[]{:S(2)}) collective-permute-start(f32[4,1,384]{2,1,0:T(1,128)S(1)} %pad_maximum_fusion.15), channel_id=1, source_target_pairs={{1,0},{2,1},{3,2},{4,3},{5,4},{6,5},{7,6},{8,7},{9,8},{10,9},{11,1... | collective-permute-start | bytes 18440 | tf_op jit(solution)/shard_map/ppermute | solution.py:22
  80.1 3.1 %collective-permute-start.8 = (f32[4,1,384]{2,1,0:T(1,128)S(1)}, f32[4,1,384]{2,1,0:T(1,128)S(1)}, u32[]{:S(2)}, u32[]{:S(2)}) collective-permute-start(f32[4,1,384]{2,1,0:T(1,128)S(1)} %slice.260), channel_id=1, source_target_pairs={{0,1},{1,2},{2,3},{3,4},{4,5},{5,6},{6,7},{7,8},{8,9},{9,10},{10,1... | collective-permute-start | bytes 18440 | tf_op jit(solution)/shard_map/ppermute | solution.py:22
  83.2 8.7 %collective-permute-start.9 = (f32[1,6,384]{2,1,0:T(8,128)S(1)}, f32[1,6,384]{2,1,0:T(8,128)S(1)}, u32[]{:S(2)}, u32[]{:S(2)}) collective-permute-start(f32[1,6,384]{2,1,0:T(8,128)S(1)} %pad_maximum_fusion.12), channel_id=1, source_target_pairs={{0,64},{64,128},{128,192},{192,256},{256,320},{320,384},{384,448},... | collective-permute-start | bytes 27656 | tf_op jit(solution)/shard_map/ppermute | solution.py:22

commit v8 on v7

--- a/solution.py
+++ b/solution.py
@@ -240,6 +240,19 @@
     return shifted(plane, BY, 1)
 
 
+def exchange(local, rows_x, rows_y):
+    from_below = lower_y(local[:, rows_y:])
+    from_above = upper_y(local[:, 0:1])
+    local = jnp.concatenate(
+        [local[:, 0:1] + from_below, local[:, 1:rows_y], local[:, rows_y:] + from_above], 1
+    )
+    from_below = lower_x(local[rows_x:])
+    from_above = upper_x(local[0:1])
+    return jnp.concatenate(
+        [local[0:1] + from_below, local[1:rows_x], local[rows_x:] + from_above], 0
+    )
+
+
 def global_sums(terms):
     return (over_axes(terms[0], BX_BY), over_axes(terms[1], BX_BY))
 
@@ -275,25 +288,32 @@
         (place_x > 0) & (place_y > 0) & (place_z > 0) & (place_x < total_x) & (place_y < total_y)
     )
     interior = jnp.where(inside, 1.0, 0.0).astype(jnp.float32)
+    wide_extent = (rows_x + 1, rows_y + 1, rows_z)
+    wide_x = lax.broadcasted_iota(jnp.int32, wide_extent, 0) + lax.axis_index(BX) * rows_x
+    wide_y = lax.broadcasted_iota(jnp.int32, wide_extent, 1) + lax.axis_index(BY) * rows_y
+    wide_z = lax.broadcasted_iota(jnp.int32, wide_extent, 2)
+    wide_inside = (
+        (wide_x > 0) & (wide_y > 0) & (wide_z > 0) & (wide_x < total_x) & (wide_y < total_y)
+    )
+    wide_interior = jnp.where(wide_inside, 1.0, 0.0).astype(jnp.float32)
     counts = pointwise.shape[4:]
     coeffs = point_layout(pointwise)
     anchor = (cotangent[0, 0, 0] * 0.0).astype(jnp.int32)
-    diagonal = collect(band_diagonal(coeffs, counts, anchor), rows_x, rows_y, rows_z)
-
-    def operator(dof_field):
-        return (
-            collect(band_operator(pad_top(widen(dof_field)), coeffs, counts, anchor), rows_x, rows_y, rows_z)
-            * interior
-        )
-
-    def local_dot(left, right):
-        return jnp.sum(left * right)
-
     residual = cotangent * interior
-    precond = residual / diagonal
-    image = operator(precond)
-    scaled = image / diagonal
-    second = operator(scaled)
+    wide_residual = widen(residual)
+    wide_diagonal = exchange(band_diagonal(coeffs, counts, anchor)[:, :, :rows_z], rows_x, rows_y)
+    diagonal = wide_diagonal[:rows_x, :rows_y]
+
+    def contributions(wide_field):
+        return band_operator(pad_top(wide_field), coeffs, counts, anchor)[:, :, :rows_z]
+
+    wide_precond = wide_residual / wide_diagonal
+    precond = wide_precond[:rows_x, :rows_y]
+    wide_image = exchange(contributions(wide_precond), rows_x, rows_y) * wide_interior
+    image = wide_image[:rows_x, :rows_y]
+    wide_scaled = wide_image / wide_diagonal
+    scaled = wide_scaled[:rows_x, :rows_y]
+    second = collect(contributions(wide_scaled), rows_x, rows_y, rows_z) * interior
     products = jnp.stack(
         [
             residual * precond,

time: 163 us -> 168 us (1.031)
  starting transfers between devices: 37.2 us -> 51.9 us
  waiting for transfers between devices: 33.5 us -> 19.5 us
  blocking collectives: 61.2 us -> 66.1 us
    ppermute x10 -> x12, starting transfers between devices: 37.2 us -> 51.9 us  [shifted(): lax.ppermute(value, axis, [(source, source + steps) for source in range(i...]
    ppermute x10 -> x12, waiting for transfers between devices: 33.5 us -> 19.5 us  [shifted(): lax.ppermute(value, axis, [(source, source + steps) for source in range(i...]
    psum x5, blocking collectives: 61.2 us -> 66.1 us  [over_axes(): value = lax.psum(value, axis)]
  transfers between devices with their start and end apart: 10 -> 12, of which waited for: 10 -> 7; matrix products, arithmetic and copies ran while one was open for 1% -> 5% of each run, Pallas kernels for 0% -> 0%
where the time goes in v8:
time: 168 us
  blocking collectives  66.1 us (39%)
  starting transfers between devices  51.9 us (31%)
  waiting for transfers between devices  19.5 us (12%)
  matrix products  13.4 us (8%)
  between operations  9.53 us (6%)
  local copies, waits for them, and re-layouts  4.25 us (3%)
  other arithmetic  2.95 us (2%)
    psum x5, blocking collectives, over_axes(): value = lax.psum(value, axis)  66.1 us
    ppermute x12, starting transfers between devices, shifted(): lax.ppermute(value, axis, [(source, source + steps) for source in range(i...  51.9 us
    ppermute x12, waiting for transfers between devices, shifted(): lax.ppermute(value, axis, [(source, source + steps) for source in range(i...  19.5 us
    dot_general x30, matrix products, mat(): return jnp.matmul(left, right, precision=lax.Precision.HIGHEST)  13.4 us
  transfers between devices with their start and end apart: 12, of which 7 were waited for; matrix products, arithmetic and copies ran while one was open for 5% of the time, Pallas kernels for 0%

profile of v8, /device:TPU:1, one launch (start us, length us, event | category | flops | bytes accessed | tf_op | source)
XLA Modules:
  0.0 167.7 jit_solution(12208614255258632422)
XLA Ops:
  0.9 0.9 select_multiply_fusion.1
  1.8 1.3 collective-permute-start
  3.1 1.2 slice.201
  5.0 1.0 fusion.179
  6.2 0.2 fusion.136
  7.1 0.2 fusion.133
  8.3 1.1 fusion.14
  9.4 1.1 convolution_add_fusion.6
  10.5 1.1 convolution_add_fusion.4
  11.7 4.6 %collective-permute-start.2 = (f32[4,1,384]{2,1,0:T(1,128)S(1)}, f32[4,1,384]{2,1,0:T(1,128)S(1)}, u32[]{:S(2)}, u32[]{:S(2)}) collective-permute-start(f32[4,1,384]{2,1,0:T(1,128)S(1)} %get-tuple-element.32), channel_id=1, source_target_pairs={{0,1},{1,2},{2,3},{3,4},{4,5},{5,6},{6,7},{7,8},{8,9},{9,10},{10,1... | collective-permute-start | bytes 18440 | tf_op jit(solution)/shard_map/ppermute | solution.py:22
  16.3 9.1 %collective-permute-start.3 = (f32[4,1,384]{2,1,0:T(1,128)S(1)}, f32[4,1,384]{2,1,0:T(1,128)S(1)}, u32[]{:S(2)}, u32[]{:S(2)}) collective-permute-start(f32[4,1,384]{2,1,0:T(1,128)S(1)} %get-tuple-element.33), channel_id=1, source_target_pairs={{1,0},{2,1},{3,2},{4,3},{5,4},{6,5},{7,6},{8,7},{9,8},{10,9},{11,1... | collective-permute-start | bytes 18440 | tf_op jit(solution)/shard_map/ppermute | solution.py:22
  25.5 0.2 bitcast_convert_fusion
  26.0 0.5 select_add_fusion.1
  26.9 1.3 collective-permute-start.5
  28.2 1.9 %collective-permute-start.1 = (f32[4,1,384]{2,1,0:T(1,128)S(1)}, f32[4,1,384]{2,1,0:T(1,128)S(1)}, u32[]{:S(2)}, u32[]{:S(2)}) collective-permute-start(f32[4,1,384]{2,1,0:T(1,128)S(1)} %pad_maximum_fusion.14), channel_id=1, source_target_pairs={{1,0},{2,1},{3,2},{4,3},{5,4},{6,5},{7,6},{8,7},{9,8},{10,9},{11,1... | collective-permute-start | bytes 18440 | tf_op jit(solution)/shard_map/ppermute | solution.py:22
  30.1 6.3 %collective-permute-done.5 = f32[1,7,384]{2,1,0:T(8,128)S(1)} collective-permute-done((f32[1,7,384]{2,1,0:T(8,128)S(1)}, f32[1,7,384]{2,1,0:T(8,128)S(1)}, u32[]{:S(2)}, u32[]{:S(2)}) %collective-permute-start.5) | collective-permute-done | bytes 10784 | tf_op jit(solution)/shard_map/ppermute | solution.py:22
  36.5 6.9 %collective-permute-start.4 = (f32[1,7,384]{2,1,0:T(8,128)S(1)}, f32[1,7,384]{2,1,0:T(8,128)S(1)}, u32[]{:S(2)}, u32[]{:S(2)}) collective-permute-start(f32[1,7,384]{2,1,0:T(8,128)S(1)} %get-tuple-element.9), channel_id=1, source_target_pairs={{0,64},{64,128},{128,192},{192,256},{256,320},{320,384},{384,448},... | collective-permute-start | bytes 32264 | tf_op jit(solution)/shard_map/ppermute | solution.py:22
  43.4 0.8 collective-permute-done.4
  44.3 1.0 fusion.29
  46.2 0.3 fusion.183
  46.5 0.3 fusion.64
  46.7 0.3 convolution_add_fusion.3
  47.0 0.3 convolution_add_fusion.2
  47.2 1.5 fusion.28
  48.8 2.3 %collective-permute-start.6 = (f32[4,1,384]{2,1,0:T(1,128)S(1)}, f32[4,1,384]{2,1,0:T(1,128)S(1)}, u32[]{:S(2)}, u32[]{:S(2)}) collective-permute-start(f32[4,1,384]{2,1,0:T(1,128)S(1)} %get-tuple-element.28), channel_id=1, source_target_pairs={{0,1},{1,2},{2,3},{3,4},{4,5},{5,6},{6,7},{7,8},{8,9},{9,10},{10,1... | collective-permute-start | bytes 18440 | tf_op jit(solution)/shard_map/ppermute | solution.py:22
  51.1 2.7 %collective-permute-start.7 = (f32[4,1,384]{2,1,0:T(1,128)S(1)}, f32[4,1,384]{2,1,0:T(1,128)S(1)}, u32[]{:S(2)}, u32[]{:S(2)}) collective-permute-start(f32[4,1,384]{2,1,0:T(1,128)S(1)} %get-tuple-element.29), channel_id=1, source_target_pairs={{1,0},{2,1},{3,2},{4,3},{5,4},{6,5},{7,6},{8,7},{9,8},{10,9},{11,1... | collective-permute-start | bytes 18440 | tf_op jit(solution)/shard_map/ppermute | solution.py:22
  53.8 2.3 %collective-permute-done.7 = f32[4,1,384]{2,1,0:T(1,128)S(1)} collective-permute-done((f32[4,1,384]{2,1,0:T(1,128)S(1)}, f32[4,1,384]{2,1,0:T(1,128)S(1)}, u32[]{:S(2)}, u32[]{:S(2)}) %collective-permute-start.7) | collective-permute-done | bytes 6176 | tf_op jit(solution)/shard_map/ppermute | solution.py:22
  56.1 8.3 %collective-permute-start.8 = (f32[1,7,384]{2,1,0:T(8,128)S(1)}, f32[1,7,384]{2,1,0:T(8,128)S(1)}, u32[]{:S(2)}, u32[]{:S(2)}) collective-permute-start(f32[1,7,384]{2,1,0:T(8,128)S(1)} %pad_maximum_fusion.10), channel_id=1, source_target_pairs={{0,64},{64,128},{128,192},{192,256},{256,320},{320,384},{384,448},... | collective-permute-start | bytes 32264 | tf_op jit(solution)/shard_map/ppermute | solution.py:22
  64.5 0.8 collective-permute-done.8
  65.3 1.3 collective-permute-start.9
  66.6 7.8 %collective-permute-done.9 = f32[1,7,384]{2,1,0:T(8,128)S(1)} collective-permute-done((f32[1,7,384]{2,1,0:T(8,128)S(1)}, f32[1,7,384]{2,1,0:T(8,128)S(1)}, u32[]{:S(2)}, u32[]{:S(2)}) %collective-permute-start.9) | collective-permute-done | bytes 10784 | tf_op jit(solution)/shard_map/ppermute | solution.py:22
  74.5 1.0 fusion.27
  76.3 0.3 fusion.184
  76.6 0.3 fusion.67
  76.8 0.3 convolution_add_fusion.1
  77.1 0.3 convolution_add_fusion
  77.4 1.5 fusion.26
  78.9 3.7 %collective-permute-start.10 = (f32[4,1,384]{2,1,0:T(1,128)S(1)}, f32[4,1,384]{2,1,0:T(1,128)S(1)}, u32[]{:S(2)}, u32[]{:S(2)}) collective-permute-start(f32[4,1,384]{2,1,0:T(1,128)S(1)} %slice.279), channel_id=1, source_target_pairs={{0,1},{1,2},{2,3},{3,4},{4,5},{5,6},{6,7},{7,8},{8,9},{9,10},{10,1... | collective-permute-start | bytes 18440 | tf_op jit(solution)/shard_map/ppermute | solution.py:22
  82.6 0.7 collective-permute-done.10
  83.4 8.5 %collective-permute-start.11 = (f32[1,6,384]{2,1,0:T(8,128)S(1)}, f32[1,6,384]{2,1,0:T(8,128)S(1)}, u32[]{:S(2)}, u32[]{:S(2)}) collective-permute-start(f32[1,6,384]{2,1,0:T(8,128)S(1)} %pad_maximum_fusion.9), channel_id=1, source_target_pairs={{0,64},{64,128},{128,192},{192,256},{256,320},{320,384},{384,448},... | collective-permute-start | bytes 27656 | tf_op jit(solution)/shard_map/ppermute | solution.py:22
  91.8 0.8 collective-permute-done.11
  93.2 18.8 %psum.35 = f32[6]{0:T(128)S(1)} all-reduce(f32[6]{0:T(128)S(1)} %reduce_sum.9), channel_id=1, replica_groups=mesh['bx_0'=4,'bx_1'=3,'by_0'=4,'by_1'=8,'by_2'=2] {'bx_0'}, use_global_device_ids=true, to_apply=%region_1.2 | all-reduce | flops 6 | bytes 48 | tf_op jit(solution)/shard_map/psum | solution.py:27
  112.0 7.7 %psum.36 = f32[6]{0:T(128)S(1)} all-reduce(f32[6]{0:T(128)S(1)} %psum.35), channel_id=1, replica_groups=mesh['bx_0'=4,'bx_1'=3,'by_0'=4,'by_1'=8,'by_2'=2] {'bx_1'}, use_global_device_ids=true, to_apply=%region_2.3 | all-reduce | flops 6 | bytes 48 | tf_op jit(solution)/shard_map/psum | solution.py:27
  119.7 12.5 %psum.37 = f32[6]{0:T(128)S(1)} all-reduce(f32[6]{0:T(128)S(1)} %psum.36), channel_id=1, replica_groups=mesh['bx_0'=4,'bx_1'=3,'by_0'=4,'by_1'=8,'by_2'=2] {'by_0'}, use_global_device_ids=true, to_apply=%region_3.4 | all-reduce | flops 6 | bytes 48 | tf_op jit(solution)/shard_map/psum | solution.py:27
  132.2 13.5 %psum.38 = f32[6]{0:T(128)S(1)} all-reduce(f32[6]{0:T(128)S(1)} %psum.37), channel_id=1, replica_groups=mesh['bx_0'=4,'bx_1'=3,'by_0'=4,'by_1'=8,'by_2'=2] {'by_1'}, use_global_device_ids=true, to_apply=%region_4.5 | all-reduce | flops 6 | bytes 48 | tf_op jit(solution)/shard_map/psum | solution.py:27
  145.7 13.6 %psum.39 = f32[6]{0:T(128)S(1)} all-reduce(f32[6]{0:T(128)S(1)} %psum.38), channel_id=1, replica_groups=mesh['bx_0'=4,'bx_1'=3,'by_0'=4,'by_1'=8,'by_2'=2] {'by_2'}, use_global_device_ids=true, to_apply=%region_5.6 | all-reduce | flops 6 | bytes 48 | tf_op jit(solution)/shard_map/psum | solution.py:27
  159.3 0.7 fusion.182
  167.0 0.7 multiply_subtract_fusion
  (156 shorter events, 4.6 us)
Async XLA Ops:
  0.6 5.5 %copy-start.5 = (f32[32,28]{1,0:T(8,128)S(1)}, f32[32,28]{1,0:T(8,128)}, u32[]{:S(2)}) copy-start(f32[32,28]{1,0:T(8,128)} %constant.111.clone) | copy-start | bytes 10756
  0.6 6.0 %copy-start.29 = (f32[4]{0:T(128)S(1)}, f32[4]{0:T(128)}, u32[]{:S(2)}) copy-start(f32[4]{0:T(128)} %constant.116.clone) | copy-start | bytes 52
  0.7 6.0 %copy-start.30 = (f32[4]{0:T(128)S(1)}, f32[4]{0:T(128)}, u32[]{:S(2)}) copy-start(f32[4]{0:T(128)} %constant.115.clone) | copy-start | bytes 52
  0.7 6.0 %copy-start.27 = (f32[4]{0:T(128)S(1)}, f32[4]{0:T(128)}, u32[]{:S(2)}) copy-start(f32[4]{0:T(128)} %constant.118.clone) | copy-start | bytes 52
  0.7 6.0 %copy-start.28 = (f32[4]{0:T(128)S(1)}, f32[4]{0:T(128)}, u32[]{:S(2)}) copy-start(f32[4]{0:T(128)} %constant.117.clone) | copy-start | bytes 52
  0.7 6.1 %copy-start.25 = (f32[4]{0:T(128)S(1)}, f32[4]{0:T(128)}, u32[]{:S(2)}) copy-start(f32[4]{0:T(128)} %constant.120.clone) | copy-start | bytes 52
  0.7 6.1 %copy-start.26 = (f32[4]{0:T(128)S(1)}, f32[4]{0:T(128)}, u32[]{:S(2)}) copy-start(f32[4]{0:T(128)} %constant.119.clone) | copy-start | bytes 52
  0.7 6.1 %copy-start.23 = (f32[4]{0:T(128)S(1)}, f32[4]{0:T(128)}, u32[]{:S(2)}) copy-start(f32[4]{0:T(128)} %constant.122.clone) | copy-start | bytes 52
  0.7 6.1 %copy-start.24 = (f32[4]{0:T(128)S(1)}, f32[4]{0:T(128)}, u32[]{:S(2)}) copy-start(f32[4]{0:T(128)} %constant.121.clone) | copy-start | bytes 52
  0.7 6.2 %copy-start.21 = (f32[4]{0:T(128)S(1)}, f32[4]{0:T(128)}, u32[]{:S(2)}) copy-start(f32[4]{0:T(128)} %constant.126.clone) | copy-start | bytes 52
  0.8 6.2 %copy-start.22 = (f32[4]{0:T(128)S(1)}, f32[4]{0:T(128)}, u32[]{:S(2)}) copy-start(f32[4]{0:T(128)} %constant.125.clone) | copy-start | bytes 52
  0.8 6.2 %copy-start.19 = (f32[4]{0:T(128)S(1)}, f32[4]{0:T(128)}, u32[]{:S(2)}) copy-start(f32[4]{0:T(128)} %constant.128.clone) | copy-start | bytes 52
  0.8 6.2 %copy-start.20 = (f32[4]{0:T(128)S(1)}, f32[4]{0:T(128)}, u32[]{:S(2)}) copy-start(f32[4]{0:T(128)} %constant.127.clone) | copy-start | bytes 52
  0.8 6.3 %copy-start.6 = (f32[32,28]{1,0:T(8,128)S(1)}, f32[32,28]{1,0:T(8,128)}, u32[]{:S(2)}) copy-start(f32[32,28]{1,0:T(8,128)} %constant.147) | copy-start | bytes 10756
  0.8 6.5 %copy-start.10 = (f32[32,28]{1,0:T(8,128)S(1)}, f32[32,28]{1,0:T(8,128)}, u32[]{:S(2)}) copy-start(f32[32,28]{1,0:T(8,128)} %constant.148) | copy-start | bytes 10756
  0.9 6.7 %copy-start.9 = (f32[32,28]{1,0:T(8,128)S(1)}, f32[32,28]{1,0:T(8,128)}, u32[]{:S(2)}) copy-start(f32[32,28]{1,0:T(8,128)} %constant.112.clone) | copy-start | bytes 10756
  1.8 26.4 %collective-permute-start = (f32[1,6,384]{2,1,0:T(8,128)S(1)}, f32[1,6,384]{2,1,0:T(8,128)S(1)}, u32[]{:S(2)}, u32[]{:S(2)}) collective-permute-start(f32[1,6,384]{2,1,0:T(8,128)S(1)} %slice.250), channel_id=1, source_target_pairs={{64,0},{128,64},{192,128},{256,192},{320,256},{384,320},{448,384},... | collective-permute-start | bytes 27656 | tf_op jit(solution)/shard_map/ppermute | solution.py:22
  4.9 2.9 %copy-start.8 = (f32[32,28]{1,0:T(8,128)S(1)}, f32[32,28]{1,0:T(8,128)}, u32[]{:S(2)}) copy-start(f32[32,28]{1,0:T(8,128)} %constant.113.clone) | copy-start | bytes 10756
  6.0 2.0 %copy-start.7 = (f32[32,28]{1,0:T(8,128)S(1)}, f32[32,28]{1,0:T(8,128)}, u32[]{:S(2)}) copy-start(f32[32,28]{1,0:T(8,128)} %constant.146) | copy-start | bytes 10756
  10.5 15.0 %copy-start.1 = (bf16[7,4,4,4,1,2,128]{6,5,4,3,2,1,0:T(2,128)(2,1)S(1)}, bf16[7,4,4,4,1,2,128]{6,5,4,3,2,1,0:T(2,128)(2,1)}, u32[]{:S(2)}) copy-start(bf16[7,4,4,4,1,2,128]{6,5,4,3,2,1,0:T(2,128)(2,1)} %param.44) | copy-start | bytes 688132
  11.6 14.1 %copy-start.17 = (f32[4]{0:T(128)S(1)}, f32[4]{0:T(128)}, u32[]{:S(2)}) copy-start(f32[4]{0:T(128)} %constant.133.clone) | copy-start | bytes 52
  11.6 14.1 %copy-start.18 = (f32[4]{0:T(128)S(1)}, f32[4]{0:T(128)}, u32[]{:S(2)}) copy-start(f32[4]{0:T(128)} %constant.132.clone) | copy-start | bytes 52
  11.6 14.2 %copy-start.15 = (f32[4]{0:T(128)S(1)}, f32[4]{0:T(128)}, u32[]{:S(2)}) copy-start(f32[4]{0:T(128)} %constant.135.clone) | copy-start | bytes 52
  11.6 14.2 %copy-start.16 = (f32[4]{0:T(128)S(1)}, f32[4]{0:T(128)}, u32[]{:S(2)}) copy-start(f32[4]{0:T(128)} %constant.134.clone) | copy-start | bytes 52
  11.6 14.2 %copy-start.13 = (f32[4]{0:T(128)S(1)}, f32[4]{0:T(128)}, u32[]{:S(2)}) copy-start(f32[4]{0:T(128)} %constant.137.clone) | copy-start | bytes 52
  11.7 14.2 %copy-start.14 = (f32[4]{0:T(128)S(1)}, f32[4]{0:T(128)}, u32[]{:S(2)}) copy-start(f32[4]{0:T(128)} %constant.136.clone) | copy-start | bytes 52
  11.7 14.3 %copy-start.11 = (f32[4]{0:T(128)S(1)}, f32[4]{0:T(128)}, u32[]{:S(2)}) copy-start(f32[4]{0:T(128)} %constant.139.clone) | copy-start | bytes 52
  11.7 14.3 %copy-start.12 = (f32[4]{0:T(128)S(1)}, f32[4]{0:T(128)}, u32[]{:S(2)}) copy-start(f32[4]{0:T(128)} %constant.138.clone) | copy-start | bytes 52
  11.7 15.1 %collective-permute-start.2 = (f32[4,1,384]{2,1,0:T(1,128)S(1)}, f32[4,1,384]{2,1,0:T(1,128)S(1)}, u32[]{:S(2)}, u32[]{:S(2)}) collective-permute-start(f32[4,1,384]{2,1,0:T(1,128)S(1)} %get-tuple-element.32), channel_id=1, source_target_pairs={{0,1},{1,2},{2,3},{3,4},{4,5},{5,6},{6,7},{7,8},{8,9},{9,10},{10,1... | collective-permute-start | bytes 18440 | tf_op jit(solution)/shard_map/ppermute | solution.py:22
  16.3 10.5 %collective-permute-start.3 = (f32[4,1,384]{2,1,0:T(1,128)S(1)}, f32[4,1,384]{2,1,0:T(1,128)S(1)}, u32[]{:S(2)}, u32[]{:S(2)}) collective-permute-start(f32[4,1,384]{2,1,0:T(1,128)S(1)} %get-tuple-element.33), channel_id=1, source_target_pairs={{1,0},{2,1},{3,2},{4,3},{5,4},{6,5},{7,6},{8,7},{9,8},{10,9},{11,1... | collective-permute-start | bytes 18440 | tf_op jit(solution)/shard_map/ppermute | solution.py:22
  26.9 9.6 %collective-permute-start.5 = (f32[1,7,384]{2,1,0:T(8,128)S(1)}, f32[1,7,384]{2,1,0:T(8,128)S(1)}, u32[]{:S(2)}, u32[]{:S(2)}) collective-permute-start(f32[1,7,384]{2,1,0:T(8,128)S(1)} %pad_maximum_fusion.13), channel_id=1, source_target_pairs={{64,0},{128,64},{192,128},{256,192},{320,256},{384,320},{448,384},... | collective-permute-start | bytes 32264 | tf_op jit(solution)/shard_map/ppermute | solution.py:22
  28.2 16.0 %collective-permute-start.1 = (f32[4,1,384]{2,1,0:T(1,128)S(1)}, f32[4,1,384]{2,1,0:T(1,128)S(1)}, u32[]{:S(2)}, u32[]{:S(2)}) collective-permute-start(f32[4,1,384]{2,1,0:T(1,128)S(1)} %pad_maximum_fusion.14), channel_id=1, source_target_pairs={{1,0},{2,1},{3,2},{4,3},{5,4},{6,5},{7,6},{8,7},{9,8},{10,9},{11,1... | collective-permute-start | bytes 18440 | tf_op jit(solution)/shard_map/ppermute | solution.py:22
  36.5 7.8 %collective-permute-start.4 = (f32[1,7,384]{2,1,0:T(8,128)S(1)}, f32[1,7,384]{2,1,0:T(8,128)S(1)}, u32[]{:S(2)}, u32[]{:S(2)}) collective-permute-start(f32[1,7,384]{2,1,0:T(8,128)S(1)} %get-tuple-element.9), channel_id=1, source_target_pairs={{0,64},{64,128},{128,192},{192,256},{256,320},{320,384},{384,448},... | collective-permute-start | bytes 32264 | tf_op jit(solution)/shard_map/ppermute | solution.py:22
  44.3 1.1 copy-start.4
  44.3 1.3 copy-start.3
  44.3 1.5 copy-start
  48.8 5.0 %collective-permute-start.6 = (f32[4,1,384]{2,1,0:T(1,128)S(1)}, f32[4,1,384]{2,1,0:T(1,128)S(1)}, u32[]{:S(2)}, u32[]{:S(2)}) collective-permute-start(f32[4,1,384]{2,1,0:T(1,128)S(1)} %get-tuple-element.28), channel_id=1, source_target_pairs={{0,1},{1,2},{2,3},{3,4},{4,5},{5,6},{6,7},{7,8},{8,9},{9,10},{10,1... | collective-permute-start | bytes 18440 | tf_op jit(solution)/shard_map/ppermute | solution.py:22
  51.1 4.9 %collective-permute-start.7 = (f32[4,1,384]{2,1,0:T(1,128)S(1)}, f32[4,1,384]{2,1,0:T(1,128)S(1)}, u32[]{:S(2)}, u32[]{:S(2)}) collective-permute-start(f32[4,1,384]{2,1,0:T(1,128)S(1)} %get-tuple-element.29), channel_id=1, source_target_pairs={{1,0},{2,1},{3,2},{4,3},{5,4},{6,5},{7,6},{8,7},{9,8},{10,9},{11,1... | collective-permute-start | bytes 18440 | tf_op jit(solution)/shard_map/ppermute | solution.py:22
  56.1 9.2 %collective-permute-start.8 = (f32[1,7,384]{2,1,0:T(8,128)S(1)}, f32[1,7,384]{2,1,0:T(8,128)S(1)}, u32[]{:S(2)}, u32[]{:S(2)}) collective-permute-start(f32[1,7,384]{2,1,0:T(8,128)S(1)} %pad_maximum_fusion.10), channel_id=1, source_target_pairs={{0,64},{64,128},{128,192},{192,256},{256,320},{320,384},{384,448},... | collective-permute-start | bytes 32264 | tf_op jit(solution)/shard_map/ppermute | solution.py:22
  65.3 9.1 %collective-permute-start.9 = (f32[1,7,384]{2,1,0:T(8,128)S(1)}, f32[1,7,384]{2,1,0:T(8,128)S(1)}, u32[]{:S(2)}, u32[]{:S(2)}) collective-permute-start(f32[1,7,384]{2,1,0:T(8,128)S(1)} %get-tuple-element.7), channel_id=1, source_target_pairs={{64,0},{128,64},{192,128},{256,192},{320,256},{384,320},{448,384},... | collective-permute-start | bytes 32264 | tf_op jit(solution)/shard_map/ppermute | solution.py:22
  77.4 15.4 %copy-start.2 = (f32[3,6,384]{2,1,0:T(8,128)S(1)}, f32[3,6,384]{2,1,0:T(8,128)}, u32[]{:S(2)}) copy-start(f32[3,6,384]{2,1,0:T(8,128)} %param.43) | copy-start | bytes 82948
  78.9 4.4 %collective-permute-start.10 = (f32[4,1,384]{2,1,0:T(1,128)S(1)}, f32[4,1,384]{2,1,0:T(1,128)S(1)}, u32[]{:S(2)}, u32[]{:S(2)}) collective-permute-start(f32[4,1,384]{2,1,0:T(1,128)S(1)} %slice.279), channel_id=1, source_target_pairs={{0,1},{1,2},{2,3},{3,4},{4,5},{5,6},{6,7},{7,8},{8,9},{9,10},{10,1... | collective-permute-start | bytes 18440 | tf_op jit(solution)/shard_map/ppermute | solution.py:22
  83.4 9.3 %collective-permute-start.11 = (f32[1,6,384]{2,1,0:T(8,128)S(1)}, f32[1,6,384]{2,1,0:T(8,128)S(1)}, u32[]{:S(2)}, u32[]{:S(2)}) collective-permute-start(f32[1,6,384]{2,1,0:T(8,128)S(1)} %pad_maximum_fusion.9), channel_id=1, source_target_pairs={{0,64},{64,128},{128,192},{192,256},{256,320},{320,384},{384,448},... | collective-permute-start | bytes 27656 | tf_op jit(solution)/shard_map/ppermute | solution.py:22

commit v9 on v7

--- a/solution.py
+++ b/solution.py
@@ -240,6 +240,29 @@
     return shifted(plane, BY, 1)
 
 
+def moved(value, steps_x, steps_y):
+    count_x = lax.axis_size(BX)
+    count_y = lax.axis_size(BY)
+    pairs = []
+    for source_x in range(count_x):
+        for source_y in range(count_y):
+            target_x, target_y = source_x + steps_x, source_y + steps_y
+            if 0 <= target_x < count_x and 0 <= target_y < count_y:
+                pairs.append((source_x * count_y + source_y, target_x * count_y + target_y))
+    return lax.ppermute(value, BX_BY, pairs)
+
+
+def gather_contributions(contributions, rows_x, rows_y, rows_z):
+    own = contributions[:rows_x, :rows_y, :rows_z]
+    from_x = lower_x(contributions[rows_x:, :rows_y, :rows_z])
+    from_y = lower_y(contributions[:rows_x, rows_y:, :rows_z])
+    from_corner = moved(contributions[rows_x:, rows_y:, :rows_z], 1, 1)
+    head = own[0:1] + from_x
+    head = jnp.concatenate([head[:, 0:1] + from_corner, head[:, 1:]], 1)
+    own = jnp.concatenate([head, own[1:]], 0)
+    return jnp.concatenate([own[:, 0:1] + from_y, own[:, 1:]], 1)
+
+
 def global_sums(terms):
     return (over_axes(terms[0], BX_BY), over_axes(terms[1], BX_BY))
 
@@ -280,31 +303,40 @@
     anchor = (cotangent[0, 0, 0] * 0.0).astype(jnp.int32)
     diagonal = collect(band_diagonal(coeffs, counts, anchor), rows_x, rows_y, rows_z)
 
-    def operator(dof_field):
-        return (
-            collect(band_operator(pad_top(widen(dof_field)), coeffs, counts, anchor), rows_x, rows_y, rows_z)
-            * interior
-        )
+    wide_extent = (rows_x + 1, rows_y + 1, rows_z)
+    wide_x = lax.broadcasted_iota(jnp.int32, wide_extent, 0) + lax.axis_index(BX) * rows_x
+    wide_y = lax.broadcasted_iota(jnp.int32, wide_extent, 1) + lax.axis_index(BY) * rows_y
+    wide_z = lax.broadcasted_iota(jnp.int32, wide_extent, 2)
+    wide_inside = (
+        (wide_x > 0) & (wide_y > 0) & (wide_z > 0) & (wide_x < total_x) & (wide_y < total_y)
+    )
+    wide_interior = jnp.where(wide_inside, 1.0, 0.0).astype(jnp.float32)
+
+    def contributions(wide_field):
+        return band_operator(pad_top(wide_field), coeffs, counts, anchor)[:, :, :rows_z]
 
     def local_dot(left, right):
         return jnp.sum(left * right)
 
     residual = cotangent * interior
     precond = residual / diagonal
-    image = operator(precond)
+    wide_precond = widen(precond)
+    image = collect(contributions(wide_precond), rows_x, rows_y, rows_z) * interior
     scaled = image / diagonal
-    second = operator(scaled)
+    wide_scaled = widen(scaled)
+    raw_second = contributions(wide_scaled)
+    masked_second = raw_second * wide_interior
     products = jnp.stack(
+        [residual * precond, precond * image, residual * scaled, image * scaled]
+    )
+    wide_products = jnp.stack([wide_precond * masked_second, wide_scaled * masked_second])
+    terms = jnp.concatenate(
         [
-            residual * precond,
-            precond * image,
-            residual * scaled,
-            image * scaled,
-            precond * second,
-            scaled * second,
+            jnp.sum(products.reshape(4, -1, products.shape[-1]), axis=(1, 2)),
+            jnp.sum(wide_products.reshape(2, -1, wide_products.shape[-1]), axis=(1, 2)),
         ]
     )
-    terms = jnp.sum(products.reshape(6, -1, products.shape[-1]), axis=(1, 2))
+    second = gather_contributions(raw_second, rows_x, rows_y, rows_z) * interior
     summed = over_axes(terms, BX_BY)
     rz_now, curvature, cross_r, cross_q, cross_z, curvature_w = [summed[k] for k in range(6)]
     alpha = rz_now / curvature

time: 163 us -> 160 us (0.982)
  blocking collectives: 61.2 us -> 56.6 us
  starting transfers between devices: 37.2 us -> 40.5 us
  waiting for transfers between devices: 33.5 us -> 31.5 us
    ppermute x0 -> x1, starting transfers between devices: none -> 6.27 us  [moved(): return lax.ppermute(value, BX_BY, pairs)]
    psum x5, blocking collectives: 61.2 us -> 56.6 us  [over_axes(): value = lax.psum(value, axis)]
    ppermute x10, starting transfers between devices: 37.2 us -> 34.3 us  [shifted(): lax.ppermute(value, axis, [(source, source + steps) for source in range(i...]
    ppermute x10, waiting for transfers between devices: 33.5 us -> 31.5 us  [shifted(): lax.ppermute(value, axis, [(source, source + steps) for source in range(i...]
  transfers between devices with their start and end apart: 10 -> 11, of which waited for: 10 -> 8; matrix products, arithmetic and copies ran while one was open for 1% -> 2% of each run, Pallas kernels for 0% -> 0%
where the time goes in v9:
time: 160 us; the launch traced here: 159 us
  blocking collectives  56.6 us (35%)
  starting transfers between devices  40.5 us (25%)
  waiting for transfers between devices  31.5 us (20%)
  matrix products  13.4 us (8%)
  between operations  9.53 us (6%)
  local copies, waits for them, and re-layouts  4.76 us (3%)
  other arithmetic  2.49 us (2%)
    psum x5, blocking collectives, over_axes(): value = lax.psum(value, axis)  56.6 us
    ppermute x10, starting transfers between devices, shifted(): lax.ppermute(value, axis, [(source, source + steps) for source in range(i...  34.3 us
    ppermute x10, waiting for transfers between devices, shifted(): lax.ppermute(value, axis, [(source, source + steps) for source in range(i...  31.5 us
    dot_general x30, matrix products, mat(): return jnp.matmul(left, right, precision=lax.Precision.HIGHEST)  13.4 us
    ppermute x1, starting transfers between devices, moved(): return lax.ppermute(value, BX_BY, pairs)  6.27 us
  transfers between devices with their start and end apart: 11, of which 8 were waited for; matrix products, arithmetic and copies ran while one was open for 2% of the time, Pallas kernels for 0%

profile of v9, /device:TPU:1, one launch (start us, length us, event | category | flops | bytes accessed | tf_op | source)
XLA Modules:
  0.0 158.8 jit_solution(15697720515162657573)
XLA Ops:
  0.8 1.2 slice.199
  2.8 1.0 fusion.180
  4.0 0.2 fusion.132
  4.2 0.2 fusion.141
  4.9 0.2 fusion.129
  6.1 1.1 fusion.14
  7.2 1.1 convolution_add_fusion.6
  8.3 1.1 convolution_add_fusion.4
  9.4 4.6 %collective-permute-start = (f32[4,1,384]{2,1,0:T(1,128)S(1)}, f32[4,1,384]{2,1,0:T(1,128)S(1)}, u32[]{:S(2)}, u32[]{:S(2)}) collective-permute-start(f32[4,1,384]{2,1,0:T(1,128)S(1)} %slice.260), channel_id=1, source_target_pairs={{0,1},{1,2},{2,3},{3,4},{4,5},{5,6},{6,7},{7,8},{8,9},{9,10},{10,1... | collective-permute-start | bytes 18440 | tf_op jit(solution)/shard_map/ppermute | solution.py:22
  14.2 0.2 bitcast_convert_fusion
  15.1 0.5 select_add_fusion.1
  15.6 6.3 %collective-permute-done = f32[4,1,384]{2,1,0:T(1,128)S(1)} collective-permute-done((f32[4,1,384]{2,1,0:T(1,128)S(1)}, f32[4,1,384]{2,1,0:T(1,128)S(1)}, u32[]{:S(2)}, u32[]{:S(2)}) %collective-permute-start) | collective-permute-done | bytes 6176 | tf_op jit(solution)/shard_map/ppermute | solution.py:22
  21.9 4.4 %collective-permute-start.1 = (f32[1,6,384]{2,1,0:T(8,128)S(1)}, f32[1,6,384]{2,1,0:T(8,128)S(1)}, u32[]{:S(2)}, u32[]{:S(2)}) collective-permute-start(f32[1,6,384]{2,1,0:T(8,128)S(1)} %pad_maximum_fusion.14), channel_id=1, source_target_pairs={{0,64},{64,128},{128,192},{192,256},{256,320},{320,384},{384,448},... | collective-permute-start | bytes 27656 | tf_op jit(solution)/shard_map/ppermute | solution.py:22
  26.3 0.8 collective-permute-done.1
  27.2 1.3 collective-permute-start.2
  29.1 7.5 %collective-permute-done.2 = f32[1,6,384]{2,1,0:T(8,128)S(1)} collective-permute-done((f32[1,6,384]{2,1,0:T(8,128)S(1)}, f32[1,6,384]{2,1,0:T(8,128)S(1)}, u32[]{:S(2)}, u32[]{:S(2)}) %collective-permute-start.2) | collective-permute-done | bytes 9248 | tf_op jit(solution)/shard_map/ppermute | solution.py:22
  36.6 2.3 %collective-permute-start.3 = (f32[4,1,384]{2,1,0:T(1,128)S(1)}, f32[4,1,384]{2,1,0:T(1,128)S(1)}, u32[]{:S(2)}, u32[]{:S(2)}) collective-permute-start(f32[4,1,384]{2,1,0:T(1,128)S(1)} %pad_maximum_fusion.16), channel_id=1, source_target_pairs={{1,0},{2,1},{3,2},{4,3},{5,4},{6,5},{7,6},{8,7},{9,8},{10,9},{11,1... | collective-permute-start | bytes 18440 | tf_op jit(solution)/shard_map/ppermute | solution.py:22
  38.9 4.0 %collective-permute-done.3 = f32[4,1,384]{2,1,0:T(1,128)S(1)} collective-permute-done((f32[4,1,384]{2,1,0:T(1,128)S(1)}, f32[4,1,384]{2,1,0:T(1,128)S(1)}, u32[]{:S(2)}, u32[]{:S(2)}) %collective-permute-start.3) | collective-permute-done | bytes 6176 | tf_op jit(solution)/shard_map/ppermute | solution.py:22
  43.0 1.0 fusion.29
  44.8 0.3 fusion.182
  45.1 0.3 fusion.64
  45.4 0.3 convolution_add_fusion.3
  45.6 0.3 convolution_add_fusion.2
  45.9 1.5 fusion.28
  47.4 1.9 %collective-permute-start.4 = (f32[4,1,384]{2,1,0:T(1,128)S(1)}, f32[4,1,384]{2,1,0:T(1,128)S(1)}, u32[]{:S(2)}, u32[]{:S(2)}) collective-permute-start(f32[4,1,384]{2,1,0:T(1,128)S(1)} %slice.273), channel_id=1, source_target_pairs={{0,1},{1,2},{2,3},{3,4},{4,5},{5,6},{6,7},{7,8},{8,9},{9,10},{10,1... | collective-permute-start | bytes 18440 | tf_op jit(solution)/shard_map/ppermute | solution.py:22
  49.4 1.1 collective-permute-done.4
  50.5 7.9 %collective-permute-start.5 = (f32[1,6,384]{2,1,0:T(8,128)S(1)}, f32[1,6,384]{2,1,0:T(8,128)S(1)}, u32[]{:S(2)}, u32[]{:S(2)}) collective-permute-start(f32[1,6,384]{2,1,0:T(8,128)S(1)} %pad_maximum_fusion.13), channel_id=1, source_target_pairs={{0,64},{64,128},{128,192},{192,256},{256,320},{320,384},{384,448},... | collective-permute-start | bytes 27656 | tf_op jit(solution)/shard_map/ppermute | solution.py:22
  58.4 0.8 collective-permute-done.5
  59.4 1.3 collective-permute-start.6
  60.8 8.1 %collective-permute-done.6 = f32[1,6,384]{2,1,0:T(8,128)S(1)} collective-permute-done((f32[1,6,384]{2,1,0:T(8,128)S(1)}, f32[1,6,384]{2,1,0:T(8,128)S(1)}, u32[]{:S(2)}, u32[]{:S(2)}) %collective-permute-start.6) | collective-permute-done | bytes 9248 | tf_op jit(solution)/shard_map/ppermute | solution.py:22
  68.9 3.8 %collective-permute-start.7 = (f32[4,1,384]{2,1,0:T(1,128)S(1)}, f32[4,1,384]{2,1,0:T(1,128)S(1)}, u32[]{:S(2)}, u32[]{:S(2)}) collective-permute-start(f32[4,1,384]{2,1,0:T(1,128)S(1)} %pad_maximum_fusion.15), channel_id=1, source_target_pairs={{1,0},{2,1},{3,2},{4,3},{5,4},{6,5},{7,6},{8,7},{9,8},{10,9},{11,1... | collective-permute-start | bytes 18440 | tf_op jit(solution)/shard_map/ppermute | solution.py:22
  72.8 2.9 %collective-permute-done.7 = f32[4,1,384]{2,1,0:T(1,128)S(1)} collective-permute-done((f32[4,1,384]{2,1,0:T(1,128)S(1)}, f32[4,1,384]{2,1,0:T(1,128)S(1)}, u32[]{:S(2)}, u32[]{:S(2)}) %collective-permute-start.7) | collective-permute-done | bytes 6176 | tf_op jit(solution)/shard_map/ppermute | solution.py:22
  75.8 1.0 fusion.27
  77.6 0.3 fusion.183
  77.9 0.3 fusion.67
  78.2 0.3 convolution_add_fusion.1
  78.4 0.3 convolution_add_fusion
  78.7 1.5 fusion.26
  80.5 12.1 %psum.35 = f32[6]{0:T(128)S(1)} all-reduce(f32[6]{0:T(128)S(1)} %pad_maximum_fusion.17), channel_id=1, replica_groups=mesh['bx_0'=4,'bx_1'=3,'by_0'=4,'by_1'=8,'by_2'=2] {'bx_0'}, use_global_device_ids=true, to_apply=%region_2.3 | all-reduce | flops 6 | bytes 48 | tf_op jit(solution)/shard_map/psum | solution.py:27
  92.6 9.9 %psum.36 = f32[6]{0:T(128)S(1)} all-reduce(f32[6]{0:T(128)S(1)} %psum.35), channel_id=1, replica_groups=mesh['bx_0'=4,'bx_1'=3,'by_0'=4,'by_1'=8,'by_2'=2] {'bx_1'}, use_global_device_ids=true, to_apply=%region_3.4 | all-reduce | flops 6 | bytes 48 | tf_op jit(solution)/shard_map/psum | solution.py:27
  102.5 12.7 %psum.37 = f32[6]{0:T(128)S(1)} all-reduce(f32[6]{0:T(128)S(1)} %psum.36), channel_id=1, replica_groups=mesh['bx_0'=4,'bx_1'=3,'by_0'=4,'by_1'=8,'by_2'=2] {'by_0'}, use_global_device_ids=true, to_apply=%region_4.5 | all-reduce | flops 6 | bytes 48 | tf_op jit(solution)/shard_map/psum | solution.py:27
  115.2 12.8 %psum.38 = f32[6]{0:T(128)S(1)} all-reduce(f32[6]{0:T(128)S(1)} %psum.37), channel_id=1, replica_groups=mesh['bx_0'=4,'bx_1'=3,'by_0'=4,'by_1'=8,'by_2'=2] {'by_1'}, use_global_device_ids=true, to_apply=%region_5.6 | all-reduce | flops 6 | bytes 48 | tf_op jit(solution)/shard_map/psum | solution.py:27
  128.0 4.6 %collective-permute-start.8 = (f32[1,6,384]{2,1,0:T(8,128)S(1)}, f32[1,6,384]{2,1,0:T(8,128)S(1)}, u32[]{:S(2)}, u32[]{:S(2)}) collective-permute-start(f32[1,6,384]{2,1,0:T(8,128)S(1)} %slice.280), channel_id=1, source_target_pairs={{0,64},{64,128},{128,192},{192,256},{256,320},{320,384},{384,448},... | collective-permute-start | bytes 27656 | tf_op jit(solution)/shard_map/ppermute | solution.py:22
  132.5 9.2 %psum.39 = f32[6]{0:T(128)S(1)} all-reduce(f32[6]{0:T(128)S(1)} %psum.38), channel_id=1, replica_groups=mesh['bx_0'=4,'bx_1'=3,'by_0'=4,'by_1'=8,'by_2'=2] {'by_2'}, use_global_device_ids=true, to_apply=%region_6.7 | all-reduce | flops 6 | bytes 48 | tf_op jit(solution)/shard_map/psum | solution.py:27
  141.7 0.6 fusion.181
  146.9 6.3 %collective-permute-start.9 = (f32[1,1,384]{2,1,0:T(1,128)S(1)}, f32[1,1,384]{2,1,0:T(1,128)S(1)}, u32[]{:S(2)}, u32[]{:S(2)}) collective-permute-start(f32[1,1,384]{2,1,0:T(1,128)S(1)} %slice.282), channel_id=1, source_target_pairs={{0,65},{1,66},{2,67},{3,68},{4,69},{5,70},{6,71},{7,72},{8,73},{9,... | collective-permute-start | bytes 4616 | tf_op jit(solution)/shard_map/ppermute | solution.py:252
  153.2 2.2 %collective-permute-start.10 = (f32[3,1,384]{2,1,0:T(1,128)S(1)}, f32[3,1,384]{2,1,0:T(1,128)S(1)}, u32[]{:S(2)}, u32[]{:S(2)}) collective-permute-start(f32[3,1,384]{2,1,0:T(1,128)S(1)} %slice.285), channel_id=1, source_target_pairs={{0,1},{1,2},{2,3},{3,4},{4,5},{5,6},{6,7},{7,8},{8,9},{9,10},{10,1... | collective-permute-start | bytes 13832 | tf_op jit(solution)/shard_map/ppermute | solution.py:22
  158.1 0.7 fusion.125
  (166 shorter events, 5.3 us)
Async XLA Ops:
  0.6 3.3 %copy-start.5 = (f32[32,28]{1,0:T(8,128)S(1)}, f32[32,28]{1,0:T(8,128)}, u32[]{:S(2)}) copy-start(f32[32,28]{1,0:T(8,128)} %constant.111.clone) | copy-start | bytes 10756
  0.6 3.8 %copy-start.29 = (f32[4]{0:T(128)S(1)}, f32[4]{0:T(128)}, u32[]{:S(2)}) copy-start(f32[4]{0:T(128)} %constant.116.clone) | copy-start | bytes 52
  0.7 3.8 %copy-start.30 = (f32[4]{0:T(128)S(1)}, f32[4]{0:T(128)}, u32[]{:S(2)}) copy-start(f32[4]{0:T(128)} %constant.115.clone) | copy-start | bytes 52
  0.7 3.8 %copy-start.27 = (f32[4]{0:T(128)S(1)}, f32[4]{0:T(128)}, u32[]{:S(2)}) copy-start(f32[4]{0:T(128)} %constant.118.clone) | copy-start | bytes 52
  0.7 3.8 %copy-start.28 = (f32[4]{0:T(128)S(1)}, f32[4]{0:T(128)}, u32[]{:S(2)}) copy-start(f32[4]{0:T(128)} %constant.117.clone) | copy-start | bytes 52
  0.7 3.9 %copy-start.25 = (f32[4]{0:T(128)S(1)}, f32[4]{0:T(128)}, u32[]{:S(2)}) copy-start(f32[4]{0:T(128)} %constant.120.clone) | copy-start | bytes 52
  0.7 3.9 %copy-start.26 = (f32[4]{0:T(128)S(1)}, f32[4]{0:T(128)}, u32[]{:S(2)}) copy-start(f32[4]{0:T(128)} %constant.119.clone) | copy-start | bytes 52
  0.7 3.9 %copy-start.23 = (f32[4]{0:T(128)S(1)}, f32[4]{0:T(128)}, u32[]{:S(2)}) copy-start(f32[4]{0:T(128)} %constant.122.clone) | copy-start | bytes 52
  0.7 3.9 %copy-start.24 = (f32[4]{0:T(128)S(1)}, f32[4]{0:T(128)}, u32[]{:S(2)}) copy-start(f32[4]{0:T(128)} %constant.121.clone) | copy-start | bytes 52
  0.7 4.0 %copy-start.21 = (f32[4]{0:T(128)S(1)}, f32[4]{0:T(128)}, u32[]{:S(2)}) copy-start(f32[4]{0:T(128)} %constant.126.clone) | copy-start | bytes 52
  0.8 4.0 %copy-start.22 = (f32[4]{0:T(128)S(1)}, f32[4]{0:T(128)}, u32[]{:S(2)}) copy-start(f32[4]{0:T(128)} %constant.125.clone) | copy-start | bytes 52
  0.8 4.0 %copy-start.19 = (f32[4]{0:T(128)S(1)}, f32[4]{0:T(128)}, u32[]{:S(2)}) copy-start(f32[4]{0:T(128)} %constant.128.clone) | copy-start | bytes 52
  0.8 4.0 %copy-start.20 = (f32[4]{0:T(128)S(1)}, f32[4]{0:T(128)}, u32[]{:S(2)}) copy-start(f32[4]{0:T(128)} %constant.127.clone) | copy-start | bytes 52
  0.8 4.1 %copy-start.6 = (f32[32,28]{1,0:T(8,128)S(1)}, f32[32,28]{1,0:T(8,128)}, u32[]{:S(2)}) copy-start(f32[32,28]{1,0:T(8,128)} %constant.147) | copy-start | bytes 10756
  0.8 4.3 %copy-start.10 = (f32[32,28]{1,0:T(8,128)S(1)}, f32[32,28]{1,0:T(8,128)}, u32[]{:S(2)}) copy-start(f32[32,28]{1,0:T(8,128)} %constant.148) | copy-start | bytes 10756
  0.8 4.5 %copy-start.9 = (f32[32,28]{1,0:T(8,128)S(1)}, f32[32,28]{1,0:T(8,128)}, u32[]{:S(2)}) copy-start(f32[32,28]{1,0:T(8,128)} %constant.112.clone) | copy-start | bytes 10756
  2.7 2.8 %copy-start.8 = (f32[32,28]{1,0:T(8,128)S(1)}, f32[32,28]{1,0:T(8,128)}, u32[]{:S(2)}) copy-start(f32[32,28]{1,0:T(8,128)} %constant.113.clone) | copy-start | bytes 10756
  3.8 2.0 %copy-start.7 = (f32[32,28]{1,0:T(8,128)S(1)}, f32[32,28]{1,0:T(8,128)}, u32[]{:S(2)}) copy-start(f32[32,28]{1,0:T(8,128)} %constant.146) | copy-start | bytes 10756
  8.3 5.8 %copy-start.1 = (bf16[7,4,4,4,1,2,128]{6,5,4,3,2,1,0:T(2,128)(2,1)S(1)}, bf16[7,4,4,4,1,2,128]{6,5,4,3,2,1,0:T(2,128)(2,1)}, u32[]{:S(2)}) copy-start(bf16[7,4,4,4,1,2,128]{6,5,4,3,2,1,0:T(2,128)(2,1)} %param.44) | copy-start | bytes 688132
  9.4 12.5 %collective-permute-start = (f32[4,1,384]{2,1,0:T(1,128)S(1)}, f32[4,1,384]{2,1,0:T(1,128)S(1)}, u32[]{:S(2)}, u32[]{:S(2)}) collective-permute-start(f32[4,1,384]{2,1,0:T(1,128)S(1)} %slice.260), channel_id=1, source_target_pairs={{0,1},{1,2},{2,3},{3,4},{4,5},{5,6},{6,7},{7,8},{8,9},{9,10},{10,1... | collective-permute-start | bytes 18440 | tf_op jit(solution)/shard_map/ppermute | solution.py:22
  14.1 0.7 copy-start.17
  14.1 0.7 copy-start.18
  14.1 0.7 copy-start.15
  14.1 0.7 copy-start.16
  14.1 0.8 copy-start.13
  14.1 0.8 copy-start.14
  14.2 0.8 copy-start.11
  14.2 0.8 copy-start.12
  15.1 12.1 %copy-start.2 = (f32[3,6,384]{2,1,0:T(8,128)S(1)}, f32[3,6,384]{2,1,0:T(8,128)}, u32[]{:S(2)}) copy-start(f32[3,6,384]{2,1,0:T(8,128)} %param.43) | copy-start | bytes 82948
  21.9 5.2 %collective-permute-start.1 = (f32[1,6,384]{2,1,0:T(8,128)S(1)}, f32[1,6,384]{2,1,0:T(8,128)S(1)}, u32[]{:S(2)}, u32[]{:S(2)}) collective-permute-start(f32[1,6,384]{2,1,0:T(8,128)S(1)} %pad_maximum_fusion.14), channel_id=1, source_target_pairs={{0,64},{64,128},{128,192},{192,256},{256,320},{320,384},{384,448},... | collective-permute-start | bytes 27656 | tf_op jit(solution)/shard_map/ppermute | solution.py:22
  27.2 9.3 %collective-permute-start.2 = (f32[1,6,384]{2,1,0:T(8,128)S(1)}, f32[1,6,384]{2,1,0:T(8,128)S(1)}, u32[]{:S(2)}, u32[]{:S(2)}) collective-permute-start(f32[1,6,384]{2,1,0:T(8,128)S(1)} %slice.263), channel_id=1, source_target_pairs={{64,0},{128,64},{192,128},{256,192},{320,256},{384,320},{448,384},... | collective-permute-start | bytes 27656 | tf_op jit(solution)/shard_map/ppermute | solution.py:22
  36.6 6.4 %collective-permute-start.3 = (f32[4,1,384]{2,1,0:T(1,128)S(1)}, f32[4,1,384]{2,1,0:T(1,128)S(1)}, u32[]{:S(2)}, u32[]{:S(2)}) collective-permute-start(f32[4,1,384]{2,1,0:T(1,128)S(1)} %pad_maximum_fusion.16), channel_id=1, source_target_pairs={{1,0},{2,1},{3,2},{4,3},{5,4},{6,5},{7,6},{8,7},{9,8},{10,9},{11,1... | collective-permute-start | bytes 18440 | tf_op jit(solution)/shard_map/ppermute | solution.py:22
  43.0 1.1 copy-start.4
  43.0 1.3 copy-start.3
  43.0 1.5 copy-start
  47.4 3.1 %collective-permute-start.4 = (f32[4,1,384]{2,1,0:T(1,128)S(1)}, f32[4,1,384]{2,1,0:T(1,128)S(1)}, u32[]{:S(2)}, u32[]{:S(2)}) collective-permute-start(f32[4,1,384]{2,1,0:T(1,128)S(1)} %slice.273), channel_id=1, source_target_pairs={{0,1},{1,2},{2,3},{3,4},{4,5},{5,6},{6,7},{7,8},{8,9},{9,10},{10,1... | collective-permute-start | bytes 18440 | tf_op jit(solution)/shard_map/ppermute | solution.py:22
  50.5 8.7 %collective-permute-start.5 = (f32[1,6,384]{2,1,0:T(8,128)S(1)}, f32[1,6,384]{2,1,0:T(8,128)S(1)}, u32[]{:S(2)}, u32[]{:S(2)}) collective-permute-start(f32[1,6,384]{2,1,0:T(8,128)S(1)} %pad_maximum_fusion.13), channel_id=1, source_target_pairs={{0,64},{64,128},{128,192},{192,256},{256,320},{320,384},{384,448},... | collective-permute-start | bytes 27656 | tf_op jit(solution)/shard_map/ppermute | solution.py:22
  59.4 9.5 %collective-permute-start.6 = (f32[1,6,384]{2,1,0:T(8,128)S(1)}, f32[1,6,384]{2,1,0:T(8,128)S(1)}, u32[]{:S(2)}, u32[]{:S(2)}) collective-permute-start(f32[1,6,384]{2,1,0:T(8,128)S(1)} %slice.275), channel_id=1, source_target_pairs={{64,0},{128,64},{192,128},{256,192},{320,256},{384,320},{448,384},... | collective-permute-start | bytes 27656 | tf_op jit(solution)/shard_map/ppermute | solution.py:22
  68.9 6.9 %collective-permute-start.7 = (f32[4,1,384]{2,1,0:T(1,128)S(1)}, f32[4,1,384]{2,1,0:T(1,128)S(1)}, u32[]{:S(2)}, u32[]{:S(2)}) collective-permute-start(f32[4,1,384]{2,1,0:T(1,128)S(1)} %pad_maximum_fusion.15), channel_id=1, source_target_pairs={{1,0},{2,1},{3,2},{4,3},{5,4},{6,5},{7,6},{8,7},{9,8},{10,9},{11,1... | collective-permute-start | bytes 18440 | tf_op jit(solution)/shard_map/ppermute | solution.py:22
  128.0 30.0 %collective-permute-start.8 = (f32[1,6,384]{2,1,0:T(8,128)S(1)}, f32[1,6,384]{2,1,0:T(8,128)S(1)}, u32[]{:S(2)}, u32[]{:S(2)}) collective-permute-start(f32[1,6,384]{2,1,0:T(8,128)S(1)} %slice.280), channel_id=1, source_target_pairs={{0,64},{64,128},{128,192},{192,256},{256,320},{320,384},{384,448},... | collective-permute-start | bytes 27656 | tf_op jit(solution)/shard_map/ppermute | solution.py:22
  146.9 11.1 %collective-permute-start.9 = (f32[1,1,384]{2,1,0:T(1,128)S(1)}, f32[1,1,384]{2,1,0:T(1,128)S(1)}, u32[]{:S(2)}, u32[]{:S(2)}) collective-permute-start(f32[1,1,384]{2,1,0:T(1,128)S(1)} %slice.282), channel_id=1, source_target_pairs={{0,65},{1,66},{2,67},{3,68},{4,69},{5,70},{6,71},{7,72},{8,73},{9,... | collective-permute-start | bytes 4616 | tf_op jit(solution)/shard_map/ppermute | solution.py:252
  153.2 4.8 %collective-permute-start.10 = (f32[3,1,384]{2,1,0:T(1,128)S(1)}, f32[3,1,384]{2,1,0:T(1,128)S(1)}, u32[]{:S(2)}, u32[]{:S(2)}) collective-permute-start(f32[3,1,384]{2,1,0:T(1,128)S(1)} %slice.285), channel_id=1, source_target_pairs={{0,1},{1,2},{2,3},{3,4},{4,5},{5,6},{6,7},{7,8},{8,9},{9,10},{10,1... | collective-permute-start | bytes 13832 | tf_op jit(solution)/shard_map/ppermute | solution.py:22

commit v10 on v9

--- a/solution.py
+++ b/solution.py
@@ -240,29 +240,6 @@
     return shifted(plane, BY, 1)
 
 
-def moved(value, steps_x, steps_y):
-    count_x = lax.axis_size(BX)
-    count_y = lax.axis_size(BY)
-    pairs = []
-    for source_x in range(count_x):
-        for source_y in range(count_y):
-            target_x, target_y = source_x + steps_x, source_y + steps_y
-            if 0 <= target_x < count_x and 0 <= target_y < count_y:
-                pairs.append((source_x * count_y + source_y, target_x * count_y + target_y))
-    return lax.ppermute(value, BX_BY, pairs)
-
-
-def gather_contributions(contributions, rows_x, rows_y, rows_z):
-    own = contributions[:rows_x, :rows_y, :rows_z]
-    from_x = lower_x(contributions[rows_x:, :rows_y, :rows_z])
-    from_y = lower_y(contributions[:rows_x, rows_y:, :rows_z])
-    from_corner = moved(contributions[rows_x:, rows_y:, :rows_z], 1, 1)
-    head = own[0:1] + from_x
-    head = jnp.concatenate([head[:, 0:1] + from_corner, head[:, 1:]], 1)
-    own = jnp.concatenate([head, own[1:]], 0)
-    return jnp.concatenate([own[:, 0:1] + from_y, own[:, 1:]], 1)
-
-
 def global_sums(terms):
     return (over_axes(terms[0], BX_BY), over_axes(terms[1], BX_BY))
 
@@ -336,8 +313,16 @@
             jnp.sum(wide_products.reshape(2, -1, wide_products.shape[-1]), axis=(1, 2)),
         ]
     )
-    second = gather_contributions(raw_second, rows_x, rows_y, rows_z) * interior
-    summed = over_axes(terms, BX_BY)
+    arrived = lower_x(raw_second[rows_x:])
+    partial = jnp.concatenate([raw_second[0:1] + arrived, raw_second[1:rows_x]], 0)
+    summed = lax.psum(terms, BX_BY[0])
+    summed, partial = lax.optimization_barrier((summed, partial))
+    arrived = lower_y(partial[:, rows_y:])
+    second = jnp.concatenate([partial[:, 0:1] + arrived, partial[:, 1:rows_y]], 1) * interior
+    summed = lax.psum(summed, BX_BY[1])
+    summed, second = lax.optimization_barrier((summed, second))
+    for axis in BX_BY[2:]:
+        summed = lax.psum(summed, axis)
     rz_now, curvature, cross_r, cross_q, cross_z, curvature_w = [summed[k] for k in range(6)]
     alpha = rz_now / curvature
     fresh = rz_now - alpha * cross_r - alpha * curvature + alpha * alpha * cross_q

time: 160 us -> 153 us (0.956)
  blocking collectives: 56.6 us -> 51.5 us
    ppermute x1 -> x0, starting transfers between devices: 6.27 us -> none  [moved(): return lax.ppermute(value, BX_BY, pairs)]
    ppermute x10, starting transfers between devices: 34.3 us -> 39.4 us  [shifted(): lax.ppermute(value, axis, [(source, source + steps) for source in range(i...]
    psum x5, blocking collectives: 56.6 us -> 51.5 us  [the longest x3 32.7 us: shards(): summed = lax.psum(summed, axis)]
  transfers between devices with their start and end apart: 11 -> 10, of which waited for: 8 -> 8; matrix products, arithmetic and copies ran while one was open for 2% -> 1% of each run, Pallas kernels for 0% -> 0%
where the time goes in v10:
time: 153 us
  blocking collectives  51.5 us (34%)
  starting transfers between devices  39.4 us (26%)
  waiting for transfers between devices  31.5 us (21%)
  matrix products  13.4 us (9%)
  between operations  9.44 us (6%)
  local copies, waits for them, and re-layouts  4.76 us (3%)
  other arithmetic  2.56 us (2%)
    ppermute x10, starting transfers between devices, shifted(): lax.ppermute(value, axis, [(source, source + steps) for source in range(i...  39.4 us
    psum x3, blocking collectives, shards(): summed = lax.psum(summed, axis)  32.7 us
    ppermute x10, waiting for transfers between devices, shifted(): lax.ppermute(value, axis, [(source, source + steps) for source in range(i...  31.5 us
    dot_general x30, matrix products, mat(): return jnp.matmul(left, right, precision=lax.Precision.HIGHEST)  13.4 us
    psum x1, blocking collectives, shards(): summed = lax.psum(summed, BX_BY[1])  11.5 us
    psum x1, blocking collectives, shards(): summed = lax.psum(terms, BX_BY[0])  7.33 us
  transfers between devices with their start and end apart: 10, of which 8 were waited for; matrix products, arithmetic and copies ran while one was open for 1% of the time, Pallas kernels for 0%

profile of v10, /device:TPU:1, one launch (start us, length us, event | category | flops | bytes accessed | tf_op | source)
XLA Modules:
  0.0 152.6 jit_solution(4581091353854409535)
XLA Ops:
  0.8 1.2 slice.186
  2.8 1.0 fusion.174
  4.0 0.2 fusion.126
  4.2 0.2 fusion.135
  4.9 0.2 fusion.123
  5.1 0.2 convolution_add_fusion.5
  6.1 1.1 fusion.14
  7.2 1.1 convolution_add_fusion.6
  8.3 1.1 convolution_add_fusion.4
  9.4 4.6 %collective-permute-start = (f32[4,1,384]{2,1,0:T(1,128)S(1)}, f32[4,1,384]{2,1,0:T(1,128)S(1)}, u32[]{:S(2)}, u32[]{:S(2)}) collective-permute-start(f32[4,1,384]{2,1,0:T(1,128)S(1)} %slice.244), channel_id=1, source_target_pairs={{0,1},{1,2},{2,3},{3,4},{4,5},{5,6},{6,7},{7,8},{8,9},{9,10},{10,1... | collective-permute-start | bytes 18440 | tf_op jit(solution)/shard_map/ppermute | solution.py:22
  14.2 0.2 bitcast_convert_fusion
  15.1 0.5 select_add_fusion.1
  15.6 6.3 %collective-permute-done = f32[4,1,384]{2,1,0:T(1,128)S(1)} collective-permute-done((f32[4,1,384]{2,1,0:T(1,128)S(1)}, f32[4,1,384]{2,1,0:T(1,128)S(1)}, u32[]{:S(2)}, u32[]{:S(2)}) %collective-permute-start) | collective-permute-done | bytes 6176 | tf_op jit(solution)/shard_map/ppermute | solution.py:22
  21.9 4.4 %collective-permute-start.1 = (f32[1,6,384]{2,1,0:T(8,128)S(1)}, f32[1,6,384]{2,1,0:T(8,128)S(1)}, u32[]{:S(2)}, u32[]{:S(2)}) collective-permute-start(f32[1,6,384]{2,1,0:T(8,128)S(1)} %pad_maximum_fusion.14), channel_id=1, source_target_pairs={{0,64},{64,128},{128,192},{192,256},{256,320},{320,384},{384,448},... | collective-permute-start | bytes 27656 | tf_op jit(solution)/shard_map/ppermute | solution.py:22
  26.3 0.8 collective-permute-done.1
  27.2 1.3 collective-permute-start.2
  29.1 7.5 %collective-permute-done.2 = f32[1,6,384]{2,1,0:T(8,128)S(1)} collective-permute-done((f32[1,6,384]{2,1,0:T(8,128)S(1)}, f32[1,6,384]{2,1,0:T(8,128)S(1)}, u32[]{:S(2)}, u32[]{:S(2)}) %collective-permute-start.2) | collective-permute-done | bytes 9248 | tf_op jit(solution)/shard_map/ppermute | solution.py:22
  36.6 2.3 %collective-permute-start.3 = (f32[4,1,384]{2,1,0:T(1,128)S(1)}, f32[4,1,384]{2,1,0:T(1,128)S(1)}, u32[]{:S(2)}, u32[]{:S(2)}) collective-permute-start(f32[4,1,384]{2,1,0:T(1,128)S(1)} %pad_maximum_fusion.16), channel_id=1, source_target_pairs={{1,0},{2,1},{3,2},{4,3},{5,4},{6,5},{7,6},{8,7},{9,8},{10,9},{11,1... | collective-permute-start | bytes 18440 | tf_op jit(solution)/shard_map/ppermute | solution.py:22
  38.9 4.0 %collective-permute-done.3 = f32[4,1,384]{2,1,0:T(1,128)S(1)} collective-permute-done((f32[4,1,384]{2,1,0:T(1,128)S(1)}, f32[4,1,384]{2,1,0:T(1,128)S(1)}, u32[]{:S(2)}, u32[]{:S(2)}) %collective-permute-start.3) | collective-permute-done | bytes 6176 | tf_op jit(solution)/shard_map/ppermute | solution.py:22
  43.0 1.0 fusion.29
  44.8 0.3 fusion.176
  45.1 0.3 fusion.64
  45.4 0.3 convolution_add_fusion.3
  45.6 0.3 convolution_add_fusion.2
  45.9 1.5 fusion.28
  47.4 1.9 %collective-permute-start.4 = (f32[4,1,384]{2,1,0:T(1,128)S(1)}, f32[4,1,384]{2,1,0:T(1,128)S(1)}, u32[]{:S(2)}, u32[]{:S(2)}) collective-permute-start(f32[4,1,384]{2,1,0:T(1,128)S(1)} %slice.257), channel_id=1, source_target_pairs={{0,1},{1,2},{2,3},{3,4},{4,5},{5,6},{6,7},{7,8},{8,9},{9,10},{10,1... | collective-permute-start | bytes 18440 | tf_op jit(solution)/shard_map/ppermute | solution.py:22
  49.4 1.1 collective-permute-done.4
  50.5 7.9 %collective-permute-start.5 = (f32[1,6,384]{2,1,0:T(8,128)S(1)}, f32[1,6,384]{2,1,0:T(8,128)S(1)}, u32[]{:S(2)}, u32[]{:S(2)}) collective-permute-start(f32[1,6,384]{2,1,0:T(8,128)S(1)} %pad_maximum_fusion.13), channel_id=1, source_target_pairs={{0,64},{64,128},{128,192},{192,256},{256,320},{320,384},{384,448},... | collective-permute-start | bytes 27656 | tf_op jit(solution)/shard_map/ppermute | solution.py:22
  58.4 0.8 collective-permute-done.5
  59.4 1.3 collective-permute-start.6
  60.8 8.1 %collective-permute-done.6 = f32[1,6,384]{2,1,0:T(8,128)S(1)} collective-permute-done((f32[1,6,384]{2,1,0:T(8,128)S(1)}, f32[1,6,384]{2,1,0:T(8,128)S(1)}, u32[]{:S(2)}, u32[]{:S(2)}) %collective-permute-start.6) | collective-permute-done | bytes 9248 | tf_op jit(solution)/shard_map/ppermute | solution.py:22
  68.9 3.8 %collective-permute-start.7 = (f32[4,1,384]{2,1,0:T(1,128)S(1)}, f32[4,1,384]{2,1,0:T(1,128)S(1)}, u32[]{:S(2)}, u32[]{:S(2)}) collective-permute-start(f32[4,1,384]{2,1,0:T(1,128)S(1)} %pad_maximum_fusion.15), channel_id=1, source_target_pairs={{1,0},{2,1},{3,2},{4,3},{5,4},{6,5},{7,6},{8,7},{9,8},{10,9},{11,1... | collective-permute-start | bytes 18440 | tf_op jit(solution)/shard_map/ppermute | solution.py:22
  72.8 2.9 %collective-permute-done.7 = f32[4,1,384]{2,1,0:T(1,128)S(1)} collective-permute-done((f32[4,1,384]{2,1,0:T(1,128)S(1)}, f32[4,1,384]{2,1,0:T(1,128)S(1)}, u32[]{:S(2)}, u32[]{:S(2)}) %collective-permute-start.7) | collective-permute-done | bytes 6176 | tf_op jit(solution)/shard_map/ppermute | solution.py:22
  75.8 1.0 fusion.27
  77.6 0.3 fusion.177
  77.9 0.3 fusion.67
  78.2 0.3 convolution_add_fusion.1
  78.4 0.3 convolution_add_fusion
  78.7 1.5 fusion.26
  80.3 7.9 %collective-permute-start.8 = (f32[1,7,384]{2,1,0:T(8,128)S(1)}, f32[1,7,384]{2,1,0:T(8,128)S(1)}, u32[]{:S(2)}, u32[]{:S(2)}) collective-permute-start(f32[1,7,384]{2,1,0:T(8,128)S(1)} %slice.264), channel_id=1, source_target_pairs={{0,64},{64,128},{128,192},{192,256},{256,320},{320,384},{384,448},... | collective-permute-start | bytes 32264 | tf_op jit(solution)/shard_map/ppermute | solution.py:22
  88.4 7.3 %psum.35 = f32[6]{0:T(128)S(1)} all-reduce(f32[6]{0:T(128)S(1)} %pad_maximum_fusion.17), channel_id=1, replica_groups=mesh['bx_0'=4,'bx_1'=3,'by_0'=4,'by_1'=8,'by_2'=2] {'bx_0'}, use_global_device_ids=true, to_apply=%region_2.3 | all-reduce | flops 6 | bytes 48 | tf_op jit(solution)/shard_map/psum | solution.py:318
  95.8 4.1 %collective-permute-start.9 = (f32[3,1,384]{2,1,0:T(1,128)S(1)}, f32[3,1,384]{2,1,0:T(1,128)S(1)}, u32[]{:S(2)}, u32[]{:S(2)}) collective-permute-start(f32[3,1,384]{2,1,0:T(1,128)S(1)} %slice.222), channel_id=1, source_target_pairs={{0,1},{1,2},{2,3},{3,4},{4,5},{5,6},{6,7},{7,8},{8,9},{9,10},{10,1... | collective-permute-start | bytes 13832 | tf_op jit(solution)/shard_map/ppermute | solution.py:22
  99.9 11.5 %psum.36 = f32[6]{0:T(128)S(1)} all-reduce(f32[6]{0:T(128)S(1)} %psum.35), channel_id=1, replica_groups=mesh['bx_0'=4,'bx_1'=3,'by_0'=4,'by_1'=8,'by_2'=2] {'bx_1'}, use_global_device_ids=true, to_apply=%region_3.4 | all-reduce | flops 6 | bytes 48 | tf_op jit(solution)/shard_map/psum | solution.py:322
  111.5 10.3 %psum.37 = f32[6]{0:T(128)S(1)} all-reduce(f32[6]{0:T(128)S(1)} %psum.36), channel_id=1, replica_groups=mesh['bx_0'=4,'bx_1'=3,'by_0'=4,'by_1'=8,'by_2'=2] {'by_0'}, use_global_device_ids=true, to_apply=%region_4.5 | all-reduce | flops 6 | bytes 48 | tf_op jit(solution)/shard_map/psum | solution.py:325
  121.8 15.6 %psum.38 = f32[6]{0:T(128)S(1)} all-reduce(f32[6]{0:T(128)S(1)} %psum.37), channel_id=1, replica_groups=mesh['bx_0'=4,'bx_1'=3,'by_0'=4,'by_1'=8,'by_2'=2] {'by_1'}, use_global_device_ids=true, to_apply=%region_5.6 | all-reduce | flops 6 | bytes 48 | tf_op jit(solution)/shard_map/psum | solution.py:325
  137.4 6.8 %psum.39 = f32[6]{0:T(128)S(1)} all-reduce(f32[6]{0:T(128)S(1)} %psum.38), channel_id=1, replica_groups=mesh['bx_0'=4,'bx_1'=3,'by_0'=4,'by_1'=8,'by_2'=2] {'by_2'}, use_global_device_ids=true, to_apply=%region_6.7 | all-reduce | flops 6 | bytes 48 | tf_op jit(solution)/shard_map/psum | solution.py:325
  144.2 0.6 fusion.175
  151.9 0.7 multiply_subtract_fusion
  (164 shorter events, 5.1 us)
Async XLA Ops:
  0.6 3.3 %copy-start.5 = (f32[32,28]{1,0:T(8,128)S(1)}, f32[32,28]{1,0:T(8,128)}, u32[]{:S(2)}) copy-start(f32[32,28]{1,0:T(8,128)} %constant.111.clone) | copy-start | bytes 10756
  0.6 3.8 %copy-start.29 = (f32[4]{0:T(128)S(1)}, f32[4]{0:T(128)}, u32[]{:S(2)}) copy-start(f32[4]{0:T(128)} %constant.116.clone) | copy-start | bytes 52
  0.7 3.8 %copy-start.30 = (f32[4]{0:T(128)S(1)}, f32[4]{0:T(128)}, u32[]{:S(2)}) copy-start(f32[4]{0:T(128)} %constant.115.clone) | copy-start | bytes 52
  0.7 3.8 %copy-start.27 = (f32[4]{0:T(128)S(1)}, f32[4]{0:T(128)}, u32[]{:S(2)}) copy-start(f32[4]{0:T(128)} %constant.118.clone) | copy-start | bytes 52
  0.7 3.8 %copy-start.28 = (f32[4]{0:T(128)S(1)}, f32[4]{0:T(128)}, u32[]{:S(2)}) copy-start(f32[4]{0:T(128)} %constant.117.clone) | copy-start | bytes 52
  0.7 3.9 %copy-start.25 = (f32[4]{0:T(128)S(1)}, f32[4]{0:T(128)}, u32[]{:S(2)}) copy-start(f32[4]{0:T(128)} %constant.120.clone) | copy-start | bytes 52
  0.7 3.9 %copy-start.26 = (f32[4]{0:T(128)S(1)}, f32[4]{0:T(128)}, u32[]{:S(2)}) copy-start(f32[4]{0:T(128)} %constant.119.clone) | copy-start | bytes 52
  0.7 3.9 %copy-start.23 = (f32[4]{0:T(128)S(1)}, f32[4]{0:T(128)}, u32[]{:S(2)}) copy-start(f32[4]{0:T(128)} %constant.122.clone) | copy-start | bytes 52
  0.7 3.9 %copy-start.24 = (f32[4]{0:T(128)S(1)}, f32[4]{0:T(128)}, u32[]{:S(2)}) copy-start(f32[4]{0:T(128)} %constant.121.clone) | copy-start | bytes 52
  0.7 4.0 %copy-start.21 = (f32[4]{0:T(128)S(1)}, f32[4]{0:T(128)}, u32[]{:S(2)}) copy-start(f32[4]{0:T(128)} %constant.126.clone) | copy-start | bytes 52
  0.8 4.0 %copy-start.22 = (f32[4]{0:T(128)S(1)}, f32[4]{0:T(128)}, u32[]{:S(2)}) copy-start(f32[4]{0:T(128)} %constant.125.clone) | copy-start | bytes 52
  0.8 4.0 %copy-start.19 = (f32[4]{0:T(128)S(1)}, f32[4]{0:T(128)}, u32[]{:S(2)}) copy-start(f32[4]{0:T(128)} %constant.128.clone) | copy-start | bytes 52
  0.8 4.0 %copy-start.20 = (f32[4]{0:T(128)S(1)}, f32[4]{0:T(128)}, u32[]{:S(2)}) copy-start(f32[4]{0:T(128)} %constant.127.clone) | copy-start | bytes 52
  0.8 4.1 %copy-start.6 = (f32[32,28]{1,0:T(8,128)S(1)}, f32[32,28]{1,0:T(8,128)}, u32[]{:S(2)}) copy-start(f32[32,28]{1,0:T(8,128)} %constant.147) | copy-start | bytes 10756
  0.8 4.3 %copy-start.10 = (f32[32,28]{1,0:T(8,128)S(1)}, f32[32,28]{1,0:T(8,128)}, u32[]{:S(2)}) copy-start(f32[32,28]{1,0:T(8,128)} %constant.148) | copy-start | bytes 10756
  0.8 4.5 %copy-start.9 = (f32[32,28]{1,0:T(8,128)S(1)}, f32[32,28]{1,0:T(8,128)}, u32[]{:S(2)}) copy-start(f32[32,28]{1,0:T(8,128)} %constant.112.clone) | copy-start | bytes 10756
  2.7 2.8 %copy-start.8 = (f32[32,28]{1,0:T(8,128)S(1)}, f32[32,28]{1,0:T(8,128)}, u32[]{:S(2)}) copy-start(f32[32,28]{1,0:T(8,128)} %constant.113.clone) | copy-start | bytes 10756
  3.8 2.0 %copy-start.7 = (f32[32,28]{1,0:T(8,128)S(1)}, f32[32,28]{1,0:T(8,128)}, u32[]{:S(2)}) copy-start(f32[32,28]{1,0:T(8,128)} %constant.146) | copy-start | bytes 10756
  8.3 5.8 %copy-start.1 = (bf16[7,4,4,4,1,2,128]{6,5,4,3,2,1,0:T(2,128)(2,1)S(1)}, bf16[7,4,4,4,1,2,128]{6,5,4,3,2,1,0:T(2,128)(2,1)}, u32[]{:S(2)}) copy-start(bf16[7,4,4,4,1,2,128]{6,5,4,3,2,1,0:T(2,128)(2,1)} %param.44) | copy-start | bytes 688132
  9.4 12.5 %collective-permute-start = (f32[4,1,384]{2,1,0:T(1,128)S(1)}, f32[4,1,384]{2,1,0:T(1,128)S(1)}, u32[]{:S(2)}, u32[]{:S(2)}) collective-permute-start(f32[4,1,384]{2,1,0:T(1,128)S(1)} %slice.244), channel_id=1, source_target_pairs={{0,1},{1,2},{2,3},{3,4},{4,5},{5,6},{6,7},{7,8},{8,9},{9,10},{10,1... | collective-permute-start | bytes 18440 | tf_op jit(solution)/shard_map/ppermute | solution.py:22
  14.1 0.7 copy-start.17
  14.1 0.7 copy-start.18
  14.1 0.7 copy-start.15
  14.1 0.7 copy-start.16
  14.1 0.8 copy-start.13
  14.1 0.8 copy-start.14
  14.2 0.8 copy-start.11
  14.2 0.8 copy-start.12
  15.1 12.1 %copy-start.2 = (f32[3,6,384]{2,1,0:T(8,128)S(1)}, f32[3,6,384]{2,1,0:T(8,128)}, u32[]{:S(2)}) copy-start(f32[3,6,384]{2,1,0:T(8,128)} %param.43) | copy-start | bytes 82948
  21.9 5.2 %collective-permute-start.1 = (f32[1,6,384]{2,1,0:T(8,128)S(1)}, f32[1,6,384]{2,1,0:T(8,128)S(1)}, u32[]{:S(2)}, u32[]{:S(2)}) collective-permute-start(f32[1,6,384]{2,1,0:T(8,128)S(1)} %pad_maximum_fusion.14), channel_id=1, source_target_pairs={{0,64},{64,128},{128,192},{192,256},{256,320},{320,384},{384,448},... | collective-permute-start | bytes 27656 | tf_op jit(solution)/shard_map/ppermute | solution.py:22
  27.2 9.3 %collective-permute-start.2 = (f32[1,6,384]{2,1,0:T(8,128)S(1)}, f32[1,6,384]{2,1,0:T(8,128)S(1)}, u32[]{:S(2)}, u32[]{:S(2)}) collective-permute-start(f32[1,6,384]{2,1,0:T(8,128)S(1)} %slice.247), channel_id=1, source_target_pairs={{64,0},{128,64},{192,128},{256,192},{320,256},{384,320},{448,384},... | collective-permute-start | bytes 27656 | tf_op jit(solution)/shard_map/ppermute | solution.py:22
  36.6 6.4 %collective-permute-start.3 = (f32[4,1,384]{2,1,0:T(1,128)S(1)}, f32[4,1,384]{2,1,0:T(1,128)S(1)}, u32[]{:S(2)}, u32[]{:S(2)}) collective-permute-start(f32[4,1,384]{2,1,0:T(1,128)S(1)} %pad_maximum_fusion.16), channel_id=1, source_target_pairs={{1,0},{2,1},{3,2},{4,3},{5,4},{6,5},{7,6},{8,7},{9,8},{10,9},{11,1... | collective-permute-start | bytes 18440 | tf_op jit(solution)/shard_map/ppermute | solution.py:22
  43.0 1.1 copy-start.4
  43.0 1.3 copy-start.3
  43.0 1.5 copy-start
  47.4 3.1 %collective-permute-start.4 = (f32[4,1,384]{2,1,0:T(1,128)S(1)}, f32[4,1,384]{2,1,0:T(1,128)S(1)}, u32[]{:S(2)}, u32[]{:S(2)}) collective-permute-start(f32[4,1,384]{2,1,0:T(1,128)S(1)} %slice.257), channel_id=1, source_target_pairs={{0,1},{1,2},{2,3},{3,4},{4,5},{5,6},{6,7},{7,8},{8,9},{9,10},{10,1... | collective-permute-start | bytes 18440 | tf_op jit(solution)/shard_map/ppermute | solution.py:22
  50.5 8.7 %collective-permute-start.5 = (f32[1,6,384]{2,1,0:T(8,128)S(1)}, f32[1,6,384]{2,1,0:T(8,128)S(1)}, u32[]{:S(2)}, u32[]{:S(2)}) collective-permute-start(f32[1,6,384]{2,1,0:T(8,128)S(1)} %pad_maximum_fusion.13), channel_id=1, source_target_pairs={{0,64},{64,128},{128,192},{192,256},{256,320},{320,384},{384,448},... | collective-permute-start | bytes 27656 | tf_op jit(solution)/shard_map/ppermute | solution.py:22
  59.4 9.5 %collective-permute-start.6 = (f32[1,6,384]{2,1,0:T(8,128)S(1)}, f32[1,6,384]{2,1,0:T(8,128)S(1)}, u32[]{:S(2)}, u32[]{:S(2)}) collective-permute-start(f32[1,6,384]{2,1,0:T(8,128)S(1)} %slice.259), channel_id=1, source_target_pairs={{64,0},{128,64},{192,128},{256,192},{320,256},{384,320},{448,384},... | collective-permute-start | bytes 27656 | tf_op jit(solution)/shard_map/ppermute | solution.py:22
  68.9 6.9 %collective-permute-start.7 = (f32[4,1,384]{2,1,0:T(1,128)S(1)}, f32[4,1,384]{2,1,0:T(1,128)S(1)}, u32[]{:S(2)}, u32[]{:S(2)}) collective-permute-start(f32[4,1,384]{2,1,0:T(1,128)S(1)} %pad_maximum_fusion.15), channel_id=1, source_target_pairs={{1,0},{2,1},{3,2},{4,3},{5,4},{6,5},{7,6},{8,7},{9,8},{10,9},{11,1... | collective-permute-start | bytes 18440 | tf_op jit(solution)/shard_map/ppermute | solution.py:22
  80.3 15.4 %collective-permute-start.8 = (f32[1,7,384]{2,1,0:T(8,128)S(1)}, f32[1,7,384]{2,1,0:T(8,128)S(1)}, u32[]{:S(2)}, u32[]{:S(2)}) collective-permute-start(f32[1,7,384]{2,1,0:T(8,128)S(1)} %slice.264), channel_id=1, source_target_pairs={{0,64},{64,128},{128,192},{192,256},{256,320},{320,384},{384,448},... | collective-permute-start | bytes 32264 | tf_op jit(solution)/shard_map/ppermute | solution.py:22
  95.8 15.7 %collective-permute-start.9 = (f32[3,1,384]{2,1,0:T(1,128)S(1)}, f32[3,1,384]{2,1,0:T(1,128)S(1)}, u32[]{:S(2)}, u32[]{:S(2)}) collective-permute-start(f32[3,1,384]{2,1,0:T(1,128)S(1)} %slice.222), channel_id=1, source_target_pairs={{0,1},{1,2},{2,3},{3,4},{4,5},{5,6},{6,7},{7,8},{8,9},{9,10},{10,1... | collective-permute-start | bytes 13832 | tf_op jit(solution)/shard_map/ppermute | solution.py:22

commit v11 on v10

--- a/solution.py
+++ b/solution.py
@@ -323,7 +323,8 @@
     summed, second = lax.optimization_barrier((summed, second))
     for axis in BX_BY[2:]:
         summed = lax.psum(summed, axis)
-    rz_now, curvature, cross_r, cross_q, cross_z, curvature_w = [summed[k] for k in range(6)]
+    parts = lax.optimization_barrier(jnp.broadcast_to(summed[:, None, None, None], (6, 1, 1, rows_z)))
+    rz_now, curvature, cross_r, cross_q, cross_z, curvature_w = [parts[k] for k in range(6)]
     alpha = rz_now / curvature
     fresh = rz_now - alpha * cross_r - alpha * curvature + alpha * alpha * cross_q
     ratio = fresh / rz_now

time: 153 us -> 146 us (0.954)
  between operations: 9.44 us -> 2.44 us
where the time goes in v11:
time: 146 us; the launch traced here: 145 us
  blocking collectives  51.5 us (35%)
  starting transfers between devices  39.4 us (27%)
  waiting for transfers between devices  31.5 us (22%)
  matrix products  13.4 us (9%)
  local copies, waits for them, and re-layouts  4.24 us (3%)
  other arithmetic  2.59 us (2%)
  between operations  2.44 us (2%)
    ppermute x10, starting transfers between devices, shifted(): lax.ppermute(value, axis, [(source, source + steps) for source in range(i...  39.4 us
    psum x3, blocking collectives, shards(): summed = lax.psum(summed, axis)  32.7 us
    ppermute x10, waiting for transfers between devices, shifted(): lax.ppermute(value, axis, [(source, source + steps) for source in range(i...  31.5 us
    dot_general x30, matrix products, mat(): return jnp.matmul(left, right, precision=lax.Precision.HIGHEST)  13.4 us
    psum x1, blocking collectives, shards(): summed = lax.psum(summed, BX_BY[1])  11.5 us
    psum x1, blocking collectives, shards(): summed = lax.psum(terms, BX_BY[0])  7.33 us
  transfers between devices with their start and end apart: 10, of which 8 were waited for; matrix products, arithmetic and copies ran while one was open for 1% of the time, Pallas kernels for 0%

profile of v11, /device:TPU:1, one launch (start us, length us, event | category | flops | bytes accessed | tf_op | source)
XLA Modules:
  0.0 145.1 jit_solution(12100820217633054078)
XLA Ops:
  0.8 1.2 slice.186
  2.8 1.0 fusion.175
  4.0 0.2 fusion.126
  4.2 0.2 fusion.135
  4.9 0.2 fusion.123
  5.1 0.2 convolution_add_fusion.5
  5.4 0.2 convolution_add_fusion.9
  6.1 1.1 fusion.14
  7.2 1.1 convolution_add_fusion.6
  8.3 1.1 convolution_add_fusion.4
  9.4 4.6 %collective-permute-start = (f32[4,1,384]{2,1,0:T(1,128)S(1)}, f32[4,1,384]{2,1,0:T(1,128)S(1)}, u32[]{:S(2)}, u32[]{:S(2)}) collective-permute-start(f32[4,1,384]{2,1,0:T(1,128)S(1)} %slice.244), channel_id=1, source_target_pairs={{0,1},{1,2},{2,3},{3,4},{4,5},{5,6},{6,7},{7,8},{8,9},{9,10},{10,1... | collective-permute-start | bytes 18440 | tf_op jit(solution)/shard_map/ppermute | solution.py:22
  14.2 0.2 bitcast_convert_fusion
  15.1 0.5 select_add_fusion.1
  15.6 6.3 %collective-permute-done = f32[4,1,384]{2,1,0:T(1,128)S(1)} collective-permute-done((f32[4,1,384]{2,1,0:T(1,128)S(1)}, f32[4,1,384]{2,1,0:T(1,128)S(1)}, u32[]{:S(2)}, u32[]{:S(2)}) %collective-permute-start) | collective-permute-done | bytes 6176 | tf_op jit(solution)/shard_map/ppermute | solution.py:22
  21.9 4.4 %collective-permute-start.1 = (f32[1,6,384]{2,1,0:T(8,128)S(1)}, f32[1,6,384]{2,1,0:T(8,128)S(1)}, u32[]{:S(2)}, u32[]{:S(2)}) collective-permute-start(f32[1,6,384]{2,1,0:T(8,128)S(1)} %pad_maximum_fusion.14), channel_id=1, source_target_pairs={{0,64},{64,128},{128,192},{192,256},{256,320},{320,384},{384,448},... | collective-permute-start | bytes 27656 | tf_op jit(solution)/shard_map/ppermute | solution.py:22
  26.3 0.8 collective-permute-done.1
  27.2 1.3 collective-permute-start.2
  29.1 7.5 %collective-permute-done.2 = f32[1,6,384]{2,1,0:T(8,128)S(1)} collective-permute-done((f32[1,6,384]{2,1,0:T(8,128)S(1)}, f32[1,6,384]{2,1,0:T(8,128)S(1)}, u32[]{:S(2)}, u32[]{:S(2)}) %collective-permute-start.2) | collective-permute-done | bytes 9248 | tf_op jit(solution)/shard_map/ppermute | solution.py:22
  36.6 2.3 %collective-permute-start.3 = (f32[4,1,384]{2,1,0:T(1,128)S(1)}, f32[4,1,384]{2,1,0:T(1,128)S(1)}, u32[]{:S(2)}, u32[]{:S(2)}) collective-permute-start(f32[4,1,384]{2,1,0:T(1,128)S(1)} %pad_maximum_fusion.16), channel_id=1, source_target_pairs={{1,0},{2,1},{3,2},{4,3},{5,4},{6,5},{7,6},{8,7},{9,8},{10,9},{11,1... | collective-permute-start | bytes 18440 | tf_op jit(solution)/shard_map/ppermute | solution.py:22
  38.9 4.0 %collective-permute-done.3 = f32[4,1,384]{2,1,0:T(1,128)S(1)} collective-permute-done((f32[4,1,384]{2,1,0:T(1,128)S(1)}, f32[4,1,384]{2,1,0:T(1,128)S(1)}, u32[]{:S(2)}, u32[]{:S(2)}) %collective-permute-start.3) | collective-permute-done | bytes 6176 | tf_op jit(solution)/shard_map/ppermute | solution.py:22
  43.0 1.0 fusion.29
  44.8 0.3 fusion.176
  45.1 0.3 fusion.64
  45.4 0.3 convolution_add_fusion.3
  45.6 0.3 convolution_add_fusion.2
  45.9 1.5 %fusion.28 = f32[28,385]{1,0:T(8,128)S(1)} fusion(f32[385,512]{1,0:T(8,128)S(1)} %get-tuple-element.41, f32[385,512]{1,0:T(8,128)S(1)} %get-tuple-element.40, f32[28,512]{1,0:T(8,128)S(1)} %fusion.64, f32[28,512]{1,0:T(8,128)S(1)} %convolution_add_fusion.2), kind=kOutput, calls=%fused_computation.44 | convolution fusion | flops 132887552 | bytes 1734768 | tf_op jit(solution)/shard_map/dot_general | solution.py:171
  47.4 1.9 %collective-permute-start.4 = (f32[4,1,384]{2,1,0:T(1,128)S(1)}, f32[4,1,384]{2,1,0:T(1,128)S(1)}, u32[]{:S(2)}, u32[]{:S(2)}) collective-permute-start(f32[4,1,384]{2,1,0:T(1,128)S(1)} %slice.257), channel_id=1, source_target_pairs={{0,1},{1,2},{2,3},{3,4},{4,5},{5,6},{6,7},{7,8},{8,9},{9,10},{10,1... | collective-permute-start | bytes 18440 | tf_op jit(solution)/shard_map/ppermute | solution.py:22
  49.4 1.1 collective-permute-done.4
  50.5 7.9 %collective-permute-start.5 = (f32[1,6,384]{2,1,0:T(8,128)S(1)}, f32[1,6,384]{2,1,0:T(8,128)S(1)}, u32[]{:S(2)}, u32[]{:S(2)}) collective-permute-start(f32[1,6,384]{2,1,0:T(8,128)S(1)} %pad_maximum_fusion.13), channel_id=1, source_target_pairs={{0,64},{64,128},{128,192},{192,256},{256,320},{320,384},{384,448},... | collective-permute-start | bytes 27656 | tf_op jit(solution)/shard_map/ppermute | solution.py:22
  58.4 0.8 collective-permute-done.5
  59.4 1.3 collective-permute-start.6
  60.8 8.1 %collective-permute-done.6 = f32[1,6,384]{2,1,0:T(8,128)S(1)} collective-permute-done((f32[1,6,384]{2,1,0:T(8,128)S(1)}, f32[1,6,384]{2,1,0:T(8,128)S(1)}, u32[]{:S(2)}, u32[]{:S(2)}) %collective-permute-start.6) | collective-permute-done | bytes 9248 | tf_op jit(solution)/shard_map/ppermute | solution.py:22
  68.9 3.8 %collective-permute-start.7 = (f32[4,1,384]{2,1,0:T(1,128)S(1)}, f32[4,1,384]{2,1,0:T(1,128)S(1)}, u32[]{:S(2)}, u32[]{:S(2)}) collective-permute-start(f32[4,1,384]{2,1,0:T(1,128)S(1)} %pad_maximum_fusion.15), channel_id=1, source_target_pairs={{1,0},{2,1},{3,2},{4,3},{5,4},{6,5},{7,6},{8,7},{9,8},{10,9},{11,1... | collective-permute-start | bytes 18440 | tf_op jit(solution)/shard_map/ppermute | solution.py:22
  72.8 2.9 %collective-permute-done.7 = f32[4,1,384]{2,1,0:T(1,128)S(1)} collective-permute-done((f32[4,1,384]{2,1,0:T(1,128)S(1)}, f32[4,1,384]{2,1,0:T(1,128)S(1)}, u32[]{:S(2)}, u32[]{:S(2)}) %collective-permute-start.7) | collective-permute-done | bytes 6176 | tf_op jit(solution)/shard_map/ppermute | solution.py:22
  75.8 1.0 fusion.27
  77.6 0.3 fusion.177
  77.9 0.3 fusion.67
  78.2 0.3 convolution_add_fusion.1
  78.4 0.3 convolution_add_fusion
  78.7 1.5 %fusion.26 = f32[28,385]{1,0:T(8,128)S(1)} fusion(f32[385,512]{1,0:T(8,128)S(1)} %get-tuple-element.41, f32[385,512]{1,0:T(8,128)S(1)} %get-tuple-element.40, f32[28,512]{1,0:T(8,128)S(1)} %fusion.67, f32[28,512]{1,0:T(8,128)S(1)} %convolution_add_fusion), kind=kOutput, calls=%fused_computation.42 | convolution fusion | flops 132887552 | bytes 1734768 | tf_op jit(solution)/shard_map/dot_general | solution.py:171
  80.3 7.9 %collective-permute-start.8 = (f32[1,7,384]{2,1,0:T(8,128)S(1)}, f32[1,7,384]{2,1,0:T(8,128)S(1)}, u32[]{:S(2)}, u32[]{:S(2)}) collective-permute-start(f32[1,7,384]{2,1,0:T(8,128)S(1)} %slice.264), channel_id=1, source_target_pairs={{0,64},{64,128},{128,192},{192,256},{256,320},{320,384},{384,448},... | collective-permute-start | bytes 32264 | tf_op jit(solution)/shard_map/ppermute | solution.py:22
  88.4 7.3 %psum.35 = f32[6]{0:T(128)S(1)} all-reduce(f32[6]{0:T(128)S(1)} %pad_maximum_fusion.17), channel_id=1, replica_groups=mesh['bx_0'=4,'bx_1'=3,'by_0'=4,'by_1'=8,'by_2'=2] {'bx_0'}, use_global_device_ids=true, to_apply=%region_2.3 | all-reduce | flops 6 | bytes 48 | tf_op jit(solution)/shard_map/psum | solution.py:318
  95.8 4.1 %collective-permute-start.9 = (f32[3,1,384]{2,1,0:T(1,128)S(1)}, f32[3,1,384]{2,1,0:T(1,128)S(1)}, u32[]{:S(2)}, u32[]{:S(2)}) collective-permute-start(f32[3,1,384]{2,1,0:T(1,128)S(1)} %slice.222), channel_id=1, source_target_pairs={{0,1},{1,2},{2,3},{3,4},{4,5},{5,6},{6,7},{7,8},{8,9},{9,10},{10,1... | collective-permute-start | bytes 13832 | tf_op jit(solution)/shard_map/ppermute | solution.py:22
  99.9 11.5 %psum.36 = f32[6]{0:T(128)S(1)} all-reduce(f32[6]{0:T(128)S(1)} %psum.35), channel_id=1, replica_groups=mesh['bx_0'=4,'bx_1'=3,'by_0'=4,'by_1'=8,'by_2'=2] {'bx_1'}, use_global_device_ids=true, to_apply=%region_3.4 | all-reduce | flops 6 | bytes 48 | tf_op jit(solution)/shard_map/psum | solution.py:322
  111.5 10.3 %psum.37 = f32[6]{0:T(128)S(1)} all-reduce(f32[6]{0:T(128)S(1)} %psum.36), channel_id=1, replica_groups=mesh['bx_0'=4,'bx_1'=3,'by_0'=4,'by_1'=8,'by_2'=2] {'by_0'}, use_global_device_ids=true, to_apply=%region_4.5 | all-reduce | flops 6 | bytes 48 | tf_op jit(solution)/shard_map/psum | solution.py:325
  121.8 15.6 %psum.38 = f32[6]{0:T(128)S(1)} all-reduce(f32[6]{0:T(128)S(1)} %psum.37), channel_id=1, replica_groups=mesh['bx_0'=4,'bx_1'=3,'by_0'=4,'by_1'=8,'by_2'=2] {'by_1'}, use_global_device_ids=true, to_apply=%region_5.6 | all-reduce | flops 6 | bytes 48 | tf_op jit(solution)/shard_map/psum | solution.py:325
  137.4 6.8 %psum.39 = f32[6]{0:T(128)S(1)} all-reduce(f32[6]{0:T(128)S(1)} %psum.38), channel_id=1, replica_groups=mesh['bx_0'=4,'bx_1'=3,'by_0'=4,'by_1'=8,'by_2'=2] {'by_2'}, use_global_device_ids=true, to_apply=%region_6.7 | all-reduce | flops 6 | bytes 48 | tf_op jit(solution)/shard_map/psum | solution.py:325
  144.4 0.7 multiply_subtract_fusion
  (167 shorter events, 5.1 us)
Async XLA Ops:
  0.6 3.3 %copy-start.5 = (f32[32,28]{1,0:T(8,128)S(1)}, f32[32,28]{1,0:T(8,128)}, u32[]{:S(2)}) copy-start(f32[32,28]{1,0:T(8,128)} %constant.112.clone) | copy-start | bytes 10756
  0.6 3.8 %copy-start.29 = (f32[4]{0:T(128)S(1)}, f32[4]{0:T(128)}, u32[]{:S(2)}) copy-start(f32[4]{0:T(128)} %constant.117.clone) | copy-start | bytes 52
  0.7 3.8 %copy-start.30 = (f32[4]{0:T(128)S(1)}, f32[4]{0:T(128)}, u32[]{:S(2)}) copy-start(f32[4]{0:T(128)} %constant.116.clone) | copy-start | bytes 52
  0.7 3.8 %copy-start.27 = (f32[4]{0:T(128)S(1)}, f32[4]{0:T(128)}, u32[]{:S(2)}) copy-start(f32[4]{0:T(128)} %constant.119.clone) | copy-start | bytes 52
  0.7 3.8 %copy-start.28 = (f32[4]{0:T(128)S(1)}, f32[4]{0:T(128)}, u32[]{:S(2)}) copy-start(f32[4]{0:T(128)} %constant.118.clone) | copy-start | bytes 52
  0.7 3.9 %copy-start.25 = (f32[4]{0:T(128)S(1)}, f32[4]{0:T(128)}, u32[]{:S(2)}) copy-start(f32[4]{0:T(128)} %constant.121.clone) | copy-start | bytes 52
  0.7 3.9 %copy-start.26 = (f32[4]{0:T(128)S(1)}, f32[4]{0:T(128)}, u32[]{:S(2)}) copy-start(f32[4]{0:T(128)} %constant.120.clone) | copy-start | bytes 52
  0.7 3.9 %copy-start.23 = (f32[4]{0:T(128)S(1)}, f32[4]{0:T(128)}, u32[]{:S(2)}) copy-start(f32[4]{0:T(128)} %constant.123.clone) | copy-start | bytes 52
  0.7 3.9 %copy-start.24 = (f32[4]{0:T(128)S(1)}, f32[4]{0:T(128)}, u32[]{:S(2)}) copy-start(f32[4]{0:T(128)} %constant.122.clone) | copy-start | bytes 52
  0.7 4.0 %copy-start.21 = (f32[4]{0:T(128)S(1)}, f32[4]{0:T(128)}, u32[]{:S(2)}) copy-start(f32[4]{0:T(128)} %constant.127.clone) | copy-start | bytes 52
  0.8 4.0 %copy-start.22 = (f32[4]{0:T(128)S(1)}, f32[4]{0:T(128)}, u32[]{:S(2)}) copy-start(f32[4]{0:T(128)} %constant.126.clone) | copy-start | bytes 52
  0.8 4.0 %copy-start.19 = (f32[4]{0:T(128)S(1)}, f32[4]{0:T(128)}, u32[]{:S(2)}) copy-start(f32[4]{0:T(128)} %constant.129.clone) | copy-start | bytes 52
  0.8 4.0 %copy-start.20 = (f32[4]{0:T(128)S(1)}, f32[4]{0:T(128)}, u32[]{:S(2)}) copy-start(f32[4]{0:T(128)} %constant.128.clone) | copy-start | bytes 52
  0.8 4.1 %copy-start.6 = (f32[32,28]{1,0:T(8,128)S(1)}, f32[32,28]{1,0:T(8,128)}, u32[]{:S(2)}) copy-start(f32[32,28]{1,0:T(8,128)} %constant.148) | copy-start | bytes 10756
  0.8 4.3 %copy-start.10 = (f32[32,28]{1,0:T(8,128)S(1)}, f32[32,28]{1,0:T(8,128)}, u32[]{:S(2)}) copy-start(f32[32,28]{1,0:T(8,128)} %constant.149) | copy-start | bytes 10756
  0.8 4.5 %copy-start.9 = (f32[32,28]{1,0:T(8,128)S(1)}, f32[32,28]{1,0:T(8,128)}, u32[]{:S(2)}) copy-start(f32[32,28]{1,0:T(8,128)} %constant.113.clone) | copy-start | bytes 10756
  2.7 2.8 %copy-start.8 = (f32[32,28]{1,0:T(8,128)S(1)}, f32[32,28]{1,0:T(8,128)}, u32[]{:S(2)}) copy-start(f32[32,28]{1,0:T(8,128)} %constant.114.clone) | copy-start | bytes 10756
  3.8 2.0 %copy-start.7 = (f32[32,28]{1,0:T(8,128)S(1)}, f32[32,28]{1,0:T(8,128)}, u32[]{:S(2)}) copy-start(f32[32,28]{1,0:T(8,128)} %constant.147) | copy-start | bytes 10756
  8.3 5.8 %copy-start.1 = (bf16[7,4,4,4,1,2,128]{6,5,4,3,2,1,0:T(2,128)(2,1)S(1)}, bf16[7,4,4,4,1,2,128]{6,5,4,3,2,1,0:T(2,128)(2,1)}, u32[]{:S(2)}) copy-start(bf16[7,4,4,4,1,2,128]{6,5,4,3,2,1,0:T(2,128)(2,1)} %param.44) | copy-start | bytes 688132
  9.4 12.5 %collective-permute-start = (f32[4,1,384]{2,1,0:T(1,128)S(1)}, f32[4,1,384]{2,1,0:T(1,128)S(1)}, u32[]{:S(2)}, u32[]{:S(2)}) collective-permute-start(f32[4,1,384]{2,1,0:T(1,128)S(1)} %slice.244), channel_id=1, source_target_pairs={{0,1},{1,2},{2,3},{3,4},{4,5},{5,6},{6,7},{7,8},{8,9},{9,10},{10,1... | collective-permute-start | bytes 18440 | tf_op jit(solution)/shard_map/ppermute | solution.py:22
  14.1 0.7 copy-start.17
  14.1 0.7 copy-start.18
  14.1 0.7 copy-start.15
  14.1 0.7 copy-start.16
  14.1 0.8 copy-start.13
  14.1 0.8 copy-start.14
  14.2 0.8 copy-start.11
  14.2 0.8 copy-start.12
  15.1 12.1 %copy-start.2 = (f32[3,6,384]{2,1,0:T(8,128)S(1)}, f32[3,6,384]{2,1,0:T(8,128)}, u32[]{:S(2)}) copy-start(f32[3,6,384]{2,1,0:T(8,128)} %param.43) | copy-start | bytes 82948
  21.9 5.2 %collective-permute-start.1 = (f32[1,6,384]{2,1,0:T(8,128)S(1)}, f32[1,6,384]{2,1,0:T(8,128)S(1)}, u32[]{:S(2)}, u32[]{:S(2)}) collective-permute-start(f32[1,6,384]{2,1,0:T(8,128)S(1)} %pad_maximum_fusion.14), channel_id=1, source_target_pairs={{0,64},{64,128},{128,192},{192,256},{256,320},{320,384},{384,448},... | collective-permute-start | bytes 27656 | tf_op jit(solution)/shard_map/ppermute | solution.py:22
  27.2 9.3 %collective-permute-start.2 = (f32[1,6,384]{2,1,0:T(8,128)S(1)}, f32[1,6,384]{2,1,0:T(8,128)S(1)}, u32[]{:S(2)}, u32[]{:S(2)}) collective-permute-start(f32[1,6,384]{2,1,0:T(8,128)S(1)} %slice.247), channel_id=1, source_target_pairs={{64,0},{128,64},{192,128},{256,192},{320,256},{384,320},{448,384},... | collective-permute-start | bytes 27656 | tf_op jit(solution)/shard_map/ppermute | solution.py:22
  36.6 6.4 %collective-permute-start.3 = (f32[4,1,384]{2,1,0:T(1,128)S(1)}, f32[4,1,384]{2,1,0:T(1,128)S(1)}, u32[]{:S(2)}, u32[]{:S(2)}) collective-permute-start(f32[4,1,384]{2,1,0:T(1,128)S(1)} %pad_maximum_fusion.16), channel_id=1, source_target_pairs={{1,0},{2,1},{3,2},{4,3},{5,4},{6,5},{7,6},{8,7},{9,8},{10,9},{11,1... | collective-permute-start | bytes 18440 | tf_op jit(solution)/shard_map/ppermute | solution.py:22
  43.0 1.1 copy-start.4
  43.0 1.3 copy-start.3
  43.0 1.5 %copy-start = (f32[32,28]{1,0:T(8,128)S(1)}, f32[32,28]{1,0:T(8,128)}, u32[]{:S(2)}) copy-start(f32[32,28]{1,0:T(8,128)} %constant.130.clone) | copy-start | bytes 10756
  47.4 3.1 %collective-permute-start.4 = (f32[4,1,384]{2,1,0:T(1,128)S(1)}, f32[4,1,384]{2,1,0:T(1,128)S(1)}, u32[]{:S(2)}, u32[]{:S(2)}) collective-permute-start(f32[4,1,384]{2,1,0:T(1,128)S(1)} %slice.257), channel_id=1, source_target_pairs={{0,1},{1,2},{2,3},{3,4},{4,5},{5,6},{6,7},{7,8},{8,9},{9,10},{10,1... | collective-permute-start | bytes 18440 | tf_op jit(solution)/shard_map/ppermute | solution.py:22
  50.5 8.7 %collective-permute-start.5 = (f32[1,6,384]{2,1,0:T(8,128)S(1)}, f32[1,6,384]{2,1,0:T(8,128)S(1)}, u32[]{:S(2)}, u32[]{:S(2)}) collective-permute-start(f32[1,6,384]{2,1,0:T(8,128)S(1)} %pad_maximum_fusion.13), channel_id=1, source_target_pairs={{0,64},{64,128},{128,192},{192,256},{256,320},{320,384},{384,448},... | collective-permute-start | bytes 27656 | tf_op jit(solution)/shard_map/ppermute | solution.py:22
  59.4 9.5 %collective-permute-start.6 = (f32[1,6,384]{2,1,0:T(8,128)S(1)}, f32[1,6,384]{2,1,0:T(8,128)S(1)}, u32[]{:S(2)}, u32[]{:S(2)}) collective-permute-start(f32[1,6,384]{2,1,0:T(8,128)S(1)} %slice.259), channel_id=1, source_target_pairs={{64,0},{128,64},{192,128},{256,192},{320,256},{384,320},{448,384},... | collective-permute-start | bytes 27656 | tf_op jit(solution)/shard_map/ppermute | solution.py:22
  68.9 6.9 %collective-permute-start.7 = (f32[4,1,384]{2,1,0:T(1,128)S(1)}, f32[4,1,384]{2,1,0:T(1,128)S(1)}, u32[]{:S(2)}, u32[]{:S(2)}) collective-permute-start(f32[4,1,384]{2,1,0:T(1,128)S(1)} %pad_maximum_fusion.15), channel_id=1, source_target_pairs={{1,0},{2,1},{3,2},{4,3},{5,4},{6,5},{7,6},{8,7},{9,8},{10,9},{11,1... | collective-permute-start | bytes 18440 | tf_op jit(solution)/shard_map/ppermute | solution.py:22
  80.3 15.4 %collective-permute-start.8 = (f32[1,7,384]{2,1,0:T(8,128)S(1)}, f32[1,7,384]{2,1,0:T(8,128)S(1)}, u32[]{:S(2)}, u32[]{:S(2)}) collective-permute-start(f32[1,7,384]{2,1,0:T(8,128)S(1)} %slice.264), channel_id=1, source_target_pairs={{0,64},{64,128},{128,192},{192,256},{256,320},{320,384},{384,448},... | collective-permute-start | bytes 32264 | tf_op jit(solution)/shard_map/ppermute | solution.py:22
  95.8 15.7 %collective-permute-start.9 = (f32[3,1,384]{2,1,0:T(1,128)S(1)}, f32[3,1,384]{2,1,0:T(1,128)S(1)}, u32[]{:S(2)}, u32[]{:S(2)}) collective-permute-start(f32[3,1,384]{2,1,0:T(1,128)S(1)} %slice.222), channel_id=1, source_target_pairs={{0,1},{1,2},{2,3},{3,4},{4,5},{5,6},{6,7},{7,8},{8,9},{9,10},{10,1... | collective-permute-start | bytes 13832 | tf_op jit(solution)/shard_map/ppermute | solution.py:22

commit v12 on v11

--- a/solution.py
+++ b/solution.py
@@ -168,7 +168,7 @@
 
 
 def mat(left, right):
-    return jnp.matmul(left, right, precision=lax.Precision.HIGHEST)
+    return jnp.matmul(left, right, precision=lax.Precision.HIGH)
 
 
 def point_layout(pointwise):

time: 146 us -> 142 us (0.973)
  matrix products: 13.4 us -> 9.38 us
    dot_general x30, matrix products: 13.4 us -> 9.38 us  [mat(): return jnp.matmul(left, right, precision=lax.Precision.HIGH)]
  transfers between devices with their start and end apart: 10 -> 10, of which waited for: 8 -> 8; matrix products, arithmetic and copies ran while one was open for 1% -> 2% of each run, Pallas kernels for 0% -> 0%
where the time goes in v12:
time: 142 us; the launch traced here: 141 us
  blocking collectives  51.5 us (36%)
  starting transfers between devices  39.5 us (28%)
  waiting for transfers between devices  31.5 us (22%)
  matrix products  9.38 us (7%)
  local copies, waits for them, and re-layouts  4.36 us (3%)
  other arithmetic  2.59 us (2%)
  between operations  2.37 us (2%)
    ppermute x10, starting transfers between devices, shifted(): lax.ppermute(value, axis, [(source, source + steps) for source in range(i...  39.5 us
    psum x3, blocking collectives, shards(): summed = lax.psum(summed, axis)  32.7 us
    ppermute x10, waiting for transfers between devices, shifted(): lax.ppermute(value, axis, [(source, source + steps) for source in range(i...  31.5 us
    psum x1, blocking collectives, shards(): summed = lax.psum(summed, BX_BY[1])  11.4 us
    dot_general x30, matrix products, mat(): return jnp.matmul(left, right, precision=lax.Precision.HIGH)  9.38 us
    psum x1, blocking collectives, shards(): summed = lax.psum(terms, BX_BY[0])  7.32 us
  transfers between devices with their start and end apart: 10, of which 8 were waited for; matrix products, arithmetic and copies ran while one was open for 2% of the time, Pallas kernels for 0%

profile of v12, /device:TPU:1, one launch (start us, length us, event | category | flops | bytes accessed | tf_op | source)
XLA Modules:
  0.0 141.1 jit_solution(14929054608039628434)
XLA Ops:
  0.8 1.2 slice.186
  2.8 1.0 fusion.175
  4.0 0.2 fusion.126
  4.2 0.2 fusion.135
  4.8 0.2 fusion.123
  5.3 0.2 convolution_add_fusion.9
  5.7 0.2 convolution_add_fusion.7
  5.9 0.8 fusion.14
  6.7 0.8 convolution_add_fusion.6
  7.5 0.8 convolution_add_fusion.4
  8.3 4.6 %collective-permute-start = (f32[4,1,384]{2,1,0:T(1,128)S(1)}, f32[4,1,384]{2,1,0:T(1,128)S(1)}, u32[]{:S(2)}, u32[]{:S(2)}) collective-permute-start(f32[4,1,384]{2,1,0:T(1,128)S(1)} %slice.244), channel_id=1, source_target_pairs={{0,1},{1,2},{2,3},{3,4},{4,5},{5,6},{6,7},{7,8},{8,9},{9,10},{10,1... | collective-permute-start | bytes 18440 | tf_op jit(solution)/shard_map/ppermute | solution.py:22
  13.0 0.2 bitcast_convert_fusion
  13.9 0.5 select_add_fusion.1
  14.5 6.3 %collective-permute-done = f32[4,1,384]{2,1,0:T(1,128)S(1)} collective-permute-done((f32[4,1,384]{2,1,0:T(1,128)S(1)}, f32[4,1,384]{2,1,0:T(1,128)S(1)}, u32[]{:S(2)}, u32[]{:S(2)}) %collective-permute-start) | collective-permute-done | bytes 6176 | tf_op jit(solution)/shard_map/ppermute | solution.py:22
  20.7 4.4 %collective-permute-start.1 = (f32[1,6,384]{2,1,0:T(8,128)S(1)}, f32[1,6,384]{2,1,0:T(8,128)S(1)}, u32[]{:S(2)}, u32[]{:S(2)}) collective-permute-start(f32[1,6,384]{2,1,0:T(8,128)S(1)} %pad_maximum_fusion.14), channel_id=1, source_target_pairs={{0,64},{64,128},{128,192},{192,256},{256,320},{320,384},{384,448},... | collective-permute-start | bytes 27656 | tf_op jit(solution)/shard_map/ppermute | solution.py:22
  25.2 0.8 collective-permute-done.1
  26.1 1.3 collective-permute-start.2
  27.9 7.5 %collective-permute-done.2 = f32[1,6,384]{2,1,0:T(8,128)S(1)} collective-permute-done((f32[1,6,384]{2,1,0:T(8,128)S(1)}, f32[1,6,384]{2,1,0:T(8,128)S(1)}, u32[]{:S(2)}, u32[]{:S(2)}) %collective-permute-start.2) | collective-permute-done | bytes 9248 | tf_op jit(solution)/shard_map/ppermute | solution.py:22
  35.4 2.3 %collective-permute-start.3 = (f32[4,1,384]{2,1,0:T(1,128)S(1)}, f32[4,1,384]{2,1,0:T(1,128)S(1)}, u32[]{:S(2)}, u32[]{:S(2)}) collective-permute-start(f32[4,1,384]{2,1,0:T(1,128)S(1)} %pad_maximum_fusion.16), channel_id=1, source_target_pairs={{1,0},{2,1},{3,2},{4,3},{5,4},{6,5},{7,6},{8,7},{9,8},{10,9},{11,1... | collective-permute-start | bytes 18440 | tf_op jit(solution)/shard_map/ppermute | solution.py:22
  37.7 4.0 %collective-permute-done.3 = f32[4,1,384]{2,1,0:T(1,128)S(1)} collective-permute-done((f32[4,1,384]{2,1,0:T(1,128)S(1)}, f32[4,1,384]{2,1,0:T(1,128)S(1)}, u32[]{:S(2)}, u32[]{:S(2)}) %collective-permute-start.3) | collective-permute-done | bytes 6176 | tf_op jit(solution)/shard_map/ppermute | solution.py:22
  41.8 0.6 fusion.29
  43.2 0.2 fusion.176
  43.4 0.2 fusion.64
  43.6 0.2 convolution_add_fusion.3
  43.9 0.2 convolution_add_fusion.2
  44.1 0.8 fusion.28
  44.9 1.9 %collective-permute-start.4 = (f32[4,1,384]{2,1,0:T(1,128)S(1)}, f32[4,1,384]{2,1,0:T(1,128)S(1)}, u32[]{:S(2)}, u32[]{:S(2)}) collective-permute-start(f32[4,1,384]{2,1,0:T(1,128)S(1)} %slice.257), channel_id=1, source_target_pairs={{0,1},{1,2},{2,3},{3,4},{4,5},{5,6},{6,7},{7,8},{8,9},{9,10},{10,1... | collective-permute-start | bytes 18440 | tf_op jit(solution)/shard_map/ppermute | solution.py:22
  46.9 1.1 collective-permute-done.4
  48.0 7.9 %collective-permute-start.5 = (f32[1,6,384]{2,1,0:T(8,128)S(1)}, f32[1,6,384]{2,1,0:T(8,128)S(1)}, u32[]{:S(2)}, u32[]{:S(2)}) collective-permute-start(f32[1,6,384]{2,1,0:T(8,128)S(1)} %pad_maximum_fusion.13), channel_id=1, source_target_pairs={{0,64},{64,128},{128,192},{192,256},{256,320},{320,384},{384,448},... | collective-permute-start | bytes 27656 | tf_op jit(solution)/shard_map/ppermute | solution.py:22
  55.9 0.8 collective-permute-done.5
  56.8 1.3 collective-permute-start.6
  58.3 8.1 %collective-permute-done.6 = f32[1,6,384]{2,1,0:T(8,128)S(1)} collective-permute-done((f32[1,6,384]{2,1,0:T(8,128)S(1)}, f32[1,6,384]{2,1,0:T(8,128)S(1)}, u32[]{:S(2)}, u32[]{:S(2)}) %collective-permute-start.6) | collective-permute-done | bytes 9248 | tf_op jit(solution)/shard_map/ppermute | solution.py:22
  66.4 3.8 %collective-permute-start.7 = (f32[4,1,384]{2,1,0:T(1,128)S(1)}, f32[4,1,384]{2,1,0:T(1,128)S(1)}, u32[]{:S(2)}, u32[]{:S(2)}) collective-permute-start(f32[4,1,384]{2,1,0:T(1,128)S(1)} %pad_maximum_fusion.15), channel_id=1, source_target_pairs={{1,0},{2,1},{3,2},{4,3},{5,4},{6,5},{7,6},{8,7},{9,8},{10,9},{11,1... | collective-permute-start | bytes 18440 | tf_op jit(solution)/shard_map/ppermute | solution.py:22
  70.3 2.9 %collective-permute-done.7 = f32[4,1,384]{2,1,0:T(1,128)S(1)} collective-permute-done((f32[4,1,384]{2,1,0:T(1,128)S(1)}, f32[4,1,384]{2,1,0:T(1,128)S(1)}, u32[]{:S(2)}, u32[]{:S(2)}) %collective-permute-start.7) | collective-permute-done | bytes 6176 | tf_op jit(solution)/shard_map/ppermute | solution.py:22
  73.3 0.6 fusion.27
  74.5 0.2 fusion.177
  74.7 0.2 fusion.67
  74.9 0.2 convolution_add_fusion.1
  75.2 0.2 convolution_add_fusion
  75.4 0.8 fusion.26
  76.3 7.9 %collective-permute-start.8 = (f32[1,7,384]{2,1,0:T(8,128)S(1)}, f32[1,7,384]{2,1,0:T(8,128)S(1)}, u32[]{:S(2)}, u32[]{:S(2)}) collective-permute-start(f32[1,7,384]{2,1,0:T(8,128)S(1)} %slice.264), channel_id=1, source_target_pairs={{0,64},{64,128},{128,192},{192,256},{256,320},{320,384},{384,448},... | collective-permute-start | bytes 32264 | tf_op jit(solution)/shard_map/ppermute | solution.py:22
  84.4 7.3 %psum.35 = f32[6]{0:T(128)S(1)} all-reduce(f32[6]{0:T(128)S(1)} %pad_maximum_fusion.17), channel_id=1, replica_groups=mesh['bx_0'=4,'bx_1'=3,'by_0'=4,'by_1'=8,'by_2'=2] {'bx_0'}, use_global_device_ids=true, to_apply=%region_2.3 | all-reduce | flops 6 | bytes 48 | tf_op jit(solution)/shard_map/psum | solution.py:318
  91.7 4.2 %collective-permute-start.9 = (f32[3,1,384]{2,1,0:T(1,128)S(1)}, f32[3,1,384]{2,1,0:T(1,128)S(1)}, u32[]{:S(2)}, u32[]{:S(2)}) collective-permute-start(f32[3,1,384]{2,1,0:T(1,128)S(1)} %slice.222), channel_id=1, source_target_pairs={{0,1},{1,2},{2,3},{3,4},{4,5},{5,6},{6,7},{7,8},{8,9},{9,10},{10,1... | collective-permute-start | bytes 13832 | tf_op jit(solution)/shard_map/ppermute | solution.py:22
  96.0 11.4 %psum.36 = f32[6]{0:T(128)S(1)} all-reduce(f32[6]{0:T(128)S(1)} %psum.35), channel_id=1, replica_groups=mesh['bx_0'=4,'bx_1'=3,'by_0'=4,'by_1'=8,'by_2'=2] {'bx_1'}, use_global_device_ids=true, to_apply=%region_3.4 | all-reduce | flops 6 | bytes 48 | tf_op jit(solution)/shard_map/psum | solution.py:322
  107.5 10.3 %psum.37 = f32[6]{0:T(128)S(1)} all-reduce(f32[6]{0:T(128)S(1)} %psum.36), channel_id=1, replica_groups=mesh['bx_0'=4,'bx_1'=3,'by_0'=4,'by_1'=8,'by_2'=2] {'by_0'}, use_global_device_ids=true, to_apply=%region_4.5 | all-reduce | flops 6 | bytes 48 | tf_op jit(solution)/shard_map/psum | solution.py:325
  117.8 15.6 %psum.38 = f32[6]{0:T(128)S(1)} all-reduce(f32[6]{0:T(128)S(1)} %psum.37), channel_id=1, replica_groups=mesh['bx_0'=4,'bx_1'=3,'by_0'=4,'by_1'=8,'by_2'=2] {'by_1'}, use_global_device_ids=true, to_apply=%region_5.6 | all-reduce | flops 6 | bytes 48 | tf_op jit(solution)/shard_map/psum | solution.py:325
  133.4 6.8 %psum.39 = f32[6]{0:T(128)S(1)} all-reduce(f32[6]{0:T(128)S(1)} %psum.38), channel_id=1, replica_groups=mesh['bx_0'=4,'bx_1'=3,'by_0'=4,'by_1'=8,'by_2'=2] {'by_2'}, use_global_device_ids=true, to_apply=%region_6.7 | all-reduce | flops 6 | bytes 48 | tf_op jit(solution)/shard_map/psum | solution.py:325
  140.4 0.7 multiply_subtract_fusion
  (167 shorter events, 4.8 us)
Async XLA Ops:
  0.6 3.3 %copy-start.5 = (f32[32,28]{1,0:T(8,128)S(1)}, f32[32,28]{1,0:T(8,128)}, u32[]{:S(2)}) copy-start(f32[32,28]{1,0:T(8,128)} %constant.112.clone) | copy-start | bytes 10756
  0.6 3.7 %copy-start.29 = (f32[4]{0:T(128)S(1)}, f32[4]{0:T(128)}, u32[]{:S(2)}) copy-start(f32[4]{0:T(128)} %constant.117.clone) | copy-start | bytes 52
  0.7 3.7 %copy-start.30 = (f32[4]{0:T(128)S(1)}, f32[4]{0:T(128)}, u32[]{:S(2)}) copy-start(f32[4]{0:T(128)} %constant.116.clone) | copy-start | bytes 52
  0.7 3.8 %copy-start.27 = (f32[4]{0:T(128)S(1)}, f32[4]{0:T(128)}, u32[]{:S(2)}) copy-start(f32[4]{0:T(128)} %constant.119.clone) | copy-start | bytes 52
  0.7 3.8 %copy-start.28 = (f32[4]{0:T(128)S(1)}, f32[4]{0:T(128)}, u32[]{:S(2)}) copy-start(f32[4]{0:T(128)} %constant.118.clone) | copy-start | bytes 52
  0.7 3.8 %copy-start.25 = (f32[4]{0:T(128)S(1)}, f32[4]{0:T(128)}, u32[]{:S(2)}) copy-start(f32[4]{0:T(128)} %constant.121.clone) | copy-start | bytes 52
  0.7 3.8 %copy-start.26 = (f32[4]{0:T(128)S(1)}, f32[4]{0:T(128)}, u32[]{:S(2)}) copy-start(f32[4]{0:T(128)} %constant.120.clone) | copy-start | bytes 52
  0.7 3.9 %copy-start.23 = (f32[4]{0:T(128)S(1)}, f32[4]{0:T(128)}, u32[]{:S(2)}) copy-start(f32[4]{0:T(128)} %constant.123.clone) | copy-start | bytes 52
  0.7 3.9 %copy-start.24 = (f32[4]{0:T(128)S(1)}, f32[4]{0:T(128)}, u32[]{:S(2)}) copy-start(f32[4]{0:T(128)} %constant.122.clone) | copy-start | bytes 52
  0.7 3.9 %copy-start.21 = (f32[4]{0:T(128)S(1)}, f32[4]{0:T(128)}, u32[]{:S(2)}) copy-start(f32[4]{0:T(128)} %constant.127.clone) | copy-start | bytes 52
  0.8 3.9 %copy-start.22 = (f32[4]{0:T(128)S(1)}, f32[4]{0:T(128)}, u32[]{:S(2)}) copy-start(f32[4]{0:T(128)} %constant.126.clone) | copy-start | bytes 52
  0.8 4.0 %copy-start.19 = (f32[4]{0:T(128)S(1)}, f32[4]{0:T(128)}, u32[]{:S(2)}) copy-start(f32[4]{0:T(128)} %constant.129.clone) | copy-start | bytes 52
  0.8 4.0 %copy-start.20 = (f32[4]{0:T(128)S(1)}, f32[4]{0:T(128)}, u32[]{:S(2)}) copy-start(f32[4]{0:T(128)} %constant.128.clone) | copy-start | bytes 52
  0.8 4.1 %copy-start.6 = (f32[32,28]{1,0:T(8,128)S(1)}, f32[32,28]{1,0:T(8,128)}, u32[]{:S(2)}) copy-start(f32[32,28]{1,0:T(8,128)} %constant.148) | copy-start | bytes 10756
  0.8 4.3 %copy-start.10 = (f32[32,28]{1,0:T(8,128)S(1)}, f32[32,28]{1,0:T(8,128)}, u32[]{:S(2)}) copy-start(f32[32,28]{1,0:T(8,128)} %constant.149) | copy-start | bytes 10756
  0.8 4.5 %copy-start.9 = (f32[32,28]{1,0:T(8,128)S(1)}, f32[32,28]{1,0:T(8,128)}, u32[]{:S(2)}) copy-start(f32[32,28]{1,0:T(8,128)} %constant.113.clone) | copy-start | bytes 10756
  2.7 2.7 %copy-start.8 = (f32[32,28]{1,0:T(8,128)S(1)}, f32[32,28]{1,0:T(8,128)}, u32[]{:S(2)}) copy-start(f32[32,28]{1,0:T(8,128)} %constant.114.clone) | copy-start | bytes 10756
  3.8 1.9 %copy-start.7 = (f32[32,28]{1,0:T(8,128)S(1)}, f32[32,28]{1,0:T(8,128)}, u32[]{:S(2)}) copy-start(f32[32,28]{1,0:T(8,128)} %constant.147) | copy-start | bytes 10756
  7.5 5.5 %copy-start.1 = (bf16[7,4,4,4,1,2,128]{6,5,4,3,2,1,0:T(2,128)(2,1)S(1)}, bf16[7,4,4,4,1,2,128]{6,5,4,3,2,1,0:T(2,128)(2,1)}, u32[]{:S(2)}) copy-start(bf16[7,4,4,4,1,2,128]{6,5,4,3,2,1,0:T(2,128)(2,1)} %param.44) | copy-start | bytes 688132
  8.3 12.4 %collective-permute-start = (f32[4,1,384]{2,1,0:T(1,128)S(1)}, f32[4,1,384]{2,1,0:T(1,128)S(1)}, u32[]{:S(2)}, u32[]{:S(2)}) collective-permute-start(f32[4,1,384]{2,1,0:T(1,128)S(1)} %slice.244), channel_id=1, source_target_pairs={{0,1},{1,2},{2,3},{3,4},{4,5},{5,6},{6,7},{7,8},{8,9},{9,10},{10,1... | collective-permute-start | bytes 18440 | tf_op jit(solution)/shard_map/ppermute | solution.py:22
  12.9 0.7 copy-start.17
  12.9 0.7 copy-start.18
  12.9 0.7 copy-start.15
  13.0 0.7 copy-start.16
  13.0 0.8 copy-start.13
  13.0 0.8 copy-start.14
  13.0 0.8 copy-start.11
  13.0 0.8 copy-start.12
  13.9 12.1 %copy-start.2 = (f32[3,6,384]{2,1,0:T(8,128)S(1)}, f32[3,6,384]{2,1,0:T(8,128)}, u32[]{:S(2)}) copy-start(f32[3,6,384]{2,1,0:T(8,128)} %param.43) | copy-start | bytes 82948
  20.7 5.2 %collective-permute-start.1 = (f32[1,6,384]{2,1,0:T(8,128)S(1)}, f32[1,6,384]{2,1,0:T(8,128)S(1)}, u32[]{:S(2)}, u32[]{:S(2)}) collective-permute-start(f32[1,6,384]{2,1,0:T(8,128)S(1)} %pad_maximum_fusion.14), channel_id=1, source_target_pairs={{0,64},{64,128},{128,192},{192,256},{256,320},{320,384},{384,448},... | collective-permute-start | bytes 27656 | tf_op jit(solution)/shard_map/ppermute | solution.py:22
  26.1 9.3 %collective-permute-start.2 = (f32[1,6,384]{2,1,0:T(8,128)S(1)}, f32[1,6,384]{2,1,0:T(8,128)S(1)}, u32[]{:S(2)}, u32[]{:S(2)}) collective-permute-start(f32[1,6,384]{2,1,0:T(8,128)S(1)} %slice.247), channel_id=1, source_target_pairs={{64,0},{128,64},{192,128},{256,192},{320,256},{384,320},{448,384},... | collective-permute-start | bytes 27656 | tf_op jit(solution)/shard_map/ppermute | solution.py:22
  35.4 6.4 %collective-permute-start.3 = (f32[4,1,384]{2,1,0:T(1,128)S(1)}, f32[4,1,384]{2,1,0:T(1,128)S(1)}, u32[]{:S(2)}, u32[]{:S(2)}) collective-permute-start(f32[4,1,384]{2,1,0:T(1,128)S(1)} %pad_maximum_fusion.16), channel_id=1, source_target_pairs={{1,0},{2,1},{3,2},{4,3},{5,4},{6,5},{7,6},{8,7},{9,8},{10,9},{11,1... | collective-permute-start | bytes 18440 | tf_op jit(solution)/shard_map/ppermute | solution.py:22
  41.8 0.7 copy-start.4
  41.8 0.9 copy-start.3
  41.8 1.0 copy-start
  44.9 3.1 %collective-permute-start.4 = (f32[4,1,384]{2,1,0:T(1,128)S(1)}, f32[4,1,384]{2,1,0:T(1,128)S(1)}, u32[]{:S(2)}, u32[]{:S(2)}) collective-permute-start(f32[4,1,384]{2,1,0:T(1,128)S(1)} %slice.257), channel_id=1, source_target_pairs={{0,1},{1,2},{2,3},{3,4},{4,5},{5,6},{6,7},{7,8},{8,9},{9,10},{10,1... | collective-permute-start | bytes 18440 | tf_op jit(solution)/shard_map/ppermute | solution.py:22
  48.0 8.7 %collective-permute-start.5 = (f32[1,6,384]{2,1,0:T(8,128)S(1)}, f32[1,6,384]{2,1,0:T(8,128)S(1)}, u32[]{:S(2)}, u32[]{:S(2)}) collective-permute-start(f32[1,6,384]{2,1,0:T(8,128)S(1)} %pad_maximum_fusion.13), channel_id=1, source_target_pairs={{0,64},{64,128},{128,192},{192,256},{256,320},{320,384},{384,448},... | collective-permute-start | bytes 27656 | tf_op jit(solution)/shard_map/ppermute | solution.py:22
  56.8 9.5 %collective-permute-start.6 = (f32[1,6,384]{2,1,0:T(8,128)S(1)}, f32[1,6,384]{2,1,0:T(8,128)S(1)}, u32[]{:S(2)}, u32[]{:S(2)}) collective-permute-start(f32[1,6,384]{2,1,0:T(8,128)S(1)} %slice.259), channel_id=1, source_target_pairs={{64,0},{128,64},{192,128},{256,192},{320,256},{384,320},{448,384},... | collective-permute-start | bytes 27656 | tf_op jit(solution)/shard_map/ppermute | solution.py:22
  66.4 6.9 %collective-permute-start.7 = (f32[4,1,384]{2,1,0:T(1,128)S(1)}, f32[4,1,384]{2,1,0:T(1,128)S(1)}, u32[]{:S(2)}, u32[]{:S(2)}) collective-permute-start(f32[4,1,384]{2,1,0:T(1,128)S(1)} %pad_maximum_fusion.15), channel_id=1, source_target_pairs={{1,0},{2,1},{3,2},{4,3},{5,4},{6,5},{7,6},{8,7},{9,8},{10,9},{11,1... | collective-permute-start | bytes 18440 | tf_op jit(solution)/shard_map/ppermute | solution.py:22
  76.3 15.4 %collective-permute-start.8 = (f32[1,7,384]{2,1,0:T(8,128)S(1)}, f32[1,7,384]{2,1,0:T(8,128)S(1)}, u32[]{:S(2)}, u32[]{:S(2)}) collective-permute-start(f32[1,7,384]{2,1,0:T(8,128)S(1)} %slice.264), channel_id=1, source_target_pairs={{0,64},{64,128},{128,192},{192,256},{256,320},{320,384},{384,448},... | collective-permute-start | bytes 32264 | tf_op jit(solution)/shard_map/ppermute | solution.py:22
  91.7 15.7 %collective-permute-start.9 = (f32[3,1,384]{2,1,0:T(1,128)S(1)}, f32[3,1,384]{2,1,0:T(1,128)S(1)}, u32[]{:S(2)}, u32[]{:S(2)}) collective-permute-start(f32[3,1,384]{2,1,0:T(1,128)S(1)} %slice.222), channel_id=1, source_target_pairs={{0,1},{1,2},{2,3},{3,4},{4,5},{5,6},{6,7},{7,8},{8,9},{9,10},{10,1... | collective-permute-start | bytes 13832 | tf_op jit(solution)/shard_map/ppermute | solution.py:22

commit v13 on v12

--- a/solution.py
+++ b/solution.py
@@ -167,8 +167,8 @@
     return band.reshape(3 * count + 1, 4 * count)
 
 
-def mat(left, right):
-    return jnp.matmul(left, right, precision=lax.Precision.HIGH)
+def mat(left, right, precision=lax.Precision.HIGHEST):
+    return jnp.matmul(left, right, precision=precision)
 
 
 def point_layout(pointwise):
@@ -219,8 +219,10 @@
     for z_table, members in groups:
         inner = 0.0
         for table_x, table_y, entry, factor in members:
-            inner = inner + mat(factor * planar(table_x, table_y, count_x, count_y).T, coeffs[entry])
-        total = total + mat(inner, long_axis(z_table, count_z, anchor).T)
+            inner = inner + mat(
+                factor * planar(table_x, table_y, count_x, count_y).T, coeffs[entry], lax.Precision.HIGH
+            )
+        total = total + mat(inner, long_axis(z_table, count_z, anchor).T, lax.Precision.HIGH)
     return total.reshape(3 * count_x + 1, 3 * count_y + 1, 3 * count_z + 1)
 
 

time: 142 us -> 145 us (1.021)
  matrix products: 9.38 us -> 12.3 us
    dot_general x30, matrix products: 9.38 us -> 12.3 us  [mat(): return jnp.matmul(left, right, precision=precision)]
where the time goes in v13:
time: 145 us; the launch traced here: 144 us
  blocking collectives  51.3 us (35%)
  starting transfers between devices  39.6 us (27%)
  waiting for transfers between devices  31.4 us (22%)
  matrix products  12.3 us (8%)
  local copies, waits for them, and re-layouts  4.24 us (3%)
  other arithmetic  2.59 us (2%)
  between operations  2.38 us (2%)
    ppermute x10, starting transfers between devices, shifted(): lax.ppermute(value, axis, [(source, source + steps) for source in range(i...  39.6 us
    psum x3, blocking collectives, shards(): summed = lax.psum(summed, axis)  32.7 us
    ppermute x10, waiting for transfers between devices, shifted(): lax.ppermute(value, axis, [(source, source + steps) for source in range(i...  31.4 us
    dot_general x30, matrix products, mat(): return jnp.matmul(left, right, precision=precision)  12.3 us
    psum x1, blocking collectives, shards(): summed = lax.psum(summed, BX_BY[1])  11.4 us
    psum x1, blocking collectives, shards(): summed = lax.psum(terms, BX_BY[0])  7.18 us
  transfers between devices with their start and end apart: 10, of which 8 were waited for; matrix products, arithmetic and copies ran while one was open for 2% of the time, Pallas kernels for 0%

profile of v13, /device:TPU:1, one launch (start us, length us, event | category | flops | bytes accessed | tf_op | source)
XLA Modules:
  0.0 144.0 jit_solution(7612172175923095491)
XLA Ops:
  0.8 1.2 slice.186
  2.8 1.0 fusion.175
  4.2 0.2 fusion.135
  4.8 0.2 fusion.123
  5.1 0.2 convolution_add_fusion.5
  5.3 0.2 convolution_add_fusion.9
  5.7 0.2 convolution_add_fusion.7
  5.9 0.8 fusion.14
  6.7 0.8 convolution_add_fusion.6
  7.5 0.8 convolution_add_fusion.4
  8.3 4.6 %collective-permute-start = (f32[4,1,384]{2,1,0:T(1,128)S(1)}, f32[4,1,384]{2,1,0:T(1,128)S(1)}, u32[]{:S(2)}, u32[]{:S(2)}) collective-permute-start(f32[4,1,384]{2,1,0:T(1,128)S(1)} %slice.244), channel_id=1, source_target_pairs={{0,1},{1,2},{2,3},{3,4},{4,5},{5,6},{6,7},{7,8},{8,9},{9,10},{10,1... | collective-permute-start | bytes 18440 | tf_op jit(solution)/shard_map/ppermute | solution.py:22
  13.0 0.2 bitcast_convert_fusion
  13.9 0.5 select_add_fusion.1
  14.5 6.3 %collective-permute-done = f32[4,1,384]{2,1,0:T(1,128)S(1)} collective-permute-done((f32[4,1,384]{2,1,0:T(1,128)S(1)}, f32[4,1,384]{2,1,0:T(1,128)S(1)}, u32[]{:S(2)}, u32[]{:S(2)}) %collective-permute-start) | collective-permute-done | bytes 6176 | tf_op jit(solution)/shard_map/ppermute | solution.py:22
  20.7 4.4 %collective-permute-start.1 = (f32[1,6,384]{2,1,0:T(8,128)S(1)}, f32[1,6,384]{2,1,0:T(8,128)S(1)}, u32[]{:S(2)}, u32[]{:S(2)}) collective-permute-start(f32[1,6,384]{2,1,0:T(8,128)S(1)} %pad_maximum_fusion.14), channel_id=1, source_target_pairs={{0,64},{64,128},{128,192},{192,256},{256,320},{320,384},{384,448},... | collective-permute-start | bytes 27656 | tf_op jit(solution)/shard_map/ppermute | solution.py:22
  25.2 0.8 collective-permute-done.1
  26.1 1.3 collective-permute-start.2
  27.9 7.5 %collective-permute-done.2 = f32[1,6,384]{2,1,0:T(8,128)S(1)} collective-permute-done((f32[1,6,384]{2,1,0:T(8,128)S(1)}, f32[1,6,384]{2,1,0:T(8,128)S(1)}, u32[]{:S(2)}, u32[]{:S(2)}) %collective-permute-start.2) | collective-permute-done | bytes 9248 | tf_op jit(solution)/shard_map/ppermute | solution.py:22
  35.4 2.3 %collective-permute-start.3 = (f32[4,1,384]{2,1,0:T(1,128)S(1)}, f32[4,1,384]{2,1,0:T(1,128)S(1)}, u32[]{:S(2)}, u32[]{:S(2)}) collective-permute-start(f32[4,1,384]{2,1,0:T(1,128)S(1)} %pad_maximum_fusion.16), channel_id=1, source_target_pairs={{1,0},{2,1},{3,2},{4,3},{5,4},{6,5},{7,6},{8,7},{9,8},{10,9},{11,1... | collective-permute-start | bytes 18440 | tf_op jit(solution)/shard_map/ppermute | solution.py:22
  37.7 4.0 %collective-permute-done.3 = f32[4,1,384]{2,1,0:T(1,128)S(1)} collective-permute-done((f32[4,1,384]{2,1,0:T(1,128)S(1)}, f32[4,1,384]{2,1,0:T(1,128)S(1)}, u32[]{:S(2)}, u32[]{:S(2)}) %collective-permute-start.3) | collective-permute-done | bytes 6176 | tf_op jit(solution)/shard_map/ppermute | solution.py:22
  41.8 1.0 fusion.29
  43.7 0.3 fusion.176
  44.0 0.3 fusion.64
  44.2 0.3 convolution_add_fusion.3
  44.5 0.3 convolution_add_fusion.2
  44.7 1.5 %fusion.28 = f32[28,385]{1,0:T(8,128)S(1)} fusion(f32[385,512]{1,0:T(8,128)S(1)} %get-tuple-element.41, f32[385,512]{1,0:T(8,128)S(1)} %get-tuple-element.40, f32[28,512]{1,0:T(8,128)S(1)} %fusion.64, f32[28,512]{1,0:T(8,128)S(1)} %convolution_add_fusion.2), kind=kOutput, calls=%fused_computation.44 | convolution fusion | flops 132887552 | bytes 1734768 | tf_op jit(solution)/shard_map/dot_general | solution.py:171
  46.3 1.9 %collective-permute-start.4 = (f32[4,1,384]{2,1,0:T(1,128)S(1)}, f32[4,1,384]{2,1,0:T(1,128)S(1)}, u32[]{:S(2)}, u32[]{:S(2)}) collective-permute-start(f32[4,1,384]{2,1,0:T(1,128)S(1)} %slice.257), channel_id=1, source_target_pairs={{0,1},{1,2},{2,3},{3,4},{4,5},{5,6},{6,7},{7,8},{8,9},{9,10},{10,1... | collective-permute-start | bytes 18440 | tf_op jit(solution)/shard_map/ppermute | solution.py:22
  48.3 1.1 collective-permute-done.4
  49.4 7.9 %collective-permute-start.5 = (f32[1,6,384]{2,1,0:T(8,128)S(1)}, f32[1,6,384]{2,1,0:T(8,128)S(1)}, u32[]{:S(2)}, u32[]{:S(2)}) collective-permute-start(f32[1,6,384]{2,1,0:T(8,128)S(1)} %pad_maximum_fusion.13), channel_id=1, source_target_pairs={{0,64},{64,128},{128,192},{192,256},{256,320},{320,384},{384,448},... | collective-permute-start | bytes 27656 | tf_op jit(solution)/shard_map/ppermute | solution.py:22
  57.3 0.8 collective-permute-done.5
  58.2 1.3 collective-permute-start.6
  59.6 8.1 %collective-permute-done.6 = f32[1,6,384]{2,1,0:T(8,128)S(1)} collective-permute-done((f32[1,6,384]{2,1,0:T(8,128)S(1)}, f32[1,6,384]{2,1,0:T(8,128)S(1)}, u32[]{:S(2)}, u32[]{:S(2)}) %collective-permute-start.6) | collective-permute-done | bytes 9248 | tf_op jit(solution)/shard_map/ppermute | solution.py:22
  67.7 3.8 %collective-permute-start.7 = (f32[4,1,384]{2,1,0:T(1,128)S(1)}, f32[4,1,384]{2,1,0:T(1,128)S(1)}, u32[]{:S(2)}, u32[]{:S(2)}) collective-permute-start(f32[4,1,384]{2,1,0:T(1,128)S(1)} %pad_maximum_fusion.15), channel_id=1, source_target_pairs={{1,0},{2,1},{3,2},{4,3},{5,4},{6,5},{7,6},{8,7},{9,8},{10,9},{11,1... | collective-permute-start | bytes 18440 | tf_op jit(solution)/shard_map/ppermute | solution.py:22
  71.6 2.9 %collective-permute-done.7 = f32[4,1,384]{2,1,0:T(1,128)S(1)} collective-permute-done((f32[4,1,384]{2,1,0:T(1,128)S(1)}, f32[4,1,384]{2,1,0:T(1,128)S(1)}, u32[]{:S(2)}, u32[]{:S(2)}) %collective-permute-start.7) | collective-permute-done | bytes 6176 | tf_op jit(solution)/shard_map/ppermute | solution.py:22
  74.6 1.0 fusion.27
  76.5 0.3 fusion.177
  76.7 0.3 fusion.67
  77.0 0.3 convolution_add_fusion.1
  77.2 0.3 convolution_add_fusion
  77.5 1.5 %fusion.26 = f32[28,385]{1,0:T(8,128)S(1)} fusion(f32[385,512]{1,0:T(8,128)S(1)} %get-tuple-element.41, f32[385,512]{1,0:T(8,128)S(1)} %get-tuple-element.40, f32[28,512]{1,0:T(8,128)S(1)} %fusion.67, f32[28,512]{1,0:T(8,128)S(1)} %convolution_add_fusion), kind=kOutput, calls=%fused_computation.42 | convolution fusion | flops 132887552 | bytes 1734768 | tf_op jit(solution)/shard_map/dot_general | solution.py:171
  79.1 8.0 %collective-permute-start.8 = (f32[1,7,384]{2,1,0:T(8,128)S(1)}, f32[1,7,384]{2,1,0:T(8,128)S(1)}, u32[]{:S(2)}, u32[]{:S(2)}) collective-permute-start(f32[1,7,384]{2,1,0:T(8,128)S(1)} %slice.264), channel_id=1, source_target_pairs={{0,64},{64,128},{128,192},{192,256},{256,320},{320,384},{384,448},... | collective-permute-start | bytes 32264 | tf_op jit(solution)/shard_map/ppermute | solution.py:22
  87.3 7.2 %psum.35 = f32[6]{0:T(128)S(1)} all-reduce(f32[6]{0:T(128)S(1)} %pad_maximum_fusion.17), channel_id=1, replica_groups=mesh['bx_0'=4,'bx_1'=3,'by_0'=4,'by_1'=8,'by_2'=2] {'bx_0'}, use_global_device_ids=true, to_apply=%region_2.3 | all-reduce | flops 6 | bytes 48 | tf_op jit(solution)/shard_map/psum | solution.py:320
  94.6 4.2 %collective-permute-start.9 = (f32[3,1,384]{2,1,0:T(1,128)S(1)}, f32[3,1,384]{2,1,0:T(1,128)S(1)}, u32[]{:S(2)}, u32[]{:S(2)}) collective-permute-start(f32[3,1,384]{2,1,0:T(1,128)S(1)} %slice.222), channel_id=1, source_target_pairs={{0,1},{1,2},{2,3},{3,4},{4,5},{5,6},{6,7},{7,8},{8,9},{9,10},{10,1... | collective-permute-start | bytes 13832 | tf_op jit(solution)/shard_map/ppermute | solution.py:22
  98.8 11.4 %psum.36 = f32[6]{0:T(128)S(1)} all-reduce(f32[6]{0:T(128)S(1)} %psum.35), channel_id=1, replica_groups=mesh['bx_0'=4,'bx_1'=3,'by_0'=4,'by_1'=8,'by_2'=2] {'bx_1'}, use_global_device_ids=true, to_apply=%region_3.4 | all-reduce | flops 6 | bytes 48 | tf_op jit(solution)/shard_map/psum | solution.py:324
  110.4 10.3 %psum.37 = f32[6]{0:T(128)S(1)} all-reduce(f32[6]{0:T(128)S(1)} %psum.36), channel_id=1, replica_groups=mesh['bx_0'=4,'bx_1'=3,'by_0'=4,'by_1'=8,'by_2'=2] {'by_0'}, use_global_device_ids=true, to_apply=%region_4.5 | all-reduce | flops 6 | bytes 48 | tf_op jit(solution)/shard_map/psum | solution.py:327
  120.6 15.6 %psum.38 = f32[6]{0:T(128)S(1)} all-reduce(f32[6]{0:T(128)S(1)} %psum.37), channel_id=1, replica_groups=mesh['bx_0'=4,'bx_1'=3,'by_0'=4,'by_1'=8,'by_2'=2] {'by_1'}, use_global_device_ids=true, to_apply=%region_5.6 | all-reduce | flops 6 | bytes 48 | tf_op jit(solution)/shard_map/psum | solution.py:327
  136.3 6.8 %psum.39 = f32[6]{0:T(128)S(1)} all-reduce(f32[6]{0:T(128)S(1)} %psum.38), channel_id=1, replica_groups=mesh['bx_0'=4,'bx_1'=3,'by_0'=4,'by_1'=8,'by_2'=2] {'by_2'}, use_global_device_ids=true, to_apply=%region_6.7 | all-reduce | flops 6 | bytes 48 | tf_op jit(solution)/shard_map/psum | solution.py:327
  143.2 0.7 multiply_subtract_fusion
  (167 shorter events, 5.0 us)
Async XLA Ops:
  0.6 3.3 %copy-start.5 = (f32[32,28]{1,0:T(8,128)S(1)}, f32[32,28]{1,0:T(8,128)}, u32[]{:S(2)}) copy-start(f32[32,28]{1,0:T(8,128)} %constant.112.clone) | copy-start | bytes 10756
  0.6 3.7 %copy-start.29 = (f32[4]{0:T(128)S(1)}, f32[4]{0:T(128)}, u32[]{:S(2)}) copy-start(f32[4]{0:T(128)} %constant.117.clone) | copy-start | bytes 52
  0.7 3.7 %copy-start.30 = (f32[4]{0:T(128)S(1)}, f32[4]{0:T(128)}, u32[]{:S(2)}) copy-start(f32[4]{0:T(128)} %constant.116.clone) | copy-start | bytes 52
  0.7 3.8 %copy-start.27 = (f32[4]{0:T(128)S(1)}, f32[4]{0:T(128)}, u32[]{:S(2)}) copy-start(f32[4]{0:T(128)} %constant.119.clone) | copy-start | bytes 52
  0.7 3.8 %copy-start.28 = (f32[4]{0:T(128)S(1)}, f32[4]{0:T(128)}, u32[]{:S(2)}) copy-start(f32[4]{0:T(128)} %constant.118.clone) | copy-start | bytes 52
  0.7 3.8 %copy-start.25 = (f32[4]{0:T(128)S(1)}, f32[4]{0:T(128)}, u32[]{:S(2)}) copy-start(f32[4]{0:T(128)} %constant.121.clone) | copy-start | bytes 52
  0.7 3.8 %copy-start.26 = (f32[4]{0:T(128)S(1)}, f32[4]{0:T(128)}, u32[]{:S(2)}) copy-start(f32[4]{0:T(128)} %constant.120.clone) | copy-start | bytes 52
  0.7 3.9 %copy-start.23 = (f32[4]{0:T(128)S(1)}, f32[4]{0:T(128)}, u32[]{:S(2)}) copy-start(f32[4]{0:T(128)} %constant.123.clone) | copy-start | bytes 52
  0.7 3.9 %copy-start.24 = (f32[4]{0:T(128)S(1)}, f32[4]{0:T(128)}, u32[]{:S(2)}) copy-start(f32[4]{0:T(128)} %constant.122.clone) | copy-start | bytes 52
  0.7 3.9 %copy-start.21 = (f32[4]{0:T(128)S(1)}, f32[4]{0:T(128)}, u32[]{:S(2)}) copy-start(f32[4]{0:T(128)} %constant.127.clone) | copy-start | bytes 52
  0.8 3.9 %copy-start.22 = (f32[4]{0:T(128)S(1)}, f32[4]{0:T(128)}, u32[]{:S(2)}) copy-start(f32[4]{0:T(128)} %constant.126.clone) | copy-start | bytes 52
  0.8 4.0 %copy-start.19 = (f32[4]{0:T(128)S(1)}, f32[4]{0:T(128)}, u32[]{:S(2)}) copy-start(f32[4]{0:T(128)} %constant.129.clone) | copy-start | bytes 52
  0.8 4.0 %copy-start.20 = (f32[4]{0:T(128)S(1)}, f32[4]{0:T(128)}, u32[]{:S(2)}) copy-start(f32[4]{0:T(128)} %constant.128.clone) | copy-start | bytes 52
  0.8 4.1 %copy-start.6 = (f32[32,28]{1,0:T(8,128)S(1)}, f32[32,28]{1,0:T(8,128)}, u32[]{:S(2)}) copy-start(f32[32,28]{1,0:T(8,128)} %constant.148) | copy-start | bytes 10756
  0.8 4.3 %copy-start.10 = (f32[32,28]{1,0:T(8,128)S(1)}, f32[32,28]{1,0:T(8,128)}, u32[]{:S(2)}) copy-start(f32[32,28]{1,0:T(8,128)} %constant.149) | copy-start | bytes 10756
  0.8 4.5 %copy-start.9 = (f32[32,28]{1,0:T(8,128)S(1)}, f32[32,28]{1,0:T(8,128)}, u32[]{:S(2)}) copy-start(f32[32,28]{1,0:T(8,128)} %constant.113.clone) | copy-start | bytes 10756
  2.7 2.7 %copy-start.8 = (f32[32,28]{1,0:T(8,128)S(1)}, f32[32,28]{1,0:T(8,128)}, u32[]{:S(2)}) copy-start(f32[32,28]{1,0:T(8,128)} %constant.114.clone) | copy-start | bytes 10756
  3.8 1.9 %copy-start.7 = (f32[32,28]{1,0:T(8,128)S(1)}, f32[32,28]{1,0:T(8,128)}, u32[]{:S(2)}) copy-start(f32[32,28]{1,0:T(8,128)} %constant.147) | copy-start | bytes 10756
  7.5 5.5 %copy-start.1 = (bf16[7,4,4,4,1,2,128]{6,5,4,3,2,1,0:T(2,128)(2,1)S(1)}, bf16[7,4,4,4,1,2,128]{6,5,4,3,2,1,0:T(2,128)(2,1)}, u32[]{:S(2)}) copy-start(bf16[7,4,4,4,1,2,128]{6,5,4,3,2,1,0:T(2,128)(2,1)} %param.44) | copy-start | bytes 688132
  8.3 12.4 %collective-permute-start = (f32[4,1,384]{2,1,0:T(1,128)S(1)}, f32[4,1,384]{2,1,0:T(1,128)S(1)}, u32[]{:S(2)}, u32[]{:S(2)}) collective-permute-start(f32[4,1,384]{2,1,0:T(1,128)S(1)} %slice.244), channel_id=1, source_target_pairs={{0,1},{1,2},{2,3},{3,4},{4,5},{5,6},{6,7},{7,8},{8,9},{9,10},{10,1... | collective-permute-start | bytes 18440 | tf_op jit(solution)/shard_map/ppermute | solution.py:22
  12.9 0.7 copy-start.17
  12.9 0.7 copy-start.18
  12.9 0.7 copy-start.15
  13.0 0.7 copy-start.16
  13.0 0.8 copy-start.13
  13.0 0.8 copy-start.14
  13.0 0.8 copy-start.11
  13.0 0.8 copy-start.12
  13.9 12.1 %copy-start.2 = (f32[3,6,384]{2,1,0:T(8,128)S(1)}, f32[3,6,384]{2,1,0:T(8,128)}, u32[]{:S(2)}) copy-start(f32[3,6,384]{2,1,0:T(8,128)} %param.43) | copy-start | bytes 82948
  20.7 5.2 %collective-permute-start.1 = (f32[1,6,384]{2,1,0:T(8,128)S(1)}, f32[1,6,384]{2,1,0:T(8,128)S(1)}, u32[]{:S(2)}, u32[]{:S(2)}) collective-permute-start(f32[1,6,384]{2,1,0:T(8,128)S(1)} %pad_maximum_fusion.14), channel_id=1, source_target_pairs={{0,64},{64,128},{128,192},{192,256},{256,320},{320,384},{384,448},... | collective-permute-start | bytes 27656 | tf_op jit(solution)/shard_map/ppermute | solution.py:22
  26.1 9.3 %collective-permute-start.2 = (f32[1,6,384]{2,1,0:T(8,128)S(1)}, f32[1,6,384]{2,1,0:T(8,128)S(1)}, u32[]{:S(2)}, u32[]{:S(2)}) collective-permute-start(f32[1,6,384]{2,1,0:T(8,128)S(1)} %slice.247), channel_id=1, source_target_pairs={{64,0},{128,64},{192,128},{256,192},{320,256},{384,320},{448,384},... | collective-permute-start | bytes 27656 | tf_op jit(solution)/shard_map/ppermute | solution.py:22
  35.4 6.4 %collective-permute-start.3 = (f32[4,1,384]{2,1,0:T(1,128)S(1)}, f32[4,1,384]{2,1,0:T(1,128)S(1)}, u32[]{:S(2)}, u32[]{:S(2)}) collective-permute-start(f32[4,1,384]{2,1,0:T(1,128)S(1)} %pad_maximum_fusion.16), channel_id=1, source_target_pairs={{1,0},{2,1},{3,2},{4,3},{5,4},{6,5},{7,6},{8,7},{9,8},{10,9},{11,1... | collective-permute-start | bytes 18440 | tf_op jit(solution)/shard_map/ppermute | solution.py:22
  41.8 1.1 copy-start.4
  41.8 1.3 copy-start.3
  41.8 1.5 %copy-start = (f32[32,28]{1,0:T(8,128)S(1)}, f32[32,28]{1,0:T(8,128)}, u32[]{:S(2)}) copy-start(f32[32,28]{1,0:T(8,128)} %constant.130.clone) | copy-start | bytes 10756
  46.3 3.1 %collective-permute-start.4 = (f32[4,1,384]{2,1,0:T(1,128)S(1)}, f32[4,1,384]{2,1,0:T(1,128)S(1)}, u32[]{:S(2)}, u32[]{:S(2)}) collective-permute-start(f32[4,1,384]{2,1,0:T(1,128)S(1)} %slice.257), channel_id=1, source_target_pairs={{0,1},{1,2},{2,3},{3,4},{4,5},{5,6},{6,7},{7,8},{8,9},{9,10},{10,1... | collective-permute-start | bytes 18440 | tf_op jit(solution)/shard_map/ppermute | solution.py:22
  49.4 8.7 %collective-permute-start.5 = (f32[1,6,384]{2,1,0:T(8,128)S(1)}, f32[1,6,384]{2,1,0:T(8,128)S(1)}, u32[]{:S(2)}, u32[]{:S(2)}) collective-permute-start(f32[1,6,384]{2,1,0:T(8,128)S(1)} %pad_maximum_fusion.13), channel_id=1, source_target_pairs={{0,64},{64,128},{128,192},{192,256},{256,320},{320,384},{384,448},... | collective-permute-start | bytes 27656 | tf_op jit(solution)/shard_map/ppermute | solution.py:22
  58.2 9.5 %collective-permute-start.6 = (f32[1,6,384]{2,1,0:T(8,128)S(1)}, f32[1,6,384]{2,1,0:T(8,128)S(1)}, u32[]{:S(2)}, u32[]{:S(2)}) collective-permute-start(f32[1,6,384]{2,1,0:T(8,128)S(1)} %slice.259), channel_id=1, source_target_pairs={{64,0},{128,64},{192,128},{256,192},{320,256},{384,320},{448,384},... | collective-permute-start | bytes 27656 | tf_op jit(solution)/shard_map/ppermute | solution.py:22
  67.7 6.9 %collective-permute-start.7 = (f32[4,1,384]{2,1,0:T(1,128)S(1)}, f32[4,1,384]{2,1,0:T(1,128)S(1)}, u32[]{:S(2)}, u32[]{:S(2)}) collective-permute-start(f32[4,1,384]{2,1,0:T(1,128)S(1)} %pad_maximum_fusion.15), channel_id=1, source_target_pairs={{1,0},{2,1},{3,2},{4,3},{5,4},{6,5},{7,6},{8,7},{9,8},{10,9},{11,1... | collective-permute-start | bytes 18440 | tf_op jit(solution)/shard_map/ppermute | solution.py:22
  79.1 15.4 %collective-permute-start.8 = (f32[1,7,384]{2,1,0:T(8,128)S(1)}, f32[1,7,384]{2,1,0:T(8,128)S(1)}, u32[]{:S(2)}, u32[]{:S(2)}) collective-permute-start(f32[1,7,384]{2,1,0:T(8,128)S(1)} %slice.264), channel_id=1, source_target_pairs={{0,64},{64,128},{128,192},{192,256},{256,320},{320,384},{384,448},... | collective-permute-start | bytes 32264 | tf_op jit(solution)/shard_map/ppermute | solution.py:22
  94.6 15.7 %collective-permute-start.9 = (f32[3,1,384]{2,1,0:T(1,128)S(1)}, f32[3,1,384]{2,1,0:T(1,128)S(1)}, u32[]{:S(2)}, u32[]{:S(2)}) collective-permute-start(f32[3,1,384]{2,1,0:T(1,128)S(1)} %slice.222), channel_id=1, source_target_pairs={{0,1},{1,2},{2,3},{3,4},{4,5},{5,6},{6,7},{7,8},{8,9},{9,10},{10,1... | collective-permute-start | bytes 13832 | tf_op jit(solution)/shard_map/ppermute | solution.py:22

commit v14 on v11

--- a/solution.py
+++ b/solution.py
@@ -188,9 +188,11 @@
     width = 4 * count_z
     through_z = mat(field.reshape(rows, field.shape[2]), z_tables)
     z_value = through_z[:, :width]
-    point_value = mat(plain, z_value)
-    grad_x = mat(along_x, z_value)
-    grad_y = mat(along_y, z_value)
+    planes = plain.shape[0]
+    stacked = mat(jnp.concatenate([plain, along_x, along_y], 0), z_value)
+    point_value = stacked[:planes]
+    grad_x = stacked[planes : 2 * planes]
+    grad_y = stacked[2 * planes :]
     grad_z = mat(plain, through_z[:, width:])
     flux_x = coeffs[1] * grad_x + coeffs[4] * grad_y + coeffs[5] * grad_z
     flux_y = coeffs[4] * grad_x + coeffs[2] * grad_y + coeffs[6] * grad_z
@@ -215,12 +217,15 @@
         (square_s, [(square_v, square_v, 3, 1.0)]),
         (mixed, [(mixed, square_v, 5, 2.0), (square_v, mixed, 6, 2.0)]),
     ]
-    total = 0.0
+    inners = []
+    bands = []
     for z_table, members in groups:
         inner = 0.0
         for table_x, table_y, entry, factor in members:
             inner = inner + mat(factor * planar(table_x, table_y, count_x, count_y).T, coeffs[entry])
-        total = total + mat(inner, long_axis(z_table, count_z, anchor).T)
+        inners.append(inner)
+        bands.append(long_axis(z_table, count_z, anchor).T)
+    total = mat(jnp.concatenate(inners, 1), jnp.concatenate(bands, 0))
     return total.reshape(3 * count_x + 1, 3 * count_y + 1, 3 * count_z + 1)
 
 

time: 146 us -> 145 us (level)
    dot_general x30 -> x24, matrix products: 13.4 us -> 12.1 us  [mat(): return jnp.matmul(left, right, precision=lax.Precision.HIGHEST)]
  transfers between devices with their start and end apart: 10 -> 10, of which waited for: 8 -> 8; matrix products, arithmetic and copies ran while one was open for 1% -> 2% of each run, Pallas kernels for 0% -> 0%
where the time goes in v14:
time: 145 us
  blocking collectives  51.3 us (35%)
  starting transfers between devices  39.3 us (27%)
  waiting for transfers between devices  32 us (22%)
  matrix products  12.1 us (8%)
  local copies, waits for them, and re-layouts  4.07 us (3%)
  other arithmetic  3.59 us (2%)
  between operations  2.45 us (2%)
    ppermute x10, starting transfers between devices, shifted(): lax.ppermute(value, axis, [(source, source + steps) for source in range(i...  39.3 us
    psum x3, blocking collectives, shards(): summed = lax.psum(summed, axis)  32.5 us
    ppermute x10, waiting for transfers between devices, shifted(): lax.ppermute(value, axis, [(source, source + steps) for source in range(i...  32 us
    dot_general x24, matrix products, mat(): return jnp.matmul(left, right, precision=lax.Precision.HIGHEST)  12.1 us
    psum x1, blocking collectives, shards(): summed = lax.psum(summed, BX_BY[1])  11.6 us
    psum x1, blocking collectives, shards(): summed = lax.psum(terms, BX_BY[0])  7.22 us
  transfers between devices with their start and end apart: 10, of which 8 were waited for; matrix products, arithmetic and copies ran while one was open for 2% of the time, Pallas kernels for 0%

profile of v14, /device:TPU:1, one launch (start us, length us, event | category | flops | bytes accessed | tf_op | source)
XLA Modules:
  0.0 144.8 jit_solution(8334300667856262336)
XLA Ops:
  0.9 1.1 fusion.139
  2.0 1.2 slice.207
  3.9 0.9 fusion.113
  5.6 0.2 fusion.101
  5.8 0.2 convolution_add_fusion.7
  6.1 0.2 convolution_add_fusion.6
  6.8 1.0 select_add_fusion.2
  7.8 1.8 %fusion = f32[28,385]{1,0:T(8,128)S(1)} fusion(f32[512,385]{1,0:T(8,128)S(1)} %get-tuple-element.44, f32[512,385]{1,0:T(8,128)S(1)} %get-tuple-element.43, f32[512,385]{1,0:T(8,128)S(1)} %get-tuple-element.42, f32[28,512]{1,0:T(8,128)S(1)} %convolution_add_fusion.4, f32[28,512]{1,0:T(8,128)S(1)} %fusion.104, f32[28,512]{1,0:T(8,128)S(1)} %convolution_add_fusion.5), kind=kOutput, calls=%fused_computation | convolution fusion | flops 199965696 | bytes 2580592 | tf_op jit(solution)/shard_map/dot_general | solution.py:171
  9.7 4.6 %collective-permute-start = (f32[4,1,384]{2,1,0:T(1,128)S(1)}, f32[4,1,384]{2,1,0:T(1,128)S(1)}, u32[]{:S(2)}, u32[]{:S(2)}) collective-permute-start(f32[4,1,384]{2,1,0:T(1,128)S(1)} %slice.268), channel_id=1, source_target_pairs={{0,1},{1,2},{2,3},{3,4},{4,5},{5,6},{6,7},{7,8},{8,9},{9,10},{10,1... | collective-permute-start | bytes 18440 | tf_op jit(solution)/shard_map/ppermute | solution.py:22
  14.4 0.2 bitcast_convert_fusion
  15.1 0.5 select_add_fusion.4
  15.7 6.5 %collective-permute-done = f32[4,1,384]{2,1,0:T(1,128)S(1)} collective-permute-done((f32[4,1,384]{2,1,0:T(1,128)S(1)}, f32[4,1,384]{2,1,0:T(1,128)S(1)}, u32[]{:S(2)}, u32[]{:S(2)}) %collective-permute-start) | collective-permute-done | bytes 6176 | tf_op jit(solution)/shard_map/ppermute | solution.py:22
  22.2 4.1 %collective-permute-start.1 = (f32[1,6,384]{2,1,0:T(8,128)S(1)}, f32[1,6,384]{2,1,0:T(8,128)S(1)}, u32[]{:S(2)}, u32[]{:S(2)}) collective-permute-start(f32[1,6,384]{2,1,0:T(8,128)S(1)} %pad_maximum_fusion.14), channel_id=1, source_target_pairs={{0,64},{64,128},{128,192},{192,256},{256,320},{320,384},{384,448},... | collective-permute-start | bytes 27656 | tf_op jit(solution)/shard_map/ppermute | solution.py:22
  26.4 0.8 collective-permute-done.1
  27.3 1.3 collective-permute-start.2
  29.1 7.5 %collective-permute-done.2 = f32[1,6,384]{2,1,0:T(8,128)S(1)} collective-permute-done((f32[1,6,384]{2,1,0:T(8,128)S(1)}, f32[1,6,384]{2,1,0:T(8,128)S(1)}, u32[]{:S(2)}, u32[]{:S(2)}) %collective-permute-start.2) | collective-permute-done | bytes 9248 | tf_op jit(solution)/shard_map/ppermute | solution.py:22
  36.6 2.3 %collective-permute-start.3 = (f32[4,1,384]{2,1,0:T(1,128)S(1)}, f32[4,1,384]{2,1,0:T(1,128)S(1)}, u32[]{:S(2)}, u32[]{:S(2)}) collective-permute-start(f32[4,1,384]{2,1,0:T(1,128)S(1)} %pad_maximum_fusion.16), channel_id=1, source_target_pairs={{1,0},{2,1},{3,2},{4,3},{5,4},{6,5},{7,6},{8,7},{9,8},{10,9},{11,1... | collective-permute-start | bytes 18440 | tf_op jit(solution)/shard_map/ppermute | solution.py:22
  38.9 4.3 %collective-permute-done.3 = f32[4,1,384]{2,1,0:T(1,128)S(1)} collective-permute-done((f32[4,1,384]{2,1,0:T(1,128)S(1)}, f32[4,1,384]{2,1,0:T(1,128)S(1)}, u32[]{:S(2)}, u32[]{:S(2)}) %collective-permute-start.3) | collective-permute-done | bytes 6176 | tf_op jit(solution)/shard_map/ppermute | solution.py:22
  43.3 1.0 fusion.17
  44.4 0.3 fusion.65
  44.9 0.3 fusion.55
  45.1 0.3 fusion.30
  45.4 0.3 convolution_add_fusion.3
  45.7 0.3 convolution_add_fusion.2
  45.9 1.5 %fusion.16 = f32[28,385]{1,0:T(8,128)S(1)} fusion(f32[385,512]{1,0:T(8,128)S(1)} %get-tuple-element.41, f32[385,512]{1,0:T(8,128)S(1)} %get-tuple-element.40, f32[28,512]{1,0:T(8,128)S(1)} %fusion.30, f32[28,512]{1,0:T(8,128)S(1)} %convolution_add_fusion.2), kind=kOutput, calls=%fused_computation.32 | convolution fusion | flops 132887552 | bytes 1734768 | tf_op jit(solution)/shard_map/dot_general | solution.py:171
  47.5 1.9 %collective-permute-start.4 = (f32[4,1,384]{2,1,0:T(1,128)S(1)}, f32[4,1,384]{2,1,0:T(1,128)S(1)}, u32[]{:S(2)}, u32[]{:S(2)}) collective-permute-start(f32[4,1,384]{2,1,0:T(1,128)S(1)} %slice.284), channel_id=1, source_target_pairs={{0,1},{1,2},{2,3},{3,4},{4,5},{5,6},{6,7},{7,8},{8,9},{9,10},{10,1... | collective-permute-start | bytes 18440 | tf_op jit(solution)/shard_map/ppermute | solution.py:22
  49.5 1.1 collective-permute-done.4
  50.6 7.8 %collective-permute-start.5 = (f32[1,6,384]{2,1,0:T(8,128)S(1)}, f32[1,6,384]{2,1,0:T(8,128)S(1)}, u32[]{:S(2)}, u32[]{:S(2)}) collective-permute-start(f32[1,6,384]{2,1,0:T(8,128)S(1)} %pad_maximum_fusion.13), channel_id=1, source_target_pairs={{0,64},{64,128},{128,192},{192,256},{256,320},{320,384},{384,448},... | collective-permute-start | bytes 27656 | tf_op jit(solution)/shard_map/ppermute | solution.py:22
  58.5 0.8 collective-permute-done.5
  59.4 1.3 collective-permute-start.6
  60.8 8.2 %collective-permute-done.6 = f32[1,6,384]{2,1,0:T(8,128)S(1)} collective-permute-done((f32[1,6,384]{2,1,0:T(8,128)S(1)}, f32[1,6,384]{2,1,0:T(8,128)S(1)}, u32[]{:S(2)}, u32[]{:S(2)}) %collective-permute-start.6) | collective-permute-done | bytes 9248 | tf_op jit(solution)/shard_map/ppermute | solution.py:22
  69.0 3.8 %collective-permute-start.7 = (f32[4,1,384]{2,1,0:T(1,128)S(1)}, f32[4,1,384]{2,1,0:T(1,128)S(1)}, u32[]{:S(2)}, u32[]{:S(2)}) collective-permute-start(f32[4,1,384]{2,1,0:T(1,128)S(1)} %pad_maximum_fusion.15), channel_id=1, source_target_pairs={{1,0},{2,1},{3,2},{4,3},{5,4},{6,5},{7,6},{8,7},{9,8},{10,9},{11,1... | collective-permute-start | bytes 18440 | tf_op jit(solution)/shard_map/ppermute | solution.py:22
  72.9 2.9 %collective-permute-done.7 = f32[4,1,384]{2,1,0:T(1,128)S(1)} collective-permute-done((f32[4,1,384]{2,1,0:T(1,128)S(1)}, f32[4,1,384]{2,1,0:T(1,128)S(1)}, u32[]{:S(2)}, u32[]{:S(2)}) %collective-permute-start.7) | collective-permute-done | bytes 6176 | tf_op jit(solution)/shard_map/ppermute | solution.py:22
  75.9 1.0 fusion.15
  76.9 0.3 fusion.60
  77.4 0.3 fusion.56
  77.7 0.3 fusion.33
  78.0 0.3 convolution_add_fusion.1
  78.2 0.3 convolution_add_fusion
  78.5 1.5 %fusion.14 = f32[28,385]{1,0:T(8,128)S(1)} fusion(f32[385,512]{1,0:T(8,128)S(1)} %get-tuple-element.41, f32[385,512]{1,0:T(8,128)S(1)} %get-tuple-element.40, f32[28,512]{1,0:T(8,128)S(1)} %fusion.33, f32[28,512]{1,0:T(8,128)S(1)} %convolution_add_fusion), kind=kOutput, calls=%fused_computation.30 | convolution fusion | flops 132887552 | bytes 1734768 | tf_op jit(solution)/shard_map/dot_general | solution.py:171
  80.0 7.9 %collective-permute-start.8 = (f32[1,7,384]{2,1,0:T(8,128)S(1)}, f32[1,7,384]{2,1,0:T(8,128)S(1)}, u32[]{:S(2)}, u32[]{:S(2)}) collective-permute-start(f32[1,7,384]{2,1,0:T(8,128)S(1)} %slice.294), channel_id=1, source_target_pairs={{0,64},{64,128},{128,192},{192,256},{256,320},{320,384},{384,448},... | collective-permute-start | bytes 32264 | tf_op jit(solution)/shard_map/ppermute | solution.py:22
  88.3 7.2 %psum.35 = f32[6]{0:T(128)S(1)} all-reduce(f32[6]{0:T(128)S(1)} %pad_maximum_fusion.17), channel_id=1, replica_groups=mesh['bx_0'=4,'bx_1'=3,'by_0'=4,'by_1'=8,'by_2'=2] {'bx_0'}, use_global_device_ids=true, to_apply=%region_2.3 | all-reduce | flops 6 | bytes 48 | tf_op jit(solution)/shard_map/psum | solution.py:323
  95.5 4.2 %collective-permute-start.9 = (f32[3,1,384]{2,1,0:T(1,128)S(1)}, f32[3,1,384]{2,1,0:T(1,128)S(1)}, u32[]{:S(2)}, u32[]{:S(2)}) collective-permute-start(f32[3,1,384]{2,1,0:T(1,128)S(1)} %slice.246), channel_id=1, source_target_pairs={{0,1},{1,2},{2,3},{3,4},{4,5},{5,6},{6,7},{7,8},{8,9},{9,10},{10,1... | collective-permute-start | bytes 13832 | tf_op jit(solution)/shard_map/ppermute | solution.py:22
  99.8 11.6 %psum.36 = f32[6]{0:T(128)S(1)} all-reduce(f32[6]{0:T(128)S(1)} %psum.35), channel_id=1, replica_groups=mesh['bx_0'=4,'bx_1'=3,'by_0'=4,'by_1'=8,'by_2'=2] {'bx_1'}, use_global_device_ids=true, to_apply=%region_3.4 | all-reduce | flops 6 | bytes 48 | tf_op jit(solution)/shard_map/psum | solution.py:327
  111.5 10.1 %psum.37 = f32[6]{0:T(128)S(1)} all-reduce(f32[6]{0:T(128)S(1)} %psum.36), channel_id=1, replica_groups=mesh['bx_0'=4,'bx_1'=3,'by_0'=4,'by_1'=8,'by_2'=2] {'by_0'}, use_global_device_ids=true, to_apply=%region_4.5 | all-reduce | flops 6 | bytes 48 | tf_op jit(solution)/shard_map/psum | solution.py:330
  121.5 15.6 %psum.38 = f32[6]{0:T(128)S(1)} all-reduce(f32[6]{0:T(128)S(1)} %psum.37), channel_id=1, replica_groups=mesh['bx_0'=4,'bx_1'=3,'by_0'=4,'by_1'=8,'by_2'=2] {'by_1'}, use_global_device_ids=true, to_apply=%region_5.6 | all-reduce | flops 6 | bytes 48 | tf_op jit(solution)/shard_map/psum | solution.py:330
  137.1 6.8 %psum.39 = f32[6]{0:T(128)S(1)} all-reduce(f32[6]{0:T(128)S(1)} %psum.38), channel_id=1, replica_groups=mesh['bx_0'=4,'bx_1'=3,'by_0'=4,'by_1'=8,'by_2'=2] {'by_2'}, use_global_device_ids=true, to_apply=%region_6.7 | all-reduce | flops 6 | bytes 48 | tf_op jit(solution)/shard_map/psum | solution.py:330
  144.1 0.7 multiply_subtract_fusion
  (164 shorter events, 3.9 us)
Async XLA Ops:
  0.6 4.3 %copy-start.4 = (f32[32,28]{1,0:T(8,128)S(1)}, f32[32,28]{1,0:T(8,128)}, u32[]{:S(2)}) copy-start(f32[32,28]{1,0:T(8,128)} %constant.112.clone) | copy-start | bytes 10756
  0.6 4.5 %copy-start.30 = (f32[4]{0:T(128)S(1)}, f32[4]{0:T(128)}, u32[]{:S(2)}) copy-start(f32[4]{0:T(128)} %constant.128.clone) | copy-start | bytes 52
  0.7 4.5 %copy-start.31 = (f32[4]{0:T(128)S(1)}, f32[4]{0:T(128)}, u32[]{:S(2)}) copy-start(f32[4]{0:T(128)} %constant.129.clone) | copy-start | bytes 52
  0.7 4.6 %copy-start.28 = (f32[4]{0:T(128)S(1)}, f32[4]{0:T(128)}, u32[]{:S(2)}) copy-start(f32[4]{0:T(128)} %constant.126.clone) | copy-start | bytes 52
  0.7 4.5 %copy-start.29 = (f32[4]{0:T(128)S(1)}, f32[4]{0:T(128)}, u32[]{:S(2)}) copy-start(f32[4]{0:T(128)} %constant.127.clone) | copy-start | bytes 52
  0.7 4.6 %copy-start.26 = (f32[4]{0:T(128)S(1)}, f32[4]{0:T(128)}, u32[]{:S(2)}) copy-start(f32[4]{0:T(128)} %constant.122.clone) | copy-start | bytes 52
  0.7 4.6 %copy-start.27 = (f32[4]{0:T(128)S(1)}, f32[4]{0:T(128)}, u32[]{:S(2)}) copy-start(f32[4]{0:T(128)} %constant.123.clone) | copy-start | bytes 52
  0.7 4.7 %copy-start.24 = (f32[4]{0:T(128)S(1)}, f32[4]{0:T(128)}, u32[]{:S(2)}) copy-start(f32[4]{0:T(128)} %constant.120.clone) | copy-start | bytes 52
  0.7 4.6 %copy-start.25 = (f32[4]{0:T(128)S(1)}, f32[4]{0:T(128)}, u32[]{:S(2)}) copy-start(f32[4]{0:T(128)} %constant.121.clone) | copy-start | bytes 52
  0.7 4.7 %copy-start.22 = (f32[4]{0:T(128)S(1)}, f32[4]{0:T(128)}, u32[]{:S(2)}) copy-start(f32[4]{0:T(128)} %constant.118.clone) | copy-start | bytes 52
  0.8 4.7 %copy-start.23 = (f32[4]{0:T(128)S(1)}, f32[4]{0:T(128)}, u32[]{:S(2)}) copy-start(f32[4]{0:T(128)} %constant.119.clone) | copy-start | bytes 52
  0.8 4.8 %copy-start.20 = (f32[4]{0:T(128)S(1)}, f32[4]{0:T(128)}, u32[]{:S(2)}) copy-start(f32[4]{0:T(128)} %constant.116.clone) | copy-start | bytes 52
  0.8 4.7 %copy-start.21 = (f32[4]{0:T(128)S(1)}, f32[4]{0:T(128)}, u32[]{:S(2)}) copy-start(f32[4]{0:T(128)} %constant.117.clone) | copy-start | bytes 52
  0.8 4.8 %copy-start.7 = (f32[32,28]{1,0:T(8,128)S(1)}, f32[32,28]{1,0:T(8,128)}, u32[]{:S(2)}) copy-start(f32[32,28]{1,0:T(8,128)} %constant.148) | copy-start | bytes 10756
  0.8 5.0 %copy-start.11 = (f32[32,28]{1,0:T(8,128)S(1)}, f32[32,28]{1,0:T(8,128)}, u32[]{:S(2)}) copy-start(f32[32,28]{1,0:T(8,128)} %constant.113.clone) | copy-start | bytes 10756
  0.8 5.3 %copy-start.10 = (f32[32,28]{1,0:T(8,128)S(1)}, f32[32,28]{1,0:T(8,128)}, u32[]{:S(2)}) copy-start(f32[32,28]{1,0:T(8,128)} %constant.114.clone) | copy-start | bytes 10756
  0.8 5.5 %copy-start.9 = (f32[32,28]{1,0:T(8,128)S(1)}, f32[32,28]{1,0:T(8,128)}, u32[]{:S(2)}) copy-start(f32[32,28]{1,0:T(8,128)} %constant.147) | copy-start | bytes 10756
  0.8 5.7 %copy-start.8 = (f32[32,28]{1,0:T(8,128)S(1)}, f32[32,28]{1,0:T(8,128)}, u32[]{:S(2)}) copy-start(f32[32,28]{1,0:T(8,128)} %constant.149) | copy-start | bytes 10756
  7.8 6.6 %copy-start = (bf16[7,4,4,4,1,2,128]{6,5,4,3,2,1,0:T(2,128)(2,1)S(1)}, bf16[7,4,4,4,1,2,128]{6,5,4,3,2,1,0:T(2,128)(2,1)}, u32[]{:S(2)}) copy-start(bf16[7,4,4,4,1,2,128]{6,5,4,3,2,1,0:T(2,128)(2,1)} %param.44) | copy-start | bytes 688132
  9.6 5.1 %copy-start.18 = (f32[4]{0:T(128)S(1)}, f32[4]{0:T(128)}, u32[]{:S(2)}) copy-start(f32[4]{0:T(128)} %constant.139.clone) | copy-start | bytes 52
  9.6 5.1 %copy-start.19 = (f32[4]{0:T(128)S(1)}, f32[4]{0:T(128)}, u32[]{:S(2)}) copy-start(f32[4]{0:T(128)} %constant.140.clone) | copy-start | bytes 52
  9.6 5.2 %copy-start.16 = (f32[4]{0:T(128)S(1)}, f32[4]{0:T(128)}, u32[]{:S(2)}) copy-start(f32[4]{0:T(128)} %constant.137.clone) | copy-start | bytes 52
  9.7 5.2 %copy-start.17 = (f32[4]{0:T(128)S(1)}, f32[4]{0:T(128)}, u32[]{:S(2)}) copy-start(f32[4]{0:T(128)} %constant.138.clone) | copy-start | bytes 52
  9.7 5.2 %copy-start.14 = (f32[4]{0:T(128)S(1)}, f32[4]{0:T(128)}, u32[]{:S(2)}) copy-start(f32[4]{0:T(128)} %constant.135.clone) | copy-start | bytes 52
  9.7 5.2 %copy-start.15 = (f32[4]{0:T(128)S(1)}, f32[4]{0:T(128)}, u32[]{:S(2)}) copy-start(f32[4]{0:T(128)} %constant.136.clone) | copy-start | bytes 52
  9.7 5.3 %copy-start.12 = (f32[4]{0:T(128)S(1)}, f32[4]{0:T(128)}, u32[]{:S(2)}) copy-start(f32[4]{0:T(128)} %constant.133.clone) | copy-start | bytes 52
  9.7 5.3 %copy-start.13 = (f32[4]{0:T(128)S(1)}, f32[4]{0:T(128)}, u32[]{:S(2)}) copy-start(f32[4]{0:T(128)} %constant.134.clone) | copy-start | bytes 52
  9.7 12.5 %collective-permute-start = (f32[4,1,384]{2,1,0:T(1,128)S(1)}, f32[4,1,384]{2,1,0:T(1,128)S(1)}, u32[]{:S(2)}, u32[]{:S(2)}) collective-permute-start(f32[4,1,384]{2,1,0:T(1,128)S(1)} %slice.268), channel_id=1, source_target_pairs={{0,1},{1,2},{2,3},{3,4},{4,5},{5,6},{6,7},{7,8},{8,9},{9,10},{10,1... | collective-permute-start | bytes 18440 | tf_op jit(solution)/shard_map/ppermute | solution.py:22
  14.7 12.5 %copy-start.2 = (f32[3,6,384]{2,1,0:T(8,128)S(1)}, f32[3,6,384]{2,1,0:T(8,128)}, u32[]{:S(2)}) copy-start(f32[3,6,384]{2,1,0:T(8,128)} %param.43) | copy-start | bytes 82948
  22.2 5.0 %collective-permute-start.1 = (f32[1,6,384]{2,1,0:T(8,128)S(1)}, f32[1,6,384]{2,1,0:T(8,128)S(1)}, u32[]{:S(2)}, u32[]{:S(2)}) collective-permute-start(f32[1,6,384]{2,1,0:T(8,128)S(1)} %pad_maximum_fusion.14), channel_id=1, source_target_pairs={{0,64},{64,128},{128,192},{192,256},{256,320},{320,384},{384,448},... | collective-permute-start | bytes 27656 | tf_op jit(solution)/shard_map/ppermute | solution.py:22
  27.3 9.3 %collective-permute-start.2 = (f32[1,6,384]{2,1,0:T(8,128)S(1)}, f32[1,6,384]{2,1,0:T(8,128)S(1)}, u32[]{:S(2)}, u32[]{:S(2)}) collective-permute-start(f32[1,6,384]{2,1,0:T(8,128)S(1)} %slice.271), channel_id=1, source_target_pairs={{64,0},{128,64},{192,128},{256,192},{320,256},{384,320},{448,384},... | collective-permute-start | bytes 27656 | tf_op jit(solution)/shard_map/ppermute | solution.py:22
  36.6 6.6 %collective-permute-start.3 = (f32[4,1,384]{2,1,0:T(1,128)S(1)}, f32[4,1,384]{2,1,0:T(1,128)S(1)}, u32[]{:S(2)}, u32[]{:S(2)}) collective-permute-start(f32[4,1,384]{2,1,0:T(1,128)S(1)} %pad_maximum_fusion.16), channel_id=1, source_target_pairs={{1,0},{2,1},{3,2},{4,3},{5,4},{6,5},{7,6},{8,7},{9,8},{10,9},{11,1... | collective-permute-start | bytes 18440 | tf_op jit(solution)/shard_map/ppermute | solution.py:22
  43.2 1.1 copy-start.3
  43.3 1.4 copy-start.1
  43.3 2.1 %copy-start.6 = (f32[32,28]{1,0:T(8,128)S(1)}, f32[32,28]{1,0:T(8,128)}, u32[]{:S(2)}) copy-start(f32[32,28]{1,0:T(8,128)} %constant.152) | copy-start | bytes 10756
  44.3 1.3 copy-start.5
  47.5 3.1 %collective-permute-start.4 = (f32[4,1,384]{2,1,0:T(1,128)S(1)}, f32[4,1,384]{2,1,0:T(1,128)S(1)}, u32[]{:S(2)}, u32[]{:S(2)}) collective-permute-start(f32[4,1,384]{2,1,0:T(1,128)S(1)} %slice.284), channel_id=1, source_target_pairs={{0,1},{1,2},{2,3},{3,4},{4,5},{5,6},{6,7},{7,8},{8,9},{9,10},{10,1... | collective-permute-start | bytes 18440 | tf_op jit(solution)/shard_map/ppermute | solution.py:22
  50.6 8.7 %collective-permute-start.5 = (f32[1,6,384]{2,1,0:T(8,128)S(1)}, f32[1,6,384]{2,1,0:T(8,128)S(1)}, u32[]{:S(2)}, u32[]{:S(2)}) collective-permute-start(f32[1,6,384]{2,1,0:T(8,128)S(1)} %pad_maximum_fusion.13), channel_id=1, source_target_pairs={{0,64},{64,128},{128,192},{192,256},{256,320},{320,384},{384,448},... | collective-permute-start | bytes 27656 | tf_op jit(solution)/shard_map/ppermute | solution.py:22
  59.4 9.6 %collective-permute-start.6 = (f32[1,6,384]{2,1,0:T(8,128)S(1)}, f32[1,6,384]{2,1,0:T(8,128)S(1)}, u32[]{:S(2)}, u32[]{:S(2)}) collective-permute-start(f32[1,6,384]{2,1,0:T(8,128)S(1)} %slice.286), channel_id=1, source_target_pairs={{64,0},{128,64},{192,128},{256,192},{320,256},{384,320},{448,384},... | collective-permute-start | bytes 27656 | tf_op jit(solution)/shard_map/ppermute | solution.py:22
  69.0 6.9 %collective-permute-start.7 = (f32[4,1,384]{2,1,0:T(1,128)S(1)}, f32[4,1,384]{2,1,0:T(1,128)S(1)}, u32[]{:S(2)}, u32[]{:S(2)}) collective-permute-start(f32[4,1,384]{2,1,0:T(1,128)S(1)} %pad_maximum_fusion.15), channel_id=1, source_target_pairs={{1,0},{2,1},{3,2},{4,3},{5,4},{6,5},{7,6},{8,7},{9,8},{10,9},{11,1... | collective-permute-start | bytes 18440 | tf_op jit(solution)/shard_map/ppermute | solution.py:22
  80.0 15.5 %collective-permute-start.8 = (f32[1,7,384]{2,1,0:T(8,128)S(1)}, f32[1,7,384]{2,1,0:T(8,128)S(1)}, u32[]{:S(2)}, u32[]{:S(2)}) collective-permute-start(f32[1,7,384]{2,1,0:T(8,128)S(1)} %slice.294), channel_id=1, source_target_pairs={{0,64},{64,128},{128,192},{192,256},{256,320},{320,384},{384,448},... | collective-permute-start | bytes 32264 | tf_op jit(solution)/shard_map/ppermute | solution.py:22
  95.5 15.8 %collective-permute-start.9 = (f32[3,1,384]{2,1,0:T(1,128)S(1)}, f32[3,1,384]{2,1,0:T(1,128)S(1)}, u32[]{:S(2)}, u32[]{:S(2)}) collective-permute-start(f32[3,1,384]{2,1,0:T(1,128)S(1)} %slice.246), channel_id=1, source_target_pairs={{0,1},{1,2},{2,3},{3,4},{4,5},{5,6},{6,7},{7,8},{8,9},{9,10},{10,1... | collective-permute-start | bytes 13832 | tf_op jit(solution)/shard_map/ppermute | solution.py:22

commit v15 on v14

--- a/solution.py
+++ b/solution.py
@@ -320,13 +320,14 @@
     )
     arrived = lower_x(raw_second[rows_x:])
     partial = jnp.concatenate([raw_second[0:1] + arrived, raw_second[1:rows_x]], 0)
-    summed = lax.psum(terms, BX_BY[0])
+    chain = ("bx_1", "by_1", "bx_0", "by_0", "by_2")
+    summed = lax.psum(terms, chain[0])
     summed, partial = lax.optimization_barrier((summed, partial))
     arrived = lower_y(partial[:, rows_y:])
     second = jnp.concatenate([partial[:, 0:1] + arrived, partial[:, 1:rows_y]], 1) * interior
-    summed = lax.psum(summed, BX_BY[1])
+    summed = lax.psum(summed, chain[1])
     summed, second = lax.optimization_barrier((summed, second))
-    for axis in BX_BY[2:]:
+    for axis in chain[2:]:
         summed = lax.psum(summed, axis)
     parts = lax.optimization_barrier(jnp.broadcast_to(summed[:, None, None, None], (6, 1, 1, rows_z)))
     rz_now, curvature, cross_r, cross_q, cross_z, curvature_w = [parts[k] for k in range(6)]

time: 145 us -> 146 us (level)
  blocking collectives: 51.3 us -> 53 us
    psum x2, blocking collectives: 18.8 us -> 28.5 us  [the longest x1 17 us: shards(): summed = lax.psum(summed, chain[1])]
    psum x3, blocking collectives: 32.5 us -> 24.5 us  [shards(): summed = lax.psum(summed, axis)]
where the time goes in v15:
time: 146 us
  blocking collectives  53 us (36%)
  starting transfers between devices  38.5 us (26%)
  waiting for transfers between devices  32 us (22%)
  matrix products  12.1 us (8%)
  local copies, waits for them, and re-layouts  4.07 us (3%)
  other arithmetic  3.59 us (2%)
  between operations  2.46 us (2%)
    ppermute x10, starting transfers between devices, shifted(): lax.ppermute(value, axis, [(source, source + steps) for source in range(i...  38.5 us
    ppermute x10, waiting for transfers between devices, shifted(): lax.ppermute(value, axis, [(source, source + steps) for source in range(i...  32 us
    psum x3, blocking collectives, shards(): summed = lax.psum(summed, axis)  24.5 us
    psum x1, blocking collectives, shards(): summed = lax.psum(summed, chain[1])  17 us
    dot_general x24, matrix products, mat(): return jnp.matmul(left, right, precision=lax.Precision.HIGHEST)  12.1 us
    psum x1, blocking collectives, shards(): summed = lax.psum(terms, chain[0])  11.5 us
  transfers between devices with their start and end apart: 10, of which 8 were waited for; matrix products, arithmetic and copies ran while one was open for 2% of the time, Pallas kernels for 0%

profile of v15, /device:TPU:1, one launch (start us, length us, event | category | flops | bytes accessed | tf_op | source)
XLA Modules:
  0.0 145.7 jit_solution(13733999352580290893)
XLA Ops:
  0.9 1.1 fusion.139
  2.0 1.2 slice.207
  3.9 0.9 fusion.113
  5.6 0.2 fusion.101
  5.8 0.2 convolution_add_fusion.7
  6.1 0.2 convolution_add_fusion.6
  6.8 1.0 select_add_fusion.2
  7.8 1.8 %fusion = f32[28,385]{1,0:T(8,128)S(1)} fusion(f32[512,385]{1,0:T(8,128)S(1)} %get-tuple-element.44, f32[512,385]{1,0:T(8,128)S(1)} %get-tuple-element.43, f32[512,385]{1,0:T(8,128)S(1)} %get-tuple-element.42, f32[28,512]{1,0:T(8,128)S(1)} %convolution_add_fusion.4, f32[28,512]{1,0:T(8,128)S(1)} %fusion.104, f32[28,512]{1,0:T(8,128)S(1)} %convolution_add_fusion.5), kind=kOutput, calls=%fused_computation | convolution fusion | flops 199965696 | bytes 2580592 | tf_op jit(solution)/shard_map/dot_general | solution.py:171
  9.7 4.6 %collective-permute-start = (f32[4,1,384]{2,1,0:T(1,128)S(1)}, f32[4,1,384]{2,1,0:T(1,128)S(1)}, u32[]{:S(2)}, u32[]{:S(2)}) collective-permute-start(f32[4,1,384]{2,1,0:T(1,128)S(1)} %slice.268), channel_id=1, source_target_pairs={{0,1},{1,2},{2,3},{3,4},{4,5},{5,6},{6,7},{7,8},{8,9},{9,10},{10,1... | collective-permute-start | bytes 18440 | tf_op jit(solution)/shard_map/ppermute | solution.py:22
  14.4 0.2 bitcast_convert_fusion
  15.1 0.5 select_add_fusion.4
  15.7 6.5 %collective-permute-done = f32[4,1,384]{2,1,0:T(1,128)S(1)} collective-permute-done((f32[4,1,384]{2,1,0:T(1,128)S(1)}, f32[4,1,384]{2,1,0:T(1,128)S(1)}, u32[]{:S(2)}, u32[]{:S(2)}) %collective-permute-start) | collective-permute-done | bytes 6176 | tf_op jit(solution)/shard_map/ppermute | solution.py:22
  22.2 4.1 %collective-permute-start.1 = (f32[1,6,384]{2,1,0:T(8,128)S(1)}, f32[1,6,384]{2,1,0:T(8,128)S(1)}, u32[]{:S(2)}, u32[]{:S(2)}) collective-permute-start(f32[1,6,384]{2,1,0:T(8,128)S(1)} %pad_maximum_fusion.14), channel_id=1, source_target_pairs={{0,64},{64,128},{128,192},{192,256},{256,320},{320,384},{384,448},... | collective-permute-start | bytes 27656 | tf_op jit(solution)/shard_map/ppermute | solution.py:22
  26.4 0.8 collective-permute-done.1
  27.3 1.3 collective-permute-start.2
  29.1 7.5 %collective-permute-done.2 = f32[1,6,384]{2,1,0:T(8,128)S(1)} collective-permute-done((f32[1,6,384]{2,1,0:T(8,128)S(1)}, f32[1,6,384]{2,1,0:T(8,128)S(1)}, u32[]{:S(2)}, u32[]{:S(2)}) %collective-permute-start.2) | collective-permute-done | bytes 9248 | tf_op jit(solution)/shard_map/ppermute | solution.py:22
  36.6 2.3 %collective-permute-start.3 = (f32[4,1,384]{2,1,0:T(1,128)S(1)}, f32[4,1,384]{2,1,0:T(1,128)S(1)}, u32[]{:S(2)}, u32[]{:S(2)}) collective-permute-start(f32[4,1,384]{2,1,0:T(1,128)S(1)} %pad_maximum_fusion.16), channel_id=1, source_target_pairs={{1,0},{2,1},{3,2},{4,3},{5,4},{6,5},{7,6},{8,7},{9,8},{10,9},{11,1... | collective-permute-start | bytes 18440 | tf_op jit(solution)/shard_map/ppermute | solution.py:22
  38.9 4.3 %collective-permute-done.3 = f32[4,1,384]{2,1,0:T(1,128)S(1)} collective-permute-done((f32[4,1,384]{2,1,0:T(1,128)S(1)}, f32[4,1,384]{2,1,0:T(1,128)S(1)}, u32[]{:S(2)}, u32[]{:S(2)}) %collective-permute-start.3) | collective-permute-done | bytes 6176 | tf_op jit(solution)/shard_map/ppermute | solution.py:22
  43.3 1.0 fusion.17
  44.4 0.3 fusion.65
  44.9 0.3 fusion.55
  45.1 0.3 fusion.30
  45.4 0.3 convolution_add_fusion.3
  45.7 0.3 convolution_add_fusion.2
  45.9 1.5 %fusion.16 = f32[28,385]{1,0:T(8,128)S(1)} fusion(f32[385,512]{1,0:T(8,128)S(1)} %get-tuple-element.41, f32[385,512]{1,0:T(8,128)S(1)} %get-tuple-element.40, f32[28,512]{1,0:T(8,128)S(1)} %fusion.30, f32[28,512]{1,0:T(8,128)S(1)} %convolution_add_fusion.2), kind=kOutput, calls=%fused_computation.32 | convolution fusion | flops 132887552 | bytes 1734768 | tf_op jit(solution)/shard_map/dot_general | solution.py:171
  47.5 1.9 %collective-permute-start.4 = (f32[4,1,384]{2,1,0:T(1,128)S(1)}, f32[4,1,384]{2,1,0:T(1,128)S(1)}, u32[]{:S(2)}, u32[]{:S(2)}) collective-permute-start(f32[4,1,384]{2,1,0:T(1,128)S(1)} %slice.284), channel_id=1, source_target_pairs={{0,1},{1,2},{2,3},{3,4},{4,5},{5,6},{6,7},{7,8},{8,9},{9,10},{10,1... | collective-permute-start | bytes 18440 | tf_op jit(solution)/shard_map/ppermute | solution.py:22
  49.5 1.1 collective-permute-done.4
  50.6 7.8 %collective-permute-start.5 = (f32[1,6,384]{2,1,0:T(8,128)S(1)}, f32[1,6,384]{2,1,0:T(8,128)S(1)}, u32[]{:S(2)}, u32[]{:S(2)}) collective-permute-start(f32[1,6,384]{2,1,0:T(8,128)S(1)} %pad_maximum_fusion.13), channel_id=1, source_target_pairs={{0,64},{64,128},{128,192},{192,256},{256,320},{320,384},{384,448},... | collective-permute-start | bytes 27656 | tf_op jit(solution)/shard_map/ppermute | solution.py:22
  58.5 0.8 collective-permute-done.5
  59.4 1.3 collective-permute-start.6
  60.8 8.2 %collective-permute-done.6 = f32[1,6,384]{2,1,0:T(8,128)S(1)} collective-permute-done((f32[1,6,384]{2,1,0:T(8,128)S(1)}, f32[1,6,384]{2,1,0:T(8,128)S(1)}, u32[]{:S(2)}, u32[]{:S(2)}) %collective-permute-start.6) | collective-permute-done | bytes 9248 | tf_op jit(solution)/shard_map/ppermute | solution.py:22
  69.0 3.8 %collective-permute-start.7 = (f32[4,1,384]{2,1,0:T(1,128)S(1)}, f32[4,1,384]{2,1,0:T(1,128)S(1)}, u32[]{:S(2)}, u32[]{:S(2)}) collective-permute-start(f32[4,1,384]{2,1,0:T(1,128)S(1)} %pad_maximum_fusion.15), channel_id=1, source_target_pairs={{1,0},{2,1},{3,2},{4,3},{5,4},{6,5},{7,6},{8,7},{9,8},{10,9},{11,1... | collective-permute-start | bytes 18440 | tf_op jit(solution)/shard_map/ppermute | solution.py:22
  72.9 2.9 %collective-permute-done.7 = f32[4,1,384]{2,1,0:T(1,128)S(1)} collective-permute-done((f32[4,1,384]{2,1,0:T(1,128)S(1)}, f32[4,1,384]{2,1,0:T(1,128)S(1)}, u32[]{:S(2)}, u32[]{:S(2)}) %collective-permute-start.7) | collective-permute-done | bytes 6176 | tf_op jit(solution)/shard_map/ppermute | solution.py:22
  75.9 1.0 fusion.15
  76.9 0.3 fusion.60
  77.4 0.3 fusion.56
  77.7 0.3 fusion.33
  78.0 0.3 convolution_add_fusion.1
  78.2 0.3 convolution_add_fusion
  78.5 1.5 %fusion.14 = f32[28,385]{1,0:T(8,128)S(1)} fusion(f32[385,512]{1,0:T(8,128)S(1)} %get-tuple-element.41, f32[385,512]{1,0:T(8,128)S(1)} %get-tuple-element.40, f32[28,512]{1,0:T(8,128)S(1)} %fusion.33, f32[28,512]{1,0:T(8,128)S(1)} %convolution_add_fusion), kind=kOutput, calls=%fused_computation.30 | convolution fusion | flops 132887552 | bytes 1734768 | tf_op jit(solution)/shard_map/dot_general | solution.py:171
  80.0 7.9 %collective-permute-start.8 = (f32[1,7,384]{2,1,0:T(8,128)S(1)}, f32[1,7,384]{2,1,0:T(8,128)S(1)}, u32[]{:S(2)}, u32[]{:S(2)}) collective-permute-start(f32[1,7,384]{2,1,0:T(8,128)S(1)} %slice.294), channel_id=1, source_target_pairs={{0,64},{64,128},{128,192},{192,256},{256,320},{320,384},{384,448},... | collective-permute-start | bytes 32264 | tf_op jit(solution)/shard_map/ppermute | solution.py:22
  88.3 11.5 %psum.35 = f32[6]{0:T(128)S(1)} all-reduce(f32[6]{0:T(128)S(1)} %pad_maximum_fusion.17), channel_id=1, replica_groups=mesh['bx_0'=4,'bx_1'=3,'by_0'=4,'by_1'=8,'by_2'=2] {'bx_1'}, use_global_device_ids=true, to_apply=%region_2.3 | all-reduce | flops 6 | bytes 48 | tf_op jit(solution)/shard_map/psum | solution.py:324
  99.8 3.4 %collective-permute-start.9 = (f32[3,1,384]{2,1,0:T(1,128)S(1)}, f32[3,1,384]{2,1,0:T(1,128)S(1)}, u32[]{:S(2)}, u32[]{:S(2)}) collective-permute-start(f32[3,1,384]{2,1,0:T(1,128)S(1)} %slice.246), channel_id=1, source_target_pairs={{0,1},{1,2},{2,3},{3,4},{4,5},{5,6},{6,7},{7,8},{8,9},{9,10},{10,1... | collective-permute-start | bytes 13832 | tf_op jit(solution)/shard_map/ppermute | solution.py:22
  103.2 17.0 %psum.36 = f32[6]{0:T(128)S(1)} all-reduce(f32[6]{0:T(128)S(1)} %psum.35), channel_id=1, replica_groups=mesh['bx_0'=4,'bx_1'=3,'by_0'=4,'by_1'=8,'by_2'=2] {'by_1'}, use_global_device_ids=true, to_apply=%region_3.4 | all-reduce | flops 6 | bytes 48 | tf_op jit(solution)/shard_map/psum | solution.py:328
  120.3 7.2 %psum.37 = f32[6]{0:T(128)S(1)} all-reduce(f32[6]{0:T(128)S(1)} %psum.36), channel_id=1, replica_groups=mesh['bx_0'=4,'bx_1'=3,'by_0'=4,'by_1'=8,'by_2'=2] {'bx_0'}, use_global_device_ids=true, to_apply=%region_4.5 | all-reduce | flops 6 | bytes 48 | tf_op jit(solution)/shard_map/psum | solution.py:331
  127.5 8.3 %psum.38 = f32[6]{0:T(128)S(1)} all-reduce(f32[6]{0:T(128)S(1)} %psum.37), channel_id=1, replica_groups=mesh['bx_0'=4,'bx_1'=3,'by_0'=4,'by_1'=8,'by_2'=2] {'by_0'}, use_global_device_ids=true, to_apply=%region_5.6 | all-reduce | flops 6 | bytes 48 | tf_op jit(solution)/shard_map/psum | solution.py:331
  135.9 9.0 %psum.39 = f32[6]{0:T(128)S(1)} all-reduce(f32[6]{0:T(128)S(1)} %psum.38), channel_id=1, replica_groups=mesh['bx_0'=4,'bx_1'=3,'by_0'=4,'by_1'=8,'by_2'=2] {'by_2'}, use_global_device_ids=true, to_apply=%region_6.7 | all-reduce | flops 6 | bytes 48 | tf_op jit(solution)/shard_map/psum | solution.py:331
  145.0 0.7 multiply_subtract_fusion
  (164 shorter events, 3.9 us)
Async XLA Ops:
  0.6 4.3 %copy-start.4 = (f32[32,28]{1,0:T(8,128)S(1)}, f32[32,28]{1,0:T(8,128)}, u32[]{:S(2)}) copy-start(f32[32,28]{1,0:T(8,128)} %constant.112.clone) | copy-start | bytes 10756
  0.6 4.5 %copy-start.30 = (f32[4]{0:T(128)S(1)}, f32[4]{0:T(128)}, u32[]{:S(2)}) copy-start(f32[4]{0:T(128)} %constant.128.clone) | copy-start | bytes 52
  0.7 4.5 %copy-start.31 = (f32[4]{0:T(128)S(1)}, f32[4]{0:T(128)}, u32[]{:S(2)}) copy-start(f32[4]{0:T(128)} %constant.129.clone) | copy-start | bytes 52
  0.7 4.6 %copy-start.28 = (f32[4]{0:T(128)S(1)}, f32[4]{0:T(128)}, u32[]{:S(2)}) copy-start(f32[4]{0:T(128)} %constant.126.clone) | copy-start | bytes 52
  0.7 4.5 %copy-start.29 = (f32[4]{0:T(128)S(1)}, f32[4]{0:T(128)}, u32[]{:S(2)}) copy-start(f32[4]{0:T(128)} %constant.127.clone) | copy-start | bytes 52
  0.7 4.6 %copy-start.26 = (f32[4]{0:T(128)S(1)}, f32[4]{0:T(128)}, u32[]{:S(2)}) copy-start(f32[4]{0:T(128)} %constant.122.clone) | copy-start | bytes 52
  0.7 4.6 %copy-start.27 = (f32[4]{0:T(128)S(1)}, f32[4]{0:T(128)}, u32[]{:S(2)}) copy-start(f32[4]{0:T(128)} %constant.123.clone) | copy-start | bytes 52
  0.7 4.7 %copy-start.24 = (f32[4]{0:T(128)S(1)}, f32[4]{0:T(128)}, u32[]{:S(2)}) copy-start(f32[4]{0:T(128)} %constant.120.clone) | copy-start | bytes 52
  0.7 4.6 %copy-start.25 = (f32[4]{0:T(128)S(1)}, f32[4]{0:T(128)}, u32[]{:S(2)}) copy-start(f32[4]{0:T(128)} %constant.121.clone) | copy-start | bytes 52
  0.7 4.7 %copy-start.22 = (f32[4]{0:T(128)S(1)}, f32[4]{0:T(128)}, u32[]{:S(2)}) copy-start(f32[4]{0:T(128)} %constant.118.clone) | copy-start | bytes 52
  0.8 4.7 %copy-start.23 = (f32[4]{0:T(128)S(1)}, f32[4]{0:T(128)}, u32[]{:S(2)}) copy-start(f32[4]{0:T(128)} %constant.119.clone) | copy-start | bytes 52
  0.8 4.8 %copy-start.20 = (f32[4]{0:T(128)S(1)}, f32[4]{0:T(128)}, u32[]{:S(2)}) copy-start(f32[4]{0:T(128)} %constant.116.clone) | copy-start | bytes 52
  0.8 4.7 %copy-start.21 = (f32[4]{0:T(128)S(1)}, f32[4]{0:T(128)}, u32[]{:S(2)}) copy-start(f32[4]{0:T(128)} %constant.117.clone) | copy-start | bytes 52
  0.8 4.8 %copy-start.7 = (f32[32,28]{1,0:T(8,128)S(1)}, f32[32,28]{1,0:T(8,128)}, u32[]{:S(2)}) copy-start(f32[32,28]{1,0:T(8,128)} %constant.148) | copy-start | bytes 10756
  0.8 5.0 %copy-start.11 = (f32[32,28]{1,0:T(8,128)S(1)}, f32[32,28]{1,0:T(8,128)}, u32[]{:S(2)}) copy-start(f32[32,28]{1,0:T(8,128)} %constant.113.clone) | copy-start | bytes 10756
  0.8 5.3 %copy-start.10 = (f32[32,28]{1,0:T(8,128)S(1)}, f32[32,28]{1,0:T(8,128)}, u32[]{:S(2)}) copy-start(f32[32,28]{1,0:T(8,128)} %constant.114.clone) | copy-start | bytes 10756
  0.8 5.5 %copy-start.9 = (f32[32,28]{1,0:T(8,128)S(1)}, f32[32,28]{1,0:T(8,128)}, u32[]{:S(2)}) copy-start(f32[32,28]{1,0:T(8,128)} %constant.147) | copy-start | bytes 10756
  0.8 5.7 %copy-start.8 = (f32[32,28]{1,0:T(8,128)S(1)}, f32[32,28]{1,0:T(8,128)}, u32[]{:S(2)}) copy-start(f32[32,28]{1,0:T(8,128)} %constant.149) | copy-start | bytes 10756
  7.8 6.6 %copy-start = (bf16[7,4,4,4,1,2,128]{6,5,4,3,2,1,0:T(2,128)(2,1)S(1)}, bf16[7,4,4,4,1,2,128]{6,5,4,3,2,1,0:T(2,128)(2,1)}, u32[]{:S(2)}) copy-start(bf16[7,4,4,4,1,2,128]{6,5,4,3,2,1,0:T(2,128)(2,1)} %param.44) | copy-start | bytes 688132
  9.6 5.1 %copy-start.18 = (f32[4]{0:T(128)S(1)}, f32[4]{0:T(128)}, u32[]{:S(2)}) copy-start(f32[4]{0:T(128)} %constant.139.clone) | copy-start | bytes 52
  9.6 5.1 %copy-start.19 = (f32[4]{0:T(128)S(1)}, f32[4]{0:T(128)}, u32[]{:S(2)}) copy-start(f32[4]{0:T(128)} %constant.140.clone) | copy-start | bytes 52
  9.6 5.2 %copy-start.16 = (f32[4]{0:T(128)S(1)}, f32[4]{0:T(128)}, u32[]{:S(2)}) copy-start(f32[4]{0:T(128)} %constant.137.clone) | copy-start | bytes 52
  9.7 5.2 %copy-start.17 = (f32[4]{0:T(128)S(1)}, f32[4]{0:T(128)}, u32[]{:S(2)}) copy-start(f32[4]{0:T(128)} %constant.138.clone) | copy-start | bytes 52
  9.7 5.2 %copy-start.14 = (f32[4]{0:T(128)S(1)}, f32[4]{0:T(128)}, u32[]{:S(2)}) copy-start(f32[4]{0:T(128)} %constant.135.clone) | copy-start | bytes 52
  9.7 5.2 %copy-start.15 = (f32[4]{0:T(128)S(1)}, f32[4]{0:T(128)}, u32[]{:S(2)}) copy-start(f32[4]{0:T(128)} %constant.136.clone) | copy-start | bytes 52
  9.7 5.3 %copy-start.12 = (f32[4]{0:T(128)S(1)}, f32[4]{0:T(128)}, u32[]{:S(2)}) copy-start(f32[4]{0:T(128)} %constant.133.clone) | copy-start | bytes 52
  9.7 5.3 %copy-start.13 = (f32[4]{0:T(128)S(1)}, f32[4]{0:T(128)}, u32[]{:S(2)}) copy-start(f32[4]{0:T(128)} %constant.134.clone) | copy-start | bytes 52
  9.7 12.5 %collective-permute-start = (f32[4,1,384]{2,1,0:T(1,128)S(1)}, f32[4,1,384]{2,1,0:T(1,128)S(1)}, u32[]{:S(2)}, u32[]{:S(2)}) collective-permute-start(f32[4,1,384]{2,1,0:T(1,128)S(1)} %slice.268), channel_id=1, source_target_pairs={{0,1},{1,2},{2,3},{3,4},{4,5},{5,6},{6,7},{7,8},{8,9},{9,10},{10,1... | collective-permute-start | bytes 18440 | tf_op jit(solution)/shard_map/ppermute | solution.py:22
  14.7 12.5 %copy-start.2 = (f32[3,6,384]{2,1,0:T(8,128)S(1)}, f32[3,6,384]{2,1,0:T(8,128)}, u32[]{:S(2)}) copy-start(f32[3,6,384]{2,1,0:T(8,128)} %param.43) | copy-start | bytes 82948
  22.2 5.0 %collective-permute-start.1 = (f32[1,6,384]{2,1,0:T(8,128)S(1)}, f32[1,6,384]{2,1,0:T(8,128)S(1)}, u32[]{:S(2)}, u32[]{:S(2)}) collective-permute-start(f32[1,6,384]{2,1,0:T(8,128)S(1)} %pad_maximum_fusion.14), channel_id=1, source_target_pairs={{0,64},{64,128},{128,192},{192,256},{256,320},{320,384},{384,448},... | collective-permute-start | bytes 27656 | tf_op jit(solution)/shard_map/ppermute | solution.py:22
  27.3 9.3 %collective-permute-start.2 = (f32[1,6,384]{2,1,0:T(8,128)S(1)}, f32[1,6,384]{2,1,0:T(8,128)S(1)}, u32[]{:S(2)}, u32[]{:S(2)}) collective-permute-start(f32[1,6,384]{2,1,0:T(8,128)S(1)} %slice.271), channel_id=1, source_target_pairs={{64,0},{128,64},{192,128},{256,192},{320,256},{384,320},{448,384},... | collective-permute-start | bytes 27656 | tf_op jit(solution)/shard_map/ppermute | solution.py:22
  36.6 6.6 %collective-permute-start.3 = (f32[4,1,384]{2,1,0:T(1,128)S(1)}, f32[4,1,384]{2,1,0:T(1,128)S(1)}, u32[]{:S(2)}, u32[]{:S(2)}) collective-permute-start(f32[4,1,384]{2,1,0:T(1,128)S(1)} %pad_maximum_fusion.16), channel_id=1, source_target_pairs={{1,0},{2,1},{3,2},{4,3},{5,4},{6,5},{7,6},{8,7},{9,8},{10,9},{11,1... | collective-permute-start | bytes 18440 | tf_op jit(solution)/shard_map/ppermute | solution.py:22
  43.2 1.1 copy-start.3
  43.3 1.4 copy-start.1
  43.3 2.1 %copy-start.6 = (f32[32,28]{1,0:T(8,128)S(1)}, f32[32,28]{1,0:T(8,128)}, u32[]{:S(2)}) copy-start(f32[32,28]{1,0:T(8,128)} %constant.152) | copy-start | bytes 10756
  44.3 1.3 copy-start.5
  47.5 3.1 %collective-permute-start.4 = (f32[4,1,384]{2,1,0:T(1,128)S(1)}, f32[4,1,384]{2,1,0:T(1,128)S(1)}, u32[]{:S(2)}, u32[]{:S(2)}) collective-permute-start(f32[4,1,384]{2,1,0:T(1,128)S(1)} %slice.284), channel_id=1, source_target_pairs={{0,1},{1,2},{2,3},{3,4},{4,5},{5,6},{6,7},{7,8},{8,9},{9,10},{10,1... | collective-permute-start | bytes 18440 | tf_op jit(solution)/shard_map/ppermute | solution.py:22
  50.6 8.7 %collective-permute-start.5 = (f32[1,6,384]{2,1,0:T(8,128)S(1)}, f32[1,6,384]{2,1,0:T(8,128)S(1)}, u32[]{:S(2)}, u32[]{:S(2)}) collective-permute-start(f32[1,6,384]{2,1,0:T(8,128)S(1)} %pad_maximum_fusion.13), channel_id=1, source_target_pairs={{0,64},{64,128},{128,192},{192,256},{256,320},{320,384},{384,448},... | collective-permute-start | bytes 27656 | tf_op jit(solution)/shard_map/ppermute | solution.py:22
  59.4 9.6 %collective-permute-start.6 = (f32[1,6,384]{2,1,0:T(8,128)S(1)}, f32[1,6,384]{2,1,0:T(8,128)S(1)}, u32[]{:S(2)}, u32[]{:S(2)}) collective-permute-start(f32[1,6,384]{2,1,0:T(8,128)S(1)} %slice.286), channel_id=1, source_target_pairs={{64,0},{128,64},{192,128},{256,192},{320,256},{384,320},{448,384},... | collective-permute-start | bytes 27656 | tf_op jit(solution)/shard_map/ppermute | solution.py:22
  69.0 6.9 %collective-permute-start.7 = (f32[4,1,384]{2,1,0:T(1,128)S(1)}, f32[4,1,384]{2,1,0:T(1,128)S(1)}, u32[]{:S(2)}, u32[]{:S(2)}) collective-permute-start(f32[4,1,384]{2,1,0:T(1,128)S(1)} %pad_maximum_fusion.15), channel_id=1, source_target_pairs={{1,0},{2,1},{3,2},{4,3},{5,4},{6,5},{7,6},{8,7},{9,8},{10,9},{11,1... | collective-permute-start | bytes 18440 | tf_op jit(solution)/shard_map/ppermute | solution.py:22
  80.0 19.8 %collective-permute-start.8 = (f32[1,7,384]{2,1,0:T(8,128)S(1)}, f32[1,7,384]{2,1,0:T(8,128)S(1)}, u32[]{:S(2)}, u32[]{:S(2)}) collective-permute-start(f32[1,7,384]{2,1,0:T(8,128)S(1)} %slice.294), channel_id=1, source_target_pairs={{0,64},{64,128},{128,192},{192,256},{256,320},{320,384},{384,448},... | collective-permute-start | bytes 32264 | tf_op jit(solution)/shard_map/ppermute | solution.py:22
  99.8 20.4 %collective-permute-start.9 = (f32[3,1,384]{2,1,0:T(1,128)S(1)}, f32[3,1,384]{2,1,0:T(1,128)S(1)}, u32[]{:S(2)}, u32[]{:S(2)}) collective-permute-start(f32[3,1,384]{2,1,0:T(1,128)S(1)} %slice.246), channel_id=1, source_target_pairs={{0,1},{1,2},{2,3},{3,4},{4,5},{5,6},{6,7},{7,8},{8,9},{9,10},{10,1... | collective-permute-start | bytes 13832 | tf_op jit(solution)/shard_map/ppermute | solution.py:22
